TPU v7x, 32 devices: a whole 2x2x4 slice. The times are simulated.
32 devices in a mesh: groups: 2 (over x), blk: 16 (over z, y, core).
Axes of the slice: x: 2, y: 2, z: 4, core: 2. Of those that a mesh axis runs over, the one named last changes fastest.
Arguments:
- paths: bfloat16 [4096, 512], P(('groups', 'blk')), parts along dimension 0, may hold values from -6 to 6
- deltas: bfloat16 [4096, 512], P(('groups', 'blk')), parts along dimension 0, may hold values from -6 to 6
- payoffs: bfloat16 [4096], P(('groups', 'blk')), parts along dimension 0, may hold values from -6 to 6
- counts: int32 [32, 16], P('groups'), parts along dimension 0, may hold values from 0 to 8, as said below
- w_first: bfloat16 [1024, 1024], P(('groups', 'blk')), parts along dimension 0, may hold values from -0.25 to 0.25
- w_second: bfloat16 [2048, 1024], P(('groups', 'blk')), parts along dimension 0, may hold values from -0.1875 to 0.1875
- w_out: bfloat16 [2048], P('groups'), parts along dimension 0, may hold values from -0.1875 to 0.1875
- mom_first: float32 [1024, 1024], P(('groups', 'blk')), parts along dimension 0, may hold values from -6 to 6
- mom_second: float32 [2048, 1024], P(('groups', 'blk')), parts along dimension 0, may hold values from -6 to 6
- mom_out: float32 [2048], P('groups'), parts along dimension 0, may hold values from -6 to 6
Outputs:
- new_first: float32 [1024, 1024], P(('groups', 'blk')), parts along dimension 0
- new_second: float32 [2048, 1024], P(('groups', 'blk')), parts along dimension 0
- new_out: float32 [2048], P('groups'), parts along dimension 0
There are 2 independent parts, one for each index of `groups`. A program takes and returns all parts, laid end to end along the dimension named above; each array names one. Nothing has to cross between parts.
Inputs may be any that keep to these rules, and one draw needn't show every extreme that they name: Source s hands its valid paths, slot 0 onward, to the trainers in order: counts[s, d] of them to trainer d. Every trainer receives 64 paths or fewer in all, and one receives exactly 64; one source hands 8 to every trainer.
All inputs are finite; a program needn't handle non-finite values.
Results may differ from a plain program's by a relative error of at most 0.00035.
The roundings to bfloat16 on the way count: a program that leaves them out, or rounds other values in their place, can miss the bound.
Values may be sent and summed in bfloat16 or wider, within the bound.
No kernel may reach another device: no remote copies, remote signals or barrier semaphores. Data moves between devices by JAX's collectives and lax.ppermute only.
A program may use at most 64 MiB of HBM per device.

v0:
```python
import jax
import jax.numpy as jnp
from jax import lax
from jax.sharding import PartitionSpec as P


def rows_product(left, right):
    return lax.dot_general(
        left, right, (((0,), (0,)), ((), ())), preferred_element_type=jnp.float32
    )


def twin_terms(x_rows, z_rows, y_rows, mask, w_one, w_two, w_three):
    w_outf = w_three.astype(jnp.float32)
    a_one = jnp.dot(x_rows, w_one, preferred_element_type=jnp.float32)
    s_one = jax.nn.sigmoid(a_one)
    h_one = jax.nn.softplus(a_one).astype(jnp.bfloat16)
    a_two = jnp.dot(h_one, w_two, preferred_element_type=jnp.float32)
    s_two = jax.nn.sigmoid(a_two)
    h_two = jax.nn.softplus(a_two)
    value = jnp.sum(h_two * w_outf[None, :], axis=1)
    g_two = (s_two * w_outf[None, :]).astype(jnp.bfloat16)
    c_one = lax.dot_general(
        g_two, w_two, (((1,), (1,)), ((), ())), preferred_element_type=jnp.float32
    )
    g_one = (c_one * s_one).astype(jnp.bfloat16)
    slope = lax.dot_general(
        g_one, w_one, (((1,), (1,)), ((), ())), preferred_element_type=jnp.float32
    )
    e_value = 2.0 * mask * (value - y_rows.astype(jnp.float32))
    e_slope = (2.0 * mask[:, None] * (slope - z_rows.astype(jnp.float32))).astype(jnp.bfloat16)
    e_gone = jnp.dot(e_slope, w_one, preferred_element_type=jnp.float32)
    e_cone = (e_gone * s_one).astype(jnp.bfloat16)
    e_sone = e_gone * c_one
    e_gtwo = jnp.dot(e_cone, w_two, preferred_element_type=jnp.float32)
    grad_three = jnp.sum(e_gtwo * s_two + e_value[:, None] * h_two, axis=0)
    e_atwo = (
        e_gtwo * w_outf[None, :] * s_two * (1.0 - s_two)
        + e_value[:, None] * w_outf[None, :] * s_two
    ).astype(jnp.bfloat16)
    e_hone = lax.dot_general(
        e_atwo, w_two, (((1,), (1,)), ((), ())), preferred_element_type=jnp.float32
    )
    e_aone = (e_sone * s_one * (1.0 - s_one) + e_hone * s_one).astype(jnp.bfloat16)
    return (e_slope, g_one, e_aone, e_cone, g_two, h_one, e_atwo, grad_three)


def normalized(grad):
    return grad / jnp.sqrt(jnp.mean(grad * grad, axis=-1, keepdims=True) + 1e-06)


def per_device(
    paths, deltas, payoffs, counts, w_first, w_second, w_out, mom_first, mom_second, mom_out
):
    position = lax.axis_index("blk")
    rows_dev = paths.shape[0]
    w_one, w_two = (
        lax.all_gather(w_first, "blk", axis=0, tiled=True),
        lax.all_gather(w_second, "blk", axis=0, tiled=True),
    )
    sending = lax.dynamic_index_in_dim(counts, position, 0, keepdims=False)
    x_rows, z_rows, y_rows = (paths, deltas, payoffs)
    total = jnp.sum(sending)
    mask = (jnp.arange(rows_dev, dtype=jnp.int32) < total).astype(jnp.float32)
    e_slope, g_one, e_aone, e_cone, g_two, h_one, e_atwo, grad_three = twin_terms(
        x_rows, z_rows, y_rows, mask, w_one, w_two, w_out
    )
    grad_one = lax.psum_scatter(
        rows_product(x_rows, e_aone) + rows_product(e_slope, g_one),
        "blk",
        scatter_dimension=0,
        tiled=True,
    )
    grad_two = lax.psum_scatter(
        rows_product(e_cone, g_two) + rows_product(h_one, e_atwo),
        "blk",
        scatter_dimension=0,
        tiled=True,
    )
    grad_out = lax.psum(grad_three, "blk")
    new_first = 0.8 * mom_first + 0.2 * normalized(grad_one)
    new_second = 0.8 * mom_second + 0.2 * normalized(grad_two)
    new_out = 0.8 * mom_out + 0.2 * normalized(grad_out)
    return (new_first, new_second, new_out)


def solution(mesh):
    in_specs = (
        P(("groups", "blk"), None),
        P(("groups", "blk"), None),
        P(("groups", "blk")),
        P("groups", None),
        P(("groups", "blk"), None),
        P(("groups", "blk"), None),
        P("groups"),
        P(("groups", "blk"), None),
        P(("groups", "blk"), None),
        P("groups"),
    )
    out_specs = (P(("groups", "blk"), None), P(("groups", "blk"), None), P("groups"))
    return jax.shard_map(
        per_device, mesh=mesh, in_specs=in_specs, out_specs=out_specs, check_vma=False
    )
```

profile of v0, /device:TPU:0, one launch (start us, length us, event | category | flops | bytes accessed | tf_op | source)
XLA Modules:
  0.0 254.4 jit_solution(2150444523015975469)
XLA Ops:
  7.2 0.7 all-gather.3.cloned.1.call-update
  8.0 0.7 all-gather.5.cloned.1.call-update
  8.7 0.7 convert_element_type.33
  9.4 1.3 dynamic-slice_reduce_fusion
  10.7 0.6 compare_select_fusion.2
  11.4 39.5 %all-gather.3.cloned.1.call-done = bf16[512,1024]{1,0:T(8,128)(2,1)} async-done(((bf16[32,1024]{1,0:T(8,128)(2,1)}), bf16[512,1024]{1,0:T(8,128)(2,1)}) %all-gather.3.cloned.1.call-update) | async-done | bytes 1048592 | tf_op jit(solution)/shard_map/all_gather | solution.py:58
  50.9 1.5 fusion.17
  52.4 41.0 %all-gather.5.cloned.1.call-done = bf16[1024,1024]{1,0:T(8,128)(2,1)} async-done(((bf16[64,1024]{1,0:T(8,128)(2,1)}), bf16[1024,1024]{1,0:T(8,128)(2,1)}) %all-gather.5.cloned.1.call-update) | async-done | bytes 2097168 | tf_op jit(solution)/shard_map/all_gather | solution.py:59
  93.4 2.6 %multiply_reduce_fusion.1 = (f32[128]{0:T(128)S(1)}, f32[128,1024]{1,0:T(8,128)S(1)}) fusion(f32[1024]{0:T(1024)S(1)} %convert_element_type.33, bf16[1024,1024]{1,0:T(8,128)(2,1)} %all-gather.5.cloned.1.call-done, f32[128,1024]{1,0:T(8,128)S(1)} %fusion.17), kind=kOutput, calls=%fused_computation.16 | convolution fusion | flops 270401408 | bytes 3150336 | tf_op jit(solution)/shard_map/dot_general | solution.py:18
  96.0 0.7 subtract_multiply_fusion
  96.7 1.7 multiply_convert_fusion.1
  98.4 0.5 fusion.4
  98.9 1.1 multiply_convert_fusion
  100.0 0.9 add_reduce_fusion
  100.9 3.0 %fusion.2 = f32[1024,512]{1,0:T(8,128)S(1)} fusion(bf16[128,512]{1,0:T(8,128)(2,1)S(1)} %copy-done, bf16[128,1024]{1,0:T(8,128)(2,1)S(1)} %get-tuple-element.10, bf16[1024,1024]{1,0:T(8,128)(2,1)} %all-gather.5.cloned.1.call-done, f32[128,1024]{1,0:T(8,128)} %get-tuple-element.14, f32[128,1024]{1,0:T(8,128)} %get-tuple-element.12, f32[128,1024]{1,0:T(8,128)S(1)} %fusion.17), kind=kOutput, calls=%fused_computation.7 | convolution fusion | flops 403963904 | bytes 6160384 | tf_op jit(solution)/shard_map/dot_general | solution.py:8
  103.9 1.8 bitcast_add_fusion
  105.7 2.9 %copy.20 = f32[512,1024]{1,0:T(8,128)} copy(f32[512,1024]{0,1:T(8,128)} %bitcast_add_fusion) | data formatting | bytes 4194304
  108.7 1.0 copy-done.4
  109.7 0.8 fusion.11
  110.5 2.8 %convolution_add_fusion = f32[1024,1024]{1,0:T(8,128)} fusion(f32[1024,1024]{1,0:T(8,128)S(1)} %fusion.11, bf16[128,1024]{1,0:T(8,128)(2,1)S(1)} %get-tuple-element.10, f32[128,1024]{1,0:T(8,128)S(1)} %fusion.17), kind=kOutput, calls=%fused_computation | convolution fusion | flops 270401536 | bytes 9175040 | tf_op jit(solution)/shard_map/dot_general | solution.py:8
  113.3 0.9 copy-done.9
  114.2 0.2 copy.16
  114.4 31.6 %psum.7 = f32[1024]{0:T(1024)S(1)} all-reduce(f32[1024]{0:T(1024)S(1)} %get-tuple-element.9), channel_id=1, replica_groups=mesh['groups'=2,'blk'=16] {'blk'}, use_global_device_ids=true, to_apply=%region_7.8 | all-reduce | flops 1024 | bytes 8192 | tf_op jit(solution)/shard_map/psum | solution.py:80
  146.1 0.6 multiply_reduce_fusion.3
  147.4 0.6 multiply_add_fusion.2
  148.0 21.5 %reduce-scatter.7.cloned.1.call-done = f32[32,1024]{1,0:T(8,128)} async-done(((f32[512,1024]{1,0:T(8,128)}), f32[32,1024]{1,0:T(8,128)}) %reduce-scatter.7.cloned.1.call-update) | async-done | bytes 131088
  169.5 1.1 copy.21
  170.6 0.2 multiply_reduce_fusion
  170.9 0.8 copy.18
  171.7 73.3 %reduce-scatter.5.cloned.1.call-done = f32[64,1024]{1,0:T(8,128)} async-done(((f32[1024,1024]{1,0:T(8,128)}), f32[64,1024]{1,0:T(8,128)}) %reduce-scatter.5.cloned.1.call-update) | async-done | bytes 262160 | tf_op jit(solution)/shard_map/reduce_scatter | solution.py:74
  245.0 1.1 multiply_reduce_fusion.2
  246.1 1.8 multiply_add_fusion.1
  (31 shorter events, 0.4 us)
Async XLA Ops:
  7.2 43.7 %copy-start = (bf16[128,512]{1,0:T(8,128)(2,1)S(1)}, bf16[128,512]{1,0:T(8,128)(2,1)}, u32[]{:S(2)}) copy-start(bf16[128,512]{1,0:T(8,128)(2,1)} %param.10) | copy-start | bytes 393220
  7.2 43.7 %all-gather.3.cloned.1.call-start = ((), (), s32[]{:S(2)}) async-start(), calls=%async_computation.2 | async-start | bytes 1114112 | tf_op jit(solution)/shard_map/all_gather | solution.py:58
  7.9 85.4 %all-gather.5.cloned.1.call-start = ((), (), s32[]{:S(2)}) async-start(), calls=%async_computation.3 | async-start | bytes 2228224 | tf_op jit(solution)/shard_map/all_gather | solution.py:59
  8.7 160.8 %reduce-scatter.7.cloned.1.call-start = ((), (), s32[]{:S(2)}) async-start(), calls=%async_computation.5 | async-start | bytes 2228224
  52.4 43.6 %copy-start.11 = (bf16[128]{0:T(256)(128)(2,1)S(1)}, bf16[128]{0:T(256)(128)(2,1)}, u32[]{:S(2)}) copy-start(bf16[128]{0:T(256)(128)(2,1)} %param.12) | copy-start | bytes 772
  93.4 3.3 %copy-start.2 = (bf16[1024,1024]{1,0:T(8,128)(2,1)S(1)}, bf16[1024,1024]{1,0:T(8,128)(2,1)}, u32[]{:S(2)}) copy-start(bf16[1024,1024]{1,0:T(8,128)(2,1)} %all-gather.5.cloned.1.call-done) | copy-start | bytes 6291460
  96.0 4.0 %copy-start.3 = (f32[128,1024]{1,0:T(8,128)}, f32[128,1024]{1,0:T(8,128)S(1)}, u32[]{:S(2)}) copy-start(f32[128,1024]{1,0:T(8,128)S(1)} %get-tuple-element.16) | copy-start | bytes 1572868
  96.7 1.7 copy-start.1
  96.7 1.7 copy-start.8
  100.0 0.9 copy-start.5
  108.6 1.0 copy-start.4
  108.6 1.1 copy-start.6
  108.7 136.4 %reduce-scatter.5.cloned.1.call-start = ((), (), s32[]{:S(2)}) async-start(), calls=%async_computation.4 | async-start | bytes 4456448 | tf_op jit(solution)/shard_map/reduce_scatter | solution.py:74
  113.3 0.9 copy-start.9
  113.3 34.0 %copy-start.10 = (f32[1024]{0:T(1024)S(1)}, f32[1024]{0:T(1024)}, u32[]{:S(2)}) copy-start(f32[1024]{0:T(1024)} %param.19) | copy-start | bytes 12292
  114.2 131.9 %copy-start.7 = (f32[64,1024]{1,0:T(8,128)S(1)}, f32[64,1024]{1,0:T(8,128)}, u32[]{:S(2)}) copy-start(f32[64,1024]{1,0:T(8,128)} %param.18) | copy-start | bytes 786436
Sparse Core Ops, SparseCore 0:
  10.2 40.6 all-gather.2
  53.0 40.3 all-gather.4
  108.8 60.6 reduce-scatter.6
  173.7 71.2 reduce-scatter.4
where the time goes:
time: 255 us; the launch traced here: 254 us
  waiting for transfers between devices  177 us (69%)
  blocking collectives  31.6 us (12%)
  matrix products  16.7 us (7%)
  between operations  14.6 us (6%)
  other arithmetic  7.63 us (3%)
  local copies, waits for them, and re-layouts  6.99 us (3%)
    reduce_scatter x1, waiting for transfers between devices, per_device(): lax.psum_scatter(rows_product(e_cone, g_two) + rows_product(h_one, e_atwo...  73.3 us
    all_gather x1, waiting for transfers between devices, per_device(): lax.all_gather(w_second, 'blk', axis=0, tiled=True)  41 us
    all_gather x1, waiting for transfers between devices, per_device(): lax.all_gather(w_first, 'blk', axis=0, tiled=True)  39.5 us
    psum x1, blocking collectives, per_device(): grad_out = lax.psum(grad_three, 'blk')  31.6 us
    unnamed x5, waiting for transfers between devices  22.9 us
    dot_general x4, matrix products, rows_product(): lax.dot_general(left, right, (((0,), (0,)), ((), ())), preferred_element_...  8.39 us
    unnamed x28, local copies, waits for them, and re-layouts  6.99 us
  transfers between devices with their start and end apart: 4, of which 4 were waited for; matrix products, arithmetic and copies ran while one was open for 4% of the time, Pallas kernels for 0%

commit v1 on v0

--- a/solution.py
+++ b/solution.py
@@ -53,11 +53,15 @@
     paths, deltas, payoffs, counts, w_first, w_second, w_out, mom_first, mom_second, mom_out
 ):
     position = lax.axis_index("blk")
+    n_blk = lax.axis_size("blk")
     rows_dev = paths.shape[0]
-    w_one, w_two = (
-        lax.all_gather(w_first, "blk", axis=0, tiled=True),
-        lax.all_gather(w_second, "blk", axis=0, tiled=True),
+    r_one, r_two = w_first.shape[0], w_second.shape[0]
+    hidden = w_first.shape[1]
+    gathered = lax.all_gather(
+        jnp.concatenate([w_first, w_second], axis=0), "blk", axis=0, tiled=False
     )
+    w_one = gathered[:, :r_one].reshape(n_blk * r_one, hidden)
+    w_two = gathered[:, r_one:].reshape(n_blk * r_two, hidden)
     sending = lax.dynamic_index_in_dim(counts, position, 0, keepdims=False)
     x_rows, z_rows, y_rows = (paths, deltas, payoffs)
     total = jnp.sum(sending)
@@ -65,18 +69,18 @@
     e_slope, g_one, e_aone, e_cone, g_two, h_one, e_atwo, grad_three = twin_terms(
         x_rows, z_rows, y_rows, mask, w_one, w_two, w_out
     )
-    grad_one = lax.psum_scatter(
-        rows_product(x_rows, e_aone) + rows_product(e_slope, g_one),
-        "blk",
-        scatter_dimension=0,
-        tiled=True,
+    part_one = rows_product(x_rows, e_aone) + rows_product(e_slope, g_one)
+    part_two = rows_product(e_cone, g_two) + rows_product(h_one, e_atwo)
+    blocks = jnp.concatenate(
+        [
+            part_one.reshape(n_blk, r_one, hidden),
+            part_two.reshape(n_blk, r_two, hidden),
+        ],
+        axis=1,
     )
-    grad_two = lax.psum_scatter(
-        rows_product(e_cone, g_two) + rows_product(h_one, e_atwo),
-        "blk",
-        scatter_dimension=0,
-        tiled=True,
-    )
+    reduced = lax.psum_scatter(blocks, "blk", scatter_dimension=0, tiled=True)[0]
+    grad_one = reduced[:r_one]
+    grad_two = reduced[r_one:]
     grad_out = lax.psum(grad_three, "blk")
     new_first = 0.8 * mom_first + 0.2 * normalized(grad_one)
     new_second = 0.8 * mom_second + 0.2 * normalized(grad_two)

time: 255 us -> 180 us (0.71)
  waiting for transfers between devices: 177 us -> 97.9 us
  other arithmetic: 7.63 us -> 15.5 us
  local copies, waits for them, and re-layouts: 6.99 us -> 3.79 us
    all_gather x2 -> x1, waiting for transfers between devices: 80.4 us -> 47.2 us  [per_device(): lax.all_gather(jnp.concatenate([w_first, w_second], axis=0), 'blk', axis=...]
    unnamed x5 -> x2, waiting for transfers between devices: 22.9 us -> 0.03 us
    reduce_scatter x1, waiting for transfers between devices: 73.3 us -> 50.7 us  [per_device(): lax.psum_scatter(blocks, 'blk', scatter_dimension=0, tiled=True)[0]]
    unnamed x28 -> x14, local copies, waits for them, and re-layouts: 6.99 us -> 0.64 us
    concatenate x0 -> x2, other arithmetic: none -> 5.41 us  [the longest x1 3.79 us: per_device(): jnp.concatenate([part_one.reshape(n_blk, r_one, hidden), part_two.reshape...]
    slice x0 -> x2, local copies, waits for them, and re-layouts: none -> 3.15 us  [the longest x1 1.86 us: per_device(): w_two = gathered[:, r_one:].reshape(n_blk * r_two, hidden)]
  transfers between devices with their start and end apart: 4 -> 2, of which waited for: 4 -> 2; matrix products, arithmetic and copies ran while one was open for 4% -> 2% of each run, Pallas kernels for 0% -> 0%
where the time goes in v1:
time: 180 us
  waiting for transfers between devices  97.9 us (54%)
  blocking collectives  31.6 us (18%)
  matrix products  16.2 us (9%)
  other arithmetic  15.5 us (9%)
  between operations  14.8 us (8%)
  local copies, waits for them, and re-layouts  3.79 us (2%)
    reduce_scatter x1, waiting for transfers between devices, per_device(): lax.psum_scatter(blocks, 'blk', scatter_dimension=0, tiled=True)[0]  50.7 us
    all_gather x1, waiting for transfers between devices, per_device(): lax.all_gather(jnp.concatenate([w_first, w_second], axis=0), 'blk', axis=...  47.2 us
    psum x1, blocking collectives, per_device(): grad_out = lax.psum(grad_three, 'blk')  31.6 us
    dot_general x4, matrix products, rows_product(): lax.dot_general(left, right, (((0,), (0,)), ((), ())), preferred_element_...  9.67 us
    concatenate x1, other arithmetic, per_device(): jnp.concatenate([part_one.reshape(n_blk, r_one, hidden), part_two.reshape...  3.79 us
  transfers between devices with their start and end apart: 2, of which 2 were waited for; matrix products, arithmetic and copies ran while one was open for 2% of the time, Pallas kernels for 0%

profile of v1, /device:TPU:0, one launch (start us, length us, event | category | flops | bytes accessed | tf_op | source)
XLA Modules:
  0.0 179.9 jit_solution(380783701327721012)
XLA Ops:
  7.2 0.0 all-gather.3.cloned.1.call-start
  7.2 1.6 pad_maximum_fusion.1
  8.9 0.0 all-gather.3.cloned.1.call-update
  8.9 0.0 reduce-scatter.2.cloned.1.call-start
  8.9 0.7 convert_element_type.33
  9.6 1.3 dynamic-slice_reduce_fusion
  10.9 0.6 compare_select_fusion.2
  11.6 47.2 %all-gather.3.cloned.1.call-done = bf16[1536,1024]{1,0:T(8,128)(2,1)} async-done(((bf16[96,1024]{1,0:T(8,128)(2,1)}), bf16[1536,1024]{1,0:T(8,128)(2,1)}) %all-gather.3.cloned.1.call-update) | async-done | bytes 3145744 | tf_op jit(solution)/shard_map/all_gather | solution.py:60
  58.8 1.3 slice.25
  60.1 1.9 %slice.24 = bf16[16,64,1024]{2,1,0:T(8,128)(2,1)S(1)} slice(bf16[16,96,1024]{2,1,0:T(8,128)(2,1)} %bitcast.48), slice={[0:16], [32:96], [0:1024]} | slice | bytes 4194304 | tf_op jit(solution)/shard_map/slice | solution.py:64
  62.0 0.5 convolution_bitcast_fusion
  62.4 1.2 multiply_reduce_fusion
  63.6 1.6 multiply_convert_fusion.1
  65.3 0.5 fusion.4
  65.8 1.4 multiply_convert_fusion
  67.1 2.7 %fusion.15 = f32[1024,1024]{1,0:T(8,128)} fusion(bf16[128,1024]{0,1:T(8,128)(2,1)S(1)} %get-tuple-element.7, f32[1024]{0:T(1024)S(1)} %convert_element_type.33, f32[128,1024]{0,1:T(8,128)S(1)} %get-tuple-element.10), kind=kOutput, calls=%fused_computation.43 | convolution fusion | flops 269090816 | bytes 4984832 | tf_op jit(solution)/shard_map/dot_general | solution.py:8
  69.9 0.6 subtract_multiply_fusion
  70.6 1.4 add_reduce_fusion
  71.9 4.0 %fusion.2 = f32[1024,512]{0,1:T(8,128)} fusion(bf16[128,512]{1,0:T(8,128)(2,1)S(1)} %copy-done, bf16[1024,1024]{1,0:T(8,128)(2,1)S(1)} %bitcast.45, bf16[128,1024]{0,1:T(8,128)(2,1)S(1)} %get-tuple-element.4, f32[128,1024]{0,1:T(8,128)} %get-tuple-element.8, f32[128,1024]{0,1:T(8,128)} %get-tuple-element.6, f32[128,1024]{0,1:T(8,128)S(1)} %convolution_bitcast_fusion), kind=kOutput, calls=%fused_computation.9 | convolution fusion | flops 403963904 | bytes 6160384 | tf_op jit(solution)/shard_map/dot_general | solution.py:8
  75.9 2.2 %bitcast_add_fusion = f32[512,1024]{1,0:T(8,128)S(1)} fusion(f32[1024,512]{0,1:T(8,128)} %fusion.2, bf16[128,512]{1,0:T(8,128)(2,1)S(1)} %fusion.4, bf16[128,1024]{0,1:T(8,128)(2,1)S(1)} %get-tuple-element.5), kind=kOutput, calls=%fused_computation.2 | convolution fusion | flops 134742016 | bytes 4587520 | tf_op jit(solution)/shard_map/dot_general | solution.py:8
  78.1 0.6 copy-done.1
  78.7 0.8 convolution_add_fusion
  79.5 3.8 %pad_maximum_fusion = f32[16,96,1024]{2,1,0:T(8,128)} fusion(f32[16,64,1024]{2,1,0:T(8,128)S(1)} %bitcast.38, f32[16,32,1024]{2,1,0:T(8,128)S(1)} %bitcast.46), kind=kLoop, calls=%fused_computation | loop fusion | flops 1572864 | bytes 12582912 | tf_op jit(solution)/shard_map/concatenate | solution.py:74
  83.3 0.0 reduce-scatter.2.cloned.1.call-update
  83.3 31.6 %psum.7 = f32[1024]{0:T(1024)S(1)} all-reduce(f32[1024]{0:T(1024)S(1)} %get-tuple-element.3), channel_id=1, replica_groups=mesh['groups'=2,'blk'=16] {'blk'}, use_global_device_ids=true, to_apply=%region_6.7 | all-reduce | flops 1024 | bytes 8192 | tf_op jit(solution)/shard_map/psum | solution.py:84
  114.9 0.6 multiply_reduce_fusion.3
  116.2 0.6 multiply_add_fusion.2
  116.8 50.7 %reduce-scatter.2.cloned.1.call-done = f32[1,96,1024]{2,1,0:T(8,128)} async-done(((f32[16,96,1024]{2,1,0:T(8,128)}), f32[1,96,1024]{2,1,0:T(8,128)}) %reduce-scatter.2.cloned.1.call-update) | async-done | bytes 393232 | tf_op jit(solution)/shard_map/reduce_scatter | solution.py:81
  167.5 1.1 multiply_reduce_fusion.1
  168.6 1.0 multiply_reduce_fusion.2
  169.6 1.7 multiply_add_fusion.1
  171.3 1.8 multiply_add_fusion
  (15 shorter events, 0.0 us)
Async XLA Ops:
  7.2 54.8 %copy-start = (bf16[128,512]{1,0:T(8,128)(2,1)S(1)}, bf16[128,512]{1,0:T(8,128)(2,1)}, u32[]{:S(2)}) copy-start(bf16[128,512]{1,0:T(8,128)(2,1)} %param.10) | copy-start | bytes 393220
  7.2 51.6 %all-gather.3.cloned.1.call-start = ((), (), s32[]{:S(2)}) async-start(), calls=%async_computation.2 | async-start | bytes 3342336 | tf_op jit(solution)/shard_map/all_gather | solution.py:60
  8.9 158.6 %reduce-scatter.2.cloned.1.call-start = ((), (), s32[]{:S(2)}) async-start(), calls=%async_computation.1 | async-start | bytes 6684672 | tf_op jit(solution)/shard_map/reduce_scatter | solution.py:81
  63.6 1.6 copy-start.3
  67.1 2.8 %copy-start.6 = (bf16[128]{0:T(256)(128)(2,1)S(1)}, bf16[128]{0:T(256)(128)(2,1)}, u32[]{:S(2)}) copy-start(bf16[128]{0:T(256)(128)(2,1)} %param.12) | copy-start | bytes 772
  75.9 2.8 %copy-start.1 = (f32[1024,1024]{1,0:T(8,128)S(1)}, f32[1024,1024]{1,0:T(8,128)}, u32[]{:S(2)}) copy-start(f32[1024,1024]{1,0:T(8,128)} %fusion.15) | copy-start | bytes 12582916
  83.3 32.9 %copy-start.5 = (f32[1024]{0:T(1024)S(1)}, f32[1024]{0:T(1024)}, u32[]{:S(2)}) copy-start(f32[1024]{0:T(1024)} %param.19) | copy-start | bytes 12292
  83.3 86.3 %copy-start.4 = (f32[32,1024]{1,0:T(8,128)S(1)}, f32[32,1024]{1,0:T(8,128)}, u32[]{:S(2)}) copy-start(f32[32,1024]{1,0:T(8,128)} %param.17) | copy-start | bytes 393220
  83.3 88.0 %copy-start.2 = (f32[64,1024]{1,0:T(8,128)S(1)}, f32[64,1024]{1,0:T(8,128)}, u32[]{:S(2)}) copy-start(f32[64,1024]{1,0:T(8,128)} %param.18) | copy-start | bytes 786436
Sparse Core Ops, SparseCore 0:
  10.9 47.8 all-gather.2
  83.4 84.0 reduce-scatter.1

commit v2 on v1

--- a/solution.py
+++ b/solution.py
@@ -1,3 +1,5 @@
+import functools
+
 import jax
 import jax.numpy as jnp
 from jax import lax
@@ -49,17 +51,99 @@
     return grad / jnp.sqrt(jnp.mean(grad * grad, axis=-1, keepdims=True) + 1e-06)
 
 
+def ring_plan(n_blk):
+    chips = n_blk // 2
+    snake = list(range(0, chips, 2)) + list(range(chips - 1, 0, -2))
+    place = [0] * chips
+    for p, q in enumerate(snake):
+        place[q] = p
+    cw = [(2 * snake[p] + c, 2 * snake[(p + 1) % chips] + c) for p in range(chips) for c in range(2)]
+    ccw = [(b, a) for a, b in cw]
+    partner = [(b, b ^ 1) for b in range(n_blk)]
+    return chips, snake, place, cw, ccw, partner
+
+
+def ring_all_gather(x, n_blk):
+    chips, snake, place, cw, ccw, partner = ring_plan(n_blk)
+    ahead = chips // 2
+    behind = chips - 1 - ahead
+    position = lax.axis_index("blk")
+    core, chip = position % 2, position // 2
+    spot = jnp.asarray(place, jnp.int32)[chip]
+    rel = [None] * chips
+    rel[0] = x
+    left = right = x
+    for s in range(1, ahead + 1):
+        left = lax.ppermute(left, "blk", cw)
+        rel[chips - s] = left
+        if s <= behind:
+            right = lax.ppermute(right, "blk", ccw)
+            rel[s] = right
+    mine = jnp.stack(rel)
+    other = lax.ppermute(mine, "blk", partner)
+    both = jnp.concatenate([mine, other], axis=0)
+    dest = jnp.arange(n_blk, dtype=jnp.int32)
+    dest_chip, dest_core = dest // 2, dest % 2
+    k = (jnp.asarray(place, jnp.int32)[dest_chip] - spot) % chips
+    index = jnp.where(dest_core == core, 0, chips) + k
+    return jnp.take(both, index, axis=0)
+
+
+def ring_reduce_scatter(blocks, extra, n_blk):
+    chips, snake, place, cw, ccw, partner = ring_plan(n_blk)
+    ahead = chips // 2
+    behind = chips - 1 - ahead
+    rows = blocks.shape[1]
+    position = lax.axis_index("blk")
+    core, chip = position % 2, position // 2
+    spot = jnp.asarray(place, jnp.int32)[chip]
+    order = jnp.asarray(snake, jnp.int32)
+    pairs = blocks.reshape(chips, 2, rows, blocks.shape[2])
+    kept = lax.dynamic_index_in_dim(pairs, core, 1, keepdims=False)
+    given = lax.dynamic_index_in_dim(pairs, 1 - core, 1, keepdims=False)
+    sent = jnp.concatenate([given.reshape(chips * rows, -1), extra[None]], axis=0)
+    got = lax.ppermute(sent, "blk", partner)
+    summed = kept + got[: chips * rows].reshape(chips, rows, -1)
+    chip_extra = extra + got[chips * rows]
+
+    def block_at(k):
+        return lax.dynamic_index_in_dim(summed, order[(spot + k) % chips], 0, keepdims=False)
+
+    rel = [None] * chips
+    rel[0] = chip_extra
+    acc = block_at(ahead)
+    carried = chip_extra
+    for s in range(1, ahead + 1):
+        got = lax.ppermute(jnp.concatenate([acc, carried[None]], axis=0), "blk", cw)
+        acc = got[:rows] + block_at(ahead - s)
+        carried = got[rows]
+        rel[chips - s] = carried
+    if behind:
+        acc_back = block_at(chips - behind)
+        carried = chip_extra
+        for s in range(1, behind + 1):
+            got = lax.ppermute(jnp.concatenate([acc_back, carried[None]], axis=0), "blk", ccw)
+            carried = got[rows]
+            rel[s] = carried
+            if s < behind:
+                acc_back = got[:rows] + block_at(chips - behind + s)
+            else:
+                acc = acc + got[:rows]
+    by_rel = jnp.stack(rel)
+    k = (jnp.asarray(place, jnp.int32) - spot) % chips
+    by_chip = jnp.take(by_rel, k, axis=0)
+    return acc, jnp.sum(by_chip, axis=0)
+
+
 def per_device(
-    paths, deltas, payoffs, counts, w_first, w_second, w_out, mom_first, mom_second, mom_out
+    paths, deltas, payoffs, counts, w_first, w_second, w_out, mom_first, mom_second, mom_out,
+    n_blk,
 ):
     position = lax.axis_index("blk")
-    n_blk = lax.axis_size("blk")
     rows_dev = paths.shape[0]
     r_one, r_two = w_first.shape[0], w_second.shape[0]
     hidden = w_first.shape[1]
-    gathered = lax.all_gather(
-        jnp.concatenate([w_first, w_second], axis=0), "blk", axis=0, tiled=False
-    )
+    gathered = ring_all_gather(jnp.concatenate([w_first, w_second], axis=0), n_blk)
     w_one = gathered[:, :r_one].reshape(n_blk * r_one, hidden)
     w_two = gathered[:, r_one:].reshape(n_blk * r_two, hidden)
     sending = lax.dynamic_index_in_dim(counts, position, 0, keepdims=False)
@@ -78,10 +162,9 @@
         ],
         axis=1,
     )
-    reduced = lax.psum_scatter(blocks, "blk", scatter_dimension=0, tiled=True)[0]
+    reduced, grad_out = ring_reduce_scatter(blocks, grad_three, n_blk)
     grad_one = reduced[:r_one]
     grad_two = reduced[r_one:]
-    grad_out = lax.psum(grad_three, "blk")
     new_first = 0.8 * mom_first + 0.2 * normalized(grad_one)
     new_second = 0.8 * mom_second + 0.2 * normalized(grad_two)
     new_out = 0.8 * mom_out + 0.2 * normalized(grad_out)
@@ -103,5 +186,6 @@
     )
     out_specs = (P(("groups", "blk"), None), P(("groups", "blk"), None), P("groups"))
     return jax.shard_map(
-        per_device, mesh=mesh, in_specs=in_specs, out_specs=out_specs, check_vma=False
+        functools.partial(per_device, n_blk=mesh.shape["blk"]),
+        mesh=mesh, in_specs=in_specs, out_specs=out_specs, check_vma=False,
     )

time: 180 us -> 150 us (0.83)
  waiting for transfers between devices: 97.9 us -> 40.5 us
  blocking collectives: 31.6 us -> 0 us
  local copies, waits for them, and re-layouts: 3.79 us -> 26.8 us
  starting transfers between devices: 0.08 us -> 15.1 us
  other arithmetic: 15.5 us -> 26.2 us
  between operations: 14.8 us -> 23.6 us
    reduce_scatter x1 -> x0, waiting for transfers between devices: 50.7 us -> none  [per_device(): lax.psum_scatter(blocks, 'blk', scatter_dimension=0, tiled=True)[0]]
    all_gather x1 -> x0, waiting for transfers between devices: 47.2 us -> none  [per_device(): lax.all_gather(jnp.concatenate([w_first, w_second], axis=0), 'blk', axis=...]
    ppermute x0 -> x16, waiting for transfers between devices: none -> 40.5 us  [the longest x4 19.2 us: ring_reduce_scatter(): got = lax.ppermute(jnp.concatenate([acc, carried[None]], axis=0), 'blk', cw)]
    psum x1 -> x0, blocking collectives: 31.6 us -> none  [per_device(): grad_out = lax.psum(grad_three, 'blk')]
    ppermute x0 -> x16, starting transfers between devices: none -> 15.1 us  [the longest x3 6.07 us: ring_all_gather(): right = lax.ppermute(right, 'blk', ccw)]
    unnamed x14 -> x38, local copies, waits for them, and re-layouts: 0.64 us -> 9.55 us
    slice x0 -> x8, local copies, waits for them, and re-layouts: none -> 7.74 us  [the longest x7 5.33 us: ring_reduce_scatter(): carried = got[rows]]
    add x0 -> x6, other arithmetic: none -> 6.72 us  [the longest x3 3.68 us: ring_reduce_scatter(): acc = got[:rows] + block_at(ahead - s)]
  transfers between devices with their start and end apart: 2 -> 16, of which waited for: 2 -> 10; matrix products, arithmetic and copies ran while one was open for 2% -> 11% of each run, Pallas kernels for 0% -> 0%
where the time goes in v2:
time: 150 us; the launch traced here: 148 us
  waiting for transfers between devices  40.5 us (27%)
  local copies, waits for them, and re-layouts  26.8 us (18%)
  other arithmetic  26.2 us (17%)
  between operations  23.6 us (16%)
  matrix products  16.3 us (11%)
  starting transfers between devices  15.1 us (10%)
    ppermute x4, waiting for transfers between devices, ring_reduce_scatter(): got = lax.ppermute(jnp.concatenate([acc, carried[None]], axis=0), 'blk', cw)  19.2 us
    dot_general x4, matrix products, rows_product(): lax.dot_general(left, right, (((0,), (0,)), ((), ())), preferred_element_...  9.77 us
    unnamed x38, local copies, waits for them, and re-layouts  9.55 us
    ppermute x4, waiting for transfers between devices, ring_all_gather(): left = lax.ppermute(left, 'blk', cw)  9.04 us
    ppermute x3, waiting for transfers between devices, ring_all_gather(): right = lax.ppermute(right, 'blk', ccw)  7.46 us
    ppermute x3, starting transfers between devices, ring_all_gather(): right = lax.ppermute(right, 'blk', ccw)  6.07 us
    slice x7, local copies, waits for them, and re-layouts, ring_reduce_scatter(): carried = got[rows]  5.33 us
    ppermute x3, waiting for transfers between devices, ring_reduce_scatter(): lax.ppermute(jnp.concatenate([acc_back, carried[None]], axis=0), 'blk', ccw)  4.75 us
  transfers between devices with their start and end apart: 16, of which 10 were waited for; matrix products, arithmetic and copies ran while one was open for 11% of the time, Pallas kernels for 0%

profile of v2, /device:TPU:0, one launch (start us, length us, event | category | flops | bytes accessed | tf_op | source)
XLA Modules:
  0.0 148.4 jit_solution(15466542566148709518)
XLA Ops:
  2.5 3.0 %collective-permute-start = (bf16[96,1024]{1,0:T(8,128)(2,1)S(1)}, bf16[96,1024]{1,0:T(8,128)(2,1)S(1)}, u32[]{:S(2)}, u32[]{:S(2)}) collective-permute-start(bf16[96,1024]{1,0:T(8,128)(2,1)S(1)} %constant_dynamic-update-slice_fusion), channel_id=1, source_target_pairs={{4,0},{5,1},{8,4},{9,5},{12,8},{13,9},{14,12},{15,13},{10,14},{11,... | collective-permute-start | bytes 589832 | tf_op jit(solution)/shard_map/ppermute | solution.py:80
  6.3 4.1 %collective-permute-done = bf16[96,1024]{1,0:T(8,128)(2,1)S(1)} collective-permute-done((bf16[96,1024]{1,0:T(8,128)(2,1)S(1)}, bf16[96,1024]{1,0:T(8,128)(2,1)S(1)}, u32[]{:S(2)}, u32[]{:S(2)}) %collective-permute-start) | collective-permute-done | bytes 196640 | tf_op jit(solution)/shard_map/ppermute | solution.py:80
  10.5 1.7 %collective-permute-start.1 = (bf16[96,1024]{1,0:T(8,128)(2,1)S(1)}, bf16[96,1024]{1,0:T(8,128)(2,1)S(1)}, u32[]{:S(2)}, u32[]{:S(2)}) collective-permute-start(bf16[96,1024]{1,0:T(8,128)(2,1)S(1)} %collective-permute-done), channel_id=1, source_target_pairs={{4,0},{5,1},{8,4},{9,5},{12,8},{13,9},{14,12},{15,13},{10,14},{11,... | collective-permute-start | bytes 589832 | tf_op jit(solution)/shard_map/ppermute | solution.py:80
  13.2 3.3 %collective-permute-done.1 = bf16[96,1024]{1,0:T(8,128)(2,1)S(1)} collective-permute-done((bf16[96,1024]{1,0:T(8,128)(2,1)S(1)}, bf16[96,1024]{1,0:T(8,128)(2,1)S(1)}, u32[]{:S(2)}, u32[]{:S(2)}) %collective-permute-start.1) | collective-permute-done | bytes 196640 | tf_op jit(solution)/shard_map/ppermute | solution.py:80
  16.5 1.4 collective-permute-start.2
  19.3 4.7 %collective-permute-done.5 = bf16[96,1024]{1,0:T(8,128)(2,1)S(1)} collective-permute-done((bf16[96,1024]{1,0:T(8,128)(2,1)S(1)}, bf16[96,1024]{1,0:T(8,128)(2,1)S(1)}, u32[]{:S(2)}, u32[]{:S(2)}) %collective-permute-start.5) | collective-permute-done | bytes 196640 | tf_op jit(solution)/shard_map/ppermute | solution.py:77
  25.4 4.3 %collective-permute-done.6 = bf16[96,1024]{1,0:T(8,128)(2,1)S(1)} collective-permute-done((bf16[96,1024]{1,0:T(8,128)(2,1)S(1)}, bf16[96,1024]{1,0:T(8,128)(2,1)S(1)}, u32[]{:S(2)}, u32[]{:S(2)}) %collective-permute-start.6) | collective-permute-done | bytes 196640 | tf_op jit(solution)/shard_map/ppermute | solution.py:77
  34.0 1.3 fusion.22
  36.7 1.3 constant_dynamic-update-slice_fusion.2
  38.0 2.6 %gather_fusion.1 = bf16[16,96,1024]{2,1,0:T(8,128)(2,1)S(1)} fusion(bf16[16,96,1024]{2,1,0:T(8,128)(2,1)} %constant_dynamic-update-slice_fusion.2, s32[1024]{0:T(1024)S(1)} %pad_clamp_fusion.1), kind=kCustom, calls=%fused_computation.1 | custom fusion | bytes 6291520 | tf_op jit(solution)/shard_map/jit(_take)/gather | solution.py:89
  43.1 1.6 %multiply_convert_fusion.1 = (bf16[128,1024]{0,1:T(8,128)(2,1)S(1)}, f32[128,1024]{0,1:T(8,128)}) fusion(f32[128,1024]{0,1:T(8,128)S(1)} %convolution_bitcast_fusion, bf16[1024,1024]{1,0:T(8,128)(2,1)S(1)} %bitcast.97, f32[1024]{0:T(1024)S(1)} %convert_element_type.33, f32[128,1024]{0,1:T(8,128)S(1)} %get-tuple-element.44), kind=kOutput, calls=%fused_computation.36 | convolution fusion | flops 269746176 | bytes 3936256 | tf_op jit(solution)/shard_map/dot_general | solution.py:25
  45.9 1.4 multiply_convert_fusion
  48.1 1.4 add_convert_fusion
  49.5 2.7 %convolution_add_fusion = f32[1024,1024]{1,0:T(8,128)} fusion(f32[1024,1024]{1,0:T(8,128)S(1)} %fusion.27, bf16[128,1024]{0,1:T(8,128)(2,1)S(1)} %get-tuple-element.11, f32[128,1024]{0,1:T(8,128)S(1)} %convolution_bitcast_fusion), kind=kOutput, calls=%fused_computation.13 | convolution fusion | flops 270401536 | bytes 9175040 | tf_op jit(solution)/shard_map/dot_general | solution.py:10
  52.2 4.0 %fusion.6 = f32[1024,512]{0,1:T(8,128)} fusion(bf16[128,512]{1,0:T(8,128)(2,1)S(1)} %copy-done, bf16[1024,1024]{1,0:T(8,128)(2,1)S(1)} %bitcast.99, bf16[128,1024]{0,1:T(8,128)(2,1)S(1)} %get-tuple-element.11, f32[128,1024]{0,1:T(8,128)} %get-tuple-element.42, f32[128,1024]{0,1:T(8,128)} %get-tuple-element.40, f32[128,1024]{0,1:T(8,128)S(1)} %convolution_bitcast_fusion), kind=kOutput, calls=%fused_computation.21 | convolution fusion | flops 403963904 | bytes 6160384 | tf_op jit(solution)/shard_map/dot_general | solution.py:10
  56.2 2.2 %bitcast_add_fusion = f32[512,1024]{1,0:T(8,128)S(1)} fusion(f32[1024,512]{0,1:T(8,128)} %fusion.6, bf16[128,512]{1,0:T(8,128)(2,1)S(1)} %fusion.8, bf16[128,1024]{0,1:T(8,128)(2,1)S(1)} %get-tuple-element.39), kind=kOutput, calls=%fused_computation.14 | convolution fusion | flops 134742016 | bytes 4587520 | tf_op jit(solution)/shard_map/dot_general | solution.py:10
  59.5 2.1 %pad_maximum_fusion = f32[769,1024]{1,0:T(8,128)} fusion(f32[1,1024]{1,0:T(1,128)S(1)} %bitcast.100, f32[768,1024]{1,0:T(8,128)S(1)} %bitcast.92), kind=kLoop, calls=%fused_computation.7 | loop fusion | flops 787456 | bytes 6299648 | tf_op jit(solution)/shard_map/concatenate | solution.py:104
  73.5 2.4 %slice.88 = f32[768,1024]{1,0:T(8,128)S(1)} slice(f32[769,1024]{1,0:T(8,128)} %collective-permute-done.8), slice={[0:768], [0:1024]} | slice | bytes 6291456 | tf_op jit(solution)/shard_map/slice | solution.py:106
  77.6 1.6 %copy-done.4 = f32[8,96,1024]{2,1,0:T(8,128)} copy-done((f32[8,96,1024]{2,1,0:T(8,128)}, f32[8,96,1024]{2,1,0:T(8,128)S(1)}, u32[]{:S(2)}) %copy-start.4) | copy-done | bytes 3145752
  83.5 1.4 collective-permute-start.13
  85.0 8.3 %collective-permute-done.9 = f32[97,1024]{1,0:T(8,128)} collective-permute-done((f32[97,1024]{1,0:T(8,128)}, f32[97,1024]{1,0:T(8,128)}, u32[]{:S(2)}, u32[]{:S(2)}) %collective-permute-start.9) | collective-permute-done | bytes 397344 | tf_op jit(solution)/shard_map/ppermute | solution.py:117
  101.2 6.0 %collective-permute-done.10 = f32[97,1024]{1,0:T(8,128)} collective-permute-done((f32[97,1024]{1,0:T(8,128)}, f32[97,1024]{1,0:T(8,128)}, u32[]{:S(2)}, u32[]{:S(2)}) %collective-permute-start.10) | collective-permute-done | bytes 397344 | tf_op jit(solution)/shard_map/ppermute | solution.py:117
  109.3 1.6 %collective-permute-start.14 = (f32[97,1024]{1,0:T(8,128)}, f32[97,1024]{1,0:T(8,128)}, u32[]{:S(2)}, u32[]{:S(2)}) collective-permute-start(f32[97,1024]{1,0:T(8,128)} %pad_maximum_fusion.6), channel_id=1, source_target_pairs={{4,0},{5,1},{8,4},{9,5},{12,8},{13,9},{14,12},{15,13},{10,14},{11,... | collective-permute-start | bytes 1191944 | tf_op jit(solution)/shard_map/ppermute | solution.py:125
  116.7 2.9 %collective-permute-done.14 = f32[97,1024]{1,0:T(8,128)} collective-permute-done((f32[97,1024]{1,0:T(8,128)}, f32[97,1024]{1,0:T(8,128)}, u32[]{:S(2)}, u32[]{:S(2)}) %collective-permute-start.14) | collective-permute-done | bytes 397344 | tf_op jit(solution)/shard_map/ppermute | solution.py:125
  120.4 2.1 %collective-permute-done.11 = f32[97,1024]{1,0:T(8,128)} collective-permute-done((f32[97,1024]{1,0:T(8,128)}, f32[97,1024]{1,0:T(8,128)}, u32[]{:S(2)}, u32[]{:S(2)}) %collective-permute-start.11) | collective-permute-done | bytes 397344 | tf_op jit(solution)/shard_map/ppermute | solution.py:117
  124.5 1.6 %collective-permute-start.15 = (f32[97,1024]{1,0:T(8,128)}, f32[97,1024]{1,0:T(8,128)}, u32[]{:S(2)}, u32[]{:S(2)}) collective-permute-start(f32[97,1024]{1,0:T(8,128)} %pad_maximum_fusion.7), channel_id=1, source_target_pairs={{4,0},{5,1},{8,4},{9,5},{12,8},{13,9},{14,12},{15,13},{10,14},{11,... | collective-permute-start | bytes 1191944 | tf_op jit(solution)/shard_map/ppermute | solution.py:125
  129.9 1.3 compare_and_fusion
  131.8 1.8 %collective-permute-done.15 = f32[97,1024]{1,0:T(8,128)} collective-permute-done((f32[97,1024]{1,0:T(8,128)}, f32[97,1024]{1,0:T(8,128)}, u32[]{:S(2)}, u32[]{:S(2)}) %collective-permute-start.15) | collective-permute-done | bytes 397344 | tf_op jit(solution)/shard_map/ppermute | solution.py:125
  133.6 2.9 %collective-permute-done.12 = f32[97,1024]{1,0:T(8,128)} collective-permute-done((f32[97,1024]{1,0:T(8,128)}, f32[97,1024]{1,0:T(8,128)}, u32[]{:S(2)}, u32[]{:S(2)}) %collective-permute-start.12) | collective-permute-done | bytes 397344 | tf_op jit(solution)/shard_map/ppermute | solution.py:117
  143.6 1.7 %multiply_add_fusion.1 = f32[32,1024]{1,0:T(8,128)} fusion(f32[32,1024]{1,0:T(8,128)} %param.22, f32[96,1024]{1,0:T(8,128)} %copy-done.6, f32[32]{0:T(128)S(1)} %add_sqrt_fusion.1), kind=kLoop, calls=%fused_computation.73 | loop fusion | flops 131072 | bytes 393344 | tf_op jit(solution)/shard_map/add | solution.py:168
  145.4 1.8 %multiply_add_fusion = f32[64,1024]{1,0:T(8,128)} fusion(f32[64,1024]{1,0:T(8,128)S(1)} %copy-done.7, f32[96,1024]{1,0:T(8,128)} %copy-done.6, f32[64]{0:T(128)S(1)} %add_sqrt_fusion), kind=kLoop, calls=%fused_computation.54 | loop fusion | flops 262144 | bytes 786688 | tf_op jit(solution)/shard_map/add | solution.py:169
  147.1 1.3 multiply_add_fusion.2
  (102 shorter events, 42.9 us)
Async XLA Ops:
  0.6 40.8 %copy-start = (bf16[128,512]{1,0:T(8,128)(2,1)S(1)}, bf16[128,512]{1,0:T(8,128)(2,1)}, u32[]{:S(2)}) copy-start(bf16[128,512]{1,0:T(8,128)(2,1)} %param.15) | copy-start | bytes 393220
  0.6 32.0 %copy-start.1 = (s32[8]{0:T(128)S(1)}, s32[8]{0:T(128)}, u32[]{:S(2)}) copy-start(s32[8]{0:T(128)} %constant.215.clone) | copy-start | bytes 100
  0.7 31.9 %copy-start.13 = (bf16[1024]{0:T(1024)(128)(2,1)S(1)}, bf16[1024]{0:T(1024)(128)(2,1)}, u32[]{:S(2)}) copy-start(bf16[1024]{0:T(1024)(128)(2,1)} %param.21) | copy-start | bytes 6148
  2.5 8.0 %collective-permute-start = (bf16[96,1024]{1,0:T(8,128)(2,1)S(1)}, bf16[96,1024]{1,0:T(8,128)(2,1)S(1)}, u32[]{:S(2)}, u32[]{:S(2)}) collective-permute-start(bf16[96,1024]{1,0:T(8,128)(2,1)S(1)} %constant_dynamic-update-slice_fusion), channel_id=1, source_target_pairs={{4,0},{5,1},{8,4},{9,5},{12,8},{13,9},{14,12},{15,13},{10,14},{11,... | collective-permute-start | bytes 589832 | tf_op jit(solution)/shard_map/ppermute | solution.py:80
  5.5 6.6 %collective-permute-start.3 = (bf16[96,1024]{1,0:T(8,128)(2,1)S(1)}, bf16[96,1024]{1,0:T(8,128)(2,1)S(1)}, u32[]{:S(2)}, u32[]{:S(2)}) collective-permute-start(bf16[96,1024]{1,0:T(8,128)(2,1)S(1)} %constant_dynamic-update-slice_fusion), channel_id=1, source_target_pairs={{0,4},{1,5},{4,8},{5,9},{8,12},{9,13},{12,14},{13,15},{14,10},{15,... | collective-permute-start | bytes 589832 | tf_op jit(solution)/shard_map/ppermute | solution.py:77
  10.5 6.1 %collective-permute-start.1 = (bf16[96,1024]{1,0:T(8,128)(2,1)S(1)}, bf16[96,1024]{1,0:T(8,128)(2,1)S(1)}, u32[]{:S(2)}, u32[]{:S(2)}) collective-permute-start(bf16[96,1024]{1,0:T(8,128)(2,1)S(1)} %collective-permute-done), channel_id=1, source_target_pairs={{4,0},{5,1},{8,4},{9,5},{12,8},{13,9},{14,12},{15,13},{10,14},{11,... | collective-permute-start | bytes 589832 | tf_op jit(solution)/shard_map/ppermute | solution.py:80
  12.1 5.8 %collective-permute-start.4 = (bf16[96,1024]{1,0:T(8,128)(2,1)S(1)}, bf16[96,1024]{1,0:T(8,128)(2,1)S(1)}, u32[]{:S(2)}, u32[]{:S(2)}) collective-permute-start(bf16[96,1024]{1,0:T(8,128)(2,1)S(1)} %collective-permute-done.3), channel_id=1, source_target_pairs={{0,4},{1,5},{4,8},{5,9},{8,12},{9,13},{12,14},{13,15},{14,10},{15,... | collective-permute-start | bytes 589832 | tf_op jit(solution)/shard_map/ppermute | solution.py:77
  16.5 8.1 %collective-permute-start.2 = (bf16[96,1024]{1,0:T(8,128)(2,1)S(1)}, bf16[96,1024]{1,0:T(8,128)(2,1)S(1)}, u32[]{:S(2)}, u32[]{:S(2)}) collective-permute-start(bf16[96,1024]{1,0:T(8,128)(2,1)S(1)} %collective-permute-done.1), channel_id=1, source_target_pairs={{4,0},{5,1},{8,4},{9,5},{12,8},{13,9},{14,12},{15,13},{10,14},{11,... | collective-permute-start | bytes 589832 | tf_op jit(solution)/shard_map/ppermute | solution.py:80
  17.9 6.1 %collective-permute-start.5 = (bf16[96,1024]{1,0:T(8,128)(2,1)S(1)}, bf16[96,1024]{1,0:T(8,128)(2,1)S(1)}, u32[]{:S(2)}, u32[]{:S(2)}) collective-permute-start(bf16[96,1024]{1,0:T(8,128)(2,1)S(1)} %collective-permute-done.4), channel_id=1, source_target_pairs={{0,4},{1,5},{4,8},{5,9},{8,12},{9,13},{12,14},{13,15},{14,10},{15,... | collective-permute-start | bytes 589832 | tf_op jit(solution)/shard_map/ppermute | solution.py:77
  24.0 5.7 %collective-permute-start.6 = (bf16[96,1024]{1,0:T(8,128)(2,1)S(1)}, bf16[96,1024]{1,0:T(8,128)(2,1)S(1)}, u32[]{:S(2)}, u32[]{:S(2)}) collective-permute-start(bf16[96,1024]{1,0:T(8,128)(2,1)S(1)} %collective-permute-done.5), channel_id=1, source_target_pairs={{0,4},{1,5},{4,8},{5,9},{8,12},{9,13},{12,14},{13,15},{14,10},{15,... | collective-permute-start | bytes 589832 | tf_op jit(solution)/shard_map/ppermute | solution.py:77
  32.6 4.1 %collective-permute-start.7 = (bf16[8,96,1024]{2,1,0:T(8,128)(2,1)S(1)}, bf16[8,96,1024]{2,1,0:T(8,128)(2,1)S(1)}, u32[]{:S(2)}, u32[]{:S(2)}) collective-permute-start(bf16[8,96,1024]{2,1,0:T(8,128)(2,1)S(1)} %get-tuple-element.13), channel_id=1, source_target_pairs={{0,1},{1,0},{2,3},{3,2},{4,5},{5,4},{6,7},{7,6},{8,9},{9,8},{10,11... | collective-permute-start | bytes 4718600 | tf_op jit(solution)/shard_map/ppermute | solution.py:83
  43.1 1.7 %copy-start.14 = (bf16[128]{0:T(256)(128)(2,1)S(1)}, bf16[128]{0:T(256)(128)(2,1)}, u32[]{:S(2)}) copy-start(bf16[128]{0:T(256)(128)(2,1)} %param.17) | copy-start | bytes 772
  43.1 2.3 %copy-start.8 = (bf16[128,512]{1,0:T(8,128)(2,1)S(1)}, bf16[128,512]{1,0:T(8,128)(2,1)}, u32[]{:S(2)}) copy-start(bf16[128,512]{1,0:T(8,128)(2,1)} %param.16) | copy-start | bytes 393220
  56.2 2.8 %copy-start.2 = (f32[1024,1024]{1,0:T(8,128)S(1)}, f32[1024,1024]{1,0:T(8,128)}, u32[]{:S(2)}) copy-start(f32[1024,1024]{1,0:T(8,128)} %convolution_add_fusion) | copy-start | bytes 12582916
  59.5 9.5 %copy-start.12 = (s32[8]{0:T(128)S(1)}, s32[8]{0:T(128)}, u32[]{:S(2)}) copy-start(s32[8]{0:T(128)} %constant.216.clone) | copy-start | bytes 100
  61.6 11.9 %collective-permute-start.8 = (f32[769,1024]{1,0:T(8,128)}, f32[769,1024]{1,0:T(8,128)}, u32[]{:S(2)}, u32[]{:S(2)}) collective-permute-start(f32[769,1024]{1,0:T(8,128)} %pad_maximum_fusion), channel_id=1, source_target_pairs={{0,1},{1,0},{2,3},{3,2},{4,5},{5,4},{6,7},{7,6},{8,9},{9,8},{10,11... | collective-permute-start | bytes 9449480 | tf_op jit(solution)/shard_map/ppermute | solution.py:105
  73.5 3.1 %copy-start.3 = (f32[1024,1024]{1,0:T(8,128)S(1)}, f32[1024,1024]{1,0:T(8,128)}, u32[]{:S(2)}) copy-start(f32[1024,1024]{1,0:T(8,128)} %convolution_add_fusion) | copy-start | bytes 12582916
  77.6 1.6 %copy-start.4 = (f32[8,96,1024]{2,1,0:T(8,128)}, f32[8,96,1024]{2,1,0:T(8,128)S(1)}, u32[]{:S(2)}) copy-start(f32[8,96,1024]{2,1,0:T(8,128)S(1)} %fusion.3) | copy-start | bytes 9437188
  79.3 27.9 %copy-start.5 = (f32[8,96,1024]{2,1,0:T(8,128)S(1)}, f32[8,96,1024]{2,1,0:T(8,128)}, u32[]{:S(2)}) copy-start(f32[8,96,1024]{2,1,0:T(8,128)} %copy-done.4) | copy-start | bytes 9437188
  81.2 12.1 %collective-permute-start.9 = (f32[97,1024]{1,0:T(8,128)}, f32[97,1024]{1,0:T(8,128)}, u32[]{:S(2)}, u32[]{:S(2)}) collective-permute-start(f32[97,1024]{1,0:T(8,128)} %get-tuple-element.29), channel_id=1, source_target_pairs={{0,4},{1,5},{4,8},{5,9},{8,12},{9,13},{12,14},{13,15},{14,10},{15,... | collective-permute-start | bytes 1191944 | tf_op jit(solution)/shard_map/ppermute | solution.py:117
  83.5 17.0 %collective-permute-start.13 = (f32[97,1024]{1,0:T(8,128)}, f32[97,1024]{1,0:T(8,128)}, u32[]{:S(2)}, u32[]{:S(2)}) collective-permute-start(f32[97,1024]{1,0:T(8,128)} %get-tuple-element.30), channel_id=1, source_target_pairs={{4,0},{5,1},{8,4},{9,5},{12,8},{13,9},{14,12},{15,13},{10,14},{11,... | collective-permute-start | bytes 1191944 | tf_op jit(solution)/shard_map/ppermute | solution.py:125
  96.0 11.2 %collective-permute-start.10 = (f32[97,1024]{1,0:T(8,128)}, f32[97,1024]{1,0:T(8,128)}, u32[]{:S(2)}, u32[]{:S(2)}) collective-permute-start(f32[97,1024]{1,0:T(8,128)} %pad_maximum_fusion.3), channel_id=1, source_target_pairs={{0,4},{1,5},{4,8},{5,9},{8,12},{9,13},{12,14},{13,15},{14,10},{15,... | collective-permute-start | bytes 1191944 | tf_op jit(solution)/shard_map/ppermute | solution.py:117
  109.3 10.3 %collective-permute-start.14 = (f32[97,1024]{1,0:T(8,128)}, f32[97,1024]{1,0:T(8,128)}, u32[]{:S(2)}, u32[]{:S(2)}) collective-permute-start(f32[97,1024]{1,0:T(8,128)} %pad_maximum_fusion.6), channel_id=1, source_target_pairs={{4,0},{5,1},{8,4},{9,5},{12,8},{13,9},{14,12},{15,13},{10,14},{11,... | collective-permute-start | bytes 1191944 | tf_op jit(solution)/shard_map/ppermute | solution.py:125
  111.6 8.0 %copy-start.9 = (f32[1,1024]{1,0:T(1,128)}, f32[1,1024]{1,0:T(1,128)S(1)}, u32[]{:S(2)}) copy-start(f32[1,1024]{1,0:T(1,128)S(1)} %slice.93) | copy-start | bytes 12292
  112.4 10.0 %collective-permute-start.11 = (f32[97,1024]{1,0:T(8,128)}, f32[97,1024]{1,0:T(8,128)}, u32[]{:S(2)}, u32[]{:S(2)}) collective-permute-start(f32[97,1024]{1,0:T(8,128)} %pad_maximum_fusion.4), channel_id=1, source_target_pairs={{0,4},{1,5},{4,8},{5,9},{8,12},{9,13},{12,14},{13,15},{14,10},{15,... | collective-permute-start | bytes 1191944 | tf_op jit(solution)/shard_map/ppermute | solution.py:117
  120.4 7.3 %copy-start.10 = (f32[1,1024]{1,0:T(1,128)}, f32[1,1024]{1,0:T(1,128)S(1)}, u32[]{:S(2)}) copy-start(f32[1,1024]{1,0:T(1,128)S(1)} %slice.100) | copy-start | bytes 12292
  120.4 25.0 %copy-start.7 = (f32[64,1024]{1,0:T(8,128)S(1)}, f32[64,1024]{1,0:T(8,128)}, u32[]{:S(2)}) copy-start(f32[64,1024]{1,0:T(8,128)} %param.23) | copy-start | bytes 786436
  124.5 9.1 %collective-permute-start.15 = (f32[97,1024]{1,0:T(8,128)}, f32[97,1024]{1,0:T(8,128)}, u32[]{:S(2)}, u32[]{:S(2)}) collective-permute-start(f32[97,1024]{1,0:T(8,128)} %pad_maximum_fusion.7), channel_id=1, source_target_pairs={{4,0},{5,1},{8,4},{9,5},{12,8},{13,9},{14,12},{15,13},{10,14},{11,... | collective-permute-start | bytes 1191944 | tf_op jit(solution)/shard_map/ppermute | solution.py:125
  126.9 1.2 copy-start.11
  127.7 8.8 %collective-permute-start.12 = (f32[97,1024]{1,0:T(8,128)}, f32[97,1024]{1,0:T(8,128)}, u32[]{:S(2)}, u32[]{:S(2)}) collective-permute-start(f32[97,1024]{1,0:T(8,128)} %pad_maximum_fusion.5), channel_id=1, source_target_pairs={{0,4},{1,5},{4,8},{5,9},{8,12},{9,13},{12,14},{13,15},{14,10},{15,... | collective-permute-start | bytes 1191944 | tf_op jit(solution)/shard_map/ppermute | solution.py:117
  137.7 0.8 copy-start.6

commit v3 on v2

--- a/solution.py
+++ b/solution.py
@@ -89,57 +89,55 @@
     return jnp.take(both, index, axis=0)
 
 
-def ring_reduce_scatter(blocks, extra, n_blk):
+def ring_reduce_scatter(summed, extra, n_blk):
     chips, snake, place, cw, ccw, partner = ring_plan(n_blk)
     ahead = chips // 2
     behind = chips - 1 - ahead
-    rows = blocks.shape[1]
     position = lax.axis_index("blk")
-    core, chip = position % 2, position // 2
+    chip = position // 2
     spot = jnp.asarray(place, jnp.int32)[chip]
     order = jnp.asarray(snake, jnp.int32)
-    pairs = blocks.reshape(chips, 2, rows, blocks.shape[2])
-    kept = lax.dynamic_index_in_dim(pairs, core, 1, keepdims=False)
-    given = lax.dynamic_index_in_dim(pairs, 1 - core, 1, keepdims=False)
-    sent = jnp.concatenate([given.reshape(chips * rows, -1), extra[None]], axis=0)
-    got = lax.ppermute(sent, "blk", partner)
-    summed = kept + got[: chips * rows].reshape(chips, rows, -1)
-    chip_extra = extra + got[chips * rows]
 
     def block_at(k):
         return lax.dynamic_index_in_dim(summed, order[(spot + k) % chips], 0, keepdims=False)
 
     rel = [None] * chips
-    rel[0] = chip_extra
+    rel[0] = extra
     acc = block_at(ahead)
-    carried = chip_extra
+    carried = extra
     for s in range(1, ahead + 1):
-        got = lax.ppermute(jnp.concatenate([acc, carried[None]], axis=0), "blk", cw)
-        acc = got[:rows] + block_at(ahead - s)
-        carried = got[rows]
+        acc = lax.ppermute(acc, "blk", cw) + block_at(ahead - s)
+        carried = lax.ppermute(carried, "blk", cw)
         rel[chips - s] = carried
     if behind:
         acc_back = block_at(chips - behind)
-        carried = chip_extra
+        carried = extra
         for s in range(1, behind + 1):
-            got = lax.ppermute(jnp.concatenate([acc_back, carried[None]], axis=0), "blk", ccw)
-            carried = got[rows]
+            acc_back = lax.ppermute(acc_back, "blk", ccw)
+            carried = lax.ppermute(carried, "blk", ccw)
             rel[s] = carried
             if s < behind:
-                acc_back = got[:rows] + block_at(chips - behind + s)
-            else:
-                acc = acc + got[:rows]
+                acc_back = acc_back + block_at(chips - behind + s)
+        acc = acc + acc_back
     by_rel = jnp.stack(rel)
     k = (jnp.asarray(place, jnp.int32) - spot) % chips
     by_chip = jnp.take(by_rel, k, axis=0)
     return acc, jnp.sum(by_chip, axis=0)
 
 
+def slots_product(left, right):
+    return lax.dot_general(
+        left, right, (((0,), (0,)), ((), ())), preferred_element_type=jnp.float32
+    )
+
+
 def per_device(
     paths, deltas, payoffs, counts, w_first, w_second, w_out, mom_first, mom_second, mom_out,
     n_blk,
 ):
+    chips, snake, place, cw, ccw, partner = ring_plan(n_blk)
     position = lax.axis_index("blk")
+    core = position % 2
     rows_dev = paths.shape[0]
     r_one, r_two = w_first.shape[0], w_second.shape[0]
     hidden = w_first.shape[1]
@@ -153,16 +151,23 @@
     e_slope, g_one, e_aone, e_cone, g_two, h_one, e_atwo, grad_three = twin_terms(
         x_rows, z_rows, y_rows, mask, w_one, w_two, w_out
     )
-    part_one = rows_product(x_rows, e_aone) + rows_product(e_slope, g_one)
-    part_two = rows_product(e_cone, g_two) + rows_product(h_one, e_atwo)
-    blocks = jnp.concatenate(
-        [
-            part_one.reshape(n_blk, r_one, hidden),
-            part_two.reshape(n_blk, r_two, hidden),
-        ],
-        axis=1,
-    )
-    reduced, grad_out = ring_reduce_scatter(blocks, grad_three, n_blk)
+    a_all = jnp.concatenate([x_rows, e_slope], axis=0).reshape(2 * rows_dev, chips, 2, r_one)
+    c_all = jnp.concatenate([e_cone, h_one], axis=0).reshape(2 * rows_dev, chips, 2, r_two)
+    b_me = jnp.concatenate([e_aone, g_one], axis=0)
+    d_me = jnp.concatenate([g_two, e_atwo], axis=0)
+    a_keep = lax.dynamic_index_in_dim(a_all, core, 2, keepdims=False)
+    a_give = lax.dynamic_index_in_dim(a_all, 1 - core, 2, keepdims=False)
+    c_keep = lax.dynamic_index_in_dim(c_all, core, 2, keepdims=False)
+    c_give = lax.dynamic_index_in_dim(c_all, 1 - core, 2, keepdims=False)
+    a_got = lax.ppermute(a_give, "blk", partner)
+    b_got = lax.ppermute(b_me, "blk", partner)
+    c_got = lax.ppermute(c_give, "blk", partner)
+    d_got = lax.ppermute(d_me, "blk", partner)
+    extra = grad_three + lax.ppermute(grad_three, "blk", partner)
+    part_one = slots_product(a_keep, b_me) + slots_product(a_got, b_got)
+    part_two = slots_product(c_keep, d_me) + slots_product(c_got, d_got)
+    summed = jnp.concatenate([part_one, part_two], axis=1)
+    reduced, grad_out = ring_reduce_scatter(summed, extra, n_blk)
     grad_one = reduced[:r_one]
     grad_two = reduced[r_one:]
     new_first = 0.8 * mom_first + 0.2 * normalized(grad_one)

time: 150 us -> 140 us (0.933)
  local copies, waits for them, and re-layouts: 26.8 us -> 15.9 us
  waiting for transfers between devices: 40.5 us -> 48.9 us
  starting transfers between devices: 15.1 us -> 22.6 us
  matrix products: 16.3 us -> 8.95 us
  other arithmetic: 26.2 us -> 19.2 us
    ppermute x8 -> x19, waiting for transfers between devices: 24 us -> 32.4 us  [the longest x4 25 us: ring_reduce_scatter(): acc = lax.ppermute(acc, 'blk', cw) + block_at(ahead - s)]
    slice x8 -> x0, local copies, waits for them, and re-layouts: 7.74 us -> none  [the longest x7 5.33 us: ring_reduce_scatter(): carried = got[rows]]
    ppermute x8 -> x19, starting transfers between devices: 7.24 us -> 14.8 us  [the longest x3 4.71 us: ring_reduce_scatter(): carried = lax.ppermute(carried, 'blk', ccw)]
    concatenate x8 -> x4, other arithmetic: 7.52 us -> 0.91 us  [the longest x1 0.82 us: per_device(): d_me = jnp.concatenate([g_two, e_atwo], axis=0)]
    dot_general x4 -> x5, matrix products: 9.77 us -> 4.46 us  [the longest x4 3.57 us: slots_product(): lax.dot_general(left, right, (((0,), (0,)), ((), ())), preferred_element_...]
    unnamed x38 -> x32, local copies, waits for them, and re-layouts: 9.55 us -> 6.51 us
    add x6, other arithmetic: 6.72 us -> 9.4 us  [the longest x3 5.79 us: ring_reduce_scatter(): acc = lax.ppermute(acc, 'blk', cw) + block_at(ahead - s)]
  transfers between devices with their start and end apart: 16 -> 27, of which waited for: 10 -> 15; matrix products, arithmetic and copies ran while one was open for 11% -> 13% of each run, Pallas kernels for 0% -> 0%
where the time goes in v3:
time: 140 us; the launch traced here: 139 us
  waiting for transfers between devices  48.9 us (35%)
  between operations  23.3 us (17%)
  starting transfers between devices  22.6 us (16%)
  other arithmetic  19.2 us (14%)
  local copies, waits for them, and re-layouts  15.9 us (11%)
  matrix products  8.95 us (6%)
    ppermute x4, waiting for transfers between devices, ring_reduce_scatter(): acc = lax.ppermute(acc, 'blk', cw) + block_at(ahead - s)  25 us
    ppermute x4, waiting for transfers between devices, ring_all_gather(): left = lax.ppermute(left, 'blk', cw)  9.08 us
    ppermute x3, waiting for transfers between devices, ring_all_gather(): right = lax.ppermute(right, 'blk', ccw)  7.49 us
    unnamed x32, local copies, waits for them, and re-layouts  6.51 us
    ppermute x3, starting transfers between devices, ring_all_gather(): right = lax.ppermute(right, 'blk', ccw)  6.07 us
    add x3, other arithmetic, ring_reduce_scatter(): acc = lax.ppermute(acc, 'blk', cw) + block_at(ahead - s)  5.79 us
    ppermute x3, starting transfers between devices, ring_reduce_scatter(): carried = lax.ppermute(carried, 'blk', ccw)  4.71 us
    ppermute x3, starting transfers between devices, ring_reduce_scatter(): acc_back = lax.ppermute(acc_back, 'blk', ccw)  4.42 us
  transfers between devices with their start and end apart: 27, of which 15 were waited for; matrix products, arithmetic and copies ran while one was open for 13% of the time, Pallas kernels for 0%

profile of v3, /device:TPU:0, one launch (start us, length us, event | category | flops | bytes accessed | tf_op | source)
XLA Modules:
  0.0 138.9 jit_solution(15437460640053023895)
XLA Ops:
  2.5 3.0 %collective-permute-start = (bf16[96,1024]{1,0:T(8,128)(2,1)S(1)}, bf16[96,1024]{1,0:T(8,128)(2,1)S(1)}, u32[]{:S(2)}, u32[]{:S(2)}) collective-permute-start(bf16[96,1024]{1,0:T(8,128)(2,1)S(1)} %constant_dynamic-update-slice_fusion), channel_id=1, source_target_pairs={{4,0},{5,1},{8,4},{9,5},{12,8},{13,9},{14,12},{15,13},{10,14},{11,... | collective-permute-start | bytes 589832 | tf_op jit(solution)/shard_map/ppermute | solution.py:80
  6.3 4.1 %collective-permute-done = bf16[96,1024]{1,0:T(8,128)(2,1)S(1)} collective-permute-done((bf16[96,1024]{1,0:T(8,128)(2,1)S(1)}, bf16[96,1024]{1,0:T(8,128)(2,1)S(1)}, u32[]{:S(2)}, u32[]{:S(2)}) %collective-permute-start) | collective-permute-done | bytes 196640 | tf_op jit(solution)/shard_map/ppermute | solution.py:80
  10.4 1.7 %collective-permute-start.1 = (bf16[96,1024]{1,0:T(8,128)(2,1)S(1)}, bf16[96,1024]{1,0:T(8,128)(2,1)S(1)}, u32[]{:S(2)}, u32[]{:S(2)}) collective-permute-start(bf16[96,1024]{1,0:T(8,128)(2,1)S(1)} %collective-permute-done), channel_id=1, source_target_pairs={{4,0},{5,1},{8,4},{9,5},{12,8},{13,9},{14,12},{15,13},{10,14},{11,... | collective-permute-start | bytes 589832 | tf_op jit(solution)/shard_map/ppermute | solution.py:80
  13.2 3.4 %collective-permute-done.1 = bf16[96,1024]{1,0:T(8,128)(2,1)S(1)} collective-permute-done((bf16[96,1024]{1,0:T(8,128)(2,1)S(1)}, bf16[96,1024]{1,0:T(8,128)(2,1)S(1)}, u32[]{:S(2)}, u32[]{:S(2)}) %collective-permute-start.1) | collective-permute-done | bytes 196640 | tf_op jit(solution)/shard_map/ppermute | solution.py:80
  16.5 1.4 collective-permute-start.2
  19.3 4.7 %collective-permute-done.5 = bf16[96,1024]{1,0:T(8,128)(2,1)S(1)} collective-permute-done((bf16[96,1024]{1,0:T(8,128)(2,1)S(1)}, bf16[96,1024]{1,0:T(8,128)(2,1)S(1)}, u32[]{:S(2)}, u32[]{:S(2)}) %collective-permute-start.5) | collective-permute-done | bytes 196640 | tf_op jit(solution)/shard_map/ppermute | solution.py:77
  25.3 4.3 %collective-permute-done.6 = bf16[96,1024]{1,0:T(8,128)(2,1)S(1)} collective-permute-done((bf16[96,1024]{1,0:T(8,128)(2,1)S(1)}, bf16[96,1024]{1,0:T(8,128)(2,1)S(1)}, u32[]{:S(2)}, u32[]{:S(2)}) %collective-permute-start.6) | collective-permute-done | bytes 196640 | tf_op jit(solution)/shard_map/ppermute | solution.py:77
  47.7 1.3 constant_dynamic-update-slice_fusion.2
  49.0 2.6 %gather_fusion.1 = bf16[16,96,1024]{2,1,0:T(8,128)(2,1)S(1)} fusion(bf16[16,96,1024]{2,1,0:T(8,128)(2,1)} %constant_dynamic-update-slice_fusion.2, s32[1024]{0:T(1024)S(1)} %pad_clamp_fusion.1), kind=kCustom, calls=%fused_computation.1 | custom fusion | bytes 6291520 | tf_op jit(solution)/shard_map/jit(_take)/gather | solution.py:89
  56.8 1.5 %add_reduce_fusion = (f32[1024]{0:T(1024)}, bf16[128,1024]{1,0:T(8,128)(2,1)S(1)}) fusion(f32[128,1024]{1,0:T(8,128)S(1)} %get-tuple-element.39, f32[128]{0:T(128)S(1)} %subtract_multiply_fusion, f32[1024]{0:T(1024)S(1)} %convert_element_type.33, bf16[128,1024]{1,0:T(8,128)(2,1)S(1)} %get-tuple-element.42, bf16[1024,1024]{1,0:T(8,128)(2,1)S(1)} %bitcast.128), kind=kOutput, calls=%fused_computation.41 | convolution fusion | flops 271186944 | bytes 3154432 | tf_op jit(solution)/shard_map/dot_general | solution.py:37
  62.6 1.3 convolution_add_fusion.1
  63.9 1.5 %convolution_add_fusion = f32[8,64,1024]{2,1,0:T(8,128)S(1)} fusion(f32[8,64,1024]{2,1,0:T(8,128)S(1)} %fusion.6, bf16[256,8,64]{0,2,1:T(8,128)(2,1)S(1)} %collective-permute-done.10, bf16[256,1024]{1,0:T(8,128)(2,1)} %collective-permute-done.11), kind=kOutput, calls=%fused_computation.20 | convolution fusion | flops 268959744 | bytes 4980736 | tf_op jit(solution)/shard_map/dot_general | solution.py:129
  68.7 9.3 %collective-permute-done.12 = f32[96,1024]{1,0:T(8,128)} collective-permute-done((f32[96,1024]{1,0:T(8,128)}, f32[96,1024]{1,0:T(8,128)}, u32[]{:S(2)}, u32[]{:S(2)}) %collective-permute-start.12) | collective-permute-done | bytes 393248 | tf_op jit(solution)/shard_map/ppermute | solution.py:109
  78.0 1.8 %fusion.18 = f32[96,1024]{1,0:T(8,128)} fusion(f32[96,1024]{1,0:T(8,128)} %collective-permute-done.12, s32[]{:T(128)S(6)} %select_n.247, f32[8,64,1024]{2,1,0:T(8,128)S(1)} %convolution_add_fusion, f32[8,32,1024]{2,1,0:T(8,128)S(1)} %convolution_add_fusion.1), kind=kLoop, calls=%fused_computation.56 | loop fusion | flops 196608 | bytes 3932164 | tf_op jit(solution)/shard_map/add | solution.py:109
  82.2 1.4 %collective-permute-start.16 = (f32[96,1024]{1,0:T(8,128)S(1)}, f32[96,1024]{1,0:T(8,128)}, u32[]{:S(2)}, u32[]{:S(2)}) collective-permute-start(f32[96,1024]{1,0:T(8,128)S(1)} %get-tuple-element.8), channel_id=1, source_target_pairs={{4,0},{5,1},{8,4},{9,5},{12,8},{13,9},{14,12},{15,13},{10,14},{11,... | collective-permute-start | bytes 1179656 | tf_op jit(solution)/shard_map/ppermute | solution.py:116
  83.7 7.2 %collective-permute-done.13 = f32[96,1024]{1,0:T(8,128)} collective-permute-done((f32[96,1024]{1,0:T(8,128)}, f32[96,1024]{1,0:T(8,128)}, u32[]{:S(2)}, u32[]{:S(2)}) %collective-permute-start.13) | collective-permute-done | bytes 393248 | tf_op jit(solution)/shard_map/ppermute | solution.py:109
  90.9 1.8 %fusion.21 = f32[96,1024]{1,0:T(8,128)} fusion(f32[96,1024]{1,0:T(8,128)} %collective-permute-done.13, s32[]{:T(128)S(6)} %select_n.250, f32[8,64,1024]{2,1,0:T(8,128)S(1)} %convolution_add_fusion, f32[8,32,1024]{2,1,0:T(8,128)S(1)} %convolution_add_fusion.1), kind=kLoop, calls=%fused_computation.59 | loop fusion | flops 196608 | bytes 3932164 | tf_op jit(solution)/shard_map/add | solution.py:109
  97.0 5.8 %collective-permute-done.14 = f32[96,1024]{1,0:T(8,128)} collective-permute-done((f32[96,1024]{1,0:T(8,128)}, f32[96,1024]{1,0:T(8,128)}, u32[]{:S(2)}, u32[]{:S(2)}) %collective-permute-start.14) | collective-permute-done | bytes 393248 | tf_op jit(solution)/shard_map/ppermute | solution.py:109
  102.8 2.1 %fusion.24 = (f32[96,1024]{1,0:T(8,128)}, f32[96,1024]{1,0:T(8,128)}) fusion(f32[96,1024]{1,0:T(8,128)} %collective-permute-done.14, s32[]{:T(128)S(6)} %select_n.253, f32[8,64,1024]{2,1,0:T(8,128)S(1)} %convolution_add_fusion, f32[8,32,1024]{2,1,0:T(8,128)S(1)} %convolution_add_fusion.1, f32[96,1024]{1,0:T(8,128)} %collective-permute-done.16, s32[]{:T(128)S(6)} %select_n.262), kind=kLoop, calls=%fused_computation.62 | loop fusion | flops 393216 | bytes 4718600 | tf_op jit(solution)/shard_map/add | solution.py:109
  104.9 1.6 %collective-permute-start.17 = (f32[96,1024]{1,0:T(8,128)}, f32[96,1024]{1,0:T(8,128)}, u32[]{:S(2)}, u32[]{:S(2)}) collective-permute-start(f32[96,1024]{1,0:T(8,128)} %get-tuple-element.6), channel_id=1, source_target_pairs={{4,0},{5,1},{8,4},{9,5},{12,8},{13,9},{14,12},{15,13},{10,14},{11,... | collective-permute-start | bytes 1179656 | tf_op jit(solution)/shard_map/ppermute | solution.py:116
  106.5 1.4 collective-permute-done.19
  109.0 1.6 %collective-permute-start.20 = (f32[1024]{0:T(1024)S(1)}, f32[1024]{0:T(1024)S(1)}, u32[]{:S(2)}, u32[]{:S(2)}) collective-permute-start(f32[1024]{0:T(1024)S(1)} %add.364), channel_id=1, source_target_pairs={{4,0},{5,1},{8,4},{9,5},{12,8},{13,9},{14,12},{15,13},{10,14},{11,... | collective-permute-start | bytes 12296 | tf_op jit(solution)/shard_map/ppermute | solution.py:117
  110.6 1.6 %collective-permute-done.23 = f32[1024]{0:T(1024)S(1)} collective-permute-done((f32[1024]{0:T(1024)S(1)}, f32[1024]{0:T(1024)S(1)}, u32[]{:S(2)}, u32[]{:S(2)}) %collective-permute-start.23) | collective-permute-done | bytes 4128 | tf_op jit(solution)/shard_map/ppermute | solution.py:110
  112.6 1.5 %collective-permute-done.20 = f32[1024]{0:T(1024)S(1)} collective-permute-done((f32[1024]{0:T(1024)S(1)}, f32[1024]{0:T(1024)S(1)}, u32[]{:S(2)}, u32[]{:S(2)}) %collective-permute-start.20) | collective-permute-done | bytes 4128 | tf_op jit(solution)/shard_map/ppermute | solution.py:117
  114.1 1.6 %collective-permute-start.21 = (f32[1024]{0:T(1024)S(1)}, f32[1024]{0:T(1024)S(1)}, u32[]{:S(2)}, u32[]{:S(2)}) collective-permute-start(f32[1024]{0:T(1024)S(1)} %collective-permute-done.20), channel_id=1, source_target_pairs={{4,0},{5,1},{8,4},{9,5},{12,8},{13,9},{14,12},{15,13},{10,14},{11,... | collective-permute-start | bytes 12296 | tf_op jit(solution)/shard_map/ppermute | solution.py:117
  116.2 1.2 compare_and_fusion
  117.8 1.6 %collective-permute-start.22 = (f32[1024]{0:T(1024)S(1)}, f32[1024]{0:T(1024)S(1)}, u32[]{:S(2)}, u32[]{:S(2)}) collective-permute-start(f32[1024]{0:T(1024)S(1)} %collective-permute-done.21), channel_id=1, source_target_pairs={{4,0},{5,1},{8,4},{9,5},{12,8},{13,9},{14,12},{15,13},{10,14},{11,... | collective-permute-start | bytes 12296 | tf_op jit(solution)/shard_map/ppermute | solution.py:117
  123.7 1.2 gather_fusion.2
  125.6 1.8 %fusion.13 = f32[96,1024]{1,0:T(8,128)} fusion(f32[96,1024]{1,0:T(8,128)} %collective-permute-done.17, s32[]{:T(128)S(6)} %select_n.265, f32[8,64,1024]{2,1,0:T(8,128)S(1)} %convolution_add_fusion, f32[8,32,1024]{2,1,0:T(8,128)S(1)} %convolution_add_fusion.1), kind=kLoop, calls=%fused_computation.51 | loop fusion | flops 196608 | bytes 3932164 | tf_op jit(solution)/shard_map/add | solution.py:120
  127.4 1.4 %collective-permute-start.18 = (f32[96,1024]{1,0:T(8,128)}, f32[96,1024]{1,0:T(8,128)}, u32[]{:S(2)}, u32[]{:S(2)}) collective-permute-start(f32[96,1024]{1,0:T(8,128)} %fusion.13), channel_id=1, source_target_pairs={{4,0},{5,1},{8,4},{9,5},{12,8},{13,9},{14,12},{15,13},{10,14},{11,... | collective-permute-start | bytes 1179656 | tf_op jit(solution)/shard_map/ppermute | solution.py:116
  130.8 2.8 %collective-permute-done.15 = f32[96,1024]{1,0:T(8,128)S(1)} collective-permute-done((f32[96,1024]{1,0:T(8,128)}, f32[96,1024]{1,0:T(8,128)S(1)}, u32[]{:S(2)}, u32[]{:S(2)}) %collective-permute-start.15) | collective-permute-done | bytes 393248 | tf_op jit(solution)/shard_map/ppermute | solution.py:109
  133.6 2.4 %collective-permute-done.18 = f32[96,1024]{1,0:T(8,128)} collective-permute-done((f32[96,1024]{1,0:T(8,128)}, f32[96,1024]{1,0:T(8,128)}, u32[]{:S(2)}, u32[]{:S(2)}) %collective-permute-start.18) | collective-permute-done | bytes 393248 | tf_op jit(solution)/shard_map/ppermute | solution.py:116
  (112 shorter events, 33.7 us)
Async XLA Ops:
  0.6 43.0 %copy-start = (s32[16,16]{1,0:T(8,128)S(1)}, s32[16,16]{1,0:T(8,128)}, u32[]{:S(2)}) copy-start(s32[16,16]{1,0:T(8,128)} %param.18) | copy-start | bytes 3076
  0.6 31.8 %copy-start.1 = (s32[8]{0:T(128)S(1)}, s32[8]{0:T(128)}, u32[]{:S(2)}) copy-start(s32[8]{0:T(128)} %constant.221.clone) | copy-start | bytes 100
  0.7 39.0 %copy-start.7 = (s32[8]{0:T(128)S(1)}, s32[8]{0:T(128)}, u32[]{:S(2)}) copy-start(s32[8]{0:T(128)} %constant.222.clone) | copy-start | bytes 100
  0.7 42.9 %copy-start.10 = (bf16[1024]{0:T(1024)(128)(2,1)S(1)}, bf16[1024]{0:T(1024)(128)(2,1)}, u32[]{:S(2)}) copy-start(bf16[1024]{0:T(1024)(128)(2,1)} %param.21) | copy-start | bytes 6148
  2.5 8.0 %collective-permute-start = (bf16[96,1024]{1,0:T(8,128)(2,1)S(1)}, bf16[96,1024]{1,0:T(8,128)(2,1)S(1)}, u32[]{:S(2)}, u32[]{:S(2)}) collective-permute-start(bf16[96,1024]{1,0:T(8,128)(2,1)S(1)} %constant_dynamic-update-slice_fusion), channel_id=1, source_target_pairs={{4,0},{5,1},{8,4},{9,5},{12,8},{13,9},{14,12},{15,13},{10,14},{11,... | collective-permute-start | bytes 589832 | tf_op jit(solution)/shard_map/ppermute | solution.py:80
  5.5 6.6 %collective-permute-start.3 = (bf16[96,1024]{1,0:T(8,128)(2,1)S(1)}, bf16[96,1024]{1,0:T(8,128)(2,1)S(1)}, u32[]{:S(2)}, u32[]{:S(2)}) collective-permute-start(bf16[96,1024]{1,0:T(8,128)(2,1)S(1)} %constant_dynamic-update-slice_fusion), channel_id=1, source_target_pairs={{0,4},{1,5},{4,8},{5,9},{8,12},{9,13},{12,14},{13,15},{14,10},{15,... | collective-permute-start | bytes 589832 | tf_op jit(solution)/shard_map/ppermute | solution.py:77
  10.4 6.1 %collective-permute-start.1 = (bf16[96,1024]{1,0:T(8,128)(2,1)S(1)}, bf16[96,1024]{1,0:T(8,128)(2,1)S(1)}, u32[]{:S(2)}, u32[]{:S(2)}) collective-permute-start(bf16[96,1024]{1,0:T(8,128)(2,1)S(1)} %collective-permute-done), channel_id=1, source_target_pairs={{4,0},{5,1},{8,4},{9,5},{12,8},{13,9},{14,12},{15,13},{10,14},{11,... | collective-permute-start | bytes 589832 | tf_op jit(solution)/shard_map/ppermute | solution.py:80
  12.1 5.8 %collective-permute-start.4 = (bf16[96,1024]{1,0:T(8,128)(2,1)S(1)}, bf16[96,1024]{1,0:T(8,128)(2,1)S(1)}, u32[]{:S(2)}, u32[]{:S(2)}) collective-permute-start(bf16[96,1024]{1,0:T(8,128)(2,1)S(1)} %collective-permute-done.3), channel_id=1, source_target_pairs={{0,4},{1,5},{4,8},{5,9},{8,12},{9,13},{12,14},{13,15},{14,10},{15,... | collective-permute-start | bytes 589832 | tf_op jit(solution)/shard_map/ppermute | solution.py:77
  16.5 8.1 %collective-permute-start.2 = (bf16[96,1024]{1,0:T(8,128)(2,1)S(1)}, bf16[96,1024]{1,0:T(8,128)(2,1)S(1)}, u32[]{:S(2)}, u32[]{:S(2)}) collective-permute-start(bf16[96,1024]{1,0:T(8,128)(2,1)S(1)} %collective-permute-done.1), channel_id=1, source_target_pairs={{4,0},{5,1},{8,4},{9,5},{12,8},{13,9},{14,12},{15,13},{10,14},{11,... | collective-permute-start | bytes 589832 | tf_op jit(solution)/shard_map/ppermute | solution.py:80
  17.9 6.1 %collective-permute-start.5 = (bf16[96,1024]{1,0:T(8,128)(2,1)S(1)}, bf16[96,1024]{1,0:T(8,128)(2,1)S(1)}, u32[]{:S(2)}, u32[]{:S(2)}) collective-permute-start(bf16[96,1024]{1,0:T(8,128)(2,1)S(1)} %collective-permute-done.4), channel_id=1, source_target_pairs={{0,4},{1,5},{4,8},{5,9},{8,12},{9,13},{12,14},{13,15},{14,10},{15,... | collective-permute-start | bytes 589832 | tf_op jit(solution)/shard_map/ppermute | solution.py:77
  24.0 5.7 %collective-permute-start.6 = (bf16[96,1024]{1,0:T(8,128)(2,1)S(1)}, bf16[96,1024]{1,0:T(8,128)(2,1)S(1)}, u32[]{:S(2)}, u32[]{:S(2)}) collective-permute-start(bf16[96,1024]{1,0:T(8,128)(2,1)S(1)} %collective-permute-done.5), channel_id=1, source_target_pairs={{0,4},{1,5},{4,8},{5,9},{8,12},{9,13},{12,14},{13,15},{14,10},{15,... | collective-permute-start | bytes 589832 | tf_op jit(solution)/shard_map/ppermute | solution.py:77
  32.5 15.2 %collective-permute-start.7 = (bf16[8,96,1024]{2,1,0:T(8,128)(2,1)S(1)}, bf16[8,96,1024]{2,1,0:T(8,128)(2,1)S(1)}, u32[]{:S(2)}, u32[]{:S(2)}) collective-permute-start(bf16[8,96,1024]{2,1,0:T(8,128)(2,1)S(1)} %get-tuple-element.13), channel_id=1, source_target_pairs={{0,1},{1,0},{2,3},{3,2},{4,5},{5,4},{6,7},{7,6},{8,9},{9,8},{10,11... | collective-permute-start | bytes 4718600 | tf_op jit(solution)/shard_map/ppermute | solution.py:83
  60.0 2.5 %collective-permute-start.9 = (bf16[256,1024]{1,0:T(8,128)(2,1)S(1)}, bf16[256,1024]{1,0:T(8,128)(2,1)}, u32[]{:S(2)}, u32[]{:S(2)}) collective-permute-start(bf16[256,1024]{1,0:T(8,128)(2,1)S(1)} %pad_maximum_fusion), channel_id=1, source_target_pairs={{0,1},{1,0},{2,3},{3,2},{4,5},{5,4},{6,7},{7,6},{8,9},{9,8},{10,11... | collective-permute-start | bytes 1572872 | tf_op jit(solution)/shard_map/ppermute | solution.py:163
  60.8 1.8 %collective-permute-start.8 = (bf16[256,8,32]{0,2,1:T(8,128)(2,1)S(1)}, bf16[256,8,32]{0,2,1:T(8,128)(2,1)S(1)}, u32[]{:S(2)}, u32[]{:S(2)}) collective-permute-start(bf16[256,8,32]{0,2,1:T(8,128)(2,1)S(1)} %dynamic-slice_bitcast_fusion.1), channel_id=1, source_target_pairs={{0,1},{1,0},{2,3},{3,2},{4,5},{5,4},{6,7},{7,6},{8,9},{9,8},{10,11... | collective-permute-start | bytes 393224 | tf_op jit(solution)/shard_map/ppermute | solution.py:162
  60.9 3.1 %collective-permute-start.11 = (bf16[256,1024]{1,0:T(8,128)(2,1)}, bf16[256,1024]{1,0:T(8,128)(2,1)}, u32[]{:S(2)}, u32[]{:S(2)}) collective-permute-start(bf16[256,1024]{1,0:T(8,128)(2,1)} %pad_maximum_fusion.2), channel_id=1, source_target_pairs={{0,1},{1,0},{2,3},{3,2},{4,5},{5,4},{6,7},{7,6},{8,9},{9,8},{10,11... | collective-permute-start | bytes 1572872 | tf_op jit(solution)/shard_map/ppermute | solution.py:165
  61.6 2.3 %collective-permute-start.10 = (bf16[256,8,64]{0,2,1:T(8,128)(2,1)S(1)}, bf16[256,8,64]{0,2,1:T(8,128)(2,1)S(1)}, u32[]{:S(2)}, u32[]{:S(2)}) collective-permute-start(bf16[256,8,64]{0,2,1:T(8,128)(2,1)S(1)} %dynamic-slice_bitcast_fusion), channel_id=1, source_target_pairs={{0,1},{1,0},{2,3},{3,2},{4,5},{5,4},{6,7},{7,6},{8,9},{9,8},{10,11... | collective-permute-start | bytes 786440 | tf_op jit(solution)/shard_map/ppermute | solution.py:164
  66.3 11.8 %collective-permute-start.12 = (f32[96,1024]{1,0:T(8,128)}, f32[96,1024]{1,0:T(8,128)}, u32[]{:S(2)}, u32[]{:S(2)}) collective-permute-start(f32[96,1024]{1,0:T(8,128)} %get-tuple-element.7), channel_id=1, source_target_pairs={{0,4},{1,5},{4,8},{5,9},{8,12},{9,13},{12,14},{13,15},{14,10},{15,... | collective-permute-start | bytes 1179656 | tf_op jit(solution)/shard_map/ppermute | solution.py:109
  79.9 11.0 %collective-permute-start.13 = (f32[96,1024]{1,0:T(8,128)}, f32[96,1024]{1,0:T(8,128)}, u32[]{:S(2)}, u32[]{:S(2)}) collective-permute-start(f32[96,1024]{1,0:T(8,128)} %fusion.18), channel_id=1, source_target_pairs={{0,4},{1,5},{4,8},{5,9},{8,12},{9,13},{12,14},{13,15},{14,10},{15,... | collective-permute-start | bytes 1179656 | tf_op jit(solution)/shard_map/ppermute | solution.py:109
  82.2 14.8 %collective-permute-start.16 = (f32[96,1024]{1,0:T(8,128)S(1)}, f32[96,1024]{1,0:T(8,128)}, u32[]{:S(2)}, u32[]{:S(2)}) collective-permute-start(f32[96,1024]{1,0:T(8,128)S(1)} %get-tuple-element.8), channel_id=1, source_target_pairs={{4,0},{5,1},{8,4},{9,5},{12,8},{13,9},{14,12},{15,13},{10,14},{11,... | collective-permute-start | bytes 1179656 | tf_op jit(solution)/shard_map/ppermute | solution.py:116
  92.7 10.1 %collective-permute-start.14 = (f32[96,1024]{1,0:T(8,128)}, f32[96,1024]{1,0:T(8,128)}, u32[]{:S(2)}, u32[]{:S(2)}) collective-permute-start(f32[96,1024]{1,0:T(8,128)} %fusion.21), channel_id=1, source_target_pairs={{0,4},{1,5},{4,8},{5,9},{8,12},{9,13},{12,14},{13,15},{14,10},{15,... | collective-permute-start | bytes 1179656 | tf_op jit(solution)/shard_map/ppermute | solution.py:109
  104.9 25.3 %copy-start.8 = (f32[1024]{0:T(1024)S(1)}, f32[1024]{0:T(1024)}, u32[]{:S(2)}) copy-start(f32[1024]{0:T(1024)} %param.24) | copy-start | bytes 12292
  104.9 20.6 %collective-permute-start.17 = (f32[96,1024]{1,0:T(8,128)}, f32[96,1024]{1,0:T(8,128)}, u32[]{:S(2)}, u32[]{:S(2)}) collective-permute-start(f32[96,1024]{1,0:T(8,128)} %get-tuple-element.6), channel_id=1, source_target_pairs={{4,0},{5,1},{8,4},{9,5},{12,8},{13,9},{14,12},{15,13},{10,14},{11,... | collective-permute-start | bytes 1179656 | tf_op jit(solution)/shard_map/ppermute | solution.py:116
  106.5 1.4 collective-permute-start.19
  108.6 3.6 %collective-permute-start.23 = (f32[1024]{0:T(1024)S(1)}, f32[1024]{0:T(1024)S(1)}, u32[]{:S(2)}, u32[]{:S(2)}) collective-permute-start(f32[1024]{0:T(1024)S(1)} %add.364), channel_id=1, source_target_pairs={{0,4},{1,5},{4,8},{5,9},{8,12},{9,13},{12,14},{13,15},{14,10},{15,... | collective-permute-start | bytes 12296 | tf_op jit(solution)/shard_map/ppermute | solution.py:110
  109.0 5.1 %collective-permute-start.20 = (f32[1024]{0:T(1024)S(1)}, f32[1024]{0:T(1024)S(1)}, u32[]{:S(2)}, u32[]{:S(2)}) collective-permute-start(f32[1024]{0:T(1024)S(1)} %add.364), channel_id=1, source_target_pairs={{4,0},{5,1},{8,4},{9,5},{12,8},{13,9},{14,12},{15,13},{10,14},{11,... | collective-permute-start | bytes 12296 | tf_op jit(solution)/shard_map/ppermute | solution.py:117
  112.2 3.6 %collective-permute-start.24 = (f32[1024]{0:T(1024)S(1)}, f32[1024]{0:T(1024)S(1)}, u32[]{:S(2)}, u32[]{:S(2)}) collective-permute-start(f32[1024]{0:T(1024)S(1)} %collective-permute-done.23), channel_id=1, source_target_pairs={{0,4},{1,5},{4,8},{5,9},{8,12},{9,13},{12,14},{13,15},{14,10},{15,... | collective-permute-start | bytes 12296 | tf_op jit(solution)/shard_map/ppermute | solution.py:110
  114.1 3.6 %collective-permute-start.21 = (f32[1024]{0:T(1024)S(1)}, f32[1024]{0:T(1024)S(1)}, u32[]{:S(2)}, u32[]{:S(2)}) collective-permute-start(f32[1024]{0:T(1024)S(1)} %collective-permute-done.20), channel_id=1, source_target_pairs={{4,0},{5,1},{8,4},{9,5},{12,8},{13,9},{14,12},{15,13},{10,14},{11,... | collective-permute-start | bytes 12296 | tf_op jit(solution)/shard_map/ppermute | solution.py:117
  115.8 3.6 %collective-permute-start.25 = (f32[1024]{0:T(1024)S(1)}, f32[1024]{0:T(1024)S(1)}, u32[]{:S(2)}, u32[]{:S(2)}) collective-permute-start(f32[1024]{0:T(1024)S(1)} %collective-permute-done.24), channel_id=1, source_target_pairs={{0,4},{1,5},{4,8},{5,9},{8,12},{9,13},{12,14},{13,15},{14,10},{15,... | collective-permute-start | bytes 12296 | tf_op jit(solution)/shard_map/ppermute | solution.py:110
  117.8 5.9 %collective-permute-start.22 = (f32[1024]{0:T(1024)S(1)}, f32[1024]{0:T(1024)S(1)}, u32[]{:S(2)}, u32[]{:S(2)}) collective-permute-start(f32[1024]{0:T(1024)S(1)} %collective-permute-done.21), channel_id=1, source_target_pairs={{4,0},{5,1},{8,4},{9,5},{12,8},{13,9},{14,12},{15,13},{10,14},{11,... | collective-permute-start | bytes 12296 | tf_op jit(solution)/shard_map/ppermute | solution.py:117
  119.4 4.3 %collective-permute-start.26 = (f32[1024]{0:T(1024)S(1)}, f32[1024]{0:T(1024)S(1)}, u32[]{:S(2)}, u32[]{:S(2)}) collective-permute-start(f32[1024]{0:T(1024)S(1)} %collective-permute-done.25), channel_id=1, source_target_pairs={{0,4},{1,5},{4,8},{5,9},{8,12},{9,13},{12,14},{13,15},{14,10},{15,... | collective-permute-start | bytes 12296 | tf_op jit(solution)/shard_map/ppermute | solution.py:110
  124.9 8.7 %collective-permute-start.15 = (f32[96,1024]{1,0:T(8,128)}, f32[96,1024]{1,0:T(8,128)S(1)}, u32[]{:S(2)}, u32[]{:S(2)}) collective-permute-start(f32[96,1024]{1,0:T(8,128)} %get-tuple-element.5), channel_id=1, source_target_pairs={{0,4},{1,5},{4,8},{5,9},{8,12},{9,13},{12,14},{13,15},{14,10},{15,... | collective-permute-start | bytes 1179656 | tf_op jit(solution)/shard_map/ppermute | solution.py:109
  127.4 8.6 %collective-permute-start.18 = (f32[96,1024]{1,0:T(8,128)}, f32[96,1024]{1,0:T(8,128)}, u32[]{:S(2)}, u32[]{:S(2)}) collective-permute-start(f32[96,1024]{1,0:T(8,128)} %fusion.13), channel_id=1, source_target_pairs={{4,0},{5,1},{8,4},{9,5},{12,8},{13,9},{14,12},{15,13},{10,14},{11,... | collective-permute-start | bytes 1179656 | tf_op jit(solution)/shard_map/ppermute | solution.py:116
  (7 other events, 25.5 us)

commit v4 on v3

--- a/solution.py
+++ b/solution.py
@@ -89,40 +89,21 @@
     return jnp.take(both, index, axis=0)
 
 
-def ring_reduce_scatter(summed, extra, n_blk):
+def ring_reduce_scatter(summed, n_blk):
     chips, snake, place, cw, ccw, partner = ring_plan(n_blk)
     ahead = chips // 2
     behind = chips - 1 - ahead
-    position = lax.axis_index("blk")
-    chip = position // 2
-    spot = jnp.asarray(place, jnp.int32)[chip]
-    order = jnp.asarray(snake, jnp.int32)
-
-    def block_at(k):
-        return lax.dynamic_index_in_dim(summed, order[(spot + k) % chips], 0, keepdims=False)
-
-    rel = [None] * chips
-    rel[0] = extra
-    acc = block_at(ahead)
-    carried = extra
+    acc = summed[ahead % chips]
     for s in range(1, ahead + 1):
-        acc = lax.ppermute(acc, "blk", cw) + block_at(ahead - s)
-        carried = lax.ppermute(carried, "blk", cw)
-        rel[chips - s] = carried
+        acc = lax.ppermute(acc, "blk", cw) + summed[(ahead - s) % chips]
     if behind:
-        acc_back = block_at(chips - behind)
-        carried = extra
+        acc_back = summed[chips - behind]
         for s in range(1, behind + 1):
             acc_back = lax.ppermute(acc_back, "blk", ccw)
-            carried = lax.ppermute(carried, "blk", ccw)
-            rel[s] = carried
             if s < behind:
-                acc_back = acc_back + block_at(chips - behind + s)
+                acc_back = acc_back + summed[chips - behind + s]
         acc = acc + acc_back
-    by_rel = jnp.stack(rel)
-    k = (jnp.asarray(place, jnp.int32) - spot) % chips
-    by_chip = jnp.take(by_rel, k, axis=0)
-    return acc, jnp.sum(by_chip, axis=0)
+    return acc
 
 
 def slots_product(left, right):
@@ -163,13 +144,24 @@
     b_got = lax.ppermute(b_me, "blk", partner)
     c_got = lax.ppermute(c_give, "blk", partner)
     d_got = lax.ppermute(d_me, "blk", partner)
-    extra = grad_three + lax.ppermute(grad_three, "blk", partner)
+    chip_out = grad_three + lax.ppermute(grad_three, "blk", partner)
+    chip = position // 2
+    spot = jnp.asarray(place, jnp.int32)[chip]
+    ring_chips = jnp.asarray(snake, jnp.int32)[(spot + jnp.arange(chips, dtype=jnp.int32)) % chips]
+    a_keep, a_got, c_keep, c_got = (
+        jnp.take(f, ring_chips, axis=1) for f in (a_keep, a_got, c_keep, c_got)
+    )
     part_one = slots_product(a_keep, b_me) + slots_product(a_got, b_got)
     part_two = slots_product(c_keep, d_me) + slots_product(c_got, d_got)
-    summed = jnp.concatenate([part_one, part_two], axis=1)
-    reduced, grad_out = ring_reduce_scatter(summed, extra, n_blk)
+    own_row = jnp.arange(chips, dtype=jnp.int32)[:, None] == chip
+    outs = jnp.where(own_row, chip_out[None, :], 0.0)
+    summed = jnp.concatenate(
+        [part_one, part_two, jnp.broadcast_to(outs, (chips,) + outs.shape)], axis=1
+    )
+    reduced = ring_reduce_scatter(summed, n_blk)
+    grad_out = jnp.sum(reduced[r_one + r_two:], axis=0)
     grad_one = reduced[:r_one]
-    grad_two = reduced[r_one:]
+    grad_two = reduced[r_one:r_one + r_two]
     new_first = 0.8 * mom_first + 0.2 * normalized(grad_one)
     new_second = 0.8 * mom_second + 0.2 * normalized(grad_two)
     new_out = 0.8 * mom_out + 0.2 * normalized(grad_out)

time: 140 us -> 117 us (0.84)
  between operations: 23.3 us -> 1.87 us
  starting transfers between devices: 22.6 us -> 16.2 us
  other arithmetic: 19.2 us -> 13.2 us
  local copies, waits for them, and re-layouts: 15.9 us -> 21.3 us
  waiting for transfers between devices: 48.9 us -> 53.1 us
  matrix products: 8.95 us -> 11 us
    add x5 -> x4, other arithmetic: 8.31 us -> 1 us  [the longest x1 0.7 us: per_device(): chip_out = grad_three + lax.ppermute(grad_three, 'blk', partner)]
    ppermute x12 -> x5, waiting for transfers between devices: 30 us -> 34.8 us  [the longest x4 34.8 us: ring_reduce_scatter(): acc = lax.ppermute(acc, 'blk', cw) + summed[(ahead - s) % chips]]
    ppermute x12 -> x5, starting transfers between devices: 9.05 us -> 4.32 us  [the longest x4 3.85 us: ring_reduce_scatter(): acc = lax.ppermute(acc, 'blk', cw) + summed[(ahead - s) % chips]]
    gather x1 -> x5, local copies, waits for them, and re-layouts: 1.17 us -> 4.73 us  [the longest x4 4.09 us: per_device(): jnp.take(f, ring_chips, axis=1)]
    dot_general x4, matrix products: 3.57 us -> 5.7 us  [slots_product(): lax.dot_general(left, right, (((0,), (0,)), ((), ())), preferred_element_...]
    select_n x0 -> x3, other arithmetic: none -> 1.96 us  [the longest x1 1.3 us: per_device(): outs = jnp.where(own_row, chip_out[None, :], 0.0)]
    unnamed x32 -> x40, local copies, waits for them, and re-layouts: 6.51 us -> 6.75 us
  transfers between devices with their start and end apart: 27 -> 20, of which waited for: 15 -> 10; matrix products, arithmetic and copies ran while one was open for 13% -> 19% of each run, Pallas kernels for 0% -> 0%
where the time goes in v4:
time: 117 us
  waiting for transfers between devices  53.1 us (45%)
  local copies, waits for them, and re-layouts  21.3 us (18%)
  starting transfers between devices  16.2 us (14%)
  other arithmetic  13.2 us (11%)
  matrix products  11 us (9%)
  between operations  1.87 us (2%)
    ppermute x4, waiting for transfers between devices, ring_reduce_scatter(): acc = lax.ppermute(acc, 'blk', cw) + summed[(ahead - s) % chips]  34.8 us
    ppermute x4, waiting for transfers between devices, ring_all_gather(): left = lax.ppermute(left, 'blk', cw)  9.04 us
    ppermute x3, waiting for transfers between devices, ring_all_gather(): right = lax.ppermute(right, 'blk', ccw)  7.46 us
    unnamed x40, local copies, waits for them, and re-layouts  6.75 us
    ppermute x3, starting transfers between devices, ring_all_gather(): right = lax.ppermute(right, 'blk', ccw)  6.07 us
    dot_general x4, matrix products, slots_product(): lax.dot_general(left, right, (((0,), (0,)), ((), ())), preferred_element_...  5.7 us
    gather x4, local copies, waits for them, and re-layouts, per_device(): jnp.take(f, ring_chips, axis=1)  4.09 us
    ppermute x4, starting transfers between devices, ring_reduce_scatter(): acc = lax.ppermute(acc, 'blk', cw) + summed[(ahead - s) % chips]  3.85 us
  transfers between devices with their start and end apart: 20, of which 10 were waited for; matrix products, arithmetic and copies ran while one was open for 19% of the time, Pallas kernels for 0%

profile of v4, /device:TPU:0, one launch (start us, length us, event | category | flops | bytes accessed | tf_op | source)
XLA Modules:
  0.0 116.8 jit_solution(1950848569485727599)
XLA Ops:
  0.7 0.9 constant_dynamic-update-slice_fusion.1
  1.5 0.9 constant_dynamic-update-slice_fusion
  2.5 3.0 %collective-permute-start = (bf16[96,1024]{1,0:T(8,128)(2,1)S(1)}, bf16[96,1024]{1,0:T(8,128)(2,1)S(1)}, u32[]{:S(2)}, u32[]{:S(2)}) collective-permute-start(bf16[96,1024]{1,0:T(8,128)(2,1)S(1)} %constant_dynamic-update-slice_fusion), channel_id=1, source_target_pairs={{4,0},{5,1},{8,4},{9,5},{12,8},{13,9},{14,12},{15,13},{10,14},{11,... | collective-permute-start | bytes 589832 | tf_op jit(solution)/shard_map/ppermute | solution.py:80
  6.3 4.1 %collective-permute-done = bf16[96,1024]{1,0:T(8,128)(2,1)S(1)} collective-permute-done((bf16[96,1024]{1,0:T(8,128)(2,1)S(1)}, bf16[96,1024]{1,0:T(8,128)(2,1)S(1)}, u32[]{:S(2)}, u32[]{:S(2)}) %collective-permute-start) | collective-permute-done | bytes 196640 | tf_op jit(solution)/shard_map/ppermute | solution.py:80
  10.4 1.7 %collective-permute-start.1 = (bf16[96,1024]{1,0:T(8,128)(2,1)S(1)}, bf16[96,1024]{1,0:T(8,128)(2,1)S(1)}, u32[]{:S(2)}, u32[]{:S(2)}) collective-permute-start(bf16[96,1024]{1,0:T(8,128)(2,1)S(1)} %collective-permute-done), channel_id=1, source_target_pairs={{4,0},{5,1},{8,4},{9,5},{12,8},{13,9},{14,12},{15,13},{10,14},{11,... | collective-permute-start | bytes 589832 | tf_op jit(solution)/shard_map/ppermute | solution.py:80
  13.2 3.3 %collective-permute-done.1 = bf16[96,1024]{1,0:T(8,128)(2,1)S(1)} collective-permute-done((bf16[96,1024]{1,0:T(8,128)(2,1)S(1)}, bf16[96,1024]{1,0:T(8,128)(2,1)S(1)}, u32[]{:S(2)}, u32[]{:S(2)}) %collective-permute-start.1) | collective-permute-done | bytes 196640 | tf_op jit(solution)/shard_map/ppermute | solution.py:80
  16.5 1.4 %collective-permute-start.2 = (bf16[96,1024]{1,0:T(8,128)(2,1)S(1)}, bf16[96,1024]{1,0:T(8,128)(2,1)S(1)}, u32[]{:S(2)}, u32[]{:S(2)}) collective-permute-start(bf16[96,1024]{1,0:T(8,128)(2,1)S(1)} %collective-permute-done.1), channel_id=1, source_target_pairs={{4,0},{5,1},{8,4},{9,5},{12,8},{13,9},{14,12},{15,13},{10,14},{11,... | collective-permute-start | bytes 589832 | tf_op jit(solution)/shard_map/ppermute | solution.py:80
  19.3 4.7 %collective-permute-done.5 = bf16[96,1024]{1,0:T(8,128)(2,1)S(1)} collective-permute-done((bf16[96,1024]{1,0:T(8,128)(2,1)S(1)}, bf16[96,1024]{1,0:T(8,128)(2,1)S(1)}, u32[]{:S(2)}, u32[]{:S(2)}) %collective-permute-start.5) | collective-permute-done | bytes 196640 | tf_op jit(solution)/shard_map/ppermute | solution.py:77
  25.4 4.3 %collective-permute-done.6 = bf16[96,1024]{1,0:T(8,128)(2,1)S(1)} collective-permute-done((bf16[96,1024]{1,0:T(8,128)(2,1)S(1)}, bf16[96,1024]{1,0:T(8,128)(2,1)S(1)}, u32[]{:S(2)}, u32[]{:S(2)}) %collective-permute-start.6) | collective-permute-done | bytes 196640 | tf_op jit(solution)/shard_map/ppermute | solution.py:77
  38.4 1.3 %constant_dynamic-update-slice_fusion.2 = bf16[16,96,1024]{2,1,0:T(8,128)(2,1)} fusion(bf16[16,96,1024]{2,1,0:T(8,128)(2,1)} %get-tuple-element.20, bf16[8,96,1024]{2,1,0:T(8,128)(2,1)S(1)} %collective-permute-done.7), kind=kLoop, calls=%fused_computation.96 | loop fusion | bytes 3145728 | tf_op jit(solution)/shard_map/concatenate | solution.py:84
  39.7 2.6 %gather_fusion.1 = bf16[16,96,1024]{2,1,0:T(8,128)(2,1)S(1)} fusion(bf16[16,96,1024]{2,1,0:T(8,128)(2,1)} %constant_dynamic-update-slice_fusion.2, s32[1024]{0:T(1024)S(1)} %pad_clamp_fusion.1), kind=kCustom, calls=%fused_computation.5 | custom fusion | bytes 6291520 | tf_op jit(solution)/shard_map/jit(_take)/gather | solution.py:89
  45.0 0.8 multiply_convert_fusion.1
  48.2 1.5 %add_convert_fusion = (bf16[128,1024]{1,0:T(8,128)(2,1)S(1)}, f32[1024]{0:T(1024)}) fusion(f32[128]{0:T(128)S(1)} %subtract_multiply_fusion, f32[1024]{0:T(1024)S(1)} %copy-done.13, f32[128,1024]{1,0:T(8,128)S(1)} %get-tuple-element.37, bf16[128,1024]{1,0:T(8,128)(2,1)S(1)} %get-tuple-element.40, bf16[1024,1024]{1,0:T(8,128)(2,1)S(1)} %bitcast.121), kind=kOutput, calls=%fused_computation.31 | convolution fusion | flops 271186944 | bytes 3154432 | tf_op jit(solution)/shard_map/dot_general | solution.py:37
  49.7 0.9 pad_maximum_fusion.3
  50.6 0.9 fusion.1
  51.5 0.9 pad_maximum_fusion.1
  52.9 1.1 copy.17
  57.2 1.5 %fusion.6 = f32[8,64,1024]{2,1,0:T(8,128)S(1)} fusion(bf16[8,256,64]{1,2,0:T(8,128)(2,1)S(1)} %gather_fusion.5, pred[8]{0:T(512)(128)(4,1)S(1)} %compare_and_fusion, bf16[128,1024]{1,0:T(8,128)(2,1)} %copy-done.4, bf16[128,1024]{1,0:T(8,128)(2,1)} %copy-done.3), kind=kOutput, calls=%fused_computation.25 | convolution fusion | flops 269615104 | bytes 2883592 | tf_op jit(solution)/shard_map/dot_general | solution.py:110
  59.2 1.3 %fusion.9 = f32[8,32,1024]{2,1,0:T(8,128)S(1)} fusion(bf16[8,256,32]{1,2,0:T(8,128)(2,1)S(1)} %gather_fusion.3, pred[8]{0:T(512)(128)(4,1)S(1)} %compare_and_fusion, bf16[128,1024]{1,0:T(8,128)(2,1)S(1)} %get-tuple-element.38, bf16[128,1024]{1,0:T(8,128)(2,1)} %copy-done.5), kind=kOutput, calls=%fused_computation.28 | convolution fusion | flops 135331840 | bytes 1703944 | tf_op jit(solution)/shard_map/dot_general | solution.py:110
  61.2 1.3 %broadcast_select_fusion.1 = f32[8,1024]{1,0:T(8,128)} fusion(f32[1024]{0:T(1024)S(1)} %add.260, pred[8]{0:T(512)(128)(4,1)} %iota_compare_fusion), kind=kLoop, calls=%fused_computation.98 | loop fusion | flops 8192 | bytes 36872 | tf_op jit(solution)/shard_map/jit(_where)/select_n | solution.py:157
  62.5 1.5 %gather_fusion.4 = bf16[8,256,32]{1,2,0:T(8,128)(2,1)S(1)} fusion(bf16[256,8,32]{0,2,1:T(8,128)(2,1)} %collective-permute-done.8, s32[1024]{0:T(1024)S(1)} %pad_clamp_fusion), kind=kCustom, calls=%fused_computation.2.clone | custom fusion | bytes 262176 | tf_op jit(solution)/shard_map/jit(_take)/gather | solution.py:152
  64.0 1.5 %gather_fusion.6 = bf16[8,256,64]{1,2,0:T(8,128)(2,1)S(1)} fusion(bf16[256,8,64]{0,2,1:T(8,128)(2,1)} %collective-permute-done.10, s32[1024]{0:T(1024)S(1)} %pad_clamp_fusion), kind=kCustom, calls=%fused_computation.3.clone | custom fusion | bytes 524320 | tf_op jit(solution)/shard_map/jit(_take)/gather | solution.py:152
  65.6 1.4 %convolution_add_fusion.1 = f32[8,32,1024]{2,1,0:T(8,128)S(1)} fusion(f32[8,32,1024]{2,1,0:T(8,128)S(1)} %fusion.9, bf16[256,1024]{1,0:T(8,128)(2,1)} %collective-permute-done.9, bf16[8,256,32]{1,2,0:T(8,128)(2,1)S(1)} %gather_fusion.4, pred[8]{0:T(512)(128)(4,1)S(1)} %compare_and_fusion), kind=kOutput, calls=%fused_computation.12 | convolution fusion | flops 134545408 | bytes 2752520 | tf_op jit(solution)/shard_map/dot_general | solution.py:110
  67.0 1.5 %convolution_add_fusion = f32[8,64,1024]{2,1,0:T(8,128)S(1)} fusion(f32[8,64,1024]{2,1,0:T(8,128)S(1)} %fusion.6, bf16[256,1024]{1,0:T(8,128)(2,1)} %collective-permute-done.11, bf16[8,256,64]{1,2,0:T(8,128)(2,1)S(1)} %gather_fusion.6, pred[8]{0:T(512)(128)(4,1)S(1)} %compare_and_fusion), kind=kOutput, calls=%fused_computation.9 | convolution fusion | flops 269090816 | bytes 4980744 | tf_op jit(solution)/shard_map/dot_general | solution.py:110
  69.8 1.4 %collective-permute-start.17 = (f32[104,1024]{1,0:T(8,128)S(1)}, f32[104,1024]{1,0:T(8,128)S(1)}, u32[]{:S(2)}, u32[]{:S(2)}) collective-permute-start(f32[104,1024]{1,0:T(8,128)S(1)} %get-tuple-element.10), channel_id=1, source_target_pairs={{4,0},{5,1},{8,4},{9,5},{12,8},{13,9},{14,12},{15,13},{10,14},{11,... | collective-permute-start | bytes 1277960 | tf_op jit(solution)/shard_map/ppermute | solution.py:102
  71.2 9.7 %collective-permute-done.13 = f32[104,1024]{1,0:T(8,128)S(1)} collective-permute-done((f32[104,1024]{1,0:T(8,128)S(1)}, f32[104,1024]{1,0:T(8,128)S(1)}, u32[]{:S(2)}, u32[]{:S(2)}) %collective-permute-start.13) | collective-permute-done | bytes 426016 | tf_op jit(solution)/shard_map/ppermute | solution.py:98
  81.7 10.3 %collective-permute-done.14 = f32[104,1024]{1,0:T(8,128)S(1)} collective-permute-done((f32[104,1024]{1,0:T(8,128)S(1)}, f32[104,1024]{1,0:T(8,128)S(1)}, u32[]{:S(2)}, u32[]{:S(2)}) %collective-permute-start.14) | collective-permute-done | bytes 426016 | tf_op jit(solution)/shard_map/ppermute | solution.py:98
  92.8 1.4 %collective-permute-start.18 = (f32[104,1024]{1,0:T(8,128)S(1)}, f32[104,1024]{1,0:T(8,128)S(1)}, u32[]{:S(2)}, u32[]{:S(2)}) collective-permute-start(f32[104,1024]{1,0:T(8,128)S(1)} %get-tuple-element.8), channel_id=1, source_target_pairs={{4,0},{5,1},{8,4},{9,5},{12,8},{13,9},{14,12},{15,13},{10,14},{11,... | collective-permute-start | bytes 1277960 | tf_op jit(solution)/shard_map/ppermute | solution.py:102
  94.2 8.0 %collective-permute-done.15 = f32[104,1024]{1,0:T(8,128)S(1)} collective-permute-done((f32[104,1024]{1,0:T(8,128)S(1)}, f32[104,1024]{1,0:T(8,128)S(1)}, u32[]{:S(2)}, u32[]{:S(2)}) %collective-permute-start.15) | collective-permute-done | bytes 426016 | tf_op jit(solution)/shard_map/ppermute | solution.py:98
  102.6 1.8 %collective-permute-start.16 = (f32[104,1024]{1,0:T(8,128)S(1)}, f32[104,1024]{1,0:T(8,128)S(1)}, u32[]{:S(2)}, u32[]{:S(2)}) collective-permute-start(f32[104,1024]{1,0:T(8,128)S(1)} %get-tuple-element.5), channel_id=1, source_target_pairs={{0,4},{1,5},{4,8},{5,9},{8,12},{9,13},{12,14},{13,15},{14,10},{15,... | collective-permute-start | bytes 1277960 | tf_op jit(solution)/shard_map/ppermute | solution.py:98
  104.7 6.8 %collective-permute-done.16 = f32[104,1024]{1,0:T(8,128)S(1)} collective-permute-done((f32[104,1024]{1,0:T(8,128)S(1)}, f32[104,1024]{1,0:T(8,128)S(1)}, u32[]{:S(2)}, u32[]{:S(2)}) %collective-permute-start.16) | collective-permute-done | bytes 426016 | tf_op jit(solution)/shard_map/ppermute | solution.py:98
  111.5 1.4 %collective-permute-done.19 = f32[104,1024]{1,0:T(8,128)S(1)} collective-permute-done((f32[104,1024]{1,0:T(8,128)S(1)}, f32[104,1024]{1,0:T(8,128)S(1)}, u32[]{:S(2)}, u32[]{:S(2)}) %collective-permute-start.19) | collective-permute-done | bytes 426016 | tf_op jit(solution)/shard_map/ppermute | solution.py:102
  (113 shorter events, 29.8 us)
Async XLA Ops:
  0.6 33.9 %copy-start = (s32[16,16]{1,0:T(8,128)S(1)}, s32[16,16]{1,0:T(8,128)}, u32[]{:S(2)}) copy-start(s32[16,16]{1,0:T(8,128)} %param.21) | copy-start | bytes 3076
  0.6 31.9 %copy-start.2 = (s32[8]{0:T(128)S(1)}, s32[8]{0:T(128)}, u32[]{:S(2)}) copy-start(s32[8]{0:T(128)} %constant.172.clone) | copy-start | bytes 100
  0.7 34.5 %copy-start.1 = (s32[8]{0:T(128)S(1)}, s32[8]{0:T(128)}, u32[]{:S(2)}) copy-start(s32[8]{0:T(128)} %constant.173.clone) | copy-start | bytes 100
  0.7 33.8 %copy-start.14 = (bf16[1024]{0:T(1024)(128)(2,1)S(1)}, bf16[1024]{0:T(1024)(128)(2,1)}, u32[]{:S(2)}) copy-start(bf16[1024]{0:T(1024)(128)(2,1)} %param.24) | copy-start | bytes 6148
  2.5 8.0 %collective-permute-start = (bf16[96,1024]{1,0:T(8,128)(2,1)S(1)}, bf16[96,1024]{1,0:T(8,128)(2,1)S(1)}, u32[]{:S(2)}, u32[]{:S(2)}) collective-permute-start(bf16[96,1024]{1,0:T(8,128)(2,1)S(1)} %constant_dynamic-update-slice_fusion), channel_id=1, source_target_pairs={{4,0},{5,1},{8,4},{9,5},{12,8},{13,9},{14,12},{15,13},{10,14},{11,... | collective-permute-start | bytes 589832 | tf_op jit(solution)/shard_map/ppermute | solution.py:80
  5.5 6.6 %collective-permute-start.3 = (bf16[96,1024]{1,0:T(8,128)(2,1)S(1)}, bf16[96,1024]{1,0:T(8,128)(2,1)S(1)}, u32[]{:S(2)}, u32[]{:S(2)}) collective-permute-start(bf16[96,1024]{1,0:T(8,128)(2,1)S(1)} %constant_dynamic-update-slice_fusion), channel_id=1, source_target_pairs={{0,4},{1,5},{4,8},{5,9},{8,12},{9,13},{12,14},{13,15},{14,10},{15,... | collective-permute-start | bytes 589832 | tf_op jit(solution)/shard_map/ppermute | solution.py:77
  10.4 6.1 %collective-permute-start.1 = (bf16[96,1024]{1,0:T(8,128)(2,1)S(1)}, bf16[96,1024]{1,0:T(8,128)(2,1)S(1)}, u32[]{:S(2)}, u32[]{:S(2)}) collective-permute-start(bf16[96,1024]{1,0:T(8,128)(2,1)S(1)} %collective-permute-done), channel_id=1, source_target_pairs={{4,0},{5,1},{8,4},{9,5},{12,8},{13,9},{14,12},{15,13},{10,14},{11,... | collective-permute-start | bytes 589832 | tf_op jit(solution)/shard_map/ppermute | solution.py:80
  12.1 5.8 %collective-permute-start.4 = (bf16[96,1024]{1,0:T(8,128)(2,1)S(1)}, bf16[96,1024]{1,0:T(8,128)(2,1)S(1)}, u32[]{:S(2)}, u32[]{:S(2)}) collective-permute-start(bf16[96,1024]{1,0:T(8,128)(2,1)S(1)} %collective-permute-done.3), channel_id=1, source_target_pairs={{0,4},{1,5},{4,8},{5,9},{8,12},{9,13},{12,14},{13,15},{14,10},{15,... | collective-permute-start | bytes 589832 | tf_op jit(solution)/shard_map/ppermute | solution.py:77
  16.5 8.1 %collective-permute-start.2 = (bf16[96,1024]{1,0:T(8,128)(2,1)S(1)}, bf16[96,1024]{1,0:T(8,128)(2,1)S(1)}, u32[]{:S(2)}, u32[]{:S(2)}) collective-permute-start(bf16[96,1024]{1,0:T(8,128)(2,1)S(1)} %collective-permute-done.1), channel_id=1, source_target_pairs={{4,0},{5,1},{8,4},{9,5},{12,8},{13,9},{14,12},{15,13},{10,14},{11,... | collective-permute-start | bytes 589832 | tf_op jit(solution)/shard_map/ppermute | solution.py:80
  17.9 6.1 %collective-permute-start.5 = (bf16[96,1024]{1,0:T(8,128)(2,1)S(1)}, bf16[96,1024]{1,0:T(8,128)(2,1)S(1)}, u32[]{:S(2)}, u32[]{:S(2)}) collective-permute-start(bf16[96,1024]{1,0:T(8,128)(2,1)S(1)} %collective-permute-done.4), channel_id=1, source_target_pairs={{0,4},{1,5},{4,8},{5,9},{8,12},{9,13},{12,14},{13,15},{14,10},{15,... | collective-permute-start | bytes 589832 | tf_op jit(solution)/shard_map/ppermute | solution.py:77
  24.0 5.7 %collective-permute-start.6 = (bf16[96,1024]{1,0:T(8,128)(2,1)S(1)}, bf16[96,1024]{1,0:T(8,128)(2,1)S(1)}, u32[]{:S(2)}, u32[]{:S(2)}) collective-permute-start(bf16[96,1024]{1,0:T(8,128)(2,1)S(1)} %collective-permute-done.5), channel_id=1, source_target_pairs={{0,4},{1,5},{4,8},{5,9},{8,12},{9,13},{12,14},{13,15},{14,10},{15,... | collective-permute-start | bytes 589832 | tf_op jit(solution)/shard_map/ppermute | solution.py:77
  32.5 5.9 %collective-permute-start.7 = (bf16[8,96,1024]{2,1,0:T(8,128)(2,1)S(1)}, bf16[8,96,1024]{2,1,0:T(8,128)(2,1)S(1)}, u32[]{:S(2)}, u32[]{:S(2)}) collective-permute-start(bf16[8,96,1024]{2,1,0:T(8,128)(2,1)S(1)} %get-tuple-element.19), channel_id=1, source_target_pairs={{0,1},{1,0},{2,3},{3,2},{4,5},{5,4},{6,7},{7,6},{8,9},{9,8},{10,11... | collective-permute-start | bytes 4718600 | tf_op jit(solution)/shard_map/ppermute | solution.py:83
  34.5 9.6 %copy-start.12 = (f32[1024]{0:T(1024)}, f32[1024]{0:T(1024)S(1)}, u32[]{:S(2)}) copy-start(f32[1024]{0:T(1024)S(1)} %convert_element_type.33) | copy-start | bytes 12292
  45.0 6.5 %copy-start.3 = (bf16[128,1024]{1,0:T(8,128)(2,1)}, bf16[128,1024]{1,0:T(8,128)(2,1)S(1)}, u32[]{:S(2)}) copy-start(bf16[128,1024]{1,0:T(8,128)(2,1)S(1)} %get-tuple-element.14) | copy-start | bytes 786436
  46.0 1.6 %copy-start.15 = (bf16[128]{0:T(256)(128)(2,1)S(1)}, bf16[128]{0:T(256)(128)(2,1)}, u32[]{:S(2)}) copy-start(bf16[128]{0:T(256)(128)(2,1)} %param.20) | copy-start | bytes 772
  46.0 2.2 %copy-start.13 = (f32[1024]{0:T(1024)S(1)}, f32[1024]{0:T(1024)}, u32[]{:S(2)}) copy-start(f32[1024]{0:T(1024)} %copy-done.12) | copy-start | bytes 12292
  49.7 5.0 %copy-start.4 = (bf16[128,1024]{1,0:T(8,128)(2,1)}, bf16[128,1024]{1,0:T(8,128)(2,1)S(1)}, u32[]{:S(2)}) copy-start(bf16[128,1024]{1,0:T(8,128)(2,1)S(1)} %get-tuple-element.11) | copy-start | bytes 786436
  52.4 13.2 %collective-permute-start.9 = (bf16[256,1024]{1,0:T(8,128)(2,1)}, bf16[256,1024]{1,0:T(8,128)(2,1)}, u32[]{:S(2)}, u32[]{:S(2)}) collective-permute-start(bf16[256,1024]{1,0:T(8,128)(2,1)} %pad_maximum_fusion.1), channel_id=1, source_target_pairs={{0,1},{1,0},{2,3},{3,2},{4,5},{5,4},{6,7},{7,6},{8,9},{9,8},{10,11... | collective-permute-start | bytes 1572872 | tf_op jit(solution)/shard_map/ppermute | solution.py:144
  54.6 7.9 %collective-permute-start.8 = (bf16[256,8,32]{0,2,1:T(8,128)(2,1)}, bf16[256,8,32]{0,2,1:T(8,128)(2,1)}, u32[]{:S(2)}, u32[]{:S(2)}) collective-permute-start(bf16[256,8,32]{0,2,1:T(8,128)(2,1)} %get-tuple-element.17), channel_id=1, source_target_pairs={{0,1},{1,0},{2,3},{3,2},{4,5},{5,4},{6,7},{7,6},{8,9},{9,8},{10,11... | collective-permute-start | bytes 393224 | tf_op jit(solution)/shard_map/ppermute | solution.py:143
  54.7 12.3 %collective-permute-start.11 = (bf16[256,1024]{1,0:T(8,128)(2,1)}, bf16[256,1024]{1,0:T(8,128)(2,1)}, u32[]{:S(2)}, u32[]{:S(2)}) collective-permute-start(bf16[256,1024]{1,0:T(8,128)(2,1)} %pad_maximum_fusion.3), channel_id=1, source_target_pairs={{0,1},{1,0},{2,3},{3,2},{4,5},{5,4},{6,7},{7,6},{8,9},{9,8},{10,11... | collective-permute-start | bytes 1572872 | tf_op jit(solution)/shard_map/ppermute | solution.py:146
  56.1 7.9 %collective-permute-start.10 = (bf16[256,8,64]{0,2,1:T(8,128)(2,1)}, bf16[256,8,64]{0,2,1:T(8,128)(2,1)}, u32[]{:S(2)}, u32[]{:S(2)}) collective-permute-start(bf16[256,8,64]{0,2,1:T(8,128)(2,1)} %get-tuple-element.15), channel_id=1, source_target_pairs={{0,1},{1,0},{2,3},{3,2},{4,5},{5,4},{6,7},{7,6},{8,9},{9,8},{10,11... | collective-permute-start | bytes 786440 | tf_op jit(solution)/shard_map/ppermute | solution.py:145
  56.1 4.4 %collective-permute-start.12 = (f32[1024]{0:T(1024)}, f32[1024]{0:T(1024)}, u32[]{:S(2)}, u32[]{:S(2)}) collective-permute-start(f32[1024]{0:T(1024)} %get-tuple-element.12), channel_id=1, source_target_pairs={{0,1},{1,0},{2,3},{3,2},{4,5},{5,4},{6,7},{7,6},{8,9},{9,8},{10,11... | collective-permute-start | bytes 12296 | tf_op jit(solution)/shard_map/ppermute | solution.py:147
  69.1 11.8 %collective-permute-start.13 = (f32[104,1024]{1,0:T(8,128)S(1)}, f32[104,1024]{1,0:T(8,128)S(1)}, u32[]{:S(2)}, u32[]{:S(2)}) collective-permute-start(f32[104,1024]{1,0:T(8,128)S(1)} %get-tuple-element.9), channel_id=1, source_target_pairs={{0,4},{1,5},{4,8},{5,9},{8,12},{9,13},{12,14},{13,15},{14,10},{15,... | collective-permute-start | bytes 1277960 | tf_op jit(solution)/shard_map/ppermute | solution.py:98
  69.8 11.9 %collective-permute-start.17 = (f32[104,1024]{1,0:T(8,128)S(1)}, f32[104,1024]{1,0:T(8,128)S(1)}, u32[]{:S(2)}, u32[]{:S(2)}) collective-permute-start(f32[104,1024]{1,0:T(8,128)S(1)} %get-tuple-element.10), channel_id=1, source_target_pairs={{4,0},{5,1},{8,4},{9,5},{12,8},{13,9},{14,12},{15,13},{10,14},{11,... | collective-permute-start | bytes 1277960 | tf_op jit(solution)/shard_map/ppermute | solution.py:102
  80.9 33.7 %copy-start.11 = (f32[1024]{0:T(1024)S(1)}, f32[1024]{0:T(1024)}, u32[]{:S(2)}) copy-start(f32[1024]{0:T(1024)} %param.27) | copy-start | bytes 12292
  81.0 34.3 %copy-start.6 = (f32[64,1024]{1,0:T(8,128)S(1)}, f32[64,1024]{1,0:T(8,128)}, u32[]{:S(2)}) copy-start(f32[64,1024]{1,0:T(8,128)} %param.26) | copy-start | bytes 786436
  81.0 11.0 %collective-permute-start.14 = (f32[104,1024]{1,0:T(8,128)S(1)}, f32[104,1024]{1,0:T(8,128)S(1)}, u32[]{:S(2)}, u32[]{:S(2)}) collective-permute-start(f32[104,1024]{1,0:T(8,128)S(1)} %fusion.17), channel_id=1, source_target_pairs={{0,4},{1,5},{4,8},{5,9},{8,12},{9,13},{12,14},{13,15},{14,10},{15,... | collective-permute-start | bytes 1277960 | tf_op jit(solution)/shard_map/ppermute | solution.py:98
  92.1 24.0 %copy-start.9 = (f32[32,1024]{1,0:T(8,128)S(1)}, f32[32,1024]{1,0:T(8,128)}, u32[]{:S(2)}) copy-start(f32[32,1024]{1,0:T(8,128)} %param.25) | copy-start | bytes 393220
  92.1 10.1 %collective-permute-start.15 = (f32[104,1024]{1,0:T(8,128)S(1)}, f32[104,1024]{1,0:T(8,128)S(1)}, u32[]{:S(2)}, u32[]{:S(2)}) collective-permute-start(f32[104,1024]{1,0:T(8,128)S(1)} %get-tuple-element.7), channel_id=1, source_target_pairs={{0,4},{1,5},{4,8},{5,9},{8,12},{9,13},{12,14},{13,15},{14,10},{15,... | collective-permute-start | bytes 1277960 | tf_op jit(solution)/shard_map/ppermute | solution.py:98
  92.8 9.7 %collective-permute-start.18 = (f32[104,1024]{1,0:T(8,128)S(1)}, f32[104,1024]{1,0:T(8,128)S(1)}, u32[]{:S(2)}, u32[]{:S(2)}) collective-permute-start(f32[104,1024]{1,0:T(8,128)S(1)} %get-tuple-element.8), channel_id=1, source_target_pairs={{4,0},{5,1},{8,4},{9,5},{12,8},{13,9},{14,12},{15,13},{10,14},{11,... | collective-permute-start | bytes 1277960 | tf_op jit(solution)/shard_map/ppermute | solution.py:102
  102.6 8.9 %collective-permute-start.16 = (f32[104,1024]{1,0:T(8,128)S(1)}, f32[104,1024]{1,0:T(8,128)S(1)}, u32[]{:S(2)}, u32[]{:S(2)}) collective-permute-start(f32[104,1024]{1,0:T(8,128)S(1)} %get-tuple-element.5), channel_id=1, source_target_pairs={{0,4},{1,5},{4,8},{5,9},{8,12},{9,13},{12,14},{13,15},{14,10},{15,... | collective-permute-start | bytes 1277960 | tf_op jit(solution)/shard_map/ppermute | solution.py:98
  104.4 8.5 %collective-permute-start.19 = (f32[104,1024]{1,0:T(8,128)S(1)}, f32[104,1024]{1,0:T(8,128)S(1)}, u32[]{:S(2)}, u32[]{:S(2)}) collective-permute-start(f32[104,1024]{1,0:T(8,128)S(1)} %get-tuple-element.6), channel_id=1, source_target_pairs={{4,0},{5,1},{8,4},{9,5},{12,8},{13,9},{14,12},{15,13},{10,14},{11,... | collective-permute-start | bytes 1277960 | tf_op jit(solution)/shard_map/ppermute | solution.py:102
  (4 other events, 4.4 us)

commit v5 on v4

--- a/solution.py
+++ b/solution.py
@@ -71,16 +71,20 @@
     core, chip = position % 2, position // 2
     spot = jnp.asarray(place, jnp.int32)[chip]
     rel = [None] * chips
+    rel_other = [None] * chips
     rel[0] = x
+    rel_other[0] = lax.ppermute(x, "blk", partner)
     left = right = x
     for s in range(1, ahead + 1):
         left = lax.ppermute(left, "blk", cw)
         rel[chips - s] = left
+        rel_other[chips - s] = lax.ppermute(left, "blk", partner)
         if s <= behind:
             right = lax.ppermute(right, "blk", ccw)
             rel[s] = right
+            rel_other[s] = lax.ppermute(right, "blk", partner)
     mine = jnp.stack(rel)
-    other = lax.ppermute(mine, "blk", partner)
+    other = jnp.stack(rel_other)
     both = jnp.concatenate([mine, other], axis=0)
     dest = jnp.arange(n_blk, dtype=jnp.int32)
     dest_chip, dest_core = dest // 2, dest % 2
@@ -132,27 +136,36 @@
     e_slope, g_one, e_aone, e_cone, g_two, h_one, e_atwo, grad_three = twin_terms(
         x_rows, z_rows, y_rows, mask, w_one, w_two, w_out
     )
-    a_all = jnp.concatenate([x_rows, e_slope], axis=0).reshape(2 * rows_dev, chips, 2, r_one)
-    c_all = jnp.concatenate([e_cone, h_one], axis=0).reshape(2 * rows_dev, chips, 2, r_two)
-    b_me = jnp.concatenate([e_aone, g_one], axis=0)
-    d_me = jnp.concatenate([g_two, e_atwo], axis=0)
-    a_keep = lax.dynamic_index_in_dim(a_all, core, 2, keepdims=False)
-    a_give = lax.dynamic_index_in_dim(a_all, 1 - core, 2, keepdims=False)
-    c_keep = lax.dynamic_index_in_dim(c_all, core, 2, keepdims=False)
-    c_give = lax.dynamic_index_in_dim(c_all, 1 - core, 2, keepdims=False)
-    a_got = lax.ppermute(a_give, "blk", partner)
-    b_got = lax.ppermute(b_me, "blk", partner)
-    c_got = lax.ppermute(c_give, "blk", partner)
-    d_got = lax.ppermute(d_me, "blk", partner)
-    chip_out = grad_three + lax.ppermute(grad_three, "blk", partner)
     chip = position // 2
     spot = jnp.asarray(place, jnp.int32)[chip]
     ring_chips = jnp.asarray(snake, jnp.int32)[(spot + jnp.arange(chips, dtype=jnp.int32)) % chips]
-    a_keep, a_got, c_keep, c_got = (
-        jnp.take(f, ring_chips, axis=1) for f in (a_keep, a_got, c_keep, c_got)
-    )
-    part_one = slots_product(a_keep, b_me) + slots_product(a_got, b_got)
-    part_two = slots_product(c_keep, d_me) + slots_product(c_got, d_got)
+
+    def split_cols(f, width):
+        f = jnp.take(f.reshape(rows_dev, chips, 2, width), ring_chips, axis=1)
+        keep = lax.dynamic_index_in_dim(f, core, 2, keepdims=False)
+        give = lax.dynamic_index_in_dim(f, 1 - core, 2, keepdims=False)
+        return keep, lax.ppermute(give, "blk", partner)
+
+    def swap(f):
+        return lax.ppermute(f, "blk", partner)
+
+    x_keep, x_got = split_cols(x_rows, r_one)
+    h_keep, h_got = split_cols(h_one, r_two)
+    g2_got = swap(g_two)
+    g1_got = swap(g_one)
+    ed_keep, ed_got = split_cols(e_slope, r_one)
+    ec_keep, ec_got = split_cols(e_cone, r_two)
+    ea2_got = swap(e_atwo)
+    ea1_got = swap(e_aone)
+    chip_out = grad_three + swap(grad_three)
+    part_two = (
+        slots_product(ec_keep, g_two) + slots_product(ec_got, g2_got)
+        + slots_product(h_keep, e_atwo) + slots_product(h_got, ea2_got)
+    )
+    part_one = (
+        slots_product(ed_keep, g_one) + slots_product(ed_got, g1_got)
+        + slots_product(x_keep, e_aone) + slots_product(x_got, ea1_got)
+    )
     own_row = jnp.arange(chips, dtype=jnp.int32)[:, None] == chip
     outs = jnp.where(own_row, chip_out[None, :], 0.0)
     summed = jnp.concatenate(

time: 117 us -> 120 us (1.026)
  other arithmetic: 13.2 us -> 9.83 us
  starting transfers between devices: 16.2 us -> 19.3 us
  local copies, waits for them, and re-layouts: 21.3 us -> 24.2 us
    unnamed x40 -> x51, local copies, waits for them, and re-layouts: 6.75 us -> 13.2 us
    ppermute x4, waiting for transfers between devices: 9.04 us -> 6.18 us  [ring_all_gather(): left = lax.ppermute(left, 'blk', cw)]
    dot_general x4 -> x8, matrix products: 5.7 us -> 2.95 us  [slots_product(): lax.dot_general(left, right, (((0,), (0,)), ((), ())), preferred_element_...]
    ppermute x4, starting transfers between devices: 3.85 us -> 6.6 us  [ring_reduce_scatter(): acc = lax.ppermute(acc, 'blk', cw) + summed[(ahead - s) % chips]]
    concatenate x4 -> x0, other arithmetic: 2.54 us -> none  [the longest x1 0.9 us: per_device(): d_me = jnp.concatenate([g_two, e_atwo], axis=0)]
    ppermute x6 -> x17, starting transfers between devices: 1.49 us -> 3.39 us  [the longest x4 1.17 us: split_cols(): return (keep, lax.ppermute(give, 'blk', partner))]
    ppermute x3, starting transfers between devices: 3.07 us -> 1.29 us  [ring_reduce_scatter(): acc_back = lax.ppermute(acc_back, 'blk', ccw)]
    gather x4, local copies, waits for them, and re-layouts: 4.09 us -> 2.34 us  [split_cols(): f = jnp.take(f.reshape(rows_dev, chips, 2, width), ring_chips, axis=1)]
  transfers between devices with their start and end apart: 20 -> 31, of which waited for: 10 -> 13; matrix products, arithmetic and copies ran while one was open for 19% -> 23% of each run, Pallas kernels for 0% -> 0%
where the time goes in v5:
time: 120 us; the launch traced here: 119 us
  waiting for transfers between devices  53.1 us (44%)
  local copies, waits for them, and re-layouts  24.2 us (20%)
  starting transfers between devices  19.3 us (16%)
  matrix products  10.9 us (9%)
  other arithmetic  9.83 us (8%)
  between operations  1.87 us (2%)
    ppermute x4, waiting for transfers between devices, ring_reduce_scatter(): acc = lax.ppermute(acc, 'blk', cw) + summed[(ahead - s) % chips]  34.3 us
    unnamed x51, local copies, waits for them, and re-layouts  13.2 us
    ppermute x3, waiting for transfers between devices, ring_all_gather(): right = lax.ppermute(right, 'blk', ccw)  8.21 us
    ppermute x3, starting transfers between devices, ring_all_gather(): right = lax.ppermute(right, 'blk', ccw)  6.66 us
    ppermute x4, starting transfers between devices, ring_reduce_scatter(): acc = lax.ppermute(acc, 'blk', cw) + summed[(ahead - s) % chips]  6.6 us
    ppermute x4, waiting for transfers between devices, ring_all_gather(): left = lax.ppermute(left, 'blk', cw)  6.18 us
    dot_general x8, matrix products, slots_product(): lax.dot_general(left, right, (((0,), (0,)), ((), ())), preferred_element_...  2.95 us
    gather x1, local copies, waits for them, and re-layouts, ring_all_gather(): return jnp.take(both, index, axis=0)  2.64 us
  transfers between devices with their start and end apart: 31, of which 13 were waited for; matrix products, arithmetic and copies ran while one was open for 23% of the time, Pallas kernels for 0%

profile of v5, /device:TPU:0, one launch (start us, length us, event | category | flops | bytes accessed | tf_op | source)
XLA Modules:
  0.0 119.1 jit_solution(14563851707387359286)
XLA Ops:
  0.6 0.9 constant_dynamic-update-slice_fusion.1
  1.5 0.9 constant_dynamic-update-slice_fusion
  2.4 3.0 %collective-permute-start = (bf16[96,1024]{1,0:T(8,128)(2,1)S(1)}, bf16[96,1024]{1,0:T(8,128)(2,1)S(1)}, u32[]{:S(2)}, u32[]{:S(2)}) collective-permute-start(bf16[96,1024]{1,0:T(8,128)(2,1)S(1)} %constant_dynamic-update-slice_fusion), channel_id=1, source_target_pairs={{4,0},{5,1},{8,4},{9,5},{12,8},{13,9},{14,12},{15,13},{10,14},{11,... | collective-permute-start | bytes 589832 | tf_op jit(solution)/shard_map/ppermute | solution.py:83
  6.3 1.2 %dynamic_slice.37 = s32[1]{0:T(128)} dynamic-slice(s32[8]{0:T(128)} %constant.180.clone, s32[]{:T(128)S(6)} %select_n.178), dynamic_slice_sizes={1} | dynamic-slice | bytes 12 | tf_op jit(solution)/shard_map/dynamic_slice | solution.py:72
  8.2 1.3 %gather_fusion.2 = s32[8]{0:T(128)S(1)} fusion(s32[8]{0:T(128)} %constant.181.clone, s32[1024]{0:T(1024)S(1)} %pad_clamp_fusion.3), kind=kCustom, calls=%fused_computation.6 | custom fusion | bytes 96 | tf_op jit(solution)/shard_map/gather | solution.py:141
  9.5 1.3 %gather_fusion = s32[16]{0:T(128)S(1)} fusion(s32[8]{0:T(128)} %constant.180.clone, s32[1024]{0:T(1024)S(1)} %get-tuple-element.27), kind=kCustom, calls=%fused_computation.4 | custom fusion | bytes 192 | tf_op jit(solution)/shard_map/gather | solution.py:91
  14.6 1.0 copy.45
  16.3 2.0 %collective-permute-start.1 = (bf16[96,1024]{1,0:T(8,128)(2,1)S(1)}, bf16[96,1024]{1,0:T(8,128)(2,1)S(1)}, u32[]{:S(2)}, u32[]{:S(2)}) collective-permute-start(bf16[96,1024]{1,0:T(8,128)(2,1)S(1)} %collective-permute-done), channel_id=1, source_target_pairs={{4,0},{5,1},{8,4},{9,5},{12,8},{13,9},{14,12},{15,13},{10,14},{11,... | collective-permute-start | bytes 589832 | tf_op jit(solution)/shard_map/ppermute | solution.py:83
  19.6 4.3 %collective-permute-done.1 = bf16[96,1024]{1,0:T(8,128)(2,1)S(1)} collective-permute-done((bf16[96,1024]{1,0:T(8,128)(2,1)S(1)}, bf16[96,1024]{1,0:T(8,128)(2,1)S(1)}, u32[]{:S(2)}, u32[]{:S(2)}) %collective-permute-start.1) | collective-permute-done | bytes 196640 | tf_op jit(solution)/shard_map/ppermute | solution.py:83
  23.9 1.7 %collective-permute-start.2 = (bf16[96,1024]{1,0:T(8,128)(2,1)S(1)}, bf16[96,1024]{1,0:T(8,128)(2,1)S(1)}, u32[]{:S(2)}, u32[]{:S(2)}) collective-permute-start(bf16[96,1024]{1,0:T(8,128)(2,1)S(1)} %collective-permute-done.1), channel_id=1, source_target_pairs={{4,0},{5,1},{8,4},{9,5},{12,8},{13,9},{14,12},{15,13},{10,14},{11,... | collective-permute-start | bytes 589832 | tf_op jit(solution)/shard_map/ppermute | solution.py:83
  26.6 3.9 %collective-permute-done.2 = bf16[96,1024]{1,0:T(8,128)(2,1)S(1)} collective-permute-done((bf16[96,1024]{1,0:T(8,128)(2,1)S(1)}, bf16[96,1024]{1,0:T(8,128)(2,1)S(1)}, u32[]{:S(2)}, u32[]{:S(2)}) %collective-permute-start.2) | collective-permute-done | bytes 196640 | tf_op jit(solution)/shard_map/ppermute | solution.py:83
  30.6 1.3 %collective-permute-done.5 = bf16[96,1024]{1,0:T(8,128)(2,1)S(1)} collective-permute-done((bf16[96,1024]{1,0:T(8,128)(2,1)S(1)}, bf16[96,1024]{1,0:T(8,128)(2,1)S(1)}, u32[]{:S(2)}, u32[]{:S(2)}) %collective-permute-start.5) | collective-permute-done | bytes 196640 | tf_op jit(solution)/shard_map/ppermute | solution.py:79
  33.0 4.9 %collective-permute-done.6 = bf16[96,1024]{1,0:T(8,128)(2,1)S(1)} collective-permute-done((bf16[96,1024]{1,0:T(8,128)(2,1)S(1)}, bf16[96,1024]{1,0:T(8,128)(2,1)S(1)}, u32[]{:S(2)}, u32[]{:S(2)}) %collective-permute-start.6) | collective-permute-done | bytes 196640 | tf_op jit(solution)/shard_map/ppermute | solution.py:79
  47.2 2.6 %gather_fusion.1 = bf16[16,96,1024]{2,1,0:T(8,128)(2,1)S(1)} fusion(bf16[16,96,1024]{2,1,0:T(8,128)(2,1)} %bitcast_dynamic-update-slice_fusion, s32[1024]{0:T(1024)S(1)} %pad_clamp_fusion.1), kind=kCustom, calls=%fused_computation.5 | custom fusion | bytes 6291520 | tf_op jit(solution)/shard_map/jit(_take)/gather | solution.py:93
  51.8 2.0 %multiply_reduce_fusion = (f32[128]{0:T(128)S(1)}, bf16[128,1024]{0,1:T(8,128)(2,1)S(1)}, f32[128,1024]{0,1:T(8,128)}) fusion(f32[1024]{0:T(1024)S(1)} %convert_element_type.33, bf16[128,1024]{0,1:T(8,128)(2,1)S(1)} %get-tuple-element.19, bf16[1024,1024]{1,0:T(8,128)(2,1)S(1)} %bitcast.154), kind=kOutput, calls=%fused_computation.25 | convolution fusion | flops 270139264 | bytes 3150336 | tf_op jit(solution)/shard_map/dot_general | solution.py:20
  53.7 1.5 %multiply_convert_fusion.1 = (bf16[128,1024]{0,1:T(8,128)(2,1)S(1)}, f32[128,1024]{0,1:T(8,128)}) fusion(f32[128,1024]{0,1:T(8,128)S(1)} %get-tuple-element.20, bf16[1024,1024]{1,0:T(8,128)(2,1)S(1)} %bitcast.155, bf16[128,1024]{0,1:T(8,128)(2,1)S(1)} %get-tuple-element.14), kind=kOutput, calls=%fused_computation.27 | convolution fusion | flops 269090816 | bytes 3670016 | tf_op jit(solution)/shard_map/dot_general | solution.py:25
  55.7 1.4 %multiply_convert_fusion = (bf16[128,1024]{0,1:T(8,128)(2,1)S(1)}, f32[128,1024]{0,1:T(8,128)}) fusion(f32[128,1024]{0,1:T(8,128)S(1)} %get-tuple-element.20, bf16[128,512]{1,0:T(8,128)(2,1)S(1)} %fusion.3, bf16[512,1024]{1,0:T(8,128)(2,1)S(1)} %bitcast.151), kind=kOutput, calls=%fused_computation.26 | convolution fusion | flops 134873088 | bytes 2490368 | tf_op jit(solution)/shard_map/dot_general | solution.py:34
  60.7 0.8 subtract_multiply_fusion
  61.7 1.4 %add_convert_fusion = (bf16[128,1024]{0,1:T(8,128)(2,1)S(1)}, f32[1024]{0:T(1024)S(1)}) fusion(f32[128]{0:T(128)S(1)} %subtract_multiply_fusion, f32[1024]{0:T(1024)S(1)} %convert_element_type.33, f32[128,1024]{0,1:T(8,128)S(1)} %copy-done.16, bf16[128,1024]{0,1:T(8,128)(2,1)S(1)} %get-tuple-element.24, bf16[1024,1024]{1,0:T(8,128)(2,1)S(1)} %bitcast.156), kind=kOutput, calls=%fused_computation.24 | convolution fusion | flops 271186944 | bytes 3154432 | tf_op jit(solution)/shard_map/dot_general | solution.py:37
  65.6 1.1 collective-permute-done.19
  70.1 1.7 %collective-permute-start.24 = (f32[104,1024]{1,0:T(8,128)S(1)}, f32[104,1024]{1,0:T(8,128)S(1)}, u32[]{:S(2)}, u32[]{:S(2)}) collective-permute-start(f32[104,1024]{1,0:T(8,128)S(1)} %get-tuple-element.9), channel_id=1, source_target_pairs={{0,4},{1,5},{4,8},{5,9},{8,12},{9,13},{12,14},{13,15},{14,10},{15,... | collective-permute-start | bytes 1277960 | tf_op jit(solution)/shard_map/ppermute | solution.py:102
  72.1 9.9 %collective-permute-done.24 = f32[104,1024]{1,0:T(8,128)S(1)} collective-permute-done((f32[104,1024]{1,0:T(8,128)S(1)}, f32[104,1024]{1,0:T(8,128)S(1)}, u32[]{:S(2)}, u32[]{:S(2)}) %collective-permute-start.24) | collective-permute-done | bytes 426016 | tf_op jit(solution)/shard_map/ppermute | solution.py:102
  82.1 1.7 %collective-permute-start.25 = (f32[104,1024]{1,0:T(8,128)S(1)}, f32[104,1024]{1,0:T(8,128)S(1)}, u32[]{:S(2)}, u32[]{:S(2)}) collective-permute-start(f32[104,1024]{1,0:T(8,128)S(1)} %fusion.11), channel_id=1, source_target_pairs={{0,4},{1,5},{4,8},{5,9},{8,12},{9,13},{12,14},{13,15},{14,10},{15,... | collective-permute-start | bytes 1277960 | tf_op jit(solution)/shard_map/ppermute | solution.py:102
  83.8 9.5 %collective-permute-done.25 = f32[104,1024]{1,0:T(8,128)S(1)} collective-permute-done((f32[104,1024]{1,0:T(8,128)S(1)}, f32[104,1024]{1,0:T(8,128)S(1)}, u32[]{:S(2)}, u32[]{:S(2)}) %collective-permute-start.25) | collective-permute-done | bytes 426016 | tf_op jit(solution)/shard_map/ppermute | solution.py:102
  93.3 1.7 %collective-permute-start.26 = (f32[104,1024]{1,0:T(8,128)S(1)}, f32[104,1024]{1,0:T(8,128)S(1)}, u32[]{:S(2)}, u32[]{:S(2)}) collective-permute-start(f32[104,1024]{1,0:T(8,128)S(1)} %get-tuple-element.7), channel_id=1, source_target_pairs={{0,4},{1,5},{4,8},{5,9},{8,12},{9,13},{12,14},{13,15},{14,10},{15,... | collective-permute-start | bytes 1277960 | tf_op jit(solution)/shard_map/ppermute | solution.py:102
  95.4 8.1 %collective-permute-done.26 = f32[104,1024]{1,0:T(8,128)S(1)} collective-permute-done((f32[104,1024]{1,0:T(8,128)S(1)}, f32[104,1024]{1,0:T(8,128)S(1)}, u32[]{:S(2)}, u32[]{:S(2)}) %collective-permute-start.26) | collective-permute-done | bytes 426016 | tf_op jit(solution)/shard_map/ppermute | solution.py:102
  103.5 1.3 %collective-permute-done.29 = f32[104,1024]{1,0:T(8,128)S(1)} collective-permute-done((f32[104,1024]{1,0:T(8,128)S(1)}, f32[104,1024]{1,0:T(8,128)S(1)}, u32[]{:S(2)}, u32[]{:S(2)}) %collective-permute-start.29) | collective-permute-done | bytes 426016 | tf_op jit(solution)/shard_map/ppermute | solution.py:106
  105.0 1.6 %collective-permute-start.27 = (f32[104,1024]{1,0:T(8,128)S(1)}, f32[104,1024]{1,0:T(8,128)S(1)}, u32[]{:S(2)}, u32[]{:S(2)}) collective-permute-start(f32[104,1024]{1,0:T(8,128)S(1)} %get-tuple-element.5), channel_id=1, source_target_pairs={{0,4},{1,5},{4,8},{5,9},{8,12},{9,13},{12,14},{13,15},{14,10},{15,... | collective-permute-start | bytes 1277960 | tf_op jit(solution)/shard_map/ppermute | solution.py:102
  107.1 6.9 %collective-permute-done.27 = f32[104,1024]{1,0:T(8,128)S(1)} collective-permute-done((f32[104,1024]{1,0:T(8,128)S(1)}, f32[104,1024]{1,0:T(8,128)S(1)}, u32[]{:S(2)}, u32[]{:S(2)}) %collective-permute-start.27) | collective-permute-done | bytes 426016 | tf_op jit(solution)/shard_map/ppermute | solution.py:102
  114.0 1.3 %collective-permute-done.30 = f32[104,1024]{1,0:T(8,128)S(1)} collective-permute-done((f32[104,1024]{1,0:T(8,128)S(1)}, f32[104,1024]{1,0:T(8,128)S(1)}, u32[]{:S(2)}, u32[]{:S(2)}) %collective-permute-start.30) | collective-permute-done | bytes 426016 | tf_op jit(solution)/shard_map/ppermute | solution.py:106
  117.6 0.8 multiply_add_fusion
  118.4 0.7 multiply_add_fusion.1
  (148 shorter events, 33.7 us)
Async XLA Ops:
  2.4 13.9 %collective-permute-start = (bf16[96,1024]{1,0:T(8,128)(2,1)S(1)}, bf16[96,1024]{1,0:T(8,128)(2,1)S(1)}, u32[]{:S(2)}, u32[]{:S(2)}) collective-permute-start(bf16[96,1024]{1,0:T(8,128)(2,1)S(1)} %constant_dynamic-update-slice_fusion), channel_id=1, source_target_pairs={{4,0},{5,1},{8,4},{9,5},{12,8},{13,9},{14,12},{15,13},{10,14},{11,... | collective-permute-start | bytes 589832 | tf_op jit(solution)/shard_map/ppermute | solution.py:83
  5.4 13.1 %collective-permute-start.3 = (bf16[96,1024]{1,0:T(8,128)(2,1)S(1)}, bf16[96,1024]{1,0:T(8,128)(2,1)S(1)}, u32[]{:S(2)}, u32[]{:S(2)}) collective-permute-start(bf16[96,1024]{1,0:T(8,128)(2,1)S(1)} %constant_dynamic-update-slice_fusion), channel_id=1, source_target_pairs={{0,4},{1,5},{4,8},{5,9},{8,12},{9,13},{12,14},{13,15},{14,10},{15,... | collective-permute-start | bytes 589832 | tf_op jit(solution)/shard_map/ppermute | solution.py:79
  5.6 35.1 %collective-permute-start.7 = (bf16[96,1024]{1,0:T(8,128)(2,1)S(1)}, bf16[96,1024]{1,0:T(8,128)(2,1)S(1)}, u32[]{:S(2)}, u32[]{:S(2)}) collective-permute-start(bf16[96,1024]{1,0:T(8,128)(2,1)S(1)} %constant_dynamic-update-slice_fusion), channel_id=1, source_target_pairs={{0,1},{1,0},{2,3},{3,2},{4,5},{5,4},{6,7},{7,6},{8,9},{9,8},{10,11... | collective-permute-start | bytes 589832 | tf_op jit(solution)/shard_map/ppermute | solution.py:76
  16.3 42.1 %copy-start.8 = (pred[8]{0:T(512)(128)(4,1)}, pred[8]{0:T(512)(128)(4,1)S(1)}, u32[]{:S(2)}) copy-start(pred[8]{0:T(512)(128)(4,1)S(1)} %compare_and_fusion) | copy-start | bytes 28
  16.3 7.6 %collective-permute-start.1 = (bf16[96,1024]{1,0:T(8,128)(2,1)S(1)}, bf16[96,1024]{1,0:T(8,128)(2,1)S(1)}, u32[]{:S(2)}, u32[]{:S(2)}) collective-permute-start(bf16[96,1024]{1,0:T(8,128)(2,1)S(1)} %collective-permute-done), channel_id=1, source_target_pairs={{4,0},{5,1},{8,4},{9,5},{12,8},{13,9},{14,12},{15,13},{10,14},{11,... | collective-permute-start | bytes 589832 | tf_op jit(solution)/shard_map/ppermute | solution.py:83
  18.3 23.6 %collective-permute-start.8 = (bf16[96,1024]{1,0:T(8,128)(2,1)S(1)}, bf16[96,1024]{1,0:T(8,128)(2,1)S(1)}, u32[]{:S(2)}, u32[]{:S(2)}) collective-permute-start(bf16[96,1024]{1,0:T(8,128)(2,1)S(1)} %collective-permute-done), channel_id=1, source_target_pairs={{0,1},{1,0},{2,3},{3,2},{4,5},{5,4},{6,7},{7,6},{8,9},{9,8},{10,11... | collective-permute-start | bytes 589832 | tf_op jit(solution)/shard_map/ppermute | solution.py:85
  18.5 7.1 %collective-permute-start.4 = (bf16[96,1024]{1,0:T(8,128)(2,1)S(1)}, bf16[96,1024]{1,0:T(8,128)(2,1)S(1)}, u32[]{:S(2)}, u32[]{:S(2)}) collective-permute-start(bf16[96,1024]{1,0:T(8,128)(2,1)S(1)} %collective-permute-done.3), channel_id=1, source_target_pairs={{0,4},{1,5},{4,8},{5,9},{8,12},{9,13},{12,14},{13,15},{14,10},{15,... | collective-permute-start | bytes 589832 | tf_op jit(solution)/shard_map/ppermute | solution.py:79
  18.9 27.7 %collective-permute-start.14 = (bf16[96,1024]{1,0:T(8,128)(2,1)S(1)}, bf16[96,1024]{1,0:T(8,128)(2,1)S(1)}, u32[]{:S(2)}, u32[]{:S(2)}) collective-permute-start(bf16[96,1024]{1,0:T(8,128)(2,1)S(1)} %collective-permute-done.3), channel_id=1, source_target_pairs={{0,1},{1,0},{2,3},{3,2},{4,5},{5,4},{6,7},{7,6},{8,9},{9,8},{10,11... | collective-permute-start | bytes 589832 | tf_op jit(solution)/shard_map/ppermute | solution.py:81
  23.9 6.7 %collective-permute-start.2 = (bf16[96,1024]{1,0:T(8,128)(2,1)S(1)}, bf16[96,1024]{1,0:T(8,128)(2,1)S(1)}, u32[]{:S(2)}, u32[]{:S(2)}) collective-permute-start(bf16[96,1024]{1,0:T(8,128)(2,1)S(1)} %collective-permute-done.1), channel_id=1, source_target_pairs={{4,0},{5,1},{8,4},{9,5},{12,8},{13,9},{14,12},{15,13},{10,14},{11,... | collective-permute-start | bytes 589832 | tf_op jit(solution)/shard_map/ppermute | solution.py:83
  25.6 6.3 %collective-permute-start.5 = (bf16[96,1024]{1,0:T(8,128)(2,1)S(1)}, bf16[96,1024]{1,0:T(8,128)(2,1)S(1)}, u32[]{:S(2)}, u32[]{:S(2)}) collective-permute-start(bf16[96,1024]{1,0:T(8,128)(2,1)S(1)} %collective-permute-done.4), channel_id=1, source_target_pairs={{0,4},{1,5},{4,8},{5,9},{8,12},{9,13},{12,14},{13,15},{14,10},{15,... | collective-permute-start | bytes 589832 | tf_op jit(solution)/shard_map/ppermute | solution.py:79
  30.6 12.0 %collective-permute-start.9 = (bf16[96,1024]{1,0:T(8,128)(2,1)S(1)}, bf16[96,1024]{1,0:T(8,128)(2,1)S(1)}, u32[]{:S(2)}, u32[]{:S(2)}) collective-permute-start(bf16[96,1024]{1,0:T(8,128)(2,1)S(1)} %collective-permute-done.1), channel_id=1, source_target_pairs={{0,1},{1,0},{2,3},{3,2},{4,5},{5,4},{6,7},{7,6},{8,9},{9,8},{10,11... | collective-permute-start | bytes 589832 | tf_op jit(solution)/shard_map/ppermute | solution.py:85
  31.9 6.0 %collective-permute-start.6 = (bf16[96,1024]{1,0:T(8,128)(2,1)S(1)}, bf16[96,1024]{1,0:T(8,128)(2,1)S(1)}, u32[]{:S(2)}, u32[]{:S(2)}) collective-permute-start(bf16[96,1024]{1,0:T(8,128)(2,1)S(1)} %collective-permute-done.5), channel_id=1, source_target_pairs={{0,4},{1,5},{4,8},{5,9},{8,12},{9,13},{12,14},{13,15},{14,10},{15,... | collective-permute-start | bytes 589832 | tf_op jit(solution)/shard_map/ppermute | solution.py:79
  37.9 8.0 %collective-permute-start.13 = (bf16[96,1024]{1,0:T(8,128)(2,1)S(1)}, bf16[96,1024]{1,0:T(8,128)(2,1)S(1)}, u32[]{:S(2)}, u32[]{:S(2)}) collective-permute-start(bf16[96,1024]{1,0:T(8,128)(2,1)S(1)} %collective-permute-done.4), channel_id=1, source_target_pairs={{0,1},{1,0},{2,3},{3,2},{4,5},{5,4},{6,7},{7,6},{8,9},{9,8},{10,11... | collective-permute-start | bytes 589832 | tf_op jit(solution)/shard_map/ppermute | solution.py:81
  40.7 3.1 %collective-permute-start.10 = (bf16[96,1024]{1,0:T(8,128)(2,1)S(1)}, bf16[96,1024]{1,0:T(8,128)(2,1)S(1)}, u32[]{:S(2)}, u32[]{:S(2)}) collective-permute-start(bf16[96,1024]{1,0:T(8,128)(2,1)S(1)} %collective-permute-done.2), channel_id=1, source_target_pairs={{0,1},{1,0},{2,3},{3,2},{4,5},{5,4},{6,7},{7,6},{8,9},{9,8},{10,11... | collective-permute-start | bytes 589832 | tf_op jit(solution)/shard_map/ppermute | solution.py:85
  41.9 3.3 %collective-permute-start.12 = (bf16[96,1024]{1,0:T(8,128)(2,1)S(1)}, bf16[96,1024]{1,0:T(8,128)(2,1)S(1)}, u32[]{:S(2)}, u32[]{:S(2)}) collective-permute-start(bf16[96,1024]{1,0:T(8,128)(2,1)S(1)} %collective-permute-done.5), channel_id=1, source_target_pairs={{0,1},{1,0},{2,3},{3,2},{4,5},{5,4},{6,7},{7,6},{8,9},{9,8},{10,11... | collective-permute-start | bytes 589832 | tf_op jit(solution)/shard_map/ppermute | solution.py:81
  42.6 1.9 %collective-permute-start.11 = (bf16[96,1024]{1,0:T(8,128)(2,1)S(1)}, bf16[96,1024]{1,0:T(8,128)(2,1)S(1)}, u32[]{:S(2)}, u32[]{:S(2)}) collective-permute-start(bf16[96,1024]{1,0:T(8,128)(2,1)S(1)} %collective-permute-done.6), channel_id=1, source_target_pairs={{0,1},{1,0},{2,3},{3,2},{4,5},{5,4},{6,7},{7,6},{8,9},{9,8},{10,11... | collective-permute-start | bytes 589832 | tf_op jit(solution)/shard_map/ppermute | solution.py:81
  57.2 10.6 %collective-permute-start.16 = (bf16[128,1024]{0,1:T(8,128)(2,1)S(1)}, bf16[128,1024]{0,1:T(8,128)(2,1)S(1)}, u32[]{:S(2)}, u32[]{:S(2)}) collective-permute-start(bf16[128,1024]{0,1:T(8,128)(2,1)S(1)} %get-tuple-element.22), channel_id=1, source_target_pairs={{0,1},{1,0},{2,3},{3,2},{4,5},{5,4},{6,7},{7,6},{8,9},{9,8},{10,11... | collective-permute-start | bytes 786440 | tf_op jit(solution)/shard_map/ppermute | solution.py:150
  57.4 9.5 %collective-permute-start.20 = (bf16[128,1024]{0,1:T(8,128)(2,1)S(1)}, bf16[128,1024]{0,1:T(8,128)(2,1)S(1)}, u32[]{:S(2)}, u32[]{:S(2)}) collective-permute-start(bf16[128,1024]{0,1:T(8,128)(2,1)S(1)} %get-tuple-element.14), channel_id=1, source_target_pairs={{0,1},{1,0},{2,3},{3,2},{4,5},{5,4},{6,7},{7,6},{8,9},{9,8},{10,11... | collective-permute-start | bytes 786440 | tf_op jit(solution)/shard_map/ppermute | solution.py:150
  63.6 5.5 %collective-permute-start.22 = (bf16[128,1024]{0,1:T(8,128)(2,1)S(1)}, bf16[128,1024]{0,1:T(8,128)(2,1)S(1)}, u32[]{:S(2)}, u32[]{:S(2)}) collective-permute-start(bf16[128,1024]{0,1:T(8,128)(2,1)S(1)} %get-tuple-element.11), channel_id=1, source_target_pairs={{0,1},{1,0},{2,3},{3,2},{4,5},{5,4},{6,7},{7,6},{8,9},{9,8},{10,11... | collective-permute-start | bytes 786440 | tf_op jit(solution)/shard_map/ppermute | solution.py:150
  63.7 3.9 %collective-permute-start.15 = (bf16[128,8,32]{0,2,1:T(8,128)(2,1)S(1)}, bf16[128,8,32]{0,2,1:T(8,128)(2,1)S(1)}, u32[]{:S(2)}, u32[]{:S(2)}) collective-permute-start(bf16[128,8,32]{0,2,1:T(8,128)(2,1)S(1)} %dynamic-slice_bitcast_fusion.3), channel_id=1, source_target_pairs={{0,1},{1,0},{2,3},{3,2},{4,5},{5,4},{6,7},{7,6},{8,9},{9,8},{10,11... | collective-permute-start | bytes 196616 | tf_op jit(solution)/shard_map/ppermute | solution.py:147
  64.1 1.2 collective-permute-start.23
  65.3 1.3 %collective-permute-start.19 = (bf16[128,8,64]{0,2,1:T(8,128)(2,1)S(1)}, bf16[128,8,64]{0,2,1:T(8,128)(2,1)S(1)}, u32[]{:S(2)}, u32[]{:S(2)}) collective-permute-start(bf16[128,8,64]{0,2,1:T(8,128)(2,1)S(1)} %dynamic-slice_bitcast_fusion.1), channel_id=1, source_target_pairs={{0,1},{1,0},{2,3},{3,2},{4,5},{5,4},{6,7},{7,6},{8,9},{9,8},{10,11... | collective-permute-start | bytes 393224 | tf_op jit(solution)/shard_map/ppermute | solution.py:147
  66.7 1.8 %collective-permute-start.18 = (bf16[128,1024]{0,1:T(8,128)(2,1)S(1)}, bf16[128,1024]{0,1:T(8,128)(2,1)S(1)}, u32[]{:S(2)}, u32[]{:S(2)}) collective-permute-start(bf16[128,1024]{0,1:T(8,128)(2,1)S(1)} %fusion.1), channel_id=1, source_target_pairs={{0,1},{1,0},{2,3},{3,2},{4,5},{5,4},{6,7},{7,6},{8,9},{9,8},{10,11... | collective-permute-start | bytes 786440 | tf_op jit(solution)/shard_map/ppermute | solution.py:150
  66.8 1.6 %collective-permute-start.17 = (bf16[128,8,32]{0,2,1:T(8,128)(2,1)S(1)}, bf16[128,8,32]{0,2,1:T(8,128)(2,1)S(1)}, u32[]{:S(2)}, u32[]{:S(2)}) collective-permute-start(bf16[128,8,32]{0,2,1:T(8,128)(2,1)S(1)} %dynamic-slice_bitcast_fusion.2), channel_id=1, source_target_pairs={{0,1},{1,0},{2,3},{3,2},{4,5},{5,4},{6,7},{7,6},{8,9},{9,8},{10,11... | collective-permute-start | bytes 196616 | tf_op jit(solution)/shard_map/ppermute | solution.py:147
  67.6 1.4 %collective-permute-start.21 = (bf16[128,8,64]{0,2,1:T(8,128)(2,1)S(1)}, bf16[128,8,64]{0,2,1:T(8,128)(2,1)S(1)}, u32[]{:S(2)}, u32[]{:S(2)}) collective-permute-start(bf16[128,8,64]{0,2,1:T(8,128)(2,1)S(1)} %dynamic-slice_bitcast_fusion), channel_id=1, source_target_pairs={{0,1},{1,0},{2,3},{3,2},{4,5},{5,4},{6,7},{7,6},{8,9},{9,8},{10,11... | collective-permute-start | bytes 393224 | tf_op jit(solution)/shard_map/ppermute | solution.py:147
  70.1 11.9 %collective-permute-start.24 = (f32[104,1024]{1,0:T(8,128)S(1)}, f32[104,1024]{1,0:T(8,128)S(1)}, u32[]{:S(2)}, u32[]{:S(2)}) collective-permute-start(f32[104,1024]{1,0:T(8,128)S(1)} %get-tuple-element.9), channel_id=1, source_target_pairs={{0,4},{1,5},{4,8},{5,9},{8,12},{9,13},{12,14},{13,15},{14,10},{15,... | collective-permute-start | bytes 1277960 | tf_op jit(solution)/shard_map/ppermute | solution.py:102
  71.7 12.0 %collective-permute-start.28 = (f32[104,1024]{1,0:T(8,128)S(1)}, f32[104,1024]{1,0:T(8,128)S(1)}, u32[]{:S(2)}, u32[]{:S(2)}) collective-permute-start(f32[104,1024]{1,0:T(8,128)S(1)} %get-tuple-element.10), channel_id=1, source_target_pairs={{4,0},{5,1},{8,4},{9,5},{12,8},{13,9},{14,12},{15,13},{10,14},{11,... | collective-permute-start | bytes 1277960 | tf_op jit(solution)/shard_map/ppermute | solution.py:106
  82.1 11.1 %collective-permute-start.25 = (f32[104,1024]{1,0:T(8,128)S(1)}, f32[104,1024]{1,0:T(8,128)S(1)}, u32[]{:S(2)}, u32[]{:S(2)}) collective-permute-start(f32[104,1024]{1,0:T(8,128)S(1)} %fusion.11), channel_id=1, source_target_pairs={{0,4},{1,5},{4,8},{5,9},{8,12},{9,13},{12,14},{13,15},{14,10},{15,... | collective-permute-start | bytes 1277960 | tf_op jit(solution)/shard_map/ppermute | solution.py:102
  93.3 10.2 %collective-permute-start.26 = (f32[104,1024]{1,0:T(8,128)S(1)}, f32[104,1024]{1,0:T(8,128)S(1)}, u32[]{:S(2)}, u32[]{:S(2)}) collective-permute-start(f32[104,1024]{1,0:T(8,128)S(1)} %get-tuple-element.7), channel_id=1, source_target_pairs={{0,4},{1,5},{4,8},{5,9},{8,12},{9,13},{12,14},{13,15},{14,10},{15,... | collective-permute-start | bytes 1277960 | tf_op jit(solution)/shard_map/ppermute | solution.py:102
  95.0 9.9 %collective-permute-start.29 = (f32[104,1024]{1,0:T(8,128)S(1)}, f32[104,1024]{1,0:T(8,128)S(1)}, u32[]{:S(2)}, u32[]{:S(2)}) collective-permute-start(f32[104,1024]{1,0:T(8,128)S(1)} %get-tuple-element.8), channel_id=1, source_target_pairs={{4,0},{5,1},{8,4},{9,5},{12,8},{13,9},{14,12},{15,13},{10,14},{11,... | collective-permute-start | bytes 1277960 | tf_op jit(solution)/shard_map/ppermute | solution.py:106
  105.0 9.0 %collective-permute-start.27 = (f32[104,1024]{1,0:T(8,128)S(1)}, f32[104,1024]{1,0:T(8,128)S(1)}, u32[]{:S(2)}, u32[]{:S(2)}) collective-permute-start(f32[104,1024]{1,0:T(8,128)S(1)} %get-tuple-element.5), channel_id=1, source_target_pairs={{0,4},{1,5},{4,8},{5,9},{8,12},{9,13},{12,14},{13,15},{14,10},{15,... | collective-permute-start | bytes 1277960 | tf_op jit(solution)/shard_map/ppermute | solution.py:102
  106.6 8.7 %collective-permute-start.30 = (f32[104,1024]{1,0:T(8,128)S(1)}, f32[104,1024]{1,0:T(8,128)S(1)}, u32[]{:S(2)}, u32[]{:S(2)}) collective-permute-start(f32[104,1024]{1,0:T(8,128)S(1)} %get-tuple-element.6), channel_id=1, source_target_pairs={{4,0},{5,1},{8,4},{9,5},{12,8},{13,9},{14,12},{15,13},{10,14},{11,... | collective-permute-start | bytes 1277960 | tf_op jit(solution)/shard_map/ppermute | solution.py:106
  (16 other events, 134.0 us)

commit v6 on v5

--- a/solution.py
+++ b/solution.py
@@ -71,20 +71,16 @@
     core, chip = position % 2, position // 2
     spot = jnp.asarray(place, jnp.int32)[chip]
     rel = [None] * chips
-    rel_other = [None] * chips
     rel[0] = x
-    rel_other[0] = lax.ppermute(x, "blk", partner)
     left = right = x
     for s in range(1, ahead + 1):
         left = lax.ppermute(left, "blk", cw)
         rel[chips - s] = left
-        rel_other[chips - s] = lax.ppermute(left, "blk", partner)
         if s <= behind:
             right = lax.ppermute(right, "blk", ccw)
             rel[s] = right
-            rel_other[s] = lax.ppermute(right, "blk", partner)
     mine = jnp.stack(rel)
-    other = jnp.stack(rel_other)
+    other = lax.ppermute(mine, "blk", partner)
     both = jnp.concatenate([mine, other], axis=0)
     dest = jnp.arange(n_blk, dtype=jnp.int32)
     dest_chip, dest_core = dest // 2, dest % 2

time: 120 us -> 115 us (0.958)
  local copies, waits for them, and re-layouts: 24.2 us -> 18.4 us
  matrix products: 10.9 us -> 13.6 us
  starting transfers between devices: 19.3 us -> 17.7 us
    unnamed x51 -> x49, local copies, waits for them, and re-layouts: 13.2 us -> 6.67 us
    ppermute x4, starting transfers between devices: 6.6 us -> 3.84 us  [ring_reduce_scatter(): acc = lax.ppermute(acc, 'blk', cw) + summed[(ahead - s) % chips]]
    ppermute x4, waiting for transfers between devices: 6.18 us -> 8.85 us  [ring_all_gather(): left = lax.ppermute(left, 'blk', cw)]
    ppermute x3, waiting for transfers between devices: 8.21 us -> 6.08 us  [ring_all_gather(): right = lax.ppermute(right, 'blk', ccw)]
    ppermute x3, starting transfers between devices: 1.29 us -> 3.08 us  [ring_reduce_scatter(): acc_back = lax.ppermute(acc_back, 'blk', ccw)]
    ppermute x4, waiting for transfers between devices: 34.3 us -> 36.1 us  [ring_reduce_scatter(): acc = lax.ppermute(acc, 'blk', cw) + summed[(ahead - s) % chips]]
    ppermute x8 -> x1, starting transfers between devices: 1.25 us -> 0.01 us  [ring_all_gather(): other = lax.ppermute(mine, 'blk', partner)]
  transfers between devices with their start and end apart: 31 -> 24, of which waited for: 13 -> 13; matrix products, arithmetic and copies ran while one was open for 23% -> 17% of each run, Pallas kernels for 0% -> 0%
where the time goes in v6:
time: 115 us
  waiting for transfers between devices  53.9 us (47%)
  local copies, waits for them, and re-layouts  18.4 us (16%)
  starting transfers between devices  17.7 us (15%)
  matrix products  13.6 us (12%)
  other arithmetic  9.61 us (8%)
  between operations  1.92 us (2%)
    ppermute x4, waiting for transfers between devices, ring_reduce_scatter(): acc = lax.ppermute(acc, 'blk', cw) + summed[(ahead - s) % chips]  36.1 us
    ppermute x4, waiting for transfers between devices, ring_all_gather(): left = lax.ppermute(left, 'blk', cw)  8.85 us
    unnamed x49, local copies, waits for them, and re-layouts  6.67 us
    ppermute x3, waiting for transfers between devices, ring_all_gather(): right = lax.ppermute(right, 'blk', ccw)  6.08 us
    ppermute x3, starting transfers between devices, ring_all_gather(): right = lax.ppermute(right, 'blk', ccw)  6.07 us
    dot_general x8, matrix products, slots_product(): lax.dot_general(left, right, (((0,), (0,)), ((), ())), preferred_element_...  4.04 us
    ppermute x4, starting transfers between devices, ring_reduce_scatter(): acc = lax.ppermute(acc, 'blk', cw) + summed[(ahead - s) % chips]  3.84 us
    ppermute x3, starting transfers between devices, ring_reduce_scatter(): acc_back = lax.ppermute(acc_back, 'blk', ccw)  3.08 us
  transfers between devices with their start and end apart: 24, of which 13 were waited for; matrix products, arithmetic and copies ran while one was open for 17% of the time, Pallas kernels for 0%

profile of v6, /device:TPU:0, one launch (start us, length us, event | category | flops | bytes accessed | tf_op | source)
XLA Modules:
  0.0 115.0 jit_solution(6651299445245889785)
XLA Ops:
  0.6 0.9 constant_dynamic-update-slice_fusion.1
  1.5 0.9 constant_dynamic-update-slice_fusion
  2.4 3.0 %collective-permute-start = (bf16[96,1024]{1,0:T(8,128)(2,1)S(1)}, bf16[96,1024]{1,0:T(8,128)(2,1)S(1)}, u32[]{:S(2)}, u32[]{:S(2)}) collective-permute-start(bf16[96,1024]{1,0:T(8,128)(2,1)S(1)} %constant_dynamic-update-slice_fusion), channel_id=1, source_target_pairs={{4,0},{5,1},{8,4},{9,5},{12,8},{13,9},{14,12},{15,13},{10,14},{11,... | collective-permute-start | bytes 589832 | tf_op jit(solution)/shard_map/ppermute | solution.py:80
  5.6 1.2 %dynamic_slice.37 = s32[1]{0:T(128)} dynamic-slice(s32[8]{0:T(128)} %constant.180.clone, s32[]{:T(128)S(6)} %select_n.178), dynamic_slice_sizes={1} | dynamic-slice | bytes 12 | tf_op jit(solution)/shard_map/dynamic_slice | solution.py:72
  7.6 2.8 %collective-permute-done = bf16[96,1024]{1,0:T(8,128)(2,1)S(1)} collective-permute-done((bf16[96,1024]{1,0:T(8,128)(2,1)S(1)}, bf16[96,1024]{1,0:T(8,128)(2,1)S(1)}, u32[]{:S(2)}, u32[]{:S(2)}) %collective-permute-start) | collective-permute-done | bytes 196640 | tf_op jit(solution)/shard_map/ppermute | solution.py:80
  10.4 1.7 %collective-permute-start.1 = (bf16[96,1024]{1,0:T(8,128)(2,1)S(1)}, bf16[96,1024]{1,0:T(8,128)(2,1)S(1)}, u32[]{:S(2)}, u32[]{:S(2)}) collective-permute-start(bf16[96,1024]{1,0:T(8,128)(2,1)S(1)} %collective-permute-done), channel_id=1, source_target_pairs={{4,0},{5,1},{8,4},{9,5},{12,8},{13,9},{14,12},{15,13},{10,14},{11,... | collective-permute-start | bytes 589832 | tf_op jit(solution)/shard_map/ppermute | solution.py:80
  13.2 3.3 %collective-permute-done.1 = bf16[96,1024]{1,0:T(8,128)(2,1)S(1)} collective-permute-done((bf16[96,1024]{1,0:T(8,128)(2,1)S(1)}, bf16[96,1024]{1,0:T(8,128)(2,1)S(1)}, u32[]{:S(2)}, u32[]{:S(2)}) %collective-permute-start.1) | collective-permute-done | bytes 196640 | tf_op jit(solution)/shard_map/ppermute | solution.py:80
  16.5 1.4 %collective-permute-start.2 = (bf16[96,1024]{1,0:T(8,128)(2,1)S(1)}, bf16[96,1024]{1,0:T(8,128)(2,1)S(1)}, u32[]{:S(2)}, u32[]{:S(2)}) collective-permute-start(bf16[96,1024]{1,0:T(8,128)(2,1)S(1)} %collective-permute-done.1), channel_id=1, source_target_pairs={{4,0},{5,1},{8,4},{9,5},{12,8},{13,9},{14,12},{15,13},{10,14},{11,... | collective-permute-start | bytes 589832 | tf_op jit(solution)/shard_map/ppermute | solution.py:80
  19.3 4.6 %collective-permute-done.5 = bf16[96,1024]{1,0:T(8,128)(2,1)S(1)} collective-permute-done((bf16[96,1024]{1,0:T(8,128)(2,1)S(1)}, bf16[96,1024]{1,0:T(8,128)(2,1)S(1)}, u32[]{:S(2)}, u32[]{:S(2)}) %collective-permute-start.5) | collective-permute-done | bytes 196640 | tf_op jit(solution)/shard_map/ppermute | solution.py:77
  24.6 0.8 bitcast_dynamic-update-slice_fusion.9
  25.4 4.2 %collective-permute-done.6 = bf16[96,1024]{1,0:T(8,128)(2,1)S(1)} collective-permute-done((bf16[96,1024]{1,0:T(8,128)(2,1)S(1)}, bf16[96,1024]{1,0:T(8,128)(2,1)S(1)}, u32[]{:S(2)}, u32[]{:S(2)}) %collective-permute-start.6) | collective-permute-done | bytes 196640 | tf_op jit(solution)/shard_map/ppermute | solution.py:77
  29.6 0.8 bitcast_dynamic-update-slice_fusion.7
  30.4 0.8 bitcast_dynamic-update-slice_fusion.5
  31.2 0.8 bitcast_dynamic-update-slice_fusion.3
  32.0 0.8 bitcast_dynamic-update-slice_fusion.1
  39.4 1.3 %constant_dynamic-update-slice_fusion.2 = bf16[16,96,1024]{2,1,0:T(8,128)(2,1)} fusion(bf16[16,96,1024]{2,1,0:T(8,128)(2,1)} %get-tuple-element.16, bf16[8,96,1024]{2,1,0:T(8,128)(2,1)S(1)} %collective-permute-done.7), kind=kLoop, calls=%fused_computation.96 | loop fusion | bytes 3145728 | tf_op jit(solution)/shard_map/concatenate | solution.py:84
  40.7 2.6 %gather_fusion.1 = bf16[16,96,1024]{2,1,0:T(8,128)(2,1)S(1)} fusion(bf16[16,96,1024]{2,1,0:T(8,128)(2,1)} %constant_dynamic-update-slice_fusion.2, s32[1024]{0:T(1024)S(1)} %pad_clamp_fusion.1), kind=kCustom, calls=%fused_computation.5 | custom fusion | bytes 6291520 | tf_op jit(solution)/shard_map/jit(_take)/gather | solution.py:89
  44.6 2.6 %multiply_reduce_fusion = (f32[128]{0:T(128)}, bf16[128,1024]{0,1:T(8,128)(2,1)}, f32[128,1024]{0,1:T(8,128)}) fusion(f32[1024]{0:T(1024)S(1)} %convert_element_type.33, bf16[128,1024]{0,1:T(8,128)(2,1)S(1)} %get-tuple-element.35, bf16[1024,1024]{1,0:T(8,128)(2,1)S(1)} %bitcast.146), kind=kOutput, calls=%fused_computation.25 | convolution fusion | flops 270139264 | bytes 3150336 | tf_op jit(solution)/shard_map/dot_general | solution.py:20
  47.2 2.5 %multiply_convert_fusion.1 = (bf16[128,1024]{0,1:T(8,128)(2,1)S(1)}, f32[128,1024]{0,1:T(8,128)}) fusion(f32[128,1024]{0,1:T(8,128)S(1)} %get-tuple-element.36, bf16[1024,1024]{1,0:T(8,128)(2,1)S(1)} %bitcast.147, bf16[128,1024]{0,1:T(8,128)(2,1)} %get-tuple-element.14), kind=kOutput, calls=%fused_computation.27 | convolution fusion | flops 269090816 | bytes 3670016 | tf_op jit(solution)/shard_map/dot_general | solution.py:25
  50.2 1.4 %multiply_convert_fusion = (bf16[128,1024]{0,1:T(8,128)(2,1)S(1)}, f32[128,1024]{0,1:T(8,128)}) fusion(f32[128,1024]{0,1:T(8,128)S(1)} %get-tuple-element.36, bf16[128,512]{1,0:T(8,128)(2,1)S(1)} %fusion.3, bf16[512,1024]{1,0:T(8,128)(2,1)S(1)} %bitcast.143), kind=kOutput, calls=%fused_computation.26 | convolution fusion | flops 134873088 | bytes 2490368 | tf_op jit(solution)/shard_map/dot_general | solution.py:34
  55.4 1.5 %fusion.17 = f32[8,64,1024]{2,1,0:T(8,128)S(1)} fusion(bf16[128,1024]{0,1:T(8,128)(2,1)} %get-tuple-element.14, bf16[128,8,2,64]{0,3,2,1:T(8,128)(2,1)S(1)} %get-tuple-element.33, s32[]{:T(128)S(6)} %select_n.189), kind=kOutput, calls=%fused_computation.51 | convolution fusion | flops 134217728 | bytes 2490372 | tf_op jit(solution)/shard_map/dot_general | solution.py:110
  57.6 1.4 %add_convert_fusion = (bf16[128,1024]{0,1:T(8,128)(2,1)S(1)}, f32[1024]{0:T(1024)S(1)}) fusion(f32[128]{0:T(128)S(1)} %subtract_multiply_fusion, f32[1024]{0:T(1024)S(1)} %convert_element_type.33, f32[128,1024]{0,1:T(8,128)S(1)} %copy-done.19, bf16[128,1024]{0,1:T(8,128)(2,1)S(1)} %get-tuple-element.40, bf16[1024,1024]{1,0:T(8,128)(2,1)S(1)} %bitcast.148), kind=kOutput, calls=%fused_computation.24 | convolution fusion | flops 271186944 | bytes 3154432 | tf_op jit(solution)/shard_map/dot_general | solution.py:37
  61.7 0.9 collective-permute-done.12
  66.8 1.4 %collective-permute-start.21 = (f32[104,1024]{1,0:T(8,128)S(1)}, f32[104,1024]{1,0:T(8,128)S(1)}, u32[]{:S(2)}, u32[]{:S(2)}) collective-permute-start(f32[104,1024]{1,0:T(8,128)S(1)} %get-tuple-element.10), channel_id=1, source_target_pairs={{4,0},{5,1},{8,4},{9,5},{12,8},{13,9},{14,12},{15,13},{10,14},{11,... | collective-permute-start | bytes 1277960 | tf_op jit(solution)/shard_map/ppermute | solution.py:102
  68.1 10.0 %collective-permute-done.17 = f32[104,1024]{1,0:T(8,128)S(1)} collective-permute-done((f32[104,1024]{1,0:T(8,128)S(1)}, f32[104,1024]{1,0:T(8,128)S(1)}, u32[]{:S(2)}, u32[]{:S(2)}) %collective-permute-start.17) | collective-permute-done | bytes 426016 | tf_op jit(solution)/shard_map/ppermute | solution.py:98
  78.9 10.6 %collective-permute-done.18 = f32[104,1024]{1,0:T(8,128)S(1)} collective-permute-done((f32[104,1024]{1,0:T(8,128)S(1)}, f32[104,1024]{1,0:T(8,128)S(1)}, u32[]{:S(2)}, u32[]{:S(2)}) %collective-permute-start.18) | collective-permute-done | bytes 426016 | tf_op jit(solution)/shard_map/ppermute | solution.py:98
  90.3 1.4 %collective-permute-start.22 = (f32[104,1024]{1,0:T(8,128)S(1)}, f32[104,1024]{1,0:T(8,128)S(1)}, u32[]{:S(2)}, u32[]{:S(2)}) collective-permute-start(f32[104,1024]{1,0:T(8,128)S(1)} %get-tuple-element.8), channel_id=1, source_target_pairs={{4,0},{5,1},{8,4},{9,5},{12,8},{13,9},{14,12},{15,13},{10,14},{11,... | collective-permute-start | bytes 1277960 | tf_op jit(solution)/shard_map/ppermute | solution.py:102
  91.7 8.3 %collective-permute-done.19 = f32[104,1024]{1,0:T(8,128)S(1)} collective-permute-done((f32[104,1024]{1,0:T(8,128)S(1)}, f32[104,1024]{1,0:T(8,128)S(1)}, u32[]{:S(2)}, u32[]{:S(2)}) %collective-permute-start.19) | collective-permute-done | bytes 426016 | tf_op jit(solution)/shard_map/ppermute | solution.py:98
  100.5 1.8 %collective-permute-start.20 = (f32[104,1024]{1,0:T(8,128)S(1)}, f32[104,1024]{1,0:T(8,128)S(1)}, u32[]{:S(2)}, u32[]{:S(2)}) collective-permute-start(f32[104,1024]{1,0:T(8,128)S(1)} %get-tuple-element.5), channel_id=1, source_target_pairs={{0,4},{1,5},{4,8},{5,9},{8,12},{9,13},{12,14},{13,15},{14,10},{15,... | collective-permute-start | bytes 1277960 | tf_op jit(solution)/shard_map/ppermute | solution.py:98
  102.6 7.1 %collective-permute-done.20 = f32[104,1024]{1,0:T(8,128)S(1)} collective-permute-done((f32[104,1024]{1,0:T(8,128)S(1)}, f32[104,1024]{1,0:T(8,128)S(1)}, u32[]{:S(2)}, u32[]{:S(2)}) %collective-permute-start.20) | collective-permute-done | bytes 426016 | tf_op jit(solution)/shard_map/ppermute | solution.py:98
  109.7 1.4 %collective-permute-done.23 = f32[104,1024]{1,0:T(8,128)S(1)} collective-permute-done((f32[104,1024]{1,0:T(8,128)S(1)}, f32[104,1024]{1,0:T(8,128)S(1)}, u32[]{:S(2)}, u32[]{:S(2)}) %collective-permute-start.23) | collective-permute-done | bytes 426016 | tf_op jit(solution)/shard_map/ppermute | solution.py:102
  113.5 0.8 multiply_add_fusion
  (133 shorter events, 28.0 us)
Async XLA Ops:
  0.6 34.4 %copy-start = (s32[16,16]{1,0:T(8,128)S(1)}, s32[16,16]{1,0:T(8,128)}, u32[]{:S(2)}) copy-start(s32[16,16]{1,0:T(8,128)} %param.21) | copy-start | bytes 3076
  2.4 8.0 %collective-permute-start = (bf16[96,1024]{1,0:T(8,128)(2,1)S(1)}, bf16[96,1024]{1,0:T(8,128)(2,1)S(1)}, u32[]{:S(2)}, u32[]{:S(2)}) collective-permute-start(bf16[96,1024]{1,0:T(8,128)(2,1)S(1)} %constant_dynamic-update-slice_fusion), channel_id=1, source_target_pairs={{4,0},{5,1},{8,4},{9,5},{12,8},{13,9},{14,12},{15,13},{10,14},{11,... | collective-permute-start | bytes 589832 | tf_op jit(solution)/shard_map/ppermute | solution.py:80
  5.4 6.6 %collective-permute-start.3 = (bf16[96,1024]{1,0:T(8,128)(2,1)S(1)}, bf16[96,1024]{1,0:T(8,128)(2,1)S(1)}, u32[]{:S(2)}, u32[]{:S(2)}) collective-permute-start(bf16[96,1024]{1,0:T(8,128)(2,1)S(1)} %constant_dynamic-update-slice_fusion), channel_id=1, source_target_pairs={{0,4},{1,5},{4,8},{5,9},{8,12},{9,13},{12,14},{13,15},{14,10},{15,... | collective-permute-start | bytes 589832 | tf_op jit(solution)/shard_map/ppermute | solution.py:77
  7.6 26.0 %copy-start.2 = (s32[8]{0:T(128)S(1)}, s32[8]{0:T(128)}, u32[]{:S(2)}) copy-start(s32[8]{0:T(128)} %constant.181.clone) | copy-start | bytes 100
  10.4 6.1 %collective-permute-start.1 = (bf16[96,1024]{1,0:T(8,128)(2,1)S(1)}, bf16[96,1024]{1,0:T(8,128)(2,1)S(1)}, u32[]{:S(2)}, u32[]{:S(2)}) collective-permute-start(bf16[96,1024]{1,0:T(8,128)(2,1)S(1)} %collective-permute-done), channel_id=1, source_target_pairs={{4,0},{5,1},{8,4},{9,5},{12,8},{13,9},{14,12},{15,13},{10,14},{11,... | collective-permute-start | bytes 589832 | tf_op jit(solution)/shard_map/ppermute | solution.py:80
  12.1 5.8 %collective-permute-start.4 = (bf16[96,1024]{1,0:T(8,128)(2,1)S(1)}, bf16[96,1024]{1,0:T(8,128)(2,1)S(1)}, u32[]{:S(2)}, u32[]{:S(2)}) collective-permute-start(bf16[96,1024]{1,0:T(8,128)(2,1)S(1)} %collective-permute-done.3), channel_id=1, source_target_pairs={{0,4},{1,5},{4,8},{5,9},{8,12},{9,13},{12,14},{13,15},{14,10},{15,... | collective-permute-start | bytes 589832 | tf_op jit(solution)/shard_map/ppermute | solution.py:77
  13.2 21.0 %copy-start.1 = (s32[8]{0:T(128)S(1)}, s32[8]{0:T(128)}, u32[]{:S(2)}) copy-start(s32[8]{0:T(128)} %constant.180.clone) | copy-start | bytes 100
  16.5 8.1 %collective-permute-start.2 = (bf16[96,1024]{1,0:T(8,128)(2,1)S(1)}, bf16[96,1024]{1,0:T(8,128)(2,1)S(1)}, u32[]{:S(2)}, u32[]{:S(2)}) collective-permute-start(bf16[96,1024]{1,0:T(8,128)(2,1)S(1)} %collective-permute-done.1), channel_id=1, source_target_pairs={{4,0},{5,1},{8,4},{9,5},{12,8},{13,9},{14,12},{15,13},{10,14},{11,... | collective-permute-start | bytes 589832 | tf_op jit(solution)/shard_map/ppermute | solution.py:80
  17.8 6.1 %collective-permute-start.5 = (bf16[96,1024]{1,0:T(8,128)(2,1)S(1)}, bf16[96,1024]{1,0:T(8,128)(2,1)S(1)}, u32[]{:S(2)}, u32[]{:S(2)}) collective-permute-start(bf16[96,1024]{1,0:T(8,128)(2,1)S(1)} %collective-permute-done.4), channel_id=1, source_target_pairs={{0,4},{1,5},{4,8},{5,9},{8,12},{9,13},{12,14},{13,15},{14,10},{15,... | collective-permute-start | bytes 589832 | tf_op jit(solution)/shard_map/ppermute | solution.py:77
  19.3 15.6 %copy-start.11 = (bf16[1024]{0:T(1024)(128)(2,1)S(1)}, bf16[1024]{0:T(1024)(128)(2,1)}, u32[]{:S(2)}) copy-start(bf16[1024]{0:T(1024)(128)(2,1)} %param.24) | copy-start | bytes 6148
  19.3 15.6 %copy-start.7 = (bf16[128,512]{1,0:T(8,128)(2,1)S(1)}, bf16[128,512]{1,0:T(8,128)(2,1)}, u32[]{:S(2)}) copy-start(bf16[128,512]{1,0:T(8,128)(2,1)} %param.18) | copy-start | bytes 393220
  24.0 5.7 %collective-permute-start.6 = (bf16[96,1024]{1,0:T(8,128)(2,1)S(1)}, bf16[96,1024]{1,0:T(8,128)(2,1)S(1)}, u32[]{:S(2)}, u32[]{:S(2)}) collective-permute-start(bf16[96,1024]{1,0:T(8,128)(2,1)S(1)} %collective-permute-done.5), channel_id=1, source_target_pairs={{0,4},{1,5},{4,8},{5,9},{8,12},{9,13},{12,14},{13,15},{14,10},{15,... | collective-permute-start | bytes 589832 | tf_op jit(solution)/shard_map/ppermute | solution.py:77
  32.8 6.6 %collective-permute-start.7 = (bf16[8,96,1024]{2,1,0:T(8,128)(2,1)}, bf16[8,96,1024]{2,1,0:T(8,128)(2,1)S(1)}, u32[]{:S(2)}, u32[]{:S(2)}) collective-permute-start(bf16[8,96,1024]{2,1,0:T(8,128)(2,1)} %get-tuple-element.15), channel_id=1, source_target_pairs={{0,1},{1,0},{2,3},{3,2},{4,5},{5,4},{6,7},{7,6},{8,9},{9,8},{10,11... | collective-permute-start | bytes 4718600 | tf_op jit(solution)/shard_map/ppermute | solution.py:83
  51.7 12.3 %collective-permute-start.9 = (bf16[128,1024]{0,1:T(8,128)(2,1)S(1)}, bf16[128,1024]{0,1:T(8,128)(2,1)S(1)}, u32[]{:S(2)}, u32[]{:S(2)}) collective-permute-start(bf16[128,1024]{0,1:T(8,128)(2,1)S(1)} %get-tuple-element.38), channel_id=1, source_target_pairs={{0,1},{1,0},{2,3},{3,2},{4,5},{5,4},{6,7},{7,6},{8,9},{9,8},{10,11... | collective-permute-start | bytes 786440 | tf_op jit(solution)/shard_map/ppermute | solution.py:146
  52.3 10.7 %collective-permute-start.13 = (bf16[128,1024]{0,1:T(8,128)(2,1)}, bf16[128,1024]{0,1:T(8,128)(2,1)S(1)}, u32[]{:S(2)}, u32[]{:S(2)}) collective-permute-start(bf16[128,1024]{0,1:T(8,128)(2,1)} %get-tuple-element.14), channel_id=1, source_target_pairs={{0,1},{1,0},{2,3},{3,2},{4,5},{5,4},{6,7},{7,6},{8,9},{9,8},{10,11... | collective-permute-start | bytes 786440 | tf_op jit(solution)/shard_map/ppermute | solution.py:146
  59.5 5.6 %collective-permute-start.15 = (bf16[128,1024]{0,1:T(8,128)(2,1)S(1)}, bf16[128,1024]{0,1:T(8,128)(2,1)S(1)}, u32[]{:S(2)}, u32[]{:S(2)}) collective-permute-start(bf16[128,1024]{0,1:T(8,128)(2,1)S(1)} %get-tuple-element.11), channel_id=1, source_target_pairs={{0,1},{1,0},{2,3},{3,2},{4,5},{5,4},{6,7},{7,6},{8,9},{9,8},{10,11... | collective-permute-start | bytes 786440 | tf_op jit(solution)/shard_map/ppermute | solution.py:146
  60.0 3.6 %collective-permute-start.8 = (bf16[128,8,32]{0,2,1:T(8,128)(2,1)}, bf16[128,8,32]{0,2,1:T(8,128)(2,1)S(1)}, u32[]{:S(2)}, u32[]{:S(2)}) collective-permute-start(bf16[128,8,32]{0,2,1:T(8,128)(2,1)} %dynamic-slice_bitcast_fusion.3), channel_id=1, source_target_pairs={{0,1},{1,0},{2,3},{3,2},{4,5},{5,4},{6,7},{7,6},{8,9},{9,8},{10,11... | collective-permute-start | bytes 196616 | tf_op jit(solution)/shard_map/ppermute | solution.py:143
  60.1 1.3 %collective-permute-start.16 = (f32[1024]{0:T(1024)S(1)}, f32[1024]{0:T(1024)S(1)}, u32[]{:S(2)}, u32[]{:S(2)}) collective-permute-start(f32[1024]{0:T(1024)S(1)} %get-tuple-element.12), channel_id=1, source_target_pairs={{0,1},{1,0},{2,3},{3,2},{4,5},{5,4},{6,7},{7,6},{8,9},{9,8},{10,11... | collective-permute-start | bytes 12296 | tf_op jit(solution)/shard_map/ppermute | solution.py:146
  61.3 1.4 %collective-permute-start.12 = (bf16[128,8,64]{0,2,1:T(8,128)(2,1)S(1)}, bf16[128,8,64]{0,2,1:T(8,128)(2,1)S(1)}, u32[]{:S(2)}, u32[]{:S(2)}) collective-permute-start(bf16[128,8,64]{0,2,1:T(8,128)(2,1)S(1)} %dynamic-slice_bitcast_fusion.1), channel_id=1, source_target_pairs={{0,1},{1,0},{2,3},{3,2},{4,5},{5,4},{6,7},{7,6},{8,9},{9,8},{10,11... | collective-permute-start | bytes 393224 | tf_op jit(solution)/shard_map/ppermute | solution.py:143
  62.7 2.0 %collective-permute-start.11 = (bf16[128,1024]{0,1:T(8,128)(2,1)S(1)}, bf16[128,1024]{0,1:T(8,128)(2,1)S(1)}, u32[]{:S(2)}, u32[]{:S(2)}) collective-permute-start(bf16[128,1024]{0,1:T(8,128)(2,1)S(1)} %fusion.1), channel_id=1, source_target_pairs={{0,1},{1,0},{2,3},{3,2},{4,5},{5,4},{6,7},{7,6},{8,9},{9,8},{10,11... | collective-permute-start | bytes 786440 | tf_op jit(solution)/shard_map/ppermute | solution.py:146
  63.0 1.6 %collective-permute-start.10 = (bf16[128,8,32]{0,2,1:T(8,128)(2,1)S(1)}, bf16[128,8,32]{0,2,1:T(8,128)(2,1)S(1)}, u32[]{:S(2)}, u32[]{:S(2)}) collective-permute-start(bf16[128,8,32]{0,2,1:T(8,128)(2,1)S(1)} %dynamic-slice_bitcast_fusion.2), channel_id=1, source_target_pairs={{0,1},{1,0},{2,3},{3,2},{4,5},{5,4},{6,7},{7,6},{8,9},{9,8},{10,11... | collective-permute-start | bytes 196616 | tf_op jit(solution)/shard_map/ppermute | solution.py:143
  63.6 1.4 %collective-permute-start.14 = (bf16[128,8,64]{0,2,1:T(8,128)(2,1)S(1)}, bf16[128,8,64]{0,2,1:T(8,128)(2,1)S(1)}, u32[]{:S(2)}, u32[]{:S(2)}) collective-permute-start(bf16[128,8,64]{0,2,1:T(8,128)(2,1)S(1)} %dynamic-slice_bitcast_fusion), channel_id=1, source_target_pairs={{0,1},{1,0},{2,3},{3,2},{4,5},{5,4},{6,7},{7,6},{8,9},{9,8},{10,11... | collective-permute-start | bytes 393224 | tf_op jit(solution)/shard_map/ppermute | solution.py:143
  66.1 12.1 %collective-permute-start.17 = (f32[104,1024]{1,0:T(8,128)S(1)}, f32[104,1024]{1,0:T(8,128)S(1)}, u32[]{:S(2)}, u32[]{:S(2)}) collective-permute-start(f32[104,1024]{1,0:T(8,128)S(1)} %get-tuple-element.9), channel_id=1, source_target_pairs={{0,4},{1,5},{4,8},{5,9},{8,12},{9,13},{12,14},{13,15},{14,10},{15,... | collective-permute-start | bytes 1277960 | tf_op jit(solution)/shard_map/ppermute | solution.py:98
  66.8 12.2 %collective-permute-start.21 = (f32[104,1024]{1,0:T(8,128)S(1)}, f32[104,1024]{1,0:T(8,128)S(1)}, u32[]{:S(2)}, u32[]{:S(2)}) collective-permute-start(f32[104,1024]{1,0:T(8,128)S(1)} %get-tuple-element.10), channel_id=1, source_target_pairs={{4,0},{5,1},{8,4},{9,5},{12,8},{13,9},{14,12},{15,13},{10,14},{11,... | collective-permute-start | bytes 1277960 | tf_op jit(solution)/shard_map/ppermute | solution.py:102
  78.2 11.3 %collective-permute-start.18 = (f32[104,1024]{1,0:T(8,128)S(1)}, f32[104,1024]{1,0:T(8,128)S(1)}, u32[]{:S(2)}, u32[]{:S(2)}) collective-permute-start(f32[104,1024]{1,0:T(8,128)S(1)} %fusion.11), channel_id=1, source_target_pairs={{0,4},{1,5},{4,8},{5,9},{8,12},{9,13},{12,14},{13,15},{14,10},{15,... | collective-permute-start | bytes 1277960 | tf_op jit(solution)/shard_map/ppermute | solution.py:98
  89.7 10.4 %collective-permute-start.19 = (f32[104,1024]{1,0:T(8,128)S(1)}, f32[104,1024]{1,0:T(8,128)S(1)}, u32[]{:S(2)}, u32[]{:S(2)}) collective-permute-start(f32[104,1024]{1,0:T(8,128)S(1)} %get-tuple-element.7), channel_id=1, source_target_pairs={{0,4},{1,5},{4,8},{5,9},{8,12},{9,13},{12,14},{13,15},{14,10},{15,... | collective-permute-start | bytes 1277960 | tf_op jit(solution)/shard_map/ppermute | solution.py:98
  90.3 22.5 %copy-start.9 = (f32[1024]{0:T(1024)S(1)}, f32[1024]{0:T(1024)}, u32[]{:S(2)}) copy-start(f32[1024]{0:T(1024)} %param.27) | copy-start | bytes 12292
  90.3 23.2 %copy-start.5 = (f32[64,1024]{1,0:T(8,128)S(1)}, f32[64,1024]{1,0:T(8,128)}, u32[]{:S(2)}) copy-start(f32[64,1024]{1,0:T(8,128)} %param.26) | copy-start | bytes 786436
  90.3 10.1 %collective-permute-start.22 = (f32[104,1024]{1,0:T(8,128)S(1)}, f32[104,1024]{1,0:T(8,128)S(1)}, u32[]{:S(2)}, u32[]{:S(2)}) collective-permute-start(f32[104,1024]{1,0:T(8,128)S(1)} %get-tuple-element.8), channel_id=1, source_target_pairs={{4,0},{5,1},{8,4},{9,5},{12,8},{13,9},{14,12},{15,13},{10,14},{11,... | collective-permute-start | bytes 1277960 | tf_op jit(solution)/shard_map/ppermute | solution.py:102
  100.5 13.8 %copy-start.8 = (f32[32,1024]{1,0:T(8,128)S(1)}, f32[32,1024]{1,0:T(8,128)}, u32[]{:S(2)}) copy-start(f32[32,1024]{1,0:T(8,128)} %param.25) | copy-start | bytes 393220
  100.5 9.2 %collective-permute-start.20 = (f32[104,1024]{1,0:T(8,128)S(1)}, f32[104,1024]{1,0:T(8,128)S(1)}, u32[]{:S(2)}, u32[]{:S(2)}) collective-permute-start(f32[104,1024]{1,0:T(8,128)S(1)} %get-tuple-element.5), channel_id=1, source_target_pairs={{0,4},{1,5},{4,8},{5,9},{8,12},{9,13},{12,14},{13,15},{14,10},{15,... | collective-permute-start | bytes 1277960 | tf_op jit(solution)/shard_map/ppermute | solution.py:98
  102.3 8.8 %collective-permute-start.23 = (f32[104,1024]{1,0:T(8,128)S(1)}, f32[104,1024]{1,0:T(8,128)S(1)}, u32[]{:S(2)}, u32[]{:S(2)}) collective-permute-start(f32[104,1024]{1,0:T(8,128)S(1)} %get-tuple-element.6), channel_id=1, source_target_pairs={{4,0},{5,1},{8,4},{9,5},{12,8},{13,9},{14,12},{15,13},{10,14},{11,... | collective-permute-start | bytes 1277960 | tf_op jit(solution)/shard_map/ppermute | solution.py:102
  (12 other events, 27.9 us)

commit v7 on v6

--- a/solution.py
+++ b/solution.py
@@ -93,17 +93,34 @@
     chips, snake, place, cw, ccw, partner = ring_plan(n_blk)
     ahead = chips // 2
     behind = chips - 1 - ahead
-    acc = summed[ahead % chips]
-    for s in range(1, ahead + 1):
-        acc = lax.ppermute(acc, "blk", cw) + summed[(ahead - s) % chips]
-    if behind:
-        acc_back = summed[chips - behind]
-        for s in range(1, behind + 1):
-            acc_back = lax.ppermute(acc_back, "blk", ccw)
-            if s < behind:
-                acc_back = acc_back + summed[chips - behind + s]
-        acc = acc + acc_back
-    return acc
+    rows = summed.shape[1]
+    split = (rows // 16) * 8
+
+    def forward(part, window):
+        acc = part[window % chips]
+        for s in range(1, window + 1):
+            acc = lax.ppermute(acc, "blk", cw) + part[(window - s) % chips]
+        return acc
+
+    def backward(part, window):
+        acc = part[chips - window]
+        for s in range(1, window + 1):
+            acc = lax.ppermute(acc, "blk", ccw)
+            if s < window:
+                acc = acc + part[chips - window + s]
+        return acc
+
+    def both_ways(part, one, other):
+        total = forward(part, one)
+        if other:
+            total = total + backward(part, other)
+        return total
+
+    if split == 0 or behind == ahead:
+        return both_ways(summed, ahead, behind)
+    first = both_ways(summed[:, :split], ahead, behind)
+    second = both_ways(summed[:, split:], behind, ahead)
+    return jnp.concatenate([first, second], axis=0)
 
 
 def slots_product(left, right):

time: 115 us -> 109 us (0.948)
  waiting for transfers between devices: 53.9 us -> 35.8 us
  starting transfers between devices: 17.7 us -> 26.8 us
  matrix products: 13.6 us -> 16.4 us
    ppermute x7 -> x14, waiting for transfers between devices: 37.9 us -> 23.7 us  [the longest x7 12.3 us: forward(): acc = lax.ppermute(acc, 'blk', cw) + part[(window - s) % chips]]
    ppermute x7 -> x14, starting transfers between devices: 6.91 us -> 15 us  [the longest x7 12.1 us: forward(): acc = lax.ppermute(acc, 'blk', cw) + part[(window - s) % chips]]
    ppermute x4, starting transfers between devices: 1.76 us -> 8.15 us  [ring_all_gather(): left = lax.ppermute(left, 'blk', cw)]
    ppermute x3, waiting for transfers between devices: 6.08 us -> 0.01 us  [ring_all_gather(): right = lax.ppermute(right, 'blk', ccw)]
    ppermute x3, starting transfers between devices: 6.07 us -> 0.79 us  [ring_all_gather(): right = lax.ppermute(right, 'blk', ccw)]
    ppermute x4, waiting for transfers between devices: 8.85 us -> 12.1 us  [ring_all_gather(): left = lax.ppermute(left, 'blk', cw)]
    dot_general x8, matrix products: 4.04 us -> 5.81 us  [slots_product(): lax.dot_general(left, right, (((0,), (0,)), ((), ())), preferred_element_...]
    unnamed x49 -> x39, local copies, waits for them, and re-layouts: 6.67 us -> 6.63 us
  transfers between devices with their start and end apart: 24 -> 31, of which waited for: 13 -> 16; matrix products, arithmetic and copies ran while one was open for 17% -> 26% of each run, Pallas kernels for 0% -> 0%
where the time goes in v7:
time: 109 us; the launch traced here: 108 us
  waiting for transfers between devices  35.8 us (33%)
  starting transfers between devices  26.8 us (25%)
  local copies, waits for them, and re-layouts  17.6 us (16%)
  matrix products  16.4 us (15%)
  other arithmetic  9.8 us (9%)
  between operations  1.91 us (2%)
    ppermute x7, waiting for transfers between devices, forward(): acc = lax.ppermute(acc, 'blk', cw) + part[(window - s) % chips]  12.3 us
    ppermute x7, starting transfers between devices, forward(): acc = lax.ppermute(acc, 'blk', cw) + part[(window - s) % chips]  12.1 us
    ppermute x4, waiting for transfers between devices, ring_all_gather(): left = lax.ppermute(left, 'blk', cw)  12.1 us
    ppermute x7, waiting for transfers between devices, backward(): acc = lax.ppermute(acc, 'blk', ccw)  11.4 us
    ppermute x4, starting transfers between devices, ring_all_gather(): left = lax.ppermute(left, 'blk', cw)  8.15 us
    unnamed x39, local copies, waits for them, and re-layouts  6.63 us
    dot_general x8, matrix products, slots_product(): lax.dot_general(left, right, (((0,), (0,)), ((), ())), preferred_element_...  5.81 us
    ppermute x7, starting transfers between devices, backward(): acc = lax.ppermute(acc, 'blk', ccw)  2.9 us
  transfers between devices with their start and end apart: 31, of which 16 were waited for; matrix products, arithmetic and copies ran while one was open for 26% of the time, Pallas kernels for 0%

profile of v7, /device:TPU:0, one launch (start us, length us, event | category | flops | bytes accessed | tf_op | source)
XLA Modules:
  0.0 108.3 jit_solution(12563728786030555371)
XLA Ops:
  2.4 3.1 %collective-permute-start.3 = (bf16[96,1024]{1,0:T(8,128)(2,1)S(1)}, bf16[96,1024]{1,0:T(8,128)(2,1)S(1)}, u32[]{:S(2)}, u32[]{:S(2)}) collective-permute-start(bf16[96,1024]{1,0:T(8,128)(2,1)S(1)} %constant_dynamic-update-slice_fusion), channel_id=1, source_target_pairs={{0,4},{1,5},{4,8},{5,9},{8,12},{9,13},{12,14},{13,15},{14,10},{15,... | collective-permute-start | bytes 589832 | tf_op jit(solution)/shard_map/ppermute | solution.py:77
  5.5 1.2 %dynamic_slice.37 = s32[1]{0:T(128)} dynamic-slice(s32[8]{0:T(128)} %constant.180.clone, s32[]{:T(128)S(6)} %select_n.178), dynamic_slice_sizes={1} | dynamic-slice | bytes 12 | tf_op jit(solution)/shard_map/dynamic_slice | solution.py:72
  7.5 2.8 %collective-permute-done.3 = bf16[96,1024]{1,0:T(8,128)(2,1)S(1)} collective-permute-done((bf16[96,1024]{1,0:T(8,128)(2,1)S(1)}, bf16[96,1024]{1,0:T(8,128)(2,1)S(1)}, u32[]{:S(2)}, u32[]{:S(2)}) %collective-permute-start.3) | collective-permute-done | bytes 196640 | tf_op jit(solution)/shard_map/ppermute | solution.py:77
  10.3 1.8 %collective-permute-start.4 = (bf16[96,1024]{1,0:T(8,128)(2,1)S(1)}, bf16[96,1024]{1,0:T(8,128)(2,1)S(1)}, u32[]{:S(2)}, u32[]{:S(2)}) collective-permute-start(bf16[96,1024]{1,0:T(8,128)(2,1)S(1)} %collective-permute-done.3), channel_id=1, source_target_pairs={{0,4},{1,5},{4,8},{5,9},{8,12},{9,13},{12,14},{13,15},{14,10},{15,... | collective-permute-start | bytes 589832 | tf_op jit(solution)/shard_map/ppermute | solution.py:77
  13.2 3.3 %collective-permute-done.4 = bf16[96,1024]{1,0:T(8,128)(2,1)S(1)} collective-permute-done((bf16[96,1024]{1,0:T(8,128)(2,1)S(1)}, bf16[96,1024]{1,0:T(8,128)(2,1)S(1)}, u32[]{:S(2)}, u32[]{:S(2)}) %collective-permute-start.4) | collective-permute-done | bytes 196640 | tf_op jit(solution)/shard_map/ppermute | solution.py:77
  16.4 1.5 %collective-permute-start.5 = (bf16[96,1024]{1,0:T(8,128)(2,1)S(1)}, bf16[96,1024]{1,0:T(8,128)(2,1)S(1)}, u32[]{:S(2)}, u32[]{:S(2)}) collective-permute-start(bf16[96,1024]{1,0:T(8,128)(2,1)S(1)} %collective-permute-done.4), channel_id=1, source_target_pairs={{0,4},{1,5},{4,8},{5,9},{8,12},{9,13},{12,14},{13,15},{14,10},{15,... | collective-permute-start | bytes 589832 | tf_op jit(solution)/shard_map/ppermute | solution.py:77
  19.3 3.0 %collective-permute-done.5 = bf16[96,1024]{1,0:T(8,128)(2,1)S(1)} collective-permute-done((bf16[96,1024]{1,0:T(8,128)(2,1)S(1)}, bf16[96,1024]{1,0:T(8,128)(2,1)S(1)}, u32[]{:S(2)}, u32[]{:S(2)}) %collective-permute-start.5) | collective-permute-done | bytes 196640 | tf_op jit(solution)/shard_map/ppermute | solution.py:77
  22.2 1.8 %collective-permute-start.6 = (bf16[96,1024]{1,0:T(8,128)(2,1)S(1)}, bf16[96,1024]{1,0:T(8,128)(2,1)S(1)}, u32[]{:S(2)}, u32[]{:S(2)}) collective-permute-start(bf16[96,1024]{1,0:T(8,128)(2,1)S(1)} %collective-permute-done.5), channel_id=1, source_target_pairs={{0,4},{1,5},{4,8},{5,9},{8,12},{9,13},{12,14},{13,15},{14,10},{15,... | collective-permute-start | bytes 589832 | tf_op jit(solution)/shard_map/ppermute | solution.py:77
  24.8 3.0 %collective-permute-done.6 = bf16[96,1024]{1,0:T(8,128)(2,1)S(1)} collective-permute-done((bf16[96,1024]{1,0:T(8,128)(2,1)S(1)}, bf16[96,1024]{1,0:T(8,128)(2,1)S(1)}, u32[]{:S(2)}, u32[]{:S(2)}) %collective-permute-start.6) | collective-permute-done | bytes 196640 | tf_op jit(solution)/shard_map/ppermute | solution.py:77
  37.6 1.3 %constant_dynamic-update-slice_fusion.2 = bf16[16,96,1024]{2,1,0:T(8,128)(2,1)} fusion(bf16[16,96,1024]{2,1,0:T(8,128)(2,1)} %get-tuple-element.22, bf16[8,96,1024]{2,1,0:T(8,128)(2,1)S(1)} %collective-permute-done.7), kind=kLoop, calls=%fused_computation.113 | loop fusion | bytes 3145728 | tf_op jit(solution)/shard_map/concatenate | solution.py:84
  38.9 2.6 %gather_fusion.1 = bf16[16,96,1024]{2,1,0:T(8,128)(2,1)S(1)} fusion(bf16[16,96,1024]{2,1,0:T(8,128)(2,1)} %constant_dynamic-update-slice_fusion.2, s32[1024]{0:T(1024)S(1)} %pad_clamp_fusion.1), kind=kCustom, calls=%fused_computation.5 | custom fusion | bytes 6291520 | tf_op jit(solution)/shard_map/jit(_take)/gather | solution.py:89
  42.7 2.6 %multiply_reduce_fusion = (f32[128]{0:T(128)}, bf16[128,1024]{0,1:T(8,128)(2,1)}, f32[128,1024]{0,1:T(8,128)}) fusion(f32[1024]{0:T(1024)S(1)} %convert_element_type.33, bf16[128,1024]{0,1:T(8,128)(2,1)S(1)} %get-tuple-element.41, bf16[1024,1024]{1,0:T(8,128)(2,1)S(1)} %bitcast.176), kind=kOutput, calls=%fused_computation.24 | convolution fusion | flops 270139264 | bytes 3150336 | tf_op jit(solution)/shard_map/dot_general | solution.py:20
  45.8 2.5 %multiply_convert_fusion.1 = (bf16[128,1024]{0,1:T(8,128)(2,1)S(1)}, f32[128,1024]{0,1:T(8,128)}) fusion(f32[128,1024]{0,1:T(8,128)S(1)} %get-tuple-element.42, bf16[1024,1024]{1,0:T(8,128)(2,1)S(1)} %bitcast.177, bf16[128,1024]{0,1:T(8,128)(2,1)} %get-tuple-element.20), kind=kOutput, calls=%fused_computation.26 | convolution fusion | flops 269090816 | bytes 3670016 | tf_op jit(solution)/shard_map/dot_general | solution.py:25
  48.8 1.4 %multiply_convert_fusion = (bf16[128,1024]{0,1:T(8,128)(2,1)S(1)}, f32[128,1024]{0,1:T(8,128)}) fusion(f32[128,1024]{0,1:T(8,128)S(1)} %get-tuple-element.42, bf16[128,512]{1,0:T(8,128)(2,1)S(1)} %fusion.3, bf16[512,1024]{1,0:T(8,128)(2,1)S(1)} %bitcast.173), kind=kOutput, calls=%fused_computation.25 | convolution fusion | flops 134873088 | bytes 2490368 | tf_op jit(solution)/shard_map/dot_general | solution.py:34
  52.2 1.3 %subtract_multiply_fusion = f32[128]{0:T(128)S(1)} fusion(f32[128]{0:T(128)} %get-tuple-element.19, bf16[128]{0:T(256)(128)(2,1)} %param.20, s32[]{:T(128)} %fusion.51), kind=kLoop, calls=%fused_computation.164 | loop fusion | flops 640 | bytes 1284 | tf_op jit(solution)/shard_map/mul | solution.py:32
  53.5 2.4 %add_reduce_fusion = (f32[1024]{0:T(1024)S(1)}, bf16[128,1024]{0,1:T(8,128)(2,1)S(1)}) fusion(f32[128,1024]{0,1:T(8,128)} %get-tuple-element.43, f32[128]{0:T(128)S(1)} %subtract_multiply_fusion, f32[1024]{0:T(1024)S(1)} %convert_element_type.33, bf16[128,1024]{0,1:T(8,128)(2,1)S(1)} %get-tuple-element.46, bf16[1024,1024]{1,0:T(8,128)(2,1)S(1)} %bitcast.178), kind=kOutput, calls=%fused_computation.22 | convolution fusion | flops 271186944 | bytes 3154432 | tf_op jit(solution)/shard_map/dot_general | solution.py:37
  57.3 1.4 %fusion.10 = f32[8,64,1024]{2,1,0:T(8,128)S(1)} fusion(bf16[128,1024]{0,1:T(8,128)(2,1)} %get-tuple-element.20, bf16[128,8,2,64]{0,3,2,1:T(8,128)(2,1)S(1)} %get-tuple-element.39, s32[]{:T(128)S(6)} %select_n.189), kind=kOutput, calls=%fused_computation.36 | convolution fusion | flops 134217728 | bytes 2490372 | tf_op jit(solution)/shard_map/dot_general | solution.py:127
  61.1 1.4 %fusion.8 = f32[8,64,1024]{2,1,0:T(8,128)S(1)} fusion(bf16[128,8,64]{0,2,1:T(8,128)(2,1)S(1)} %collective-permute-done.12, bf16[128,1024]{0,1:T(8,128)(2,1)} %collective-permute-done.13), kind=kOutput, calls=%fused_computation.34 | convolution fusion | flops 134217728 | bytes 2490368 | tf_op jit(solution)/shard_map/dot_general | solution.py:127
  62.9 1.2 %convolution_add_fusion.2 = f32[8,32,1024]{2,1,0:T(8,128)S(1)} fusion(f32[8,32,1024]{2,1,0:T(8,128)S(1)} %fusion.15, bf16[128,8,32]{0,2,1:T(8,128)(2,1)S(1)} %collective-permute-done.8, bf16[128,1024]{0,1:T(8,128)(2,1)} %collective-permute-done.9), kind=kOutput, calls=%fused_computation.13 | convolution fusion | flops 67371008 | bytes 2424832 | tf_op jit(solution)/shard_map/dot_general | solution.py:127
  65.3 1.8 %collective-permute-start.16 = (f32[48,1024]{1,0:T(8,128)S(1)}, f32[48,1024]{1,0:T(8,128)S(1)}, u32[]{:S(2)}, u32[]{:S(2)}) collective-permute-start(f32[48,1024]{1,0:T(8,128)S(1)} %get-tuple-element.9), channel_id=1, source_target_pairs={{0,4},{1,5},{4,8},{5,9},{8,12},{9,13},{12,14},{13,15},{14,10},{15,... | collective-permute-start | bytes 589832 | tf_op jit(solution)/shard_map/ppermute | solution.py:102
  67.7 1.7 %collective-permute-start.24 = (f32[56,1024]{1,0:T(8,128)S(1)}, f32[56,1024]{1,0:T(8,128)S(1)}, u32[]{:S(2)}, u32[]{:S(2)}) collective-permute-start(f32[56,1024]{1,0:T(8,128)S(1)} %get-tuple-element.15), channel_id=1, source_target_pairs={{0,4},{1,5},{4,8},{5,9},{8,12},{9,13},{12,14},{13,15},{14,10},{15,... | collective-permute-start | bytes 688136 | tf_op jit(solution)/shard_map/ppermute | solution.py:102
  69.7 3.3 %collective-permute-done.16 = f32[48,1024]{1,0:T(8,128)S(1)} collective-permute-done((f32[48,1024]{1,0:T(8,128)S(1)}, f32[48,1024]{1,0:T(8,128)S(1)}, u32[]{:S(2)}, u32[]{:S(2)}) %collective-permute-start.16) | collective-permute-done | bytes 196640 | tf_op jit(solution)/shard_map/ppermute | solution.py:102
  73.1 1.8 %collective-permute-start.17 = (f32[48,1024]{1,0:T(8,128)S(1)}, f32[48,1024]{1,0:T(8,128)S(1)}, u32[]{:S(2)}, u32[]{:S(2)}) collective-permute-start(f32[48,1024]{1,0:T(8,128)S(1)} %fusion.32), channel_id=1, source_target_pairs={{0,4},{1,5},{4,8},{5,9},{8,12},{9,13},{12,14},{13,15},{14,10},{15,... | collective-permute-start | bytes 589832 | tf_op jit(solution)/shard_map/ppermute | solution.py:102
  74.9 3.0 %collective-permute-done.24 = f32[56,1024]{1,0:T(8,128)S(1)} collective-permute-done((f32[56,1024]{1,0:T(8,128)S(1)}, f32[56,1024]{1,0:T(8,128)S(1)}, u32[]{:S(2)}, u32[]{:S(2)}) %collective-permute-start.24) | collective-permute-done | bytes 229408 | tf_op jit(solution)/shard_map/ppermute | solution.py:102
  78.9 1.6 %collective-permute-start.25 = (f32[56,1024]{1,0:T(8,128)S(1)}, f32[56,1024]{1,0:T(8,128)S(1)}, u32[]{:S(2)}, u32[]{:S(2)}) collective-permute-start(f32[56,1024]{1,0:T(8,128)S(1)} %get-tuple-element.13), channel_id=1, source_target_pairs={{0,4},{1,5},{4,8},{5,9},{8,12},{9,13},{12,14},{13,15},{14,10},{15,... | collective-permute-start | bytes 688136 | tf_op jit(solution)/shard_map/ppermute | solution.py:102
  82.3 1.8 %collective-permute-start.18 = (f32[48,1024]{1,0:T(8,128)S(1)}, f32[48,1024]{1,0:T(8,128)S(1)}, u32[]{:S(2)}, u32[]{:S(2)}) collective-permute-start(f32[48,1024]{1,0:T(8,128)S(1)} %get-tuple-element.7), channel_id=1, source_target_pairs={{0,4},{1,5},{4,8},{5,9},{8,12},{9,13},{12,14},{13,15},{14,10},{15,... | collective-permute-start | bytes 589832 | tf_op jit(solution)/shard_map/ppermute | solution.py:102
  84.3 3.2 %collective-permute-done.25 = f32[56,1024]{1,0:T(8,128)S(1)} collective-permute-done((f32[56,1024]{1,0:T(8,128)S(1)}, f32[56,1024]{1,0:T(8,128)S(1)}, u32[]{:S(2)}, u32[]{:S(2)}) %collective-permute-start.25) | collective-permute-done | bytes 229408 | tf_op jit(solution)/shard_map/ppermute | solution.py:102
  88.6 1.6 %collective-permute-start.26 = (f32[56,1024]{1,0:T(8,128)S(1)}, f32[56,1024]{1,0:T(8,128)S(1)}, u32[]{:S(2)}, u32[]{:S(2)}) collective-permute-start(f32[56,1024]{1,0:T(8,128)S(1)} %get-tuple-element.11), channel_id=1, source_target_pairs={{0,4},{1,5},{4,8},{5,9},{8,12},{9,13},{12,14},{13,15},{14,10},{15,... | collective-permute-start | bytes 688136 | tf_op jit(solution)/shard_map/ppermute | solution.py:102
  92.2 1.6 %collective-permute-start.19 = (f32[48,1024]{1,0:T(8,128)S(1)}, f32[48,1024]{1,0:T(8,128)S(1)}, u32[]{:S(2)}, u32[]{:S(2)}) collective-permute-start(f32[48,1024]{1,0:T(8,128)S(1)} %get-tuple-element.5), channel_id=1, source_target_pairs={{0,4},{1,5},{4,8},{5,9},{8,12},{9,13},{12,14},{13,15},{14,10},{15,... | collective-permute-start | bytes 589832 | tf_op jit(solution)/shard_map/ppermute | solution.py:102
  94.3 4.3 %collective-permute-done.29 = f32[56,1024]{1,0:T(8,128)S(1)} collective-permute-done((f32[56,1024]{1,0:T(8,128)S(1)}, f32[56,1024]{1,0:T(8,128)S(1)}, u32[]{:S(2)}, u32[]{:S(2)}) %collective-permute-start.29) | collective-permute-done | bytes 229408 | tf_op jit(solution)/shard_map/ppermute | solution.py:108
  99.7 3.1 %collective-permute-done.22 = f32[48,1024]{1,0:T(8,128)S(1)} collective-permute-done((f32[48,1024]{1,0:T(8,128)S(1)}, f32[48,1024]{1,0:T(8,128)S(1)}, u32[]{:S(2)}, u32[]{:S(2)}) %collective-permute-start.22) | collective-permute-done | bytes 196640 | tf_op jit(solution)/shard_map/ppermute | solution.py:108
  103.7 1.7 %collective-permute-done.30 = f32[56,1024]{1,0:T(8,128)S(1)} collective-permute-done((f32[56,1024]{1,0:T(8,128)S(1)}, f32[56,1024]{1,0:T(8,128)S(1)}, u32[]{:S(2)}, u32[]{:S(2)}) %collective-permute-start.30) | collective-permute-done | bytes 229408 | tf_op jit(solution)/shard_map/ppermute | solution.py:108
  (141 shorter events, 36.2 us)
Async XLA Ops:
  0.6 32.7 %copy-start = (s32[16,16]{1,0:T(8,128)S(1)}, s32[16,16]{1,0:T(8,128)}, u32[]{:S(2)}) copy-start(s32[16,16]{1,0:T(8,128)} %param.21) | copy-start | bytes 3076
  2.4 7.9 %collective-permute-start.3 = (bf16[96,1024]{1,0:T(8,128)(2,1)S(1)}, bf16[96,1024]{1,0:T(8,128)(2,1)S(1)}, u32[]{:S(2)}, u32[]{:S(2)}) collective-permute-start(bf16[96,1024]{1,0:T(8,128)(2,1)S(1)} %constant_dynamic-update-slice_fusion), channel_id=1, source_target_pairs={{0,4},{1,5},{4,8},{5,9},{8,12},{9,13},{12,14},{13,15},{14,10},{15,... | collective-permute-start | bytes 589832 | tf_op jit(solution)/shard_map/ppermute | solution.py:77
  5.5 6.6 %collective-permute-start = (bf16[96,1024]{1,0:T(8,128)(2,1)S(1)}, bf16[96,1024]{1,0:T(8,128)(2,1)S(1)}, u32[]{:S(2)}, u32[]{:S(2)}) collective-permute-start(bf16[96,1024]{1,0:T(8,128)(2,1)S(1)} %constant_dynamic-update-slice_fusion), channel_id=1, source_target_pairs={{4,0},{5,1},{8,4},{9,5},{12,8},{13,9},{14,12},{15,13},{10,14},{11,... | collective-permute-start | bytes 589832 | tf_op jit(solution)/shard_map/ppermute | solution.py:80
  10.3 6.1 %collective-permute-start.4 = (bf16[96,1024]{1,0:T(8,128)(2,1)S(1)}, bf16[96,1024]{1,0:T(8,128)(2,1)S(1)}, u32[]{:S(2)}, u32[]{:S(2)}) collective-permute-start(bf16[96,1024]{1,0:T(8,128)(2,1)S(1)} %collective-permute-done.3), channel_id=1, source_target_pairs={{0,4},{1,5},{4,8},{5,9},{8,12},{9,13},{12,14},{13,15},{14,10},{15,... | collective-permute-start | bytes 589832 | tf_op jit(solution)/shard_map/ppermute | solution.py:77
  12.1 5.8 %collective-permute-start.1 = (bf16[96,1024]{1,0:T(8,128)(2,1)S(1)}, bf16[96,1024]{1,0:T(8,128)(2,1)S(1)}, u32[]{:S(2)}, u32[]{:S(2)}) collective-permute-start(bf16[96,1024]{1,0:T(8,128)(2,1)S(1)} %collective-permute-done), channel_id=1, source_target_pairs={{4,0},{5,1},{8,4},{9,5},{12,8},{13,9},{14,12},{15,13},{10,14},{11,... | collective-permute-start | bytes 589832 | tf_op jit(solution)/shard_map/ppermute | solution.py:80
  16.4 5.8 %collective-permute-start.5 = (bf16[96,1024]{1,0:T(8,128)(2,1)S(1)}, bf16[96,1024]{1,0:T(8,128)(2,1)S(1)}, u32[]{:S(2)}, u32[]{:S(2)}) collective-permute-start(bf16[96,1024]{1,0:T(8,128)(2,1)S(1)} %collective-permute-done.4), channel_id=1, source_target_pairs={{0,4},{1,5},{4,8},{5,9},{8,12},{9,13},{12,14},{13,15},{14,10},{15,... | collective-permute-start | bytes 589832 | tf_op jit(solution)/shard_map/ppermute | solution.py:77
  17.9 6.1 %collective-permute-start.2 = (bf16[96,1024]{1,0:T(8,128)(2,1)S(1)}, bf16[96,1024]{1,0:T(8,128)(2,1)S(1)}, u32[]{:S(2)}, u32[]{:S(2)}) collective-permute-start(bf16[96,1024]{1,0:T(8,128)(2,1)S(1)} %collective-permute-done.1), channel_id=1, source_target_pairs={{4,0},{5,1},{8,4},{9,5},{12,8},{13,9},{14,12},{15,13},{10,14},{11,... | collective-permute-start | bytes 589832 | tf_op jit(solution)/shard_map/ppermute | solution.py:80
  22.2 5.7 %collective-permute-start.6 = (bf16[96,1024]{1,0:T(8,128)(2,1)S(1)}, bf16[96,1024]{1,0:T(8,128)(2,1)S(1)}, u32[]{:S(2)}, u32[]{:S(2)}) collective-permute-start(bf16[96,1024]{1,0:T(8,128)(2,1)S(1)} %collective-permute-done.5), channel_id=1, source_target_pairs={{0,4},{1,5},{4,8},{5,9},{8,12},{9,13},{12,14},{13,15},{14,10},{15,... | collective-permute-start | bytes 589832 | tf_op jit(solution)/shard_map/ppermute | solution.py:77
  31.1 6.5 %collective-permute-start.7 = (bf16[8,96,1024]{2,1,0:T(8,128)(2,1)}, bf16[8,96,1024]{2,1,0:T(8,128)(2,1)S(1)}, u32[]{:S(2)}, u32[]{:S(2)}) collective-permute-start(bf16[8,96,1024]{2,1,0:T(8,128)(2,1)} %get-tuple-element.21), channel_id=1, source_target_pairs={{0,1},{1,0},{2,3},{3,2},{4,5},{5,4},{6,7},{7,6},{8,9},{9,8},{10,11... | collective-permute-start | bytes 4718600 | tf_op jit(solution)/shard_map/ppermute | solution.py:83
  45.3 15.6 %collective-permute-start.13 = (bf16[128,1024]{0,1:T(8,128)(2,1)}, bf16[128,1024]{0,1:T(8,128)(2,1)}, u32[]{:S(2)}, u32[]{:S(2)}) collective-permute-start(bf16[128,1024]{0,1:T(8,128)(2,1)} %get-tuple-element.20), channel_id=1, source_target_pairs={{0,1},{1,0},{2,3},{3,2},{4,5},{5,4},{6,7},{7,6},{8,9},{9,8},{10,11... | collective-permute-start | bytes 786440 | tf_op jit(solution)/shard_map/ppermute | solution.py:163
  50.3 12.5 %collective-permute-start.9 = (bf16[128,1024]{0,1:T(8,128)(2,1)S(1)}, bf16[128,1024]{0,1:T(8,128)(2,1)}, u32[]{:S(2)}, u32[]{:S(2)}) collective-permute-start(bf16[128,1024]{0,1:T(8,128)(2,1)S(1)} %get-tuple-element.44), channel_id=1, source_target_pairs={{0,1},{1,0},{2,3},{3,2},{4,5},{5,4},{6,7},{7,6},{8,9},{9,8},{10,11... | collective-permute-start | bytes 786440 | tf_op jit(solution)/shard_map/ppermute | solution.py:163
  55.9 4.4 %collective-permute-start.23 = (f32[1024]{0:T(1024)S(1)}, f32[1024]{0:T(1024)S(1)}, u32[]{:S(2)}, u32[]{:S(2)}) collective-permute-start(f32[1024]{0:T(1024)S(1)} %get-tuple-element.17), channel_id=1, source_target_pairs={{0,1},{1,0},{2,3},{3,2},{4,5},{5,4},{6,7},{7,6},{8,9},{9,8},{10,11... | collective-permute-start | bytes 12296 | tf_op jit(solution)/shard_map/ppermute | solution.py:163
  56.7 3.8 %collective-permute-start.12 = (bf16[128,8,64]{0,2,1:T(8,128)(2,1)S(1)}, bf16[128,8,64]{0,2,1:T(8,128)(2,1)S(1)}, u32[]{:S(2)}, u32[]{:S(2)}) collective-permute-start(bf16[128,8,64]{0,2,1:T(8,128)(2,1)S(1)} %dynamic-slice_bitcast_fusion.1), channel_id=1, source_target_pairs={{0,1},{1,0},{2,3},{3,2},{4,5},{5,4},{6,7},{7,6},{8,9},{9,8},{10,11... | collective-permute-start | bytes 393224 | tf_op jit(solution)/shard_map/ppermute | solution.py:160
  56.9 7.9 %collective-permute-start.15 = (bf16[128,1024]{0,1:T(8,128)(2,1)S(1)}, bf16[128,1024]{0,1:T(8,128)(2,1)S(1)}, u32[]{:S(2)}, u32[]{:S(2)}) collective-permute-start(bf16[128,1024]{0,1:T(8,128)(2,1)S(1)} %get-tuple-element.18), channel_id=1, source_target_pairs={{0,1},{1,0},{2,3},{3,2},{4,5},{5,4},{6,7},{7,6},{8,9},{9,8},{10,11... | collective-permute-start | bytes 786440 | tf_op jit(solution)/shard_map/ppermute | solution.py:163
  60.3 2.2 %collective-permute-start.8 = (bf16[128,8,32]{0,2,1:T(8,128)(2,1)S(1)}, bf16[128,8,32]{0,2,1:T(8,128)(2,1)S(1)}, u32[]{:S(2)}, u32[]{:S(2)}) collective-permute-start(bf16[128,8,32]{0,2,1:T(8,128)(2,1)S(1)} %dynamic-slice_bitcast_fusion.3), channel_id=1, source_target_pairs={{0,1},{1,0},{2,3},{3,2},{4,5},{5,4},{6,7},{7,6},{8,9},{9,8},{10,11... | collective-permute-start | bytes 196616 | tf_op jit(solution)/shard_map/ppermute | solution.py:160
  60.6 3.9 %collective-permute-start.10 = (bf16[128,8,32]{0,2,1:T(8,128)(2,1)S(1)}, bf16[128,8,32]{0,2,1:T(8,128)(2,1)S(1)}, u32[]{:S(2)}, u32[]{:S(2)}) collective-permute-start(bf16[128,8,32]{0,2,1:T(8,128)(2,1)S(1)} %dynamic-slice_bitcast_fusion.2), channel_id=1, source_target_pairs={{0,1},{1,0},{2,3},{3,2},{4,5},{5,4},{6,7},{7,6},{8,9},{9,8},{10,11... | collective-permute-start | bytes 196616 | tf_op jit(solution)/shard_map/ppermute | solution.py:160
  60.9 3.9 %collective-permute-start.14 = (bf16[128,8,64]{0,2,1:T(8,128)(2,1)S(1)}, bf16[128,8,64]{0,2,1:T(8,128)(2,1)S(1)}, u32[]{:S(2)}, u32[]{:S(2)}) collective-permute-start(bf16[128,8,64]{0,2,1:T(8,128)(2,1)S(1)} %dynamic-slice_bitcast_fusion), channel_id=1, source_target_pairs={{0,1},{1,0},{2,3},{3,2},{4,5},{5,4},{6,7},{7,6},{8,9},{9,8},{10,11... | collective-permute-start | bytes 393224 | tf_op jit(solution)/shard_map/ppermute | solution.py:160
  62.5 2.0 %collective-permute-start.11 = (bf16[128,1024]{0,1:T(8,128)(2,1)S(1)}, bf16[128,1024]{0,1:T(8,128)(2,1)S(1)}, u32[]{:S(2)}, u32[]{:S(2)}) collective-permute-start(bf16[128,1024]{0,1:T(8,128)(2,1)S(1)} %fusion.1), channel_id=1, source_target_pairs={{0,1},{1,0},{2,3},{3,2},{4,5},{5,4},{6,7},{7,6},{8,9},{9,8},{10,11... | collective-permute-start | bytes 786440 | tf_op jit(solution)/shard_map/ppermute | solution.py:163
  65.3 7.8 %collective-permute-start.16 = (f32[48,1024]{1,0:T(8,128)S(1)}, f32[48,1024]{1,0:T(8,128)S(1)}, u32[]{:S(2)}, u32[]{:S(2)}) collective-permute-start(f32[48,1024]{1,0:T(8,128)S(1)} %get-tuple-element.9), channel_id=1, source_target_pairs={{0,4},{1,5},{4,8},{5,9},{8,12},{9,13},{12,14},{13,15},{14,10},{15,... | collective-permute-start | bytes 589832 | tf_op jit(solution)/shard_map/ppermute | solution.py:102
  67.2 13.8 %collective-permute-start.20 = (f32[48,1024]{1,0:T(8,128)S(1)}, f32[48,1024]{1,0:T(8,128)S(1)}, u32[]{:S(2)}, u32[]{:S(2)}) collective-permute-start(f32[48,1024]{1,0:T(8,128)S(1)} %get-tuple-element.10), channel_id=1, source_target_pairs={{4,0},{5,1},{8,4},{9,5},{12,8},{13,9},{14,12},{15,13},{10,14},{11,... | collective-permute-start | bytes 589832 | tf_op jit(solution)/shard_map/ppermute | solution.py:108
  67.7 10.3 %collective-permute-start.24 = (f32[56,1024]{1,0:T(8,128)S(1)}, f32[56,1024]{1,0:T(8,128)S(1)}, u32[]{:S(2)}, u32[]{:S(2)}) collective-permute-start(f32[56,1024]{1,0:T(8,128)S(1)} %get-tuple-element.15), channel_id=1, source_target_pairs={{0,4},{1,5},{4,8},{5,9},{8,12},{9,13},{12,14},{13,15},{14,10},{15,... | collective-permute-start | bytes 688136 | tf_op jit(solution)/shard_map/ppermute | solution.py:102
  69.3 9.5 %collective-permute-start.27 = (f32[56,1024]{1,0:T(8,128)S(1)}, f32[56,1024]{1,0:T(8,128)S(1)}, u32[]{:S(2)}, u32[]{:S(2)}) collective-permute-start(f32[56,1024]{1,0:T(8,128)S(1)} %get-tuple-element.16), channel_id=1, source_target_pairs={{4,0},{5,1},{8,4},{9,5},{12,8},{13,9},{14,12},{15,13},{10,14},{11,... | collective-permute-start | bytes 688136 | tf_op jit(solution)/shard_map/ppermute | solution.py:108
  73.1 9.1 %collective-permute-start.17 = (f32[48,1024]{1,0:T(8,128)S(1)}, f32[48,1024]{1,0:T(8,128)S(1)}, u32[]{:S(2)}, u32[]{:S(2)}) collective-permute-start(f32[48,1024]{1,0:T(8,128)S(1)} %fusion.32), channel_id=1, source_target_pairs={{0,4},{1,5},{4,8},{5,9},{8,12},{9,13},{12,14},{13,15},{14,10},{15,... | collective-permute-start | bytes 589832 | tf_op jit(solution)/shard_map/ppermute | solution.py:102
  78.9 8.6 %collective-permute-start.25 = (f32[56,1024]{1,0:T(8,128)S(1)}, f32[56,1024]{1,0:T(8,128)S(1)}, u32[]{:S(2)}, u32[]{:S(2)}) collective-permute-start(f32[56,1024]{1,0:T(8,128)S(1)} %get-tuple-element.13), channel_id=1, source_target_pairs={{0,4},{1,5},{4,8},{5,9},{8,12},{9,13},{12,14},{13,15},{14,10},{15,... | collective-permute-start | bytes 688136 | tf_op jit(solution)/shard_map/ppermute | solution.py:102
  80.5 8.0 %collective-permute-start.28 = (f32[56,1024]{1,0:T(8,128)S(1)}, f32[56,1024]{1,0:T(8,128)S(1)}, u32[]{:S(2)}, u32[]{:S(2)}) collective-permute-start(f32[56,1024]{1,0:T(8,128)S(1)} %get-tuple-element.14), channel_id=1, source_target_pairs={{4,0},{5,1},{8,4},{9,5},{12,8},{13,9},{14,12},{15,13},{10,14},{11,... | collective-permute-start | bytes 688136 | tf_op jit(solution)/shard_map/ppermute | solution.py:108
  82.3 9.4 %collective-permute-start.18 = (f32[48,1024]{1,0:T(8,128)S(1)}, f32[48,1024]{1,0:T(8,128)S(1)}, u32[]{:S(2)}, u32[]{:S(2)}) collective-permute-start(f32[48,1024]{1,0:T(8,128)S(1)} %get-tuple-element.7), channel_id=1, source_target_pairs={{0,4},{1,5},{4,8},{5,9},{8,12},{9,13},{12,14},{13,15},{14,10},{15,... | collective-permute-start | bytes 589832 | tf_op jit(solution)/shard_map/ppermute | solution.py:102
  84.1 8.1 %collective-permute-start.21 = (f32[48,1024]{1,0:T(8,128)S(1)}, f32[48,1024]{1,0:T(8,128)S(1)}, u32[]{:S(2)}, u32[]{:S(2)}) collective-permute-start(f32[48,1024]{1,0:T(8,128)S(1)} %get-tuple-element.8), channel_id=1, source_target_pairs={{4,0},{5,1},{8,4},{9,5},{12,8},{13,9},{14,12},{15,13},{10,14},{11,... | collective-permute-start | bytes 589832 | tf_op jit(solution)/shard_map/ppermute | solution.py:108
  88.6 15.1 %collective-permute-start.26 = (f32[56,1024]{1,0:T(8,128)S(1)}, f32[56,1024]{1,0:T(8,128)S(1)}, u32[]{:S(2)}, u32[]{:S(2)}) collective-permute-start(f32[56,1024]{1,0:T(8,128)S(1)} %get-tuple-element.11), channel_id=1, source_target_pairs={{0,4},{1,5},{4,8},{5,9},{8,12},{9,13},{12,14},{13,15},{14,10},{15,... | collective-permute-start | bytes 688136 | tf_op jit(solution)/shard_map/ppermute | solution.py:102
  90.3 8.3 %collective-permute-start.29 = (f32[56,1024]{1,0:T(8,128)S(1)}, f32[56,1024]{1,0:T(8,128)S(1)}, u32[]{:S(2)}, u32[]{:S(2)}) collective-permute-start(f32[56,1024]{1,0:T(8,128)S(1)} %get-tuple-element.12), channel_id=1, source_target_pairs={{4,0},{5,1},{8,4},{9,5},{12,8},{13,9},{14,12},{15,13},{10,14},{11,... | collective-permute-start | bytes 688136 | tf_op jit(solution)/shard_map/ppermute | solution.py:108
  92.2 7.5 %collective-permute-start.19 = (f32[48,1024]{1,0:T(8,128)S(1)}, f32[48,1024]{1,0:T(8,128)S(1)}, u32[]{:S(2)}, u32[]{:S(2)}) collective-permute-start(f32[48,1024]{1,0:T(8,128)S(1)} %get-tuple-element.5), channel_id=1, source_target_pairs={{0,4},{1,5},{4,8},{5,9},{8,12},{9,13},{12,14},{13,15},{14,10},{15,... | collective-permute-start | bytes 589832 | tf_op jit(solution)/shard_map/ppermute | solution.py:102
  93.8 9.0 %collective-permute-start.22 = (f32[48,1024]{1,0:T(8,128)S(1)}, f32[48,1024]{1,0:T(8,128)S(1)}, u32[]{:S(2)}, u32[]{:S(2)}) collective-permute-start(f32[48,1024]{1,0:T(8,128)S(1)} %get-tuple-element.6), channel_id=1, source_target_pairs={{4,0},{5,1},{8,4},{9,5},{12,8},{13,9},{14,12},{15,13},{10,14},{11,... | collective-permute-start | bytes 589832 | tf_op jit(solution)/shard_map/ppermute | solution.py:108
  98.6 6.8 %collective-permute-start.30 = (f32[56,1024]{1,0:T(8,128)S(1)}, f32[56,1024]{1,0:T(8,128)S(1)}, u32[]{:S(2)}, u32[]{:S(2)}) collective-permute-start(f32[56,1024]{1,0:T(8,128)S(1)} %fusion.18), channel_id=1, source_target_pairs={{4,0},{5,1},{8,4},{9,5},{12,8},{13,9},{14,12},{15,13},{10,14},{11,... | collective-permute-start | bytes 688136 | tf_op jit(solution)/shard_map/ppermute | solution.py:108
  (14 other events, 114.7 us)

commit v8 on v7

--- a/solution.py
+++ b/solution.py
@@ -182,12 +182,12 @@
     own_row = jnp.arange(chips, dtype=jnp.int32)[:, None] == chip
     outs = jnp.where(own_row, chip_out[None, :], 0.0)
     summed = jnp.concatenate(
-        [part_one, part_two, jnp.broadcast_to(outs, (chips,) + outs.shape)], axis=1
+        [part_two, jnp.broadcast_to(outs, (chips,) + outs.shape), part_one], axis=1
     )
     reduced = ring_reduce_scatter(summed, n_blk)
-    grad_out = jnp.sum(reduced[r_one + r_two:], axis=0)
-    grad_one = reduced[:r_one]
-    grad_two = reduced[r_one:r_one + r_two]
+    grad_two = reduced[:r_two]
+    grad_out = jnp.sum(reduced[r_two:r_two + chips], axis=0)
+    grad_one = reduced[r_two + chips:]
     new_first = 0.8 * mom_first + 0.2 * normalized(grad_one)
     new_second = 0.8 * mom_second + 0.2 * normalized(grad_two)
     new_out = 0.8 * mom_out + 0.2 * normalized(grad_out)

time: 109 us -> 107 us (0.982)
  matrix products: 16.4 us -> 12.4 us
  waiting for transfers between devices: 35.8 us -> 39.4 us
  starting transfers between devices: 26.8 us -> 24.7 us
  local copies, waits for them, and re-layouts: 17.6 us -> 18.7 us
    ppermute x7, starting transfers between devices: 12.1 us -> 5.46 us  [forward(): acc = lax.ppermute(acc, 'blk', cw) + part[(window - s) % chips]]
    ppermute x4, starting transfers between devices: 8.15 us -> 1.76 us  [ring_all_gather(): left = lax.ppermute(left, 'blk', cw)]
    ppermute x3, waiting for transfers between devices: 0.01 us -> 6.06 us  [ring_all_gather(): right = lax.ppermute(right, 'blk', ccw)]
    ppermute x7, starting transfers between devices: 2.9 us -> 8.91 us  [backward(): acc = lax.ppermute(acc, 'blk', ccw)]
    ppermute x3, starting transfers between devices: 0.79 us -> 6.07 us  [ring_all_gather(): right = lax.ppermute(right, 'blk', ccw)]
    ppermute x7, waiting for transfers between devices: 11.4 us -> 7.73 us  [backward(): acc = lax.ppermute(acc, 'blk', ccw)]
    ppermute x4, waiting for transfers between devices: 12.1 us -> 8.85 us  [ring_all_gather(): left = lax.ppermute(left, 'blk', cw)]
    dot_general x8, matrix products: 5.81 us -> 2.93 us  [slots_product(): lax.dot_general(left, right, (((0,), (0,)), ((), ())), preferred_element_...]
  transfers between devices with their start and end apart: 31 -> 31, of which waited for: 16 -> 16; matrix products, arithmetic and copies ran while one was open for 26% -> 22% of each run, Pallas kernels for 0% -> 0%
where the time goes in v8:
time: 107 us
  waiting for transfers between devices  39.4 us (37%)
  starting transfers between devices  24.7 us (23%)
  local copies, waits for them, and re-layouts  18.7 us (17%)
  matrix products  12.4 us (12%)
  other arithmetic  9.69 us (9%)
  between operations  1.95 us (2%)
    ppermute x7, waiting for transfers between devices, forward(): acc = lax.ppermute(acc, 'blk', cw) + part[(window - s) % chips]  14.9 us
    ppermute x7, starting transfers between devices, backward(): acc = lax.ppermute(acc, 'blk', ccw)  8.91 us
    ppermute x4, waiting for transfers between devices, ring_all_gather(): left = lax.ppermute(left, 'blk', cw)  8.85 us
    ppermute x7, waiting for transfers between devices, backward(): acc = lax.ppermute(acc, 'blk', ccw)  7.73 us
    unnamed x61, local copies, waits for them, and re-layouts  7.1 us
    ppermute x3, starting transfers between devices, ring_all_gather(): right = lax.ppermute(right, 'blk', ccw)  6.07 us
    ppermute x3, waiting for transfers between devices, ring_all_gather(): right = lax.ppermute(right, 'blk', ccw)  6.06 us
    ppermute x7, starting transfers between devices, forward(): acc = lax.ppermute(acc, 'blk', cw) + part[(window - s) % chips]  5.46 us
  transfers between devices with their start and end apart: 31, of which 16 were waited for; matrix products, arithmetic and copies ran while one was open for 22% of the time, Pallas kernels for 0%

profile of v8, /device:TPU:0, one launch (start us, length us, event | category | flops | bytes accessed | tf_op | source)
XLA Modules:
  0.0 106.9 jit_solution(1698130289326121165)
XLA Ops:
  1.5 0.9 constant_dynamic-update-slice_fusion
  2.4 3.0 %collective-permute-start = (bf16[96,1024]{1,0:T(8,128)(2,1)S(1)}, bf16[96,1024]{1,0:T(8,128)(2,1)S(1)}, u32[]{:S(2)}, u32[]{:S(2)}) collective-permute-start(bf16[96,1024]{1,0:T(8,128)(2,1)S(1)} %constant_dynamic-update-slice_fusion), channel_id=1, source_target_pairs={{4,0},{5,1},{8,4},{9,5},{12,8},{13,9},{14,12},{15,13},{10,14},{11,... | collective-permute-start | bytes 589832 | tf_op jit(solution)/shard_map/ppermute | solution.py:80
  5.6 1.2 %dynamic_slice.37 = s32[1]{0:T(128)} dynamic-slice(s32[8]{0:T(128)} %constant.180.clone, s32[]{:T(128)S(6)} %select_n.178), dynamic_slice_sizes={1} | dynamic-slice | bytes 12 | tf_op jit(solution)/shard_map/dynamic_slice | solution.py:72
  7.6 2.8 %collective-permute-done = bf16[96,1024]{1,0:T(8,128)(2,1)S(1)} collective-permute-done((bf16[96,1024]{1,0:T(8,128)(2,1)S(1)}, bf16[96,1024]{1,0:T(8,128)(2,1)S(1)}, u32[]{:S(2)}, u32[]{:S(2)}) %collective-permute-start) | collective-permute-done | bytes 196640 | tf_op jit(solution)/shard_map/ppermute | solution.py:80
  10.4 1.7 %collective-permute-start.1 = (bf16[96,1024]{1,0:T(8,128)(2,1)S(1)}, bf16[96,1024]{1,0:T(8,128)(2,1)S(1)}, u32[]{:S(2)}, u32[]{:S(2)}) collective-permute-start(bf16[96,1024]{1,0:T(8,128)(2,1)S(1)} %collective-permute-done), channel_id=1, source_target_pairs={{4,0},{5,1},{8,4},{9,5},{12,8},{13,9},{14,12},{15,13},{10,14},{11,... | collective-permute-start | bytes 589832 | tf_op jit(solution)/shard_map/ppermute | solution.py:80
  13.2 3.3 %collective-permute-done.1 = bf16[96,1024]{1,0:T(8,128)(2,1)S(1)} collective-permute-done((bf16[96,1024]{1,0:T(8,128)(2,1)S(1)}, bf16[96,1024]{1,0:T(8,128)(2,1)S(1)}, u32[]{:S(2)}, u32[]{:S(2)}) %collective-permute-start.1) | collective-permute-done | bytes 196640 | tf_op jit(solution)/shard_map/ppermute | solution.py:80
  16.5 1.4 %collective-permute-start.2 = (bf16[96,1024]{1,0:T(8,128)(2,1)S(1)}, bf16[96,1024]{1,0:T(8,128)(2,1)S(1)}, u32[]{:S(2)}, u32[]{:S(2)}) collective-permute-start(bf16[96,1024]{1,0:T(8,128)(2,1)S(1)} %collective-permute-done.1), channel_id=1, source_target_pairs={{4,0},{5,1},{8,4},{9,5},{12,8},{13,9},{14,12},{15,13},{10,14},{11,... | collective-permute-start | bytes 589832 | tf_op jit(solution)/shard_map/ppermute | solution.py:80
  19.3 4.6 %collective-permute-done.5 = bf16[96,1024]{1,0:T(8,128)(2,1)S(1)} collective-permute-done((bf16[96,1024]{1,0:T(8,128)(2,1)S(1)}, bf16[96,1024]{1,0:T(8,128)(2,1)S(1)}, u32[]{:S(2)}, u32[]{:S(2)}) %collective-permute-start.5) | collective-permute-done | bytes 196640 | tf_op jit(solution)/shard_map/ppermute | solution.py:77
  25.4 4.2 %collective-permute-done.6 = bf16[96,1024]{1,0:T(8,128)(2,1)S(1)} collective-permute-done((bf16[96,1024]{1,0:T(8,128)(2,1)S(1)}, bf16[96,1024]{1,0:T(8,128)(2,1)S(1)}, u32[]{:S(2)}, u32[]{:S(2)}) %collective-permute-start.6) | collective-permute-done | bytes 196640 | tf_op jit(solution)/shard_map/ppermute | solution.py:77
  36.8 1.2 %compare_select_fusion.15 = f32[128]{0:T(128)} fusion(s32[]{:T(128)} %fusion.50), kind=kLoop, calls=%fused_computation.148 | loop fusion | flops 256 | bytes 516 | tf_op jit(solution)/shard_map/mul | solution.py:33
  39.9 1.3 %constant_dynamic-update-slice_fusion.2 = bf16[16,96,1024]{2,1,0:T(8,128)(2,1)} fusion(bf16[16,96,1024]{2,1,0:T(8,128)(2,1)} %get-tuple-element.22, bf16[8,96,1024]{2,1,0:T(8,128)(2,1)S(1)} %collective-permute-done.7), kind=kLoop, calls=%fused_computation.113 | loop fusion | bytes 3145728 | tf_op jit(solution)/shard_map/concatenate | solution.py:84
  41.1 2.6 %gather_fusion.1 = bf16[16,96,1024]{2,1,0:T(8,128)(2,1)S(1)} fusion(bf16[16,96,1024]{2,1,0:T(8,128)(2,1)} %constant_dynamic-update-slice_fusion.2, s32[1024]{0:T(1024)S(1)} %pad_clamp_fusion.1), kind=kCustom, calls=%fused_computation.5 | custom fusion | bytes 6291520 | tf_op jit(solution)/shard_map/jit(_take)/gather | solution.py:89
  45.0 2.5 %multiply_reduce_fusion = (f32[128]{0:T(128)}, bf16[128,1024]{0,1:T(8,128)(2,1)S(1)}, f32[128,1024]{0,1:T(8,128)}) fusion(f32[1024]{0:T(1024)S(1)} %convert_element_type.33, bf16[128,1024]{0,1:T(8,128)(2,1)S(1)} %get-tuple-element.41, bf16[1024,1024]{1,0:T(8,128)(2,1)S(1)} %bitcast.176), kind=kOutput, calls=%fused_computation.24 | convolution fusion | flops 270139264 | bytes 3150336 | tf_op jit(solution)/shard_map/dot_general | solution.py:20
  47.5 1.5 %multiply_convert_fusion.1 = (bf16[128,1024]{0,1:T(8,128)(2,1)S(1)}, f32[128,1024]{0,1:T(8,128)}) fusion(f32[128,1024]{0,1:T(8,128)S(1)} %get-tuple-element.42, bf16[1024,1024]{1,0:T(8,128)(2,1)S(1)} %bitcast.177, bf16[128,1024]{0,1:T(8,128)(2,1)S(1)} %get-tuple-element.20), kind=kOutput, calls=%fused_computation.26 | convolution fusion | flops 269090816 | bytes 3670016 | tf_op jit(solution)/shard_map/dot_general | solution.py:25
  50.2 2.4 %multiply_convert_fusion = (bf16[128,1024]{0,1:T(8,128)(2,1)S(1)}, f32[128,1024]{0,1:T(8,128)}) fusion(f32[128,1024]{0,1:T(8,128)} %copy-done.21, bf16[128,512]{1,0:T(8,128)(2,1)S(1)} %fusion.3, bf16[512,1024]{1,0:T(8,128)(2,1)S(1)} %bitcast.173), kind=kOutput, calls=%fused_computation.25 | convolution fusion | flops 134873088 | bytes 2490368 | tf_op jit(solution)/shard_map/dot_general | solution.py:34
  57.1 1.3 %add_reduce_fusion = (f32[1024]{0:T(1024)S(1)}, bf16[128,1024]{0,1:T(8,128)(2,1)S(1)}) fusion(f32[128,1024]{0,1:T(8,128)S(1)} %copy-done.25, f32[128]{0:T(128)S(1)} %subtract_multiply_fusion, f32[1024]{0:T(1024)S(1)} %convert_element_type.33, bf16[128,1024]{0,1:T(8,128)(2,1)S(1)} %get-tuple-element.46, bf16[1024,1024]{1,0:T(8,128)(2,1)S(1)} %bitcast.178), kind=kOutput, calls=%fused_computation.22 | convolution fusion | flops 271186944 | bytes 3154432 | tf_op jit(solution)/shard_map/dot_general | solution.py:37
  61.1 1.0 collective-permute-done.8
  66.3 1.8 %collective-permute-start.17 = (f32[56,1024]{1,0:T(8,128)S(1)}, f32[56,1024]{1,0:T(8,128)S(1)}, u32[]{:S(2)}, u32[]{:S(2)}) collective-permute-start(f32[56,1024]{1,0:T(8,128)S(1)} %get-tuple-element.9), channel_id=1, source_target_pairs={{0,4},{1,5},{4,8},{5,9},{8,12},{9,13},{12,14},{13,15},{14,10},{15,... | collective-permute-start | bytes 688136 | tf_op jit(solution)/shard_map/ppermute | solution.py:102
  68.4 1.4 %collective-permute-start.28 = (f32[48,1024]{1,0:T(8,128)S(1)}, f32[48,1024]{1,0:T(8,128)S(1)}, u32[]{:S(2)}, u32[]{:S(2)}) collective-permute-start(f32[48,1024]{1,0:T(8,128)S(1)} %get-tuple-element.16), channel_id=1, source_target_pairs={{4,0},{5,1},{8,4},{9,5},{12,8},{13,9},{14,12},{15,13},{10,14},{11,... | collective-permute-start | bytes 589832 | tf_op jit(solution)/shard_map/ppermute | solution.py:108
  69.8 3.2 %collective-permute-done.24 = f32[48,1024]{1,0:T(8,128)S(1)} collective-permute-done((f32[48,1024]{1,0:T(8,128)S(1)}, f32[48,1024]{1,0:T(8,128)S(1)}, u32[]{:S(2)}, u32[]{:S(2)}) %collective-permute-start.24) | collective-permute-done | bytes 196640 | tf_op jit(solution)/shard_map/ppermute | solution.py:102
  73.7 4.2 %collective-permute-done.17 = f32[56,1024]{1,0:T(8,128)S(1)} collective-permute-done((f32[56,1024]{1,0:T(8,128)S(1)}, f32[56,1024]{1,0:T(8,128)S(1)}, u32[]{:S(2)}, u32[]{:S(2)}) %collective-permute-start.17) | collective-permute-done | bytes 229408 | tf_op jit(solution)/shard_map/ppermute | solution.py:102
  78.7 1.4 %collective-permute-start.21 = (f32[56,1024]{1,0:T(8,128)S(1)}, f32[56,1024]{1,0:T(8,128)S(1)}, u32[]{:S(2)}, u32[]{:S(2)}) collective-permute-start(f32[56,1024]{1,0:T(8,128)S(1)} %get-tuple-element.8), channel_id=1, source_target_pairs={{4,0},{5,1},{8,4},{9,5},{12,8},{13,9},{14,12},{15,13},{10,14},{11,... | collective-permute-start | bytes 688136 | tf_op jit(solution)/shard_map/ppermute | solution.py:108
  80.1 2.1 %collective-permute-done.25 = f32[48,1024]{1,0:T(8,128)S(1)} collective-permute-done((f32[48,1024]{1,0:T(8,128)S(1)}, f32[48,1024]{1,0:T(8,128)S(1)}, u32[]{:S(2)}, u32[]{:S(2)}) %collective-permute-start.25) | collective-permute-done | bytes 196640 | tf_op jit(solution)/shard_map/ppermute | solution.py:102
  82.9 1.4 %collective-permute-start.29 = (f32[48,1024]{1,0:T(8,128)S(1)}, f32[48,1024]{1,0:T(8,128)S(1)}, u32[]{:S(2)}, u32[]{:S(2)}) collective-permute-start(f32[48,1024]{1,0:T(8,128)S(1)} %get-tuple-element.14), channel_id=1, source_target_pairs={{4,0},{5,1},{8,4},{9,5},{12,8},{13,9},{14,12},{15,13},{10,14},{11,... | collective-permute-start | bytes 589832 | tf_op jit(solution)/shard_map/ppermute | solution.py:108
  84.3 2.8 %collective-permute-done.18 = f32[56,1024]{1,0:T(8,128)S(1)} collective-permute-done((f32[56,1024]{1,0:T(8,128)S(1)}, f32[56,1024]{1,0:T(8,128)S(1)}, u32[]{:S(2)}, u32[]{:S(2)}) %collective-permute-start.18) | collective-permute-done | bytes 229408 | tf_op jit(solution)/shard_map/ppermute | solution.py:102
  87.1 1.6 %collective-permute-start.22 = (f32[56,1024]{1,0:T(8,128)S(1)}, f32[56,1024]{1,0:T(8,128)S(1)}, u32[]{:S(2)}, u32[]{:S(2)}) collective-permute-start(f32[56,1024]{1,0:T(8,128)S(1)} %get-tuple-element.6), channel_id=1, source_target_pairs={{4,0},{5,1},{8,4},{9,5},{12,8},{13,9},{14,12},{15,13},{10,14},{11,... | collective-permute-start | bytes 688136 | tf_op jit(solution)/shard_map/ppermute | solution.py:108
  89.2 2.1 %collective-permute-done.26 = f32[48,1024]{1,0:T(8,128)S(1)} collective-permute-done((f32[48,1024]{1,0:T(8,128)S(1)}, f32[48,1024]{1,0:T(8,128)S(1)}, u32[]{:S(2)}, u32[]{:S(2)}) %collective-permute-start.26) | collective-permute-done | bytes 196640 | tf_op jit(solution)/shard_map/ppermute | solution.py:102
  91.3 1.6 %collective-permute-start.30 = (f32[48,1024]{1,0:T(8,128)S(1)}, f32[48,1024]{1,0:T(8,128)S(1)}, u32[]{:S(2)}, u32[]{:S(2)}) collective-permute-start(f32[48,1024]{1,0:T(8,128)S(1)} %get-tuple-element.12), channel_id=1, source_target_pairs={{4,0},{5,1},{8,4},{9,5},{12,8},{13,9},{14,12},{15,13},{10,14},{11,... | collective-permute-start | bytes 589832 | tf_op jit(solution)/shard_map/ppermute | solution.py:108
  93.4 1.6 %collective-permute-done.22 = f32[56,1024]{1,0:T(8,128)S(1)} collective-permute-done((f32[56,1024]{1,0:T(8,128)S(1)}, f32[56,1024]{1,0:T(8,128)S(1)}, u32[]{:S(2)}, u32[]{:S(2)}) %collective-permute-start.22) | collective-permute-done | bytes 229408 | tf_op jit(solution)/shard_map/ppermute | solution.py:108
  95.0 1.2 %collective-permute-start.23 = (f32[56,1024]{1,0:T(8,128)S(1)}, f32[56,1024]{1,0:T(8,128)S(1)}, u32[]{:S(2)}, u32[]{:S(2)}) collective-permute-start(f32[56,1024]{1,0:T(8,128)S(1)} %fusion.18), channel_id=1, source_target_pairs={{4,0},{5,1},{8,4},{9,5},{12,8},{13,9},{14,12},{15,13},{10,14},{11,... | collective-permute-start | bytes 688136 | tf_op jit(solution)/shard_map/ppermute | solution.py:108
  96.2 3.0 %collective-permute-done.30 = f32[48,1024]{1,0:T(8,128)S(1)} collective-permute-done((f32[48,1024]{1,0:T(8,128)S(1)}, f32[48,1024]{1,0:T(8,128)S(1)}, u32[]{:S(2)}, u32[]{:S(2)}) %collective-permute-start.30) | collective-permute-done | bytes 196640 | tf_op jit(solution)/shard_map/ppermute | solution.py:108
  99.9 3.2 %collective-permute-done.23 = f32[56,1024]{1,0:T(8,128)S(1)} collective-permute-done((f32[56,1024]{1,0:T(8,128)S(1)}, f32[56,1024]{1,0:T(8,128)S(1)}, u32[]{:S(2)}, u32[]{:S(2)}) %collective-permute-start.23) | collective-permute-done | bytes 229408 | tf_op jit(solution)/shard_map/ppermute | solution.py:108
  (163 shorter events, 35.5 us)
Async XLA Ops:
  0.6 35.0 %copy-start = (s32[16,16]{1,0:T(8,128)S(1)}, s32[16,16]{1,0:T(8,128)}, u32[]{:S(2)}) copy-start(s32[16,16]{1,0:T(8,128)} %param.21) | copy-start | bytes 3076
  2.4 8.0 %collective-permute-start = (bf16[96,1024]{1,0:T(8,128)(2,1)S(1)}, bf16[96,1024]{1,0:T(8,128)(2,1)S(1)}, u32[]{:S(2)}, u32[]{:S(2)}) collective-permute-start(bf16[96,1024]{1,0:T(8,128)(2,1)S(1)} %constant_dynamic-update-slice_fusion), channel_id=1, source_target_pairs={{4,0},{5,1},{8,4},{9,5},{12,8},{13,9},{14,12},{15,13},{10,14},{11,... | collective-permute-start | bytes 589832 | tf_op jit(solution)/shard_map/ppermute | solution.py:80
  5.4 6.6 %collective-permute-start.3 = (bf16[96,1024]{1,0:T(8,128)(2,1)S(1)}, bf16[96,1024]{1,0:T(8,128)(2,1)S(1)}, u32[]{:S(2)}, u32[]{:S(2)}) collective-permute-start(bf16[96,1024]{1,0:T(8,128)(2,1)S(1)} %constant_dynamic-update-slice_fusion), channel_id=1, source_target_pairs={{0,4},{1,5},{4,8},{5,9},{8,12},{9,13},{12,14},{13,15},{14,10},{15,... | collective-permute-start | bytes 589832 | tf_op jit(solution)/shard_map/ppermute | solution.py:77
  10.4 6.1 %collective-permute-start.1 = (bf16[96,1024]{1,0:T(8,128)(2,1)S(1)}, bf16[96,1024]{1,0:T(8,128)(2,1)S(1)}, u32[]{:S(2)}, u32[]{:S(2)}) collective-permute-start(bf16[96,1024]{1,0:T(8,128)(2,1)S(1)} %collective-permute-done), channel_id=1, source_target_pairs={{4,0},{5,1},{8,4},{9,5},{12,8},{13,9},{14,12},{15,13},{10,14},{11,... | collective-permute-start | bytes 589832 | tf_op jit(solution)/shard_map/ppermute | solution.py:80
  12.1 5.8 %collective-permute-start.4 = (bf16[96,1024]{1,0:T(8,128)(2,1)S(1)}, bf16[96,1024]{1,0:T(8,128)(2,1)S(1)}, u32[]{:S(2)}, u32[]{:S(2)}) collective-permute-start(bf16[96,1024]{1,0:T(8,128)(2,1)S(1)} %collective-permute-done.3), channel_id=1, source_target_pairs={{0,4},{1,5},{4,8},{5,9},{8,12},{9,13},{12,14},{13,15},{14,10},{15,... | collective-permute-start | bytes 589832 | tf_op jit(solution)/shard_map/ppermute | solution.py:77
  16.5 8.1 %collective-permute-start.2 = (bf16[96,1024]{1,0:T(8,128)(2,1)S(1)}, bf16[96,1024]{1,0:T(8,128)(2,1)S(1)}, u32[]{:S(2)}, u32[]{:S(2)}) collective-permute-start(bf16[96,1024]{1,0:T(8,128)(2,1)S(1)} %collective-permute-done.1), channel_id=1, source_target_pairs={{4,0},{5,1},{8,4},{9,5},{12,8},{13,9},{14,12},{15,13},{10,14},{11,... | collective-permute-start | bytes 589832 | tf_op jit(solution)/shard_map/ppermute | solution.py:80
  17.8 6.1 %collective-permute-start.5 = (bf16[96,1024]{1,0:T(8,128)(2,1)S(1)}, bf16[96,1024]{1,0:T(8,128)(2,1)S(1)}, u32[]{:S(2)}, u32[]{:S(2)}) collective-permute-start(bf16[96,1024]{1,0:T(8,128)(2,1)S(1)} %collective-permute-done.4), channel_id=1, source_target_pairs={{0,4},{1,5},{4,8},{5,9},{8,12},{9,13},{12,14},{13,15},{14,10},{15,... | collective-permute-start | bytes 589832 | tf_op jit(solution)/shard_map/ppermute | solution.py:77
  24.0 5.7 %collective-permute-start.6 = (bf16[96,1024]{1,0:T(8,128)(2,1)S(1)}, bf16[96,1024]{1,0:T(8,128)(2,1)S(1)}, u32[]{:S(2)}, u32[]{:S(2)}) collective-permute-start(bf16[96,1024]{1,0:T(8,128)(2,1)S(1)} %collective-permute-done.5), channel_id=1, source_target_pairs={{0,4},{1,5},{4,8},{5,9},{8,12},{9,13},{12,14},{13,15},{14,10},{15,... | collective-permute-start | bytes 589832 | tf_op jit(solution)/shard_map/ppermute | solution.py:77
  32.8 7.0 %collective-permute-start.7 = (bf16[8,96,1024]{2,1,0:T(8,128)(2,1)}, bf16[8,96,1024]{2,1,0:T(8,128)(2,1)S(1)}, u32[]{:S(2)}, u32[]{:S(2)}) collective-permute-start(bf16[8,96,1024]{2,1,0:T(8,128)(2,1)} %get-tuple-element.21), channel_id=1, source_target_pairs={{0,1},{1,0},{2,3},{3,2},{4,5},{5,4},{6,7},{7,6},{8,9},{9,8},{10,11... | collective-permute-start | bytes 4718600 | tf_op jit(solution)/shard_map/ppermute | solution.py:83
  49.0 14.4 %collective-permute-start.14 = (bf16[128,1024]{0,1:T(8,128)(2,1)S(1)}, bf16[128,1024]{0,1:T(8,128)(2,1)S(1)}, u32[]{:S(2)}, u32[]{:S(2)}) collective-permute-start(bf16[128,1024]{0,1:T(8,128)(2,1)S(1)} %get-tuple-element.44), channel_id=1, source_target_pairs={{0,1},{1,0},{2,3},{3,2},{4,5},{5,4},{6,7},{7,6},{8,9},{9,8},{10,11... | collective-permute-start | bytes 786440 | tf_op jit(solution)/shard_map/ppermute | solution.py:163
  56.1 6.3 %collective-permute-start.9 = (bf16[128,1024]{0,1:T(8,128)(2,1)S(1)}, bf16[128,1024]{0,1:T(8,128)(2,1)S(1)}, u32[]{:S(2)}, u32[]{:S(2)}) collective-permute-start(bf16[128,1024]{0,1:T(8,128)(2,1)S(1)} %copy-done.9), channel_id=1, source_target_pairs={{0,1},{1,0},{2,3},{3,2},{4,5},{5,4},{6,7},{7,6},{8,9},{9,8},{10,11... | collective-permute-start | bytes 786440 | tf_op jit(solution)/shard_map/ppermute | solution.py:163
  59.0 5.5 %collective-permute-start.11 = (bf16[128,1024]{0,1:T(8,128)(2,1)S(1)}, bf16[128,1024]{0,1:T(8,128)(2,1)S(1)}, u32[]{:S(2)}, u32[]{:S(2)}) collective-permute-start(bf16[128,1024]{0,1:T(8,128)(2,1)S(1)} %get-tuple-element.18), channel_id=1, source_target_pairs={{0,1},{1,0},{2,3},{3,2},{4,5},{5,4},{6,7},{7,6},{8,9},{9,8},{10,11... | collective-permute-start | bytes 786440 | tf_op jit(solution)/shard_map/ppermute | solution.py:163
  59.3 3.7 %collective-permute-start.13 = (bf16[128,8,32]{0,2,1:T(8,128)(2,1)S(1)}, bf16[128,8,32]{0,2,1:T(8,128)(2,1)S(1)}, u32[]{:S(2)}, u32[]{:S(2)}) collective-permute-start(bf16[128,8,32]{0,2,1:T(8,128)(2,1)S(1)} %copy-done.13), channel_id=1, source_target_pairs={{0,1},{1,0},{2,3},{3,2},{4,5},{5,4},{6,7},{7,6},{8,9},{9,8},{10,11... | collective-permute-start | bytes 196616 | tf_op jit(solution)/shard_map/ppermute | solution.py:160
  59.6 1.2 %collective-permute-start.12 = (f32[1024]{0:T(1024)S(1)}, f32[1024]{0:T(1024)S(1)}, u32[]{:S(2)}, u32[]{:S(2)}) collective-permute-start(f32[1024]{0:T(1024)S(1)} %get-tuple-element.17), channel_id=1, source_target_pairs={{0,1},{1,0},{2,3},{3,2},{4,5},{5,4},{6,7},{7,6},{8,9},{9,8},{10,11... | collective-permute-start | bytes 12296 | tf_op jit(solution)/shard_map/ppermute | solution.py:163
  60.7 1.3 %collective-permute-start.8 = (bf16[128,8,64]{0,2,1:T(8,128)(2,1)S(1)}, bf16[128,8,64]{0,2,1:T(8,128)(2,1)S(1)}, u32[]{:S(2)}, u32[]{:S(2)}) collective-permute-start(bf16[128,8,64]{0,2,1:T(8,128)(2,1)S(1)} %dynamic-slice_bitcast_fusion.1), channel_id=1, source_target_pairs={{0,1},{1,0},{2,3},{3,2},{4,5},{5,4},{6,7},{7,6},{8,9},{9,8},{10,11... | collective-permute-start | bytes 393224 | tf_op jit(solution)/shard_map/ppermute | solution.py:160
  62.1 3.9 %collective-permute-start.15 = (bf16[128,8,32]{0,2,1:T(8,128)(2,1)S(1)}, bf16[128,8,32]{0,2,1:T(8,128)(2,1)S(1)}, u32[]{:S(2)}, u32[]{:S(2)}) collective-permute-start(bf16[128,8,32]{0,2,1:T(8,128)(2,1)S(1)} %dynamic-slice_bitcast_fusion.2), channel_id=1, source_target_pairs={{0,1},{1,0},{2,3},{3,2},{4,5},{5,4},{6,7},{7,6},{8,9},{9,8},{10,11... | collective-permute-start | bytes 196616 | tf_op jit(solution)/shard_map/ppermute | solution.py:160
  62.4 3.6 %collective-permute-start.16 = (bf16[128,1024]{0,1:T(8,128)(2,1)S(1)}, bf16[128,1024]{0,1:T(8,128)(2,1)S(1)}, u32[]{:S(2)}, u32[]{:S(2)}) collective-permute-start(bf16[128,1024]{0,1:T(8,128)(2,1)S(1)} %fusion.1), channel_id=1, source_target_pairs={{0,1},{1,0},{2,3},{3,2},{4,5},{5,4},{6,7},{7,6},{8,9},{9,8},{10,11... | collective-permute-start | bytes 786440 | tf_op jit(solution)/shard_map/ppermute | solution.py:163
  63.0 1.4 %collective-permute-start.10 = (bf16[128,8,64]{0,2,1:T(8,128)(2,1)S(1)}, bf16[128,8,64]{0,2,1:T(8,128)(2,1)S(1)}, u32[]{:S(2)}, u32[]{:S(2)}) collective-permute-start(bf16[128,8,64]{0,2,1:T(8,128)(2,1)S(1)} %dynamic-slice_bitcast_fusion), channel_id=1, source_target_pairs={{0,1},{1,0},{2,3},{3,2},{4,5},{5,4},{6,7},{7,6},{8,9},{9,8},{10,11... | collective-permute-start | bytes 393224 | tf_op jit(solution)/shard_map/ppermute | solution.py:160
  65.2 7.8 %collective-permute-start.24 = (f32[48,1024]{1,0:T(8,128)S(1)}, f32[48,1024]{1,0:T(8,128)S(1)}, u32[]{:S(2)}, u32[]{:S(2)}) collective-permute-start(f32[48,1024]{1,0:T(8,128)S(1)} %get-tuple-element.15), channel_id=1, source_target_pairs={{0,4},{1,5},{4,8},{5,9},{8,12},{9,13},{12,14},{13,15},{14,10},{15,... | collective-permute-start | bytes 589832 | tf_op jit(solution)/shard_map/ppermute | solution.py:102
  66.3 11.6 %collective-permute-start.17 = (f32[56,1024]{1,0:T(8,128)S(1)}, f32[56,1024]{1,0:T(8,128)S(1)}, u32[]{:S(2)}, u32[]{:S(2)}) collective-permute-start(f32[56,1024]{1,0:T(8,128)S(1)} %get-tuple-element.9), channel_id=1, source_target_pairs={{0,4},{1,5},{4,8},{5,9},{8,12},{9,13},{12,14},{13,15},{14,10},{15,... | collective-permute-start | bytes 688136 | tf_op jit(solution)/shard_map/ppermute | solution.py:102
  68.1 9.8 %collective-permute-start.20 = (f32[56,1024]{1,0:T(8,128)S(1)}, f32[56,1024]{1,0:T(8,128)S(1)}, u32[]{:S(2)}, u32[]{:S(2)}) collective-permute-start(f32[56,1024]{1,0:T(8,128)S(1)} %get-tuple-element.10), channel_id=1, source_target_pairs={{4,0},{5,1},{8,4},{9,5},{12,8},{13,9},{14,12},{15,13},{10,14},{11,... | collective-permute-start | bytes 688136 | tf_op jit(solution)/shard_map/ppermute | solution.py:108
  68.4 11.7 %collective-permute-start.28 = (f32[48,1024]{1,0:T(8,128)S(1)}, f32[48,1024]{1,0:T(8,128)S(1)}, u32[]{:S(2)}, u32[]{:S(2)}) collective-permute-start(f32[48,1024]{1,0:T(8,128)S(1)} %get-tuple-element.16), channel_id=1, source_target_pairs={{4,0},{5,1},{8,4},{9,5},{12,8},{13,9},{14,12},{15,13},{10,14},{11,... | collective-permute-start | bytes 589832 | tf_op jit(solution)/shard_map/ppermute | solution.py:108
  73.0 9.1 %collective-permute-start.25 = (f32[48,1024]{1,0:T(8,128)S(1)}, f32[48,1024]{1,0:T(8,128)S(1)}, u32[]{:S(2)}, u32[]{:S(2)}) collective-permute-start(f32[48,1024]{1,0:T(8,128)S(1)} %fusion.31), channel_id=1, source_target_pairs={{0,4},{1,5},{4,8},{5,9},{8,12},{9,13},{12,14},{13,15},{14,10},{15,... | collective-permute-start | bytes 589832 | tf_op jit(solution)/shard_map/ppermute | solution.py:102
  78.0 9.1 %collective-permute-start.18 = (f32[56,1024]{1,0:T(8,128)S(1)}, f32[56,1024]{1,0:T(8,128)S(1)}, u32[]{:S(2)}, u32[]{:S(2)}) collective-permute-start(f32[56,1024]{1,0:T(8,128)S(1)} %get-tuple-element.7), channel_id=1, source_target_pairs={{0,4},{1,5},{4,8},{5,9},{8,12},{9,13},{12,14},{13,15},{14,10},{15,... | collective-permute-start | bytes 688136 | tf_op jit(solution)/shard_map/ppermute | solution.py:102
  78.7 8.4 %collective-permute-start.21 = (f32[56,1024]{1,0:T(8,128)S(1)}, f32[56,1024]{1,0:T(8,128)S(1)}, u32[]{:S(2)}, u32[]{:S(2)}) collective-permute-start(f32[56,1024]{1,0:T(8,128)S(1)} %get-tuple-element.8), channel_id=1, source_target_pairs={{4,0},{5,1},{8,4},{9,5},{12,8},{13,9},{14,12},{15,13},{10,14},{11,... | collective-permute-start | bytes 688136 | tf_op jit(solution)/shard_map/ppermute | solution.py:108
  82.2 9.1 %collective-permute-start.26 = (f32[48,1024]{1,0:T(8,128)S(1)}, f32[48,1024]{1,0:T(8,128)S(1)}, u32[]{:S(2)}, u32[]{:S(2)}) collective-permute-start(f32[48,1024]{1,0:T(8,128)S(1)} %get-tuple-element.13), channel_id=1, source_target_pairs={{0,4},{1,5},{4,8},{5,9},{8,12},{9,13},{12,14},{13,15},{14,10},{15,... | collective-permute-start | bytes 589832 | tf_op jit(solution)/shard_map/ppermute | solution.py:102
  82.9 8.4 %collective-permute-start.29 = (f32[48,1024]{1,0:T(8,128)S(1)}, f32[48,1024]{1,0:T(8,128)S(1)}, u32[]{:S(2)}, u32[]{:S(2)}) collective-permute-start(f32[48,1024]{1,0:T(8,128)S(1)} %get-tuple-element.14), channel_id=1, source_target_pairs={{4,0},{5,1},{8,4},{9,5},{12,8},{13,9},{14,12},{15,13},{10,14},{11,... | collective-permute-start | bytes 589832 | tf_op jit(solution)/shard_map/ppermute | solution.py:108
  87.1 7.8 %collective-permute-start.22 = (f32[56,1024]{1,0:T(8,128)S(1)}, f32[56,1024]{1,0:T(8,128)S(1)}, u32[]{:S(2)}, u32[]{:S(2)}) collective-permute-start(f32[56,1024]{1,0:T(8,128)S(1)} %get-tuple-element.6), channel_id=1, source_target_pairs={{4,0},{5,1},{8,4},{9,5},{12,8},{13,9},{14,12},{15,13},{10,14},{11,... | collective-permute-start | bytes 688136 | tf_op jit(solution)/shard_map/ppermute | solution.py:108
  88.8 11.1 %collective-permute-start.19 = (f32[56,1024]{1,0:T(8,128)S(1)}, f32[56,1024]{1,0:T(8,128)S(1)}, u32[]{:S(2)}, u32[]{:S(2)}) collective-permute-start(f32[56,1024]{1,0:T(8,128)S(1)} %get-tuple-element.5), channel_id=1, source_target_pairs={{0,4},{1,5},{4,8},{5,9},{8,12},{9,13},{12,14},{13,15},{14,10},{15,... | collective-permute-start | bytes 688136 | tf_op jit(solution)/shard_map/ppermute | solution.py:102
  91.3 7.8 %collective-permute-start.30 = (f32[48,1024]{1,0:T(8,128)S(1)}, f32[48,1024]{1,0:T(8,128)S(1)}, u32[]{:S(2)}, u32[]{:S(2)}) collective-permute-start(f32[48,1024]{1,0:T(8,128)S(1)} %get-tuple-element.12), channel_id=1, source_target_pairs={{4,0},{5,1},{8,4},{9,5},{12,8},{13,9},{14,12},{15,13},{10,14},{11,... | collective-permute-start | bytes 589832 | tf_op jit(solution)/shard_map/ppermute | solution.py:108
  93.0 6.8 %collective-permute-start.27 = (f32[48,1024]{1,0:T(8,128)S(1)}, f32[48,1024]{1,0:T(8,128)S(1)}, u32[]{:S(2)}, u32[]{:S(2)}) collective-permute-start(f32[48,1024]{1,0:T(8,128)S(1)} %get-tuple-element.11), channel_id=1, source_target_pairs={{0,4},{1,5},{4,8},{5,9},{8,12},{9,13},{12,14},{13,15},{14,10},{15,... | collective-permute-start | bytes 589832 | tf_op jit(solution)/shard_map/ppermute | solution.py:102
  95.0 8.1 %collective-permute-start.23 = (f32[56,1024]{1,0:T(8,128)S(1)}, f32[56,1024]{1,0:T(8,128)S(1)}, u32[]{:S(2)}, u32[]{:S(2)}) collective-permute-start(f32[56,1024]{1,0:T(8,128)S(1)} %fusion.18), channel_id=1, source_target_pairs={{4,0},{5,1},{8,4},{9,5},{12,8},{13,9},{14,12},{15,13},{10,14},{11,... | collective-permute-start | bytes 688136 | tf_op jit(solution)/shard_map/ppermute | solution.py:108
  (25 other events, 129.1 us)

commit v9 on v8

--- a/solution.py
+++ b/solution.py
@@ -79,13 +79,20 @@
         if s <= behind:
             right = lax.ppermute(right, "blk", ccw)
             rel[s] = right
+    half = ahead // 2
+    early = [0] + [chips - s for s in range(1, half + 1)] + [s for s in range(1, min(half, behind) + 1)]
+    late = [k for k in range(chips) if k not in early]
+    slot = [0] * chips
+    for i, k in enumerate(early + late):
+        slot[k] = i
     mine = jnp.stack(rel)
-    other = lax.ppermute(mine, "blk", partner)
-    both = jnp.concatenate([mine, other], axis=0)
+    other_early = lax.ppermute(jnp.stack([rel[k] for k in early]), "blk", partner)
+    other_late = lax.ppermute(jnp.stack([rel[k] for k in late]), "blk", partner)
+    both = jnp.concatenate([mine, other_early, other_late], axis=0)
     dest = jnp.arange(n_blk, dtype=jnp.int32)
     dest_chip, dest_core = dest // 2, dest % 2
     k = (jnp.asarray(place, jnp.int32)[dest_chip] - spot) % chips
-    index = jnp.where(dest_core == core, 0, chips) + k
+    index = jnp.where(dest_core == core, k, chips + jnp.asarray(slot, jnp.int32)[k])
     return jnp.take(both, index, axis=0)
 
 

time: 107 us -> 113 us (1.056)
  waiting for transfers between devices: 39.4 us -> 34.2 us
  local copies, waits for them, and re-layouts: 18.7 us -> 23.8 us
  matrix products: 12.4 us -> 15.8 us
  starting transfers between devices: 24.7 us -> 26.2 us
  other arithmetic: 9.69 us -> 11 us
    ppermute x4, starting transfers between devices: 1.76 us -> 8.57 us  [ring_all_gather(): left = lax.ppermute(left, 'blk', cw)]
    ppermute x3, starting transfers between devices: 6.07 us -> 0.31 us  [ring_all_gather(): right = lax.ppermute(right, 'blk', ccw)]
    ppermute x3, waiting for transfers between devices: 6.06 us -> 0.69 us  [ring_all_gather(): right = lax.ppermute(right, 'blk', ccw)]
    ppermute x7, starting transfers between devices: 8.91 us -> 4.48 us  [backward(): acc = lax.ppermute(acc, 'blk', ccw)]
    ppermute x7, starting transfers between devices: 5.46 us -> 9.84 us  [forward(): acc = lax.ppermute(acc, 'blk', cw) + part[(window - s) % chips]]
    ppermute x7, waiting for transfers between devices: 7.73 us -> 11.2 us  [backward(): acc = lax.ppermute(acc, 'blk', ccw)]
    unnamed x61 -> x50, local copies, waits for them, and re-layouts: 7.1 us -> 10 us
    ppermute x7, waiting for transfers between devices: 14.9 us -> 12.7 us  [forward(): acc = lax.ppermute(acc, 'blk', cw) + part[(window - s) % chips]]
  transfers between devices with their start and end apart: 31 -> 32, of which waited for: 16 -> 17; matrix products, arithmetic and copies ran while one was open for 22% -> 31% of each run, Pallas kernels for 0% -> 0%
where the time goes in v9:
time: 113 us
  waiting for transfers between devices  34.2 us (30%)
  starting transfers between devices  26.2 us (23%)
  local copies, waits for them, and re-layouts  23.8 us (21%)
  matrix products  15.8 us (14%)
  other arithmetic  11 us (10%)
  between operations  1.91 us (2%)
    ppermute x7, waiting for transfers between devices, forward(): acc = lax.ppermute(acc, 'blk', cw) + part[(window - s) % chips]  12.7 us
    ppermute x7, waiting for transfers between devices, backward(): acc = lax.ppermute(acc, 'blk', ccw)  11.2 us
    unnamed x50, local copies, waits for them, and re-layouts  10 us
    ppermute x7, starting transfers between devices, forward(): acc = lax.ppermute(acc, 'blk', cw) + part[(window - s) % chips]  9.84 us
    ppermute x4, starting transfers between devices, ring_all_gather(): left = lax.ppermute(left, 'blk', cw)  8.57 us
    ppermute x4, waiting for transfers between devices, ring_all_gather(): left = lax.ppermute(left, 'blk', cw)  7.84 us
    ppermute x7, starting transfers between devices, backward(): acc = lax.ppermute(acc, 'blk', ccw)  4.48 us
    dot_general x8, matrix products, slots_product(): lax.dot_general(left, right, (((0,), (0,)), ((), ())), preferred_element_...  4.02 us
  transfers between devices with their start and end apart: 32, of which 17 were waited for; matrix products, arithmetic and copies ran while one was open for 31% of the time, Pallas kernels for 0%

profile of v9, /device:TPU:0, one launch (start us, length us, event | category | flops | bytes accessed | tf_op | source)
XLA Modules:
  0.0 112.9 jit_solution(10678935983610623502)
XLA Ops:
  2.4 3.1 %collective-permute-start.3 = (bf16[96,1024]{1,0:T(8,128)(2,1)S(1)}, bf16[96,1024]{1,0:T(8,128)(2,1)S(1)}, u32[]{:S(2)}, u32[]{:S(2)}) collective-permute-start(bf16[96,1024]{1,0:T(8,128)(2,1)S(1)} %constant_dynamic-update-slice_fusion), channel_id=1, source_target_pairs={{0,4},{1,5},{4,8},{5,9},{8,12},{9,13},{12,14},{13,15},{14,10},{15,... | collective-permute-start | bytes 589832 | tf_op jit(solution)/shard_map/ppermute | solution.py:77
  6.3 1.2 %dynamic_slice.37 = s32[1]{0:T(128)} dynamic-slice(s32[8]{0:T(128)} %constant.182.clone, s32[]{:T(128)S(6)} %select_n.190), dynamic_slice_sizes={1} | dynamic-slice | bytes 12 | tf_op jit(solution)/shard_map/dynamic_slice | solution.py:72
  8.2 1.3 %gather_fusion.3 = s32[8]{0:T(128)S(1)} fusion(s32[8]{0:T(128)} %constant.184.clone, s32[1024]{0:T(1024)S(1)} %pad_clamp_fusion.4), kind=kCustom, calls=%fused_computation.7 | custom fusion | bytes 96 | tf_op jit(solution)/shard_map/gather | solution.py:161
  9.5 1.3 %gather_fusion = s32[16]{0:T(128)S(1)} fusion(s32[8]{0:T(128)} %constant.182.clone, s32[1024]{0:T(1024)S(1)} %pad_clamp_fusion.3), kind=kCustom, calls=%fused_computation.4 | custom fusion | bytes 192 | tf_op jit(solution)/shard_map/gather | solution.py:94
  11.5 1.3 %gather_fusion.1 = s32[16]{0:T(128)S(1)} fusion(s32[8]{0:T(128)} %constant.183.clone, s32[1024]{0:T(1024)S(1)} %get-tuple-element.39), kind=kCustom, calls=%fused_computation.5 | custom fusion | bytes 192 | tf_op jit(solution)/shard_map/gather | solution.py:95
  19.4 2.0 %collective-permute-start.4 = (bf16[96,1024]{1,0:T(8,128)(2,1)S(1)}, bf16[96,1024]{1,0:T(8,128)(2,1)S(1)}, u32[]{:S(2)}, u32[]{:S(2)}) collective-permute-start(bf16[96,1024]{1,0:T(8,128)(2,1)S(1)} %collective-permute-done.3), channel_id=1, source_target_pairs={{0,4},{1,5},{4,8},{5,9},{8,12},{9,13},{12,14},{13,15},{14,10},{15,... | collective-permute-start | bytes 589832 | tf_op jit(solution)/shard_map/ppermute | solution.py:77
  22.1 3.7 %collective-permute-done.4 = bf16[96,1024]{1,0:T(8,128)(2,1)S(1)} collective-permute-done((bf16[96,1024]{1,0:T(8,128)(2,1)S(1)}, bf16[96,1024]{1,0:T(8,128)(2,1)S(1)}, u32[]{:S(2)}, u32[]{:S(2)}) %collective-permute-start.4) | collective-permute-done | bytes 196640 | tf_op jit(solution)/shard_map/ppermute | solution.py:77
  25.8 1.7 %collective-permute-start.5 = (bf16[96,1024]{1,0:T(8,128)(2,1)S(1)}, bf16[96,1024]{1,0:T(8,128)(2,1)S(1)}, u32[]{:S(2)}, u32[]{:S(2)}) collective-permute-start(bf16[96,1024]{1,0:T(8,128)(2,1)S(1)} %collective-permute-done.4), channel_id=1, source_target_pairs={{0,4},{1,5},{4,8},{5,9},{8,12},{9,13},{12,14},{13,15},{14,10},{15,... | collective-permute-start | bytes 589832 | tf_op jit(solution)/shard_map/ppermute | solution.py:77
  30.1 1.4 %collective-permute-done.5 = bf16[96,1024]{1,0:T(8,128)(2,1)S(1)} collective-permute-done((bf16[96,1024]{1,0:T(8,128)(2,1)S(1)}, bf16[96,1024]{1,0:T(8,128)(2,1)S(1)}, u32[]{:S(2)}, u32[]{:S(2)}) %collective-permute-start.5) | collective-permute-done | bytes 196640 | tf_op jit(solution)/shard_map/ppermute | solution.py:77
  31.4 1.7 %collective-permute-start.6 = (bf16[96,1024]{1,0:T(8,128)(2,1)S(1)}, bf16[96,1024]{1,0:T(8,128)(2,1)S(1)}, u32[]{:S(2)}, u32[]{:S(2)}) collective-permute-start(bf16[96,1024]{1,0:T(8,128)(2,1)S(1)} %collective-permute-done.5), channel_id=1, source_target_pairs={{0,4},{1,5},{4,8},{5,9},{8,12},{9,13},{12,14},{13,15},{14,10},{15,... | collective-permute-start | bytes 589832 | tf_op jit(solution)/shard_map/ppermute | solution.py:77
  34.6 2.8 %collective-permute-done.6 = bf16[96,1024]{1,0:T(8,128)(2,1)S(1)} collective-permute-done((bf16[96,1024]{1,0:T(8,128)(2,1)S(1)}, bf16[96,1024]{1,0:T(8,128)(2,1)S(1)}, u32[]{:S(2)}, u32[]{:S(2)}) %collective-permute-start.6) | collective-permute-done | bytes 196640 | tf_op jit(solution)/shard_map/ppermute | solution.py:77
  42.2 2.6 %gather_fusion.2 = bf16[16,96,1024]{2,1,0:T(8,128)(2,1)S(1)} fusion(bf16[16,96,1024]{2,1,0:T(8,128)(2,1)} %constant_dynamic-update-slice_fusion.2, s32[1024]{0:T(1024)S(1)} %pad_clamp_fusion.1), kind=kCustom, calls=%fused_computation.6 | custom fusion | bytes 6291520 | tf_op jit(solution)/shard_map/jit(_take)/gather | solution.py:96
  46.7 2.6 %multiply_reduce_fusion = (f32[128]{0:T(128)}, bf16[128,1024]{0,1:T(8,128)(2,1)}, f32[128,1024]{0,1:T(8,128)}) fusion(f32[1024]{0:T(1024)S(1)} %convert_element_type.33, bf16[128,1024]{0,1:T(8,128)(2,1)S(1)} %get-tuple-element.31, bf16[1024,1024]{1,0:T(8,128)(2,1)S(1)} %bitcast.183), kind=kOutput, calls=%fused_computation.26 | convolution fusion | flops 270139264 | bytes 3150336 | tf_op jit(solution)/shard_map/dot_general | solution.py:20
  49.3 2.5 %multiply_convert_fusion.1 = (bf16[128,1024]{0,1:T(8,128)(2,1)S(1)}, f32[128,1024]{0,1:T(8,128)}) fusion(f32[128,1024]{0,1:T(8,128)S(1)} %get-tuple-element.32, bf16[1024,1024]{1,0:T(8,128)(2,1)S(1)} %bitcast.184, bf16[128,1024]{0,1:T(8,128)(2,1)} %get-tuple-element.20), kind=kOutput, calls=%fused_computation.28 | convolution fusion | flops 269090816 | bytes 3670016 | tf_op jit(solution)/shard_map/dot_general | solution.py:25
  52.9 2.4 %multiply_convert_fusion = (bf16[128,1024]{0,1:T(8,128)(2,1)S(1)}, f32[128,1024]{0,1:T(8,128)}) fusion(f32[128,1024]{0,1:T(8,128)} %copy-done.15, bf16[128,512]{1,0:T(8,128)(2,1)S(1)} %fusion.3, bf16[512,1024]{1,0:T(8,128)(2,1)S(1)} %bitcast.180), kind=kOutput, calls=%fused_computation.27 | convolution fusion | flops 134873088 | bytes 2490368 | tf_op jit(solution)/shard_map/dot_general | solution.py:34
  58.3 1.5 %fusion.15 = f32[8,64,1024]{2,1,0:T(8,128)S(1)} fusion(bf16[128,1024]{0,1:T(8,128)(2,1)} %get-tuple-element.20, bf16[128,8,2,64]{0,3,2,1:T(8,128)(2,1)S(1)} %get-tuple-element.27, s32[]{:T(128)S(6)} %select_n.203), kind=kOutput, calls=%fused_computation.43 | convolution fusion | flops 134217728 | bytes 2490372 | tf_op jit(solution)/shard_map/dot_general | solution.py:134
  60.7 2.5 %add_reduce_fusion = (f32[1024]{0:T(1024)S(1)}, bf16[128,1024]{0,1:T(8,128)(2,1)S(1)}) fusion(f32[128,1024]{0,1:T(8,128)} %get-tuple-element.33, f32[128]{0:T(128)S(1)} %subtract_multiply_fusion, f32[1024]{0:T(1024)S(1)} %convert_element_type.33, bf16[128,1024]{0,1:T(8,128)(2,1)S(1)} %get-tuple-element.36, bf16[1024,1024]{1,0:T(8,128)(2,1)S(1)} %bitcast.185), kind=kOutput, calls=%fused_computation.24 | convolution fusion | flops 271186944 | bytes 3154432 | tf_op jit(solution)/shard_map/dot_general | solution.py:37
  70.1 1.8 %collective-permute-start.25 = (f32[48,1024]{1,0:T(8,128)S(1)}, f32[48,1024]{1,0:T(8,128)S(1)}, u32[]{:S(2)}, u32[]{:S(2)}) collective-permute-start(f32[48,1024]{1,0:T(8,128)S(1)} %get-tuple-element.15), channel_id=1, source_target_pairs={{0,4},{1,5},{4,8},{5,9},{8,12},{9,13},{12,14},{13,15},{14,10},{15,... | collective-permute-start | bytes 589832 | tf_op jit(solution)/shard_map/ppermute | solution.py:109
  72.2 1.6 %collective-permute-start.18 = (f32[56,1024]{1,0:T(8,128)S(1)}, f32[56,1024]{1,0:T(8,128)S(1)}, u32[]{:S(2)}, u32[]{:S(2)}) collective-permute-start(f32[56,1024]{1,0:T(8,128)S(1)} %get-tuple-element.9), channel_id=1, source_target_pairs={{0,4},{1,5},{4,8},{5,9},{8,12},{9,13},{12,14},{13,15},{14,10},{15,... | collective-permute-start | bytes 688136 | tf_op jit(solution)/shard_map/ppermute | solution.py:109
  74.6 3.2 %collective-permute-done.25 = f32[48,1024]{1,0:T(8,128)S(1)} collective-permute-done((f32[48,1024]{1,0:T(8,128)S(1)}, f32[48,1024]{1,0:T(8,128)S(1)}, u32[]{:S(2)}, u32[]{:S(2)}) %collective-permute-start.25) | collective-permute-done | bytes 196640 | tf_op jit(solution)/shard_map/ppermute | solution.py:109
  77.8 1.8 %collective-permute-start.26 = (f32[48,1024]{1,0:T(8,128)S(1)}, f32[48,1024]{1,0:T(8,128)S(1)}, u32[]{:S(2)}, u32[]{:S(2)}) collective-permute-start(f32[48,1024]{1,0:T(8,128)S(1)} %fusion.31), channel_id=1, source_target_pairs={{0,4},{1,5},{4,8},{5,9},{8,12},{9,13},{12,14},{13,15},{14,10},{15,... | collective-permute-start | bytes 589832 | tf_op jit(solution)/shard_map/ppermute | solution.py:109
  79.6 3.1 %collective-permute-done.18 = f32[56,1024]{1,0:T(8,128)S(1)} collective-permute-done((f32[56,1024]{1,0:T(8,128)S(1)}, f32[56,1024]{1,0:T(8,128)S(1)}, u32[]{:S(2)}, u32[]{:S(2)}) %collective-permute-start.18) | collective-permute-done | bytes 229408 | tf_op jit(solution)/shard_map/ppermute | solution.py:109
  82.8 1.8 %collective-permute-start.19 = (f32[56,1024]{1,0:T(8,128)S(1)}, f32[56,1024]{1,0:T(8,128)S(1)}, u32[]{:S(2)}, u32[]{:S(2)}) collective-permute-start(f32[56,1024]{1,0:T(8,128)S(1)} %get-tuple-element.7), channel_id=1, source_target_pairs={{0,4},{1,5},{4,8},{5,9},{8,12},{9,13},{12,14},{13,15},{14,10},{15,... | collective-permute-start | bytes 688136 | tf_op jit(solution)/shard_map/ppermute | solution.py:109
  85.4 1.6 %collective-permute-done.26 = f32[48,1024]{1,0:T(8,128)S(1)} collective-permute-done((f32[48,1024]{1,0:T(8,128)S(1)}, f32[48,1024]{1,0:T(8,128)S(1)}, u32[]{:S(2)}, u32[]{:S(2)}) %collective-permute-start.26) | collective-permute-done | bytes 196640 | tf_op jit(solution)/shard_map/ppermute | solution.py:109
  87.0 1.8 %collective-permute-start.27 = (f32[48,1024]{1,0:T(8,128)S(1)}, f32[48,1024]{1,0:T(8,128)S(1)}, u32[]{:S(2)}, u32[]{:S(2)}) collective-permute-start(f32[48,1024]{1,0:T(8,128)S(1)} %get-tuple-element.13), channel_id=1, source_target_pairs={{0,4},{1,5},{4,8},{5,9},{8,12},{9,13},{12,14},{13,15},{14,10},{15,... | collective-permute-start | bytes 589832 | tf_op jit(solution)/shard_map/ppermute | solution.py:109
  89.1 2.8 %collective-permute-done.19 = f32[56,1024]{1,0:T(8,128)S(1)} collective-permute-done((f32[56,1024]{1,0:T(8,128)S(1)}, f32[56,1024]{1,0:T(8,128)S(1)}, u32[]{:S(2)}, u32[]{:S(2)}) %collective-permute-start.19) | collective-permute-done | bytes 229408 | tf_op jit(solution)/shard_map/ppermute | solution.py:109
  91.9 1.7 %collective-permute-start.23 = (f32[56,1024]{1,0:T(8,128)S(1)}, f32[56,1024]{1,0:T(8,128)S(1)}, u32[]{:S(2)}, u32[]{:S(2)}) collective-permute-start(f32[56,1024]{1,0:T(8,128)S(1)} %get-tuple-element.6), channel_id=1, source_target_pairs={{4,0},{5,1},{8,4},{9,5},{12,8},{13,9},{14,12},{15,13},{10,14},{11,... | collective-permute-start | bytes 688136 | tf_op jit(solution)/shard_map/ppermute | solution.py:115
  94.0 2.0 %collective-permute-done.27 = f32[48,1024]{1,0:T(8,128)S(1)} collective-permute-done((f32[48,1024]{1,0:T(8,128)S(1)}, f32[48,1024]{1,0:T(8,128)S(1)}, u32[]{:S(2)}, u32[]{:S(2)}) %collective-permute-start.27) | collective-permute-done | bytes 196640 | tf_op jit(solution)/shard_map/ppermute | solution.py:109
  96.5 1.4 %collective-permute-start.31 = (f32[48,1024]{1,0:T(8,128)S(1)}, f32[48,1024]{1,0:T(8,128)S(1)}, u32[]{:S(2)}, u32[]{:S(2)}) collective-permute-start(f32[48,1024]{1,0:T(8,128)S(1)} %get-tuple-element.12), channel_id=1, source_target_pairs={{4,0},{5,1},{8,4},{9,5},{12,8},{13,9},{14,12},{15,13},{10,14},{11,... | collective-permute-start | bytes 589832 | tf_op jit(solution)/shard_map/ppermute | solution.py:115
  98.6 2.8 %collective-permute-done.23 = f32[56,1024]{1,0:T(8,128)S(1)} collective-permute-done((f32[56,1024]{1,0:T(8,128)S(1)}, f32[56,1024]{1,0:T(8,128)S(1)}, u32[]{:S(2)}, u32[]{:S(2)}) %collective-permute-start.23) | collective-permute-done | bytes 229408 | tf_op jit(solution)/shard_map/ppermute | solution.py:115
  101.5 4.1 %collective-permute-done.31 = f32[48,1024]{1,0:T(8,128)S(1)} collective-permute-done((f32[48,1024]{1,0:T(8,128)S(1)}, f32[48,1024]{1,0:T(8,128)S(1)}, u32[]{:S(2)}, u32[]{:S(2)}) %collective-permute-start.31) | collective-permute-done | bytes 196640 | tf_op jit(solution)/shard_map/ppermute | solution.py:115
  105.7 3.4 %collective-permute-done.24 = f32[56,1024]{1,0:T(8,128)S(1)} collective-permute-done((f32[56,1024]{1,0:T(8,128)S(1)}, f32[56,1024]{1,0:T(8,128)S(1)}, u32[]{:S(2)}, u32[]{:S(2)}) %collective-permute-start.24) | collective-permute-done | bytes 229408 | tf_op jit(solution)/shard_map/ppermute | solution.py:115
  (158 shorter events, 40.4 us)
Async XLA Ops:
  2.4 17.0 %collective-permute-start.3 = (bf16[96,1024]{1,0:T(8,128)(2,1)S(1)}, bf16[96,1024]{1,0:T(8,128)(2,1)S(1)}, u32[]{:S(2)}, u32[]{:S(2)}) collective-permute-start(bf16[96,1024]{1,0:T(8,128)(2,1)S(1)} %constant_dynamic-update-slice_fusion), channel_id=1, source_target_pairs={{0,4},{1,5},{4,8},{5,9},{8,12},{9,13},{12,14},{13,15},{14,10},{15,... | collective-permute-start | bytes 589832 | tf_op jit(solution)/shard_map/ppermute | solution.py:77
  5.5 15.9 %collective-permute-start = (bf16[96,1024]{1,0:T(8,128)(2,1)S(1)}, bf16[96,1024]{1,0:T(8,128)(2,1)S(1)}, u32[]{:S(2)}, u32[]{:S(2)}) collective-permute-start(bf16[96,1024]{1,0:T(8,128)(2,1)S(1)} %constant_dynamic-update-slice_fusion), channel_id=1, source_target_pairs={{4,0},{5,1},{8,4},{9,5},{12,8},{13,9},{14,12},{15,13},{10,14},{11,... | collective-permute-start | bytes 589832 | tf_op jit(solution)/shard_map/ppermute | solution.py:80
  19.4 6.4 %collective-permute-start.4 = (bf16[96,1024]{1,0:T(8,128)(2,1)S(1)}, bf16[96,1024]{1,0:T(8,128)(2,1)S(1)}, u32[]{:S(2)}, u32[]{:S(2)}) collective-permute-start(bf16[96,1024]{1,0:T(8,128)(2,1)S(1)} %collective-permute-done.3), channel_id=1, source_target_pairs={{0,4},{1,5},{4,8},{5,9},{8,12},{9,13},{12,14},{13,15},{14,10},{15,... | collective-permute-start | bytes 589832 | tf_op jit(solution)/shard_map/ppermute | solution.py:77
  21.4 6.8 %collective-permute-start.1 = (bf16[96,1024]{1,0:T(8,128)(2,1)S(1)}, bf16[96,1024]{1,0:T(8,128)(2,1)S(1)}, u32[]{:S(2)}, u32[]{:S(2)}) collective-permute-start(bf16[96,1024]{1,0:T(8,128)(2,1)S(1)} %collective-permute-done), channel_id=1, source_target_pairs={{4,0},{5,1},{8,4},{9,5},{12,8},{13,9},{14,12},{15,13},{10,14},{11,... | collective-permute-start | bytes 589832 | tf_op jit(solution)/shard_map/ppermute | solution.py:80
  25.8 5.7 %collective-permute-start.5 = (bf16[96,1024]{1,0:T(8,128)(2,1)S(1)}, bf16[96,1024]{1,0:T(8,128)(2,1)S(1)}, u32[]{:S(2)}, u32[]{:S(2)}) collective-permute-start(bf16[96,1024]{1,0:T(8,128)(2,1)S(1)} %collective-permute-done.4), channel_id=1, source_target_pairs={{0,4},{1,5},{4,8},{5,9},{8,12},{9,13},{12,14},{13,15},{14,10},{15,... | collective-permute-start | bytes 589832 | tf_op jit(solution)/shard_map/ppermute | solution.py:77
  28.2 5.7 %collective-permute-start.2 = (bf16[96,1024]{1,0:T(8,128)(2,1)S(1)}, bf16[96,1024]{1,0:T(8,128)(2,1)S(1)}, u32[]{:S(2)}, u32[]{:S(2)}) collective-permute-start(bf16[96,1024]{1,0:T(8,128)(2,1)S(1)} %collective-permute-done.1), channel_id=1, source_target_pairs={{4,0},{5,1},{8,4},{9,5},{12,8},{13,9},{14,12},{15,13},{10,14},{11,... | collective-permute-start | bytes 589832 | tf_op jit(solution)/shard_map/ppermute | solution.py:80
  30.1 10.2 %collective-permute-start.7 = (bf16[5,96,1024]{2,1,0:T(8,128)(2,1)}, bf16[5,96,1024]{2,1,0:T(8,128)(2,1)S(1)}, u32[]{:S(2)}, u32[]{:S(2)}) collective-permute-start(bf16[5,96,1024]{2,1,0:T(8,128)(2,1)} %get-tuple-element.21), channel_id=1, source_target_pairs={{0,1},{1,0},{2,3},{3,2},{4,5},{5,4},{6,7},{7,6},{8,9},{9,8},{10,11... | collective-permute-start | bytes 2949128 | tf_op jit(solution)/shard_map/ppermute | solution.py:89
  31.4 6.0 %collective-permute-start.6 = (bf16[96,1024]{1,0:T(8,128)(2,1)S(1)}, bf16[96,1024]{1,0:T(8,128)(2,1)S(1)}, u32[]{:S(2)}, u32[]{:S(2)}) collective-permute-start(bf16[96,1024]{1,0:T(8,128)(2,1)S(1)} %collective-permute-done.5), channel_id=1, source_target_pairs={{0,4},{1,5},{4,8},{5,9},{8,12},{9,13},{12,14},{13,15},{14,10},{15,... | collective-permute-start | bytes 589832 | tf_op jit(solution)/shard_map/ppermute | solution.py:77
  37.5 3.8 %collective-permute-start.8 = (bf16[3,96,1024]{2,1,0:T(8,128)(2,1)S(1)}, bf16[3,96,1024]{2,1,0:T(8,128)(2,1)S(1)}, u32[]{:S(2)}, u32[]{:S(2)}) collective-permute-start(bf16[3,96,1024]{2,1,0:T(8,128)(2,1)S(1)} %pad_maximum_fusion), channel_id=1, source_target_pairs={{0,1},{1,0},{2,3},{3,2},{4,5},{5,4},{6,7},{7,6},{8,9},{9,8},{10,11... | collective-permute-start | bytes 1769480 | tf_op jit(solution)/shard_map/ppermute | solution.py:90
  51.8 16.5 %collective-permute-start.15 = (bf16[128,1024]{0,1:T(8,128)(2,1)S(1)}, bf16[128,1024]{0,1:T(8,128)(2,1)S(1)}, u32[]{:S(2)}, u32[]{:S(2)}) collective-permute-start(bf16[128,1024]{0,1:T(8,128)(2,1)S(1)} %get-tuple-element.34), channel_id=1, source_target_pairs={{0,1},{1,0},{2,3},{3,2},{4,5},{5,4},{6,7},{7,6},{8,9},{9,8},{10,11... | collective-permute-start | bytes 786440 | tf_op jit(solution)/shard_map/ppermute | solution.py:170
  59.9 7.3 %collective-permute-start.10 = (bf16[128,1024]{0,1:T(8,128)(2,1)}, bf16[128,1024]{0,1:T(8,128)(2,1)S(1)}, u32[]{:S(2)}, u32[]{:S(2)}) collective-permute-start(bf16[128,1024]{0,1:T(8,128)(2,1)} %get-tuple-element.20), channel_id=1, source_target_pairs={{0,1},{1,0},{2,3},{3,2},{4,5},{5,4},{6,7},{7,6},{8,9},{9,8},{10,11... | collective-permute-start | bytes 786440 | tf_op jit(solution)/shard_map/ppermute | solution.py:170
  63.7 5.6 %collective-permute-start.12 = (bf16[128,1024]{0,1:T(8,128)(2,1)S(1)}, bf16[128,1024]{0,1:T(8,128)(2,1)S(1)}, u32[]{:S(2)}, u32[]{:S(2)}) collective-permute-start(bf16[128,1024]{0,1:T(8,128)(2,1)S(1)} %get-tuple-element.18), channel_id=1, source_target_pairs={{0,1},{1,0},{2,3},{3,2},{4,5},{5,4},{6,7},{7,6},{8,9},{9,8},{10,11... | collective-permute-start | bytes 786440 | tf_op jit(solution)/shard_map/ppermute | solution.py:170
  64.2 3.6 %collective-permute-start.14 = (bf16[128,8,32]{0,2,1:T(8,128)(2,1)}, bf16[128,8,32]{0,2,1:T(8,128)(2,1)S(1)}, u32[]{:S(2)}, u32[]{:S(2)}) collective-permute-start(bf16[128,8,32]{0,2,1:T(8,128)(2,1)} %dynamic-slice_bitcast_fusion.3), channel_id=1, source_target_pairs={{0,1},{1,0},{2,3},{3,2},{4,5},{5,4},{6,7},{7,6},{8,9},{9,8},{10,11... | collective-permute-start | bytes 196616 | tf_op jit(solution)/shard_map/ppermute | solution.py:167
  64.3 1.3 %collective-permute-start.13 = (f32[1024]{0:T(1024)S(1)}, f32[1024]{0:T(1024)S(1)}, u32[]{:S(2)}, u32[]{:S(2)}) collective-permute-start(f32[1024]{0:T(1024)S(1)} %get-tuple-element.17), channel_id=1, source_target_pairs={{0,1},{1,0},{2,3},{3,2},{4,5},{5,4},{6,7},{7,6},{8,9},{9,8},{10,11... | collective-permute-start | bytes 12296 | tf_op jit(solution)/shard_map/ppermute | solution.py:170
  65.5 1.3 %collective-permute-start.9 = (bf16[128,8,64]{0,2,1:T(8,128)(2,1)S(1)}, bf16[128,8,64]{0,2,1:T(8,128)(2,1)S(1)}, u32[]{:S(2)}, u32[]{:S(2)}) collective-permute-start(bf16[128,8,64]{0,2,1:T(8,128)(2,1)S(1)} %dynamic-slice_bitcast_fusion.1), channel_id=1, source_target_pairs={{0,1},{1,0},{2,3},{3,2},{4,5},{5,4},{6,7},{7,6},{8,9},{9,8},{10,11... | collective-permute-start | bytes 393224 | tf_op jit(solution)/shard_map/ppermute | solution.py:167
  66.9 5.0 %collective-permute-start.16 = (bf16[128,8,32]{0,2,1:T(8,128)(2,1)S(1)}, bf16[128,8,32]{0,2,1:T(8,128)(2,1)S(1)}, u32[]{:S(2)}, u32[]{:S(2)}) collective-permute-start(bf16[128,8,32]{0,2,1:T(8,128)(2,1)S(1)} %dynamic-slice_bitcast_fusion.2), channel_id=1, source_target_pairs={{0,1},{1,0},{2,3},{3,2},{4,5},{5,4},{6,7},{7,6},{8,9},{9,8},{10,11... | collective-permute-start | bytes 196616 | tf_op jit(solution)/shard_map/ppermute | solution.py:167
  67.2 4.6 %collective-permute-start.17 = (bf16[128,1024]{0,1:T(8,128)(2,1)S(1)}, bf16[128,1024]{0,1:T(8,128)(2,1)S(1)}, u32[]{:S(2)}, u32[]{:S(2)}) collective-permute-start(bf16[128,1024]{0,1:T(8,128)(2,1)S(1)} %fusion.1), channel_id=1, source_target_pairs={{0,1},{1,0},{2,3},{3,2},{4,5},{5,4},{6,7},{7,6},{8,9},{9,8},{10,11... | collective-permute-start | bytes 786440 | tf_op jit(solution)/shard_map/ppermute | solution.py:170
  67.8 1.4 %collective-permute-start.11 = (bf16[128,8,64]{0,2,1:T(8,128)(2,1)S(1)}, bf16[128,8,64]{0,2,1:T(8,128)(2,1)S(1)}, u32[]{:S(2)}, u32[]{:S(2)}) collective-permute-start(bf16[128,8,64]{0,2,1:T(8,128)(2,1)S(1)} %dynamic-slice_bitcast_fusion), channel_id=1, source_target_pairs={{0,1},{1,0},{2,3},{3,2},{4,5},{5,4},{6,7},{7,6},{8,9},{9,8},{10,11... | collective-permute-start | bytes 393224 | tf_op jit(solution)/shard_map/ppermute | solution.py:167
  70.1 7.8 %collective-permute-start.25 = (f32[48,1024]{1,0:T(8,128)S(1)}, f32[48,1024]{1,0:T(8,128)S(1)}, u32[]{:S(2)}, u32[]{:S(2)}) collective-permute-start(f32[48,1024]{1,0:T(8,128)S(1)} %get-tuple-element.15), channel_id=1, source_target_pairs={{0,4},{1,5},{4,8},{5,9},{8,12},{9,13},{12,14},{13,15},{14,10},{15,... | collective-permute-start | bytes 589832 | tf_op jit(solution)/shard_map/ppermute | solution.py:109
  72.2 10.5 %collective-permute-start.18 = (f32[56,1024]{1,0:T(8,128)S(1)}, f32[56,1024]{1,0:T(8,128)S(1)}, u32[]{:S(2)}, u32[]{:S(2)}) collective-permute-start(f32[56,1024]{1,0:T(8,128)S(1)} %get-tuple-element.9), channel_id=1, source_target_pairs={{0,4},{1,5},{4,8},{5,9},{8,12},{9,13},{12,14},{13,15},{14,10},{15,... | collective-permute-start | bytes 688136 | tf_op jit(solution)/shard_map/ppermute | solution.py:109
  73.9 8.9 %collective-permute-start.21 = (f32[56,1024]{1,0:T(8,128)S(1)}, f32[56,1024]{1,0:T(8,128)S(1)}, u32[]{:S(2)}, u32[]{:S(2)}) collective-permute-start(f32[56,1024]{1,0:T(8,128)S(1)} %get-tuple-element.10), channel_id=1, source_target_pairs={{4,0},{5,1},{8,4},{9,5},{12,8},{13,9},{14,12},{15,13},{10,14},{11,... | collective-permute-start | bytes 688136 | tf_op jit(solution)/shard_map/ppermute | solution.py:115
  74.3 11.1 %collective-permute-start.29 = (f32[48,1024]{1,0:T(8,128)S(1)}, f32[48,1024]{1,0:T(8,128)S(1)}, u32[]{:S(2)}, u32[]{:S(2)}) collective-permute-start(f32[48,1024]{1,0:T(8,128)S(1)} %get-tuple-element.16), channel_id=1, source_target_pairs={{4,0},{5,1},{8,4},{9,5},{12,8},{13,9},{14,12},{15,13},{10,14},{11,... | collective-permute-start | bytes 589832 | tf_op jit(solution)/shard_map/ppermute | solution.py:115
  77.8 9.1 %collective-permute-start.26 = (f32[48,1024]{1,0:T(8,128)S(1)}, f32[48,1024]{1,0:T(8,128)S(1)}, u32[]{:S(2)}, u32[]{:S(2)}) collective-permute-start(f32[48,1024]{1,0:T(8,128)S(1)} %fusion.31), channel_id=1, source_target_pairs={{0,4},{1,5},{4,8},{5,9},{8,12},{9,13},{12,14},{13,15},{14,10},{15,... | collective-permute-start | bytes 589832 | tf_op jit(solution)/shard_map/ppermute | solution.py:109
  82.8 9.1 %collective-permute-start.19 = (f32[56,1024]{1,0:T(8,128)S(1)}, f32[56,1024]{1,0:T(8,128)S(1)}, u32[]{:S(2)}, u32[]{:S(2)}) collective-permute-start(f32[56,1024]{1,0:T(8,128)S(1)} %get-tuple-element.7), channel_id=1, source_target_pairs={{0,4},{1,5},{4,8},{5,9},{8,12},{9,13},{12,14},{13,15},{14,10},{15,... | collective-permute-start | bytes 688136 | tf_op jit(solution)/shard_map/ppermute | solution.py:109
  84.6 7.3 %collective-permute-start.22 = (f32[56,1024]{1,0:T(8,128)S(1)}, f32[56,1024]{1,0:T(8,128)S(1)}, u32[]{:S(2)}, u32[]{:S(2)}) collective-permute-start(f32[56,1024]{1,0:T(8,128)S(1)} %get-tuple-element.8), channel_id=1, source_target_pairs={{4,0},{5,1},{8,4},{9,5},{12,8},{13,9},{14,12},{15,13},{10,14},{11,... | collective-permute-start | bytes 688136 | tf_op jit(solution)/shard_map/ppermute | solution.py:115
  87.0 9.0 %collective-permute-start.27 = (f32[48,1024]{1,0:T(8,128)S(1)}, f32[48,1024]{1,0:T(8,128)S(1)}, u32[]{:S(2)}, u32[]{:S(2)}) collective-permute-start(f32[48,1024]{1,0:T(8,128)S(1)} %get-tuple-element.13), channel_id=1, source_target_pairs={{0,4},{1,5},{4,8},{5,9},{8,12},{9,13},{12,14},{13,15},{14,10},{15,... | collective-permute-start | bytes 589832 | tf_op jit(solution)/shard_map/ppermute | solution.py:109
  88.8 7.7 %collective-permute-start.30 = (f32[48,1024]{1,0:T(8,128)S(1)}, f32[48,1024]{1,0:T(8,128)S(1)}, u32[]{:S(2)}, u32[]{:S(2)}) collective-permute-start(f32[48,1024]{1,0:T(8,128)S(1)} %get-tuple-element.14), channel_id=1, source_target_pairs={{4,0},{5,1},{8,4},{9,5},{12,8},{13,9},{14,12},{15,13},{10,14},{11,... | collective-permute-start | bytes 589832 | tf_op jit(solution)/shard_map/ppermute | solution.py:115
  91.9 9.4 %collective-permute-start.23 = (f32[56,1024]{1,0:T(8,128)S(1)}, f32[56,1024]{1,0:T(8,128)S(1)}, u32[]{:S(2)}, u32[]{:S(2)}) collective-permute-start(f32[56,1024]{1,0:T(8,128)S(1)} %get-tuple-element.6), channel_id=1, source_target_pairs={{4,0},{5,1},{8,4},{9,5},{12,8},{13,9},{14,12},{15,13},{10,14},{11,... | collective-permute-start | bytes 688136 | tf_op jit(solution)/shard_map/ppermute | solution.py:115
  93.7 12.0 %collective-permute-start.20 = (f32[56,1024]{1,0:T(8,128)S(1)}, f32[56,1024]{1,0:T(8,128)S(1)}, u32[]{:S(2)}, u32[]{:S(2)}) collective-permute-start(f32[56,1024]{1,0:T(8,128)S(1)} %get-tuple-element.5), channel_id=1, source_target_pairs={{0,4},{1,5},{4,8},{5,9},{8,12},{9,13},{12,14},{13,15},{14,10},{15,... | collective-permute-start | bytes 688136 | tf_op jit(solution)/shard_map/ppermute | solution.py:109
  96.5 9.1 %collective-permute-start.31 = (f32[48,1024]{1,0:T(8,128)S(1)}, f32[48,1024]{1,0:T(8,128)S(1)}, u32[]{:S(2)}, u32[]{:S(2)}) collective-permute-start(f32[48,1024]{1,0:T(8,128)S(1)} %get-tuple-element.12), channel_id=1, source_target_pairs={{4,0},{5,1},{8,4},{9,5},{12,8},{13,9},{14,12},{15,13},{10,14},{11,... | collective-permute-start | bytes 589832 | tf_op jit(solution)/shard_map/ppermute | solution.py:115
  97.9 7.7 %collective-permute-start.28 = (f32[48,1024]{1,0:T(8,128)S(1)}, f32[48,1024]{1,0:T(8,128)S(1)}, u32[]{:S(2)}, u32[]{:S(2)}) collective-permute-start(f32[48,1024]{1,0:T(8,128)S(1)} %get-tuple-element.11), channel_id=1, source_target_pairs={{0,4},{1,5},{4,8},{5,9},{8,12},{9,13},{12,14},{13,15},{14,10},{15,... | collective-permute-start | bytes 589832 | tf_op jit(solution)/shard_map/ppermute | solution.py:109
  101.4 7.6 %collective-permute-start.24 = (f32[56,1024]{1,0:T(8,128)S(1)}, f32[56,1024]{1,0:T(8,128)S(1)}, u32[]{:S(2)}, u32[]{:S(2)}) collective-permute-start(f32[56,1024]{1,0:T(8,128)S(1)} %fusion.18), channel_id=1, source_target_pairs={{4,0},{5,1},{8,4},{9,5},{12,8},{13,9},{14,12},{15,13},{10,14},{11,... | collective-permute-start | bytes 688136 | tf_op jit(solution)/shard_map/ppermute | solution.py:115
  (19 other events, 96.2 us)

commit v10 on v8

--- a/solution.py
+++ b/solution.py
@@ -3,6 +3,8 @@
 import jax
 import jax.numpy as jnp
 from jax import lax
+from jax.experimental import pallas as pl
+from jax.experimental.pallas import tpu as pltpu
 from jax.sharding import PartitionSpec as P
 
 
@@ -45,6 +47,83 @@
     )
     e_aone = (e_sone * s_one * (1.0 - s_one) + e_hone * s_one).astype(jnp.bfloat16)
     return (e_slope, g_one, e_aone, e_cone, g_two, h_one, e_atwo, grad_three)
+
+
+def _nt(left, right):
+    return lax.dot_general(left, right, (((1,), (1,)), ((), ())), preferred_element_type=jnp.float32)
+
+
+def _sigmoid(a):
+    return 1.0 / (1.0 + jnp.exp(-a))
+
+
+def _softplus(a):
+    return jnp.maximum(a, 0.0) + jnp.log1p(jnp.exp(-jnp.abs(a)))
+
+
+def twin_body(x_ref, z_ref, y_ref, m_ref, w1_ref, w2_ref, wo_ref,
+              es_ref, g1_ref, ea1_ref, ec1_ref, g2_ref, h1_ref, ea2_ref, g3_ref):
+    w1 = w1_ref[...]
+    w2 = w2_ref[...]
+    wo = wo_ref[...]
+    mask = m_ref[...]
+    a1 = jnp.dot(x_ref[...], w1, preferred_element_type=jnp.float32)
+    s1 = _sigmoid(a1)
+    h1 = _softplus(a1).astype(jnp.bfloat16)
+    a2 = jnp.dot(h1, w2, preferred_element_type=jnp.float32)
+    s2 = _sigmoid(a2)
+    h2 = _softplus(a2)
+    value = jnp.sum(h2 * wo, axis=1, keepdims=True)
+    g2 = (s2 * wo).astype(jnp.bfloat16)
+    c1 = _nt(g2, w2)
+    g1 = (c1 * s1).astype(jnp.bfloat16)
+    slope = _nt(g1, w1)
+    ev = 2.0 * mask * (value - y_ref[...])
+    ed = (2.0 * mask * (slope - z_ref[...].astype(jnp.float32))).astype(jnp.bfloat16)
+    eg1 = jnp.dot(ed, w1, preferred_element_type=jnp.float32)
+    ec1 = (eg1 * s1).astype(jnp.bfloat16)
+    es1 = eg1 * c1
+    eg2 = jnp.dot(ec1, w2, preferred_element_type=jnp.float32)
+    g3_ref[...] = jnp.sum(eg2 * s2 + ev * h2, axis=0, keepdims=True)
+    ea2 = (eg2 * wo * s2 * (1.0 - s2) + ev * wo * s2).astype(jnp.bfloat16)
+    eh1 = _nt(ea2, w2)
+    ea1 = (es1 * s1 * (1.0 - s1) + eh1 * s1).astype(jnp.bfloat16)
+    es_ref[...] = ed
+    g1_ref[...] = g1
+    ea1_ref[...] = ea1
+    ec1_ref[...] = ec1
+    g2_ref[...] = g2
+    h1_ref[...] = h1
+    ea2_ref[...] = ea2
+
+
+def twin_fused(x_rows, z_rows, y_rows, mask, w_one, w_two, w_three):
+    rows, assets = x_rows.shape
+    hidden = w_one.shape[1]
+    bf, f32 = jnp.bfloat16, jnp.float32
+    shapes = (
+        jax.ShapeDtypeStruct((rows, assets), bf),
+        jax.ShapeDtypeStruct((rows, hidden), bf),
+        jax.ShapeDtypeStruct((rows, hidden), bf),
+        jax.ShapeDtypeStruct((rows, hidden), bf),
+        jax.ShapeDtypeStruct((rows, hidden), bf),
+        jax.ShapeDtypeStruct((rows, hidden), bf),
+        jax.ShapeDtypeStruct((rows, hidden), bf),
+        jax.ShapeDtypeStruct((1, hidden), f32),
+    )
+    vmem = pl.BlockSpec(memory_space=pltpu.VMEM)
+    flops = 2 * rows * hidden * (3 * assets + 4 * hidden)
+    e_slope, g_one, e_aone, e_cone, g_two, h_one, e_atwo, grad_three = pl.pallas_call(
+        twin_body,
+        out_shape=shapes,
+        in_specs=[vmem] * 7,
+        out_specs=[vmem] * 8,
+        cost_estimate=pl.CostEstimate(
+            flops=flops, transcendentals=6 * rows * hidden,
+            bytes_accessed=2 * (assets + 2 * hidden) * hidden + 16 * rows * hidden),
+    )(x_rows, z_rows, y_rows.astype(f32)[:, None], mask[:, None], w_one, w_two,
+      w_three.astype(f32)[None, :])
+    return (e_slope, g_one, e_aone, e_cone, g_two, h_one, e_atwo, grad_three[0])
 
 
 def normalized(grad):
@@ -146,7 +225,7 @@
     x_rows, z_rows, y_rows = (paths, deltas, payoffs)
     total = jnp.sum(sending)
     mask = (jnp.arange(rows_dev, dtype=jnp.int32) < total).astype(jnp.float32)
-    e_slope, g_one, e_aone, e_cone, g_two, h_one, e_atwo, grad_three = twin_terms(
+    e_slope, g_one, e_aone, e_cone, g_two, h_one, e_atwo, grad_three = twin_fused(
         x_rows, z_rows, y_rows, mask, w_one, w_two, w_out
     )
     chip = position // 2

time: 107 us -> 110 us (1.028)
  matrix products: 12.4 us -> 6.24 us
  Pallas kernels: 0 us -> 6.05 us
  local copies, waits for them, and re-layouts: 18.7 us -> 23.1 us
  waiting for transfers between devices: 39.4 us -> 38 us
    dot_general x7 -> x0, matrix products: 9.51 us -> none  [the longest x1 2.46 us: twin_terms(): a_two = jnp.dot(h_one, w_two, preferred_element_type=jnp.float32)]
    pallas_call x0 -> x1, Pallas kernels: none -> 6.05 us  [twin_fused(): pl.pallas_call(twin_body, out_shape=shapes, in_specs=[vmem] * 7, out_spec...]
    dot_general x8, matrix products: 2.93 us -> 6.24 us  [slots_product(): lax.dot_general(left, right, (((0,), (0,)), ((), ())), preferred_element_...]
    ppermute x7, waiting for transfers between devices: 7.73 us -> 4.52 us  [backward(): acc = lax.ppermute(acc, 'blk', ccw)]
    ppermute x7, waiting for transfers between devices: 14.9 us -> 18 us  [forward(): acc = lax.ppermute(acc, 'blk', cw) + part[(window - s) % chips]]
    pallas_call x0 -> x3, local copies, waits for them, and re-layouts: none -> 2.36 us  [twin_fused(): pl.pallas_call(twin_body, out_shape=shapes, in_specs=[vmem] * 7, out_spec...]
    mul x2 -> x0, other arithmetic: 1.89 us -> none  [the longest x1 1.21 us: twin_terms(): 2.0 * mask[:, None] * (slope - z_rows.astype(jnp.float32))]
    slice x1, local copies, waits for them, and re-layouts: 0.17 us -> 1.58 us  [per_device(): w_two = gathered[:, r_one:].reshape(n_blk * r_two, hidden)]
  transfers between devices with their start and end apart: 31 -> 31, of which waited for: 16 -> 15; matrix products, arithmetic and copies ran while one was open for 22% -> 19% of each run, Pallas kernels for 0% -> 0%
where the time goes in v10:
time: 110 us
  waiting for transfers between devices  38 us (35%)
  starting transfers between devices  25.2 us (23%)
  local copies, waits for them, and re-layouts  23.1 us (21%)
  other arithmetic  9.77 us (9%)
  matrix products  6.24 us (6%)
  Pallas kernels  6.05 us (6%)
  between operations  1.82 us (2%)
    ppermute x7, waiting for transfers between devices, forward(): acc = lax.ppermute(acc, 'blk', cw) + part[(window - s) % chips]  18 us
    ppermute x4, waiting for transfers between devices, ring_all_gather(): left = lax.ppermute(left, 'blk', cw)  8.85 us
    ppermute x7, starting transfers between devices, backward(): acc = lax.ppermute(acc, 'blk', ccw)  8.5 us
    unnamed x41, local copies, waits for them, and re-layouts  6.7 us
    dot_general x8, matrix products, slots_product(): lax.dot_general(left, right, (((0,), (0,)), ((), ())), preferred_element_...  6.24 us
    ppermute x7, starting transfers between devices, forward(): acc = lax.ppermute(acc, 'blk', cw) + part[(window - s) % chips]  6.09 us
    ppermute x3, starting transfers between devices, ring_all_gather(): right = lax.ppermute(right, 'blk', ccw)  6.07 us
    pallas_call x1, Pallas kernels, twin_fused(): pl.pallas_call(twin_body, out_shape=shapes, in_specs=[vmem] * 7, out_spec...  6.05 us
  transfers between devices with their start and end apart: 31, of which 15 were waited for; matrix products, arithmetic and copies ran while one was open for 19% of the time, Pallas kernels for 0%

profile of v10, /device:TPU:0, one launch (start us, length us, event | category | flops | bytes accessed | tf_op | source)
XLA Modules:
  0.0 110.1 jit_solution(2313594612489060757)
XLA Ops:
  2.4 3.0 %collective-permute-start = (bf16[96,1024]{1,0:T(8,128)(2,1)S(1)}, bf16[96,1024]{1,0:T(8,128)(2,1)S(1)}, u32[]{:S(2)}, u32[]{:S(2)}) collective-permute-start(bf16[96,1024]{1,0:T(8,128)(2,1)S(1)} %constant_dynamic-update-slice_fusion), channel_id=1, source_target_pairs={{4,0},{5,1},{8,4},{9,5},{12,8},{13,9},{14,12},{15,13},{10,14},{11,... | collective-permute-start | bytes 589832 | tf_op jit(solution)/shard_map/ppermute | solution.py:159
  5.6 1.2 %dynamic_slice.37 = s32[1]{0:T(128)} dynamic-slice(s32[8]{0:T(128)} %constant.170.clone, s32[]{:T(128)S(6)} %select_n.171), dynamic_slice_sizes={1} | dynamic-slice | bytes 12 | tf_op jit(solution)/shard_map/dynamic_slice | solution.py:151
  8.3 2.1 %collective-permute-done = bf16[96,1024]{1,0:T(8,128)(2,1)S(1)} collective-permute-done((bf16[96,1024]{1,0:T(8,128)(2,1)S(1)}, bf16[96,1024]{1,0:T(8,128)(2,1)S(1)}, u32[]{:S(2)}, u32[]{:S(2)}) %collective-permute-start) | collective-permute-done | bytes 196640 | tf_op jit(solution)/shard_map/ppermute | solution.py:159
  10.4 1.7 %collective-permute-start.1 = (bf16[96,1024]{1,0:T(8,128)(2,1)S(1)}, bf16[96,1024]{1,0:T(8,128)(2,1)S(1)}, u32[]{:S(2)}, u32[]{:S(2)}) collective-permute-start(bf16[96,1024]{1,0:T(8,128)(2,1)S(1)} %collective-permute-done), channel_id=1, source_target_pairs={{4,0},{5,1},{8,4},{9,5},{12,8},{13,9},{14,12},{15,13},{10,14},{11,... | collective-permute-start | bytes 589832 | tf_op jit(solution)/shard_map/ppermute | solution.py:159
  13.2 3.3 %collective-permute-done.1 = bf16[96,1024]{1,0:T(8,128)(2,1)S(1)} collective-permute-done((bf16[96,1024]{1,0:T(8,128)(2,1)S(1)}, bf16[96,1024]{1,0:T(8,128)(2,1)S(1)}, u32[]{:S(2)}, u32[]{:S(2)}) %collective-permute-start.1) | collective-permute-done | bytes 196640 | tf_op jit(solution)/shard_map/ppermute | solution.py:159
  16.5 1.4 %collective-permute-start.2 = (bf16[96,1024]{1,0:T(8,128)(2,1)S(1)}, bf16[96,1024]{1,0:T(8,128)(2,1)S(1)}, u32[]{:S(2)}, u32[]{:S(2)}) collective-permute-start(bf16[96,1024]{1,0:T(8,128)(2,1)S(1)} %collective-permute-done.1), channel_id=1, source_target_pairs={{4,0},{5,1},{8,4},{9,5},{12,8},{13,9},{14,12},{15,13},{10,14},{11,... | collective-permute-start | bytes 589832 | tf_op jit(solution)/shard_map/ppermute | solution.py:159
  19.3 4.6 %collective-permute-done.5 = bf16[96,1024]{1,0:T(8,128)(2,1)S(1)} collective-permute-done((bf16[96,1024]{1,0:T(8,128)(2,1)S(1)}, bf16[96,1024]{1,0:T(8,128)(2,1)S(1)}, u32[]{:S(2)}, u32[]{:S(2)}) %collective-permute-start.5) | collective-permute-done | bytes 196640 | tf_op jit(solution)/shard_map/ppermute | solution.py:156
  25.4 4.2 %collective-permute-done.6 = bf16[96,1024]{1,0:T(8,128)(2,1)S(1)} collective-permute-done((bf16[96,1024]{1,0:T(8,128)(2,1)S(1)}, bf16[96,1024]{1,0:T(8,128)(2,1)S(1)}, u32[]{:S(2)}, u32[]{:S(2)}) %collective-permute-start.6) | collective-permute-done | bytes 196640 | tf_op jit(solution)/shard_map/ppermute | solution.py:156
  38.1 1.3 %fusion.35.m_ref = f32[128,1]{1,0:T(8,128)} fusion(s32[]{:T(128)} %fusion.46), kind=kLoop, calls=%fused_computation.94 | loop fusion | flops 256 | bytes 516 | tf_op jit(solution)/shard_map/convert_element_type | solution.py:227
  40.1 1.3 %constant_dynamic-update-slice_fusion.2 = bf16[16,96,1024]{2,1,0:T(8,128)(2,1)} fusion(bf16[16,96,1024]{2,1,0:T(8,128)(2,1)} %get-tuple-element.34, bf16[8,96,1024]{2,1,0:T(8,128)(2,1)S(1)} %collective-permute-done.7), kind=kLoop, calls=%fused_computation.97 | loop fusion | bytes 3145728 | tf_op jit(solution)/shard_map/concatenate | solution.py:163
  41.4 2.6 %gather_fusion.1 = bf16[16,96,1024]{2,1,0:T(8,128)(2,1)S(1)} fusion(bf16[16,96,1024]{2,1,0:T(8,128)(2,1)} %constant_dynamic-update-slice_fusion.2, s32[1024]{0:T(1024)S(1)} %pad_clamp_fusion.1), kind=kCustom, calls=%fused_computation.5 | custom fusion | bytes 6291520 | tf_op jit(solution)/shard_map/jit(_take)/gather | solution.py:168
  44.4 1.6 %slice.117 = bf16[16,64,1024]{2,1,0:T(8,128)(2,1)} slice(bf16[16,96,1024]{2,1,0:T(8,128)(2,1)S(1)} %broadcast_select_fusion), slice={[0:16], [32:96], [0:1024]} | slice | bytes 4194304 | tf_op jit(solution)/shard_map/slice | solution.py:223
  47.1 6.0 %shard_map.157 = (bf16[128,512]{1,0:T(8,128)(2,1)}, bf16[128,1024]{1,0:T(8,128)(2,1)}, bf16[128,1024]{1,0:T(8,128)(2,1)}, bf16[128,1024]{1,0:T(8,128)(2,1)}, bf1...) custom-call(bf16[128,512]{1,0:T(8,128)(2,1)} %x_ref.1, ...), custom_call_target="tpu_custom_call" | custom-call | flops 1476395008 | bytes 7340032 | tf_op jit(solution)/shard_map/pallas_call | solution.py:116
  53.1 1.1 %copy.25 = bf16[128,1024]{0,1:T(8,128)(2,1)S(1)} copy(bf16[128,1024]{1,0:T(8,128)(2,1)} %get-tuple-element.13) | data formatting | bytes 524288 | tf_op jit(solution)/shard_map/pallas_call | solution.py:116
  54.9 1.1 %copy.26 = bf16[128,1024]{0,1:T(8,128)(2,1)S(1)} copy(bf16[128,1024]{1,0:T(8,128)(2,1)} %get-tuple-element.15) | data formatting | bytes 524288 | tf_op jit(solution)/shard_map/pallas_call | solution.py:116
  57.3 1.4 %fusion.10 = f32[8,64,1024]{2,1,0:T(8,128)S(1)} fusion(bf16[128,1024]{1,0:T(8,128)(2,1)} %get-tuple-element.14, bf16[128,8,2,64]{0,3,2,1:T(8,128)(2,1)S(1)} %get-tuple-element.49, s32[]{:T(128)S(6)} %select_n.181), kind=kOutput, calls=%fused_computation.23 | convolution fusion | flops 134217728 | bytes 2490372 | tf_op jit(solution)/shard_map/dot_general | solution.py:206
  58.8 2.8 %fusion.6 = f32[8,64,1024]{2,1,0:T(8,128)} fusion(bf16[128,1024]{1,0:T(8,128)(2,1)} %get-tuple-element.16, bf16[128,8,2,64]{0,3,2,1:T(8,128)(2,1)S(1)} %get-tuple-element.50, s32[]{:T(128)S(6)} %select_n.181), kind=kOutput, calls=%fused_computation.19 | convolution fusion | flops 134217728 | bytes 2490372 | tf_op jit(solution)/shard_map/dot_general | solution.py:206
  69.4 1.8 %collective-permute-start.17 = (f32[56,1024]{1,0:T(8,128)S(1)}, f32[56,1024]{1,0:T(8,128)S(1)}, u32[]{:S(2)}, u32[]{:S(2)}) collective-permute-start(f32[56,1024]{1,0:T(8,128)S(1)} %get-tuple-element.25), channel_id=1, source_target_pairs={{0,4},{1,5},{4,8},{5,9},{8,12},{9,13},{12,14},{13,15},{14,10},{15,... | collective-permute-start | bytes 688136 | tf_op jit(solution)/shard_map/ppermute | solution.py:181
  71.5 1.4 %collective-permute-start.28 = (f32[48,1024]{1,0:T(8,128)S(1)}, f32[48,1024]{1,0:T(8,128)S(1)}, u32[]{:S(2)}, u32[]{:S(2)}) collective-permute-start(f32[48,1024]{1,0:T(8,128)S(1)} %get-tuple-element.32), channel_id=1, source_target_pairs={{4,0},{5,1},{8,4},{9,5},{12,8},{13,9},{14,12},{15,13},{10,14},{11,... | collective-permute-start | bytes 589832 | tf_op jit(solution)/shard_map/ppermute | solution.py:187
  72.9 3.2 %collective-permute-done.24 = f32[48,1024]{1,0:T(8,128)S(1)} collective-permute-done((f32[48,1024]{1,0:T(8,128)S(1)}, f32[48,1024]{1,0:T(8,128)S(1)}, u32[]{:S(2)}, u32[]{:S(2)}) %collective-permute-start.24) | collective-permute-done | bytes 196640 | tf_op jit(solution)/shard_map/ppermute | solution.py:181
  76.8 4.2 %collective-permute-done.17 = f32[56,1024]{1,0:T(8,128)S(1)} collective-permute-done((f32[56,1024]{1,0:T(8,128)S(1)}, f32[56,1024]{1,0:T(8,128)S(1)}, u32[]{:S(2)}, u32[]{:S(2)}) %collective-permute-start.17) | collective-permute-done | bytes 229408 | tf_op jit(solution)/shard_map/ppermute | solution.py:181
  81.8 1.4 %collective-permute-start.21 = (f32[56,1024]{1,0:T(8,128)S(1)}, f32[56,1024]{1,0:T(8,128)S(1)}, u32[]{:S(2)}, u32[]{:S(2)}) collective-permute-start(f32[56,1024]{1,0:T(8,128)S(1)} %get-tuple-element.24), channel_id=1, source_target_pairs={{4,0},{5,1},{8,4},{9,5},{12,8},{13,9},{14,12},{15,13},{10,14},{11,... | collective-permute-start | bytes 688136 | tf_op jit(solution)/shard_map/ppermute | solution.py:187
  83.2 2.1 %collective-permute-done.25 = f32[48,1024]{1,0:T(8,128)S(1)} collective-permute-done((f32[48,1024]{1,0:T(8,128)S(1)}, f32[48,1024]{1,0:T(8,128)S(1)}, u32[]{:S(2)}, u32[]{:S(2)}) %collective-permute-start.25) | collective-permute-done | bytes 196640 | tf_op jit(solution)/shard_map/ppermute | solution.py:181
  86.0 1.4 %collective-permute-start.29 = (f32[48,1024]{1,0:T(8,128)S(1)}, f32[48,1024]{1,0:T(8,128)S(1)}, u32[]{:S(2)}, u32[]{:S(2)}) collective-permute-start(f32[48,1024]{1,0:T(8,128)S(1)} %get-tuple-element.30), channel_id=1, source_target_pairs={{4,0},{5,1},{8,4},{9,5},{12,8},{13,9},{14,12},{15,13},{10,14},{11,... | collective-permute-start | bytes 589832 | tf_op jit(solution)/shard_map/ppermute | solution.py:187
  87.4 2.8 %collective-permute-done.18 = f32[56,1024]{1,0:T(8,128)S(1)} collective-permute-done((f32[56,1024]{1,0:T(8,128)S(1)}, f32[56,1024]{1,0:T(8,128)S(1)}, u32[]{:S(2)}, u32[]{:S(2)}) %collective-permute-start.18) | collective-permute-done | bytes 229408 | tf_op jit(solution)/shard_map/ppermute | solution.py:181
  90.2 1.6 %collective-permute-start.22 = (f32[56,1024]{1,0:T(8,128)S(1)}, f32[56,1024]{1,0:T(8,128)S(1)}, u32[]{:S(2)}, u32[]{:S(2)}) collective-permute-start(f32[56,1024]{1,0:T(8,128)S(1)} %get-tuple-element.22), channel_id=1, source_target_pairs={{4,0},{5,1},{8,4},{9,5},{12,8},{13,9},{14,12},{15,13},{10,14},{11,... | collective-permute-start | bytes 688136 | tf_op jit(solution)/shard_map/ppermute | solution.py:187
  92.3 2.1 %collective-permute-done.26 = f32[48,1024]{1,0:T(8,128)S(1)} collective-permute-done((f32[48,1024]{1,0:T(8,128)S(1)}, f32[48,1024]{1,0:T(8,128)S(1)}, u32[]{:S(2)}, u32[]{:S(2)}) %collective-permute-start.26) | collective-permute-done | bytes 196640 | tf_op jit(solution)/shard_map/ppermute | solution.py:181
  94.4 1.1 collective-permute-start.27
  96.5 1.3 %collective-permute-done.22 = f32[56,1024]{1,0:T(8,128)S(1)} collective-permute-done((f32[56,1024]{1,0:T(8,128)S(1)}, f32[56,1024]{1,0:T(8,128)S(1)}, u32[]{:S(2)}, u32[]{:S(2)}) %collective-permute-start.22) | collective-permute-done | bytes 229408 | tf_op jit(solution)/shard_map/ppermute | solution.py:187
  97.8 1.4 %collective-permute-start.23 = (f32[56,1024]{1,0:T(8,128)S(1)}, f32[56,1024]{1,0:T(8,128)S(1)}, u32[]{:S(2)}, u32[]{:S(2)}) collective-permute-start(f32[56,1024]{1,0:T(8,128)S(1)} %fusion.13), channel_id=1, source_target_pairs={{4,0},{5,1},{8,4},{9,5},{12,8},{13,9},{14,12},{15,13},{10,14},{11,... | collective-permute-start | bytes 688136 | tf_op jit(solution)/shard_map/ppermute | solution.py:187
  99.2 3.7 %collective-permute-done.27 = f32[48,1024]{1,0:T(8,128)S(1)} collective-permute-done((f32[48,1024]{1,0:T(8,128)S(1)}, f32[48,1024]{1,0:T(8,128)S(1)}, u32[]{:S(2)}, u32[]{:S(2)}) %collective-permute-start.27) | collective-permute-done | bytes 196640 | tf_op jit(solution)/shard_map/ppermute | solution.py:181
  103.4 2.8 %collective-permute-done.23 = f32[56,1024]{1,0:T(8,128)S(1)} collective-permute-done((f32[56,1024]{1,0:T(8,128)S(1)}, f32[56,1024]{1,0:T(8,128)S(1)}, u32[]{:S(2)}, u32[]{:S(2)}) %collective-permute-start.23) | collective-permute-done | bytes 229408 | tf_op jit(solution)/shard_map/ppermute | solution.py:187
  (140 shorter events, 35.2 us)
Async XLA Ops:
  0.6 35.1 %copy-start = (s32[16,16]{1,0:T(8,128)S(1)}, s32[16,16]{1,0:T(8,128)}, u32[]{:S(2)}) copy-start(s32[16,16]{1,0:T(8,128)} %param.21) | copy-start | bytes 3076
  2.4 8.0 %collective-permute-start = (bf16[96,1024]{1,0:T(8,128)(2,1)S(1)}, bf16[96,1024]{1,0:T(8,128)(2,1)S(1)}, u32[]{:S(2)}, u32[]{:S(2)}) collective-permute-start(bf16[96,1024]{1,0:T(8,128)(2,1)S(1)} %constant_dynamic-update-slice_fusion), channel_id=1, source_target_pairs={{4,0},{5,1},{8,4},{9,5},{12,8},{13,9},{14,12},{15,13},{10,14},{11,... | collective-permute-start | bytes 589832 | tf_op jit(solution)/shard_map/ppermute | solution.py:159
  5.4 6.6 %collective-permute-start.3 = (bf16[96,1024]{1,0:T(8,128)(2,1)S(1)}, bf16[96,1024]{1,0:T(8,128)(2,1)S(1)}, u32[]{:S(2)}, u32[]{:S(2)}) collective-permute-start(bf16[96,1024]{1,0:T(8,128)(2,1)S(1)} %constant_dynamic-update-slice_fusion), channel_id=1, source_target_pairs={{0,4},{1,5},{4,8},{5,9},{8,12},{9,13},{12,14},{13,15},{14,10},{15,... | collective-permute-start | bytes 589832 | tf_op jit(solution)/shard_map/ppermute | solution.py:156
  10.4 6.1 %collective-permute-start.1 = (bf16[96,1024]{1,0:T(8,128)(2,1)S(1)}, bf16[96,1024]{1,0:T(8,128)(2,1)S(1)}, u32[]{:S(2)}, u32[]{:S(2)}) collective-permute-start(bf16[96,1024]{1,0:T(8,128)(2,1)S(1)} %collective-permute-done), channel_id=1, source_target_pairs={{4,0},{5,1},{8,4},{9,5},{12,8},{13,9},{14,12},{15,13},{10,14},{11,... | collective-permute-start | bytes 589832 | tf_op jit(solution)/shard_map/ppermute | solution.py:159
  12.1 5.8 %collective-permute-start.4 = (bf16[96,1024]{1,0:T(8,128)(2,1)S(1)}, bf16[96,1024]{1,0:T(8,128)(2,1)S(1)}, u32[]{:S(2)}, u32[]{:S(2)}) collective-permute-start(bf16[96,1024]{1,0:T(8,128)(2,1)S(1)} %collective-permute-done.3), channel_id=1, source_target_pairs={{0,4},{1,5},{4,8},{5,9},{8,12},{9,13},{12,14},{13,15},{14,10},{15,... | collective-permute-start | bytes 589832 | tf_op jit(solution)/shard_map/ppermute | solution.py:156
  16.5 8.1 %collective-permute-start.2 = (bf16[96,1024]{1,0:T(8,128)(2,1)S(1)}, bf16[96,1024]{1,0:T(8,128)(2,1)S(1)}, u32[]{:S(2)}, u32[]{:S(2)}) collective-permute-start(bf16[96,1024]{1,0:T(8,128)(2,1)S(1)} %collective-permute-done.1), channel_id=1, source_target_pairs={{4,0},{5,1},{8,4},{9,5},{12,8},{13,9},{14,12},{15,13},{10,14},{11,... | collective-permute-start | bytes 589832 | tf_op jit(solution)/shard_map/ppermute | solution.py:159
  17.8 6.1 %collective-permute-start.5 = (bf16[96,1024]{1,0:T(8,128)(2,1)S(1)}, bf16[96,1024]{1,0:T(8,128)(2,1)S(1)}, u32[]{:S(2)}, u32[]{:S(2)}) collective-permute-start(bf16[96,1024]{1,0:T(8,128)(2,1)S(1)} %collective-permute-done.4), channel_id=1, source_target_pairs={{0,4},{1,5},{4,8},{5,9},{8,12},{9,13},{12,14},{13,15},{14,10},{15,... | collective-permute-start | bytes 589832 | tf_op jit(solution)/shard_map/ppermute | solution.py:156
  24.0 5.7 %collective-permute-start.6 = (bf16[96,1024]{1,0:T(8,128)(2,1)S(1)}, bf16[96,1024]{1,0:T(8,128)(2,1)S(1)}, u32[]{:S(2)}, u32[]{:S(2)}) collective-permute-start(bf16[96,1024]{1,0:T(8,128)(2,1)S(1)} %collective-permute-done.5), channel_id=1, source_target_pairs={{0,4},{1,5},{4,8},{5,9},{8,12},{9,13},{12,14},{13,15},{14,10},{15,... | collective-permute-start | bytes 589832 | tf_op jit(solution)/shard_map/ppermute | solution.py:156
  32.8 7.3 %collective-permute-start.7 = (bf16[8,96,1024]{2,1,0:T(8,128)(2,1)}, bf16[8,96,1024]{2,1,0:T(8,128)(2,1)S(1)}, u32[]{:S(2)}, u32[]{:S(2)}) collective-permute-start(bf16[8,96,1024]{2,1,0:T(8,128)(2,1)} %get-tuple-element.33), channel_id=1, source_target_pairs={{0,1},{1,0},{2,3},{3,2},{4,5},{5,4},{6,7},{7,6},{8,9},{9,8},{10,11... | collective-permute-start | bytes 4718600 | tf_op jit(solution)/shard_map/ppermute | solution.py:162
  56.6 9.3 %collective-permute-start.9 = (bf16[128,1024]{1,0:T(8,128)(2,1)}, bf16[128,1024]{1,0:T(8,128)(2,1)S(1)}, u32[]{:S(2)}, u32[]{:S(2)}) collective-permute-start(bf16[128,1024]{1,0:T(8,128)(2,1)} %get-tuple-element.14), channel_id=1, source_target_pairs={{0,1},{1,0},{2,3},{3,2},{4,5},{5,4},{6,7},{7,6},{8,9},{9,8},{10,11... | collective-permute-start | bytes 786440 | tf_op jit(solution)/shard_map/ppermute | solution.py:242
  61.5 5.9 %collective-permute-start.11 = (bf16[128,1024]{1,0:T(8,128)(2,1)}, bf16[128,1024]{1,0:T(8,128)(2,1)S(1)}, u32[]{:S(2)}, u32[]{:S(2)}) collective-permute-start(bf16[128,1024]{1,0:T(8,128)(2,1)} %get-tuple-element.16), channel_id=1, source_target_pairs={{0,1},{1,0},{2,3},{3,2},{4,5},{5,4},{6,7},{7,6},{8,9},{9,8},{10,11... | collective-permute-start | bytes 786440 | tf_op jit(solution)/shard_map/ppermute | solution.py:242
  63.3 3.8 %collective-permute-start.14 = (bf16[128,1024]{1,0:T(8,128)(2,1)S(1)}, bf16[128,1024]{1,0:T(8,128)(2,1)S(1)}, u32[]{:S(2)}, u32[]{:S(2)}) collective-permute-start(bf16[128,1024]{1,0:T(8,128)(2,1)S(1)} %copy-done.5), channel_id=1, source_target_pairs={{0,1},{1,0},{2,3},{3,2},{4,5},{5,4},{6,7},{7,6},{8,9},{9,8},{10,11... | collective-permute-start | bytes 786440 | tf_op jit(solution)/shard_map/ppermute | solution.py:242
  63.9 1.8 %collective-permute-start.8 = (bf16[128,8,64]{0,2,1:T(8,128)(2,1)S(1)}, bf16[128,8,64]{0,2,1:T(8,128)(2,1)S(1)}, u32[]{:S(2)}, u32[]{:S(2)}) collective-permute-start(bf16[128,8,64]{0,2,1:T(8,128)(2,1)S(1)} %dynamic-slice_bitcast_fusion.1), channel_id=1, source_target_pairs={{0,1},{1,0},{2,3},{3,2},{4,5},{5,4},{6,7},{7,6},{8,9},{9,8},{10,11... | collective-permute-start | bytes 393224 | tf_op jit(solution)/shard_map/ppermute | solution.py:239
  63.9 1.3 %collective-permute-start.12 = (f32[1024]{0:T(1024)S(1)}, f32[1024]{0:T(1024)S(1)}, u32[]{:S(2)}, u32[]{:S(2)}) collective-permute-start(f32[1024]{0:T(1024)S(1)} %bitcast.166), channel_id=1, source_target_pairs={{0,1},{1,0},{2,3},{3,2},{4,5},{5,4},{6,7},{7,6},{8,9},{9,8},{10,11... | collective-permute-start | bytes 12296 | tf_op jit(solution)/shard_map/ppermute | solution.py:242
  65.2 2.2 %collective-permute-start.10 = (bf16[128,8,64]{0,2,1:T(8,128)(2,1)S(1)}, bf16[128,8,64]{0,2,1:T(8,128)(2,1)S(1)}, u32[]{:S(2)}, u32[]{:S(2)}) collective-permute-start(bf16[128,8,64]{0,2,1:T(8,128)(2,1)S(1)} %dynamic-slice_bitcast_fusion), channel_id=1, source_target_pairs={{0,1},{1,0},{2,3},{3,2},{4,5},{5,4},{6,7},{7,6},{8,9},{9,8},{10,11... | collective-permute-start | bytes 393224 | tf_op jit(solution)/shard_map/ppermute | solution.py:239
  65.7 1.3 %collective-permute-start.13 = (bf16[128,8,32]{0,2,1:T(8,128)(2,1)S(1)}, bf16[128,8,32]{0,2,1:T(8,128)(2,1)S(1)}, u32[]{:S(2)}, u32[]{:S(2)}) collective-permute-start(bf16[128,8,32]{0,2,1:T(8,128)(2,1)S(1)} %dynamic-slice_bitcast_fusion.3), channel_id=1, source_target_pairs={{0,1},{1,0},{2,3},{3,2},{4,5},{5,4},{6,7},{7,6},{8,9},{9,8},{10,11... | collective-permute-start | bytes 196616 | tf_op jit(solution)/shard_map/ppermute | solution.py:239
  65.9 3.2 %collective-permute-start.15 = (bf16[128,8,32]{0,2,1:T(8,128)(2,1)S(1)}, bf16[128,8,32]{0,2,1:T(8,128)(2,1)S(1)}, u32[]{:S(2)}, u32[]{:S(2)}) collective-permute-start(bf16[128,8,32]{0,2,1:T(8,128)(2,1)S(1)} %dynamic-slice_bitcast_fusion.2), channel_id=1, source_target_pairs={{0,1},{1,0},{2,3},{3,2},{4,5},{5,4},{6,7},{7,6},{8,9},{9,8},{10,11... | collective-permute-start | bytes 196616 | tf_op jit(solution)/shard_map/ppermute | solution.py:239
  67.0 2.0 %collective-permute-start.16 = (bf16[128,1024]{1,0:T(8,128)(2,1)S(1)}, bf16[128,1024]{1,0:T(8,128)(2,1)S(1)}, u32[]{:S(2)}, u32[]{:S(2)}) collective-permute-start(bf16[128,1024]{1,0:T(8,128)(2,1)S(1)} %copy-done.6), channel_id=1, source_target_pairs={{0,1},{1,0},{2,3},{3,2},{4,5},{5,4},{6,7},{7,6},{8,9},{9,8},{10,11... | collective-permute-start | bytes 786440 | tf_op jit(solution)/shard_map/ppermute | solution.py:242
  68.3 7.8 %collective-permute-start.24 = (f32[48,1024]{1,0:T(8,128)S(1)}, f32[48,1024]{1,0:T(8,128)S(1)}, u32[]{:S(2)}, u32[]{:S(2)}) collective-permute-start(f32[48,1024]{1,0:T(8,128)S(1)} %get-tuple-element.31), channel_id=1, source_target_pairs={{0,4},{1,5},{4,8},{5,9},{8,12},{9,13},{12,14},{13,15},{14,10},{15,... | collective-permute-start | bytes 589832 | tf_op jit(solution)/shard_map/ppermute | solution.py:181
  69.4 11.6 %collective-permute-start.17 = (f32[56,1024]{1,0:T(8,128)S(1)}, f32[56,1024]{1,0:T(8,128)S(1)}, u32[]{:S(2)}, u32[]{:S(2)}) collective-permute-start(f32[56,1024]{1,0:T(8,128)S(1)} %get-tuple-element.25), channel_id=1, source_target_pairs={{0,4},{1,5},{4,8},{5,9},{8,12},{9,13},{12,14},{13,15},{14,10},{15,... | collective-permute-start | bytes 688136 | tf_op jit(solution)/shard_map/ppermute | solution.py:181
  71.2 9.8 %collective-permute-start.20 = (f32[56,1024]{1,0:T(8,128)S(1)}, f32[56,1024]{1,0:T(8,128)S(1)}, u32[]{:S(2)}, u32[]{:S(2)}) collective-permute-start(f32[56,1024]{1,0:T(8,128)S(1)} %get-tuple-element.26), channel_id=1, source_target_pairs={{4,0},{5,1},{8,4},{9,5},{12,8},{13,9},{14,12},{15,13},{10,14},{11,... | collective-permute-start | bytes 688136 | tf_op jit(solution)/shard_map/ppermute | solution.py:187
  71.5 11.7 %collective-permute-start.28 = (f32[48,1024]{1,0:T(8,128)S(1)}, f32[48,1024]{1,0:T(8,128)S(1)}, u32[]{:S(2)}, u32[]{:S(2)}) collective-permute-start(f32[48,1024]{1,0:T(8,128)S(1)} %get-tuple-element.32), channel_id=1, source_target_pairs={{4,0},{5,1},{8,4},{9,5},{12,8},{13,9},{14,12},{15,13},{10,14},{11,... | collective-permute-start | bytes 589832 | tf_op jit(solution)/shard_map/ppermute | solution.py:187
  76.1 9.1 %collective-permute-start.25 = (f32[48,1024]{1,0:T(8,128)S(1)}, f32[48,1024]{1,0:T(8,128)S(1)}, u32[]{:S(2)}, u32[]{:S(2)}) collective-permute-start(f32[48,1024]{1,0:T(8,128)S(1)} %fusion.26), channel_id=1, source_target_pairs={{0,4},{1,5},{4,8},{5,9},{8,12},{9,13},{12,14},{13,15},{14,10},{15,... | collective-permute-start | bytes 589832 | tf_op jit(solution)/shard_map/ppermute | solution.py:181
  81.1 9.1 %collective-permute-start.18 = (f32[56,1024]{1,0:T(8,128)S(1)}, f32[56,1024]{1,0:T(8,128)S(1)}, u32[]{:S(2)}, u32[]{:S(2)}) collective-permute-start(f32[56,1024]{1,0:T(8,128)S(1)} %get-tuple-element.23), channel_id=1, source_target_pairs={{0,4},{1,5},{4,8},{5,9},{8,12},{9,13},{12,14},{13,15},{14,10},{15,... | collective-permute-start | bytes 688136 | tf_op jit(solution)/shard_map/ppermute | solution.py:181
  81.8 8.4 %collective-permute-start.21 = (f32[56,1024]{1,0:T(8,128)S(1)}, f32[56,1024]{1,0:T(8,128)S(1)}, u32[]{:S(2)}, u32[]{:S(2)}) collective-permute-start(f32[56,1024]{1,0:T(8,128)S(1)} %get-tuple-element.24), channel_id=1, source_target_pairs={{4,0},{5,1},{8,4},{9,5},{12,8},{13,9},{14,12},{15,13},{10,14},{11,... | collective-permute-start | bytes 688136 | tf_op jit(solution)/shard_map/ppermute | solution.py:187
  85.3 9.1 %collective-permute-start.26 = (f32[48,1024]{1,0:T(8,128)S(1)}, f32[48,1024]{1,0:T(8,128)S(1)}, u32[]{:S(2)}, u32[]{:S(2)}) collective-permute-start(f32[48,1024]{1,0:T(8,128)S(1)} %get-tuple-element.29), channel_id=1, source_target_pairs={{0,4},{1,5},{4,8},{5,9},{8,12},{9,13},{12,14},{13,15},{14,10},{15,... | collective-permute-start | bytes 589832 | tf_op jit(solution)/shard_map/ppermute | solution.py:181
  86.0 8.4 %collective-permute-start.29 = (f32[48,1024]{1,0:T(8,128)S(1)}, f32[48,1024]{1,0:T(8,128)S(1)}, u32[]{:S(2)}, u32[]{:S(2)}) collective-permute-start(f32[48,1024]{1,0:T(8,128)S(1)} %get-tuple-element.30), channel_id=1, source_target_pairs={{4,0},{5,1},{8,4},{9,5},{12,8},{13,9},{14,12},{15,13},{10,14},{11,... | collective-permute-start | bytes 589832 | tf_op jit(solution)/shard_map/ppermute | solution.py:187
  90.2 7.5 %collective-permute-start.22 = (f32[56,1024]{1,0:T(8,128)S(1)}, f32[56,1024]{1,0:T(8,128)S(1)}, u32[]{:S(2)}, u32[]{:S(2)}) collective-permute-start(f32[56,1024]{1,0:T(8,128)S(1)} %get-tuple-element.22), channel_id=1, source_target_pairs={{4,0},{5,1},{8,4},{9,5},{12,8},{13,9},{14,12},{15,13},{10,14},{11,... | collective-permute-start | bytes 688136 | tf_op jit(solution)/shard_map/ppermute | solution.py:187
  91.9 11.6 %collective-permute-start.19 = (f32[56,1024]{1,0:T(8,128)S(1)}, f32[56,1024]{1,0:T(8,128)S(1)}, u32[]{:S(2)}, u32[]{:S(2)}) collective-permute-start(f32[56,1024]{1,0:T(8,128)S(1)} %get-tuple-element.21), channel_id=1, source_target_pairs={{0,4},{1,5},{4,8},{5,9},{8,12},{9,13},{12,14},{13,15},{14,10},{15,... | collective-permute-start | bytes 688136 | tf_op jit(solution)/shard_map/ppermute | solution.py:181
  94.4 8.5 %collective-permute-start.27 = (f32[48,1024]{1,0:T(8,128)S(1)}, f32[48,1024]{1,0:T(8,128)S(1)}, u32[]{:S(2)}, u32[]{:S(2)}) collective-permute-start(f32[48,1024]{1,0:T(8,128)S(1)} %get-tuple-element.27), channel_id=1, source_target_pairs={{0,4},{1,5},{4,8},{5,9},{8,12},{9,13},{12,14},{13,15},{14,10},{15,... | collective-permute-start | bytes 589832 | tf_op jit(solution)/shard_map/ppermute | solution.py:181
  95.5 7.8 %collective-permute-start.30 = (f32[48,1024]{1,0:T(8,128)S(1)}, f32[48,1024]{1,0:T(8,128)S(1)}, u32[]{:S(2)}, u32[]{:S(2)}) collective-permute-start(f32[48,1024]{1,0:T(8,128)S(1)} %get-tuple-element.28), channel_id=1, source_target_pairs={{4,0},{5,1},{8,4},{9,5},{12,8},{13,9},{14,12},{15,13},{10,14},{11,... | collective-permute-start | bytes 589832 | tf_op jit(solution)/shard_map/ppermute | solution.py:187
  97.8 8.5 %collective-permute-start.23 = (f32[56,1024]{1,0:T(8,128)S(1)}, f32[56,1024]{1,0:T(8,128)S(1)}, u32[]{:S(2)}, u32[]{:S(2)}) collective-permute-start(f32[56,1024]{1,0:T(8,128)S(1)} %fusion.13), channel_id=1, source_target_pairs={{4,0},{5,1},{8,4},{9,5},{12,8},{13,9},{14,12},{15,13},{10,14},{11,... | collective-permute-start | bytes 688136 | tf_op jit(solution)/shard_map/ppermute | solution.py:187
  (15 other events, 144.4 us)

commit v11 on v10

--- a/solution.py
+++ b/solution.py
@@ -61,10 +61,11 @@
     return jnp.maximum(a, 0.0) + jnp.log1p(jnp.exp(-jnp.abs(a)))
 
 
-def twin_body(x_ref, z_ref, y_ref, m_ref, w1_ref, w2_ref, wo_ref,
+def twin_body(r_one, x_ref, z_ref, y_ref, m_ref, w_ref, wo_ref,
               es_ref, g1_ref, ea1_ref, ec1_ref, g2_ref, h1_ref, ea2_ref, g3_ref):
-    w1 = w1_ref[...]
-    w2 = w2_ref[...]
+    blocks, width, hidden = w_ref.shape
+    w1 = w_ref[:, :r_one, :].reshape(blocks * r_one, hidden)
+    w2 = w_ref[:, r_one:, :].reshape(blocks * (width - r_one), hidden)
     wo = wo_ref[...]
     mask = m_ref[...]
     a1 = jnp.dot(x_ref[...], w1, preferred_element_type=jnp.float32)
@@ -97,9 +98,9 @@
     ea2_ref[...] = ea2
 
 
-def twin_fused(x_rows, z_rows, y_rows, mask, w_one, w_two, w_three):
+def twin_fused(x_rows, z_rows, y_rows, mask, w_blocks, r_one, w_three):
     rows, assets = x_rows.shape
-    hidden = w_one.shape[1]
+    blocks, width, hidden = w_blocks.shape
     bf, f32 = jnp.bfloat16, jnp.float32
     shapes = (
         jax.ShapeDtypeStruct((rows, assets), bf),
@@ -114,14 +115,14 @@
     vmem = pl.BlockSpec(memory_space=pltpu.VMEM)
     flops = 2 * rows * hidden * (3 * assets + 4 * hidden)
     e_slope, g_one, e_aone, e_cone, g_two, h_one, e_atwo, grad_three = pl.pallas_call(
-        twin_body,
+        functools.partial(twin_body, r_one),
         out_shape=shapes,
-        in_specs=[vmem] * 7,
+        in_specs=[vmem] * 6,
         out_specs=[vmem] * 8,
         cost_estimate=pl.CostEstimate(
             flops=flops, transcendentals=6 * rows * hidden,
-            bytes_accessed=2 * (assets + 2 * hidden) * hidden + 16 * rows * hidden),
-    )(x_rows, z_rows, y_rows.astype(f32)[:, None], mask[:, None], w_one, w_two,
+            bytes_accessed=2 * blocks * width * hidden + 16 * rows * hidden),
+    )(x_rows, z_rows, y_rows.astype(f32)[:, None], mask[:, None], w_blocks,
       w_three.astype(f32)[None, :])
     return (e_slope, g_one, e_aone, e_cone, g_two, h_one, e_atwo, grad_three[0])
 
@@ -219,14 +220,19 @@
     r_one, r_two = w_first.shape[0], w_second.shape[0]
     hidden = w_first.shape[1]
     gathered = ring_all_gather(jnp.concatenate([w_first, w_second], axis=0), n_blk)
-    w_one = gathered[:, :r_one].reshape(n_blk * r_one, hidden)
-    w_two = gathered[:, r_one:].reshape(n_blk * r_two, hidden)
+    if r_one % 16 or r_two % 16:
+        gathered = jnp.concatenate(
+            [gathered[:, :r_one].reshape(1, n_blk * r_one, hidden),
+             gathered[:, r_one:].reshape(1, n_blk * r_two, hidden)], axis=1)
+        split_at = n_blk * r_one
+    else:
+        split_at = r_one
     sending = lax.dynamic_index_in_dim(counts, position, 0, keepdims=False)
     x_rows, z_rows, y_rows = (paths, deltas, payoffs)
     total = jnp.sum(sending)
     mask = (jnp.arange(rows_dev, dtype=jnp.int32) < total).astype(jnp.float32)
     e_slope, g_one, e_aone, e_cone, g_two, h_one, e_atwo, grad_three = twin_fused(
-        x_rows, z_rows, y_rows, mask, w_one, w_two, w_out
+        x_rows, z_rows, y_rows, mask, gathered, split_at, w_out
     )
     chip = position // 2
     spot = jnp.asarray(place, jnp.int32)[chip]

time: 110 us -> 111 us (level)
  other arithmetic: 9.77 us -> 12.1 us
  local copies, waits for them, and re-layouts: 23.1 us -> 21.6 us
    slice x2 -> x0, local copies, waits for them, and re-layouts: 2.64 us -> none  [the longest x1 1.58 us: per_device(): w_two = gathered[:, r_one:].reshape(n_blk * r_two, hidden)]
    select_n x2, other arithmetic: 1.02 us -> 2.66 us  [ring_all_gather(): return jnp.take(both, index, axis=0)]
    squeeze x4, local copies, waits for them, and re-layouts: 0.05 us -> 1.36 us  [split_cols(): give = lax.dynamic_index_in_dim(f, 1 - core, 2, keepdims=False)]
    unnamed x41 -> x39, local copies, waits for them, and re-layouts: 6.7 us -> 6.62 us
  transfers between devices with their start and end apart: 31 -> 31, of which waited for: 15 -> 15; matrix products, arithmetic and copies ran while one was open for 19% -> 20% of each run, Pallas kernels for 0% -> 0%
where the time goes in v11:
time: 111 us
  waiting for transfers between devices  38 us (34%)
  starting transfers between devices  25.2 us (23%)
  local copies, waits for them, and re-layouts  21.6 us (19%)
  other arithmetic  12.1 us (11%)
  matrix products  6.26 us (6%)
  Pallas kernels  6.11 us (6%)
  between operations  1.77 us (2%)
    ppermute x7, waiting for transfers between devices, forward(): acc = lax.ppermute(acc, 'blk', cw) + part[(window - s) % chips]  18 us
    ppermute x4, waiting for transfers between devices, ring_all_gather(): left = lax.ppermute(left, 'blk', cw)  8.88 us
    ppermute x7, starting transfers between devices, backward(): acc = lax.ppermute(acc, 'blk', ccw)  8.48 us
    unnamed x39, local copies, waits for them, and re-layouts  6.62 us
    dot_general x8, matrix products, slots_product(): lax.dot_general(left, right, (((0,), (0,)), ((), ())), preferred_element_...  6.26 us
    ppermute x7, starting transfers between devices, forward(): acc = lax.ppermute(acc, 'blk', cw) + part[(window - s) % chips]  6.11 us
    pallas_call x1, Pallas kernels, twin_fused(): pl.pallas_call(functools.partial(twin_body, r_one), out_shape=shapes, in_...  6.11 us
    ppermute x3, starting transfers between devices, ring_all_gather(): right = lax.ppermute(right, 'blk', ccw)  6.07 us
  transfers between devices with their start and end apart: 31, of which 15 were waited for; matrix products, arithmetic and copies ran while one was open for 20% of the time, Pallas kernels for 0%

profile of v11, /device:TPU:0, one launch (start us, length us, event | category | flops | bytes accessed | tf_op | source)
XLA Modules:
  0.0 111.1 jit_solution(3876436747934638588)
XLA Ops:
  2.4 3.0 %collective-permute-start = (bf16[96,1024]{1,0:T(8,128)(2,1)S(1)}, bf16[96,1024]{1,0:T(8,128)(2,1)S(1)}, u32[]{:S(2)}, u32[]{:S(2)}) collective-permute-start(bf16[96,1024]{1,0:T(8,128)(2,1)S(1)} %constant_dynamic-update-slice_fusion), channel_id=1, source_target_pairs={{4,0},{5,1},{8,4},{9,5},{12,8},{13,9},{14,12},{15,13},{10,14},{11,... | collective-permute-start | bytes 589832 | tf_op jit(solution)/shard_map/ppermute | solution.py:160
  5.6 1.2 %dynamic_slice.37 = s32[1]{0:T(128)} dynamic-slice(s32[8]{0:T(128)} %constant.170.clone, s32[]{:T(128)S(6)} %select_n.171), dynamic_slice_sizes={1} | dynamic-slice | bytes 12 | tf_op jit(solution)/shard_map/dynamic_slice | solution.py:152
  8.3 2.1 %collective-permute-done = bf16[96,1024]{1,0:T(8,128)(2,1)S(1)} collective-permute-done((bf16[96,1024]{1,0:T(8,128)(2,1)S(1)}, bf16[96,1024]{1,0:T(8,128)(2,1)S(1)}, u32[]{:S(2)}, u32[]{:S(2)}) %collective-permute-start) | collective-permute-done | bytes 196640 | tf_op jit(solution)/shard_map/ppermute | solution.py:160
  10.4 1.7 %collective-permute-start.1 = (bf16[96,1024]{1,0:T(8,128)(2,1)S(1)}, bf16[96,1024]{1,0:T(8,128)(2,1)S(1)}, u32[]{:S(2)}, u32[]{:S(2)}) collective-permute-start(bf16[96,1024]{1,0:T(8,128)(2,1)S(1)} %collective-permute-done), channel_id=1, source_target_pairs={{4,0},{5,1},{8,4},{9,5},{12,8},{13,9},{14,12},{15,13},{10,14},{11,... | collective-permute-start | bytes 589832 | tf_op jit(solution)/shard_map/ppermute | solution.py:160
  13.2 3.3 %collective-permute-done.1 = bf16[96,1024]{1,0:T(8,128)(2,1)S(1)} collective-permute-done((bf16[96,1024]{1,0:T(8,128)(2,1)S(1)}, bf16[96,1024]{1,0:T(8,128)(2,1)S(1)}, u32[]{:S(2)}, u32[]{:S(2)}) %collective-permute-start.1) | collective-permute-done | bytes 196640 | tf_op jit(solution)/shard_map/ppermute | solution.py:160
  16.5 1.4 %collective-permute-start.2 = (bf16[96,1024]{1,0:T(8,128)(2,1)S(1)}, bf16[96,1024]{1,0:T(8,128)(2,1)S(1)}, u32[]{:S(2)}, u32[]{:S(2)}) collective-permute-start(bf16[96,1024]{1,0:T(8,128)(2,1)S(1)} %collective-permute-done.1), channel_id=1, source_target_pairs={{4,0},{5,1},{8,4},{9,5},{12,8},{13,9},{14,12},{15,13},{10,14},{11,... | collective-permute-start | bytes 589832 | tf_op jit(solution)/shard_map/ppermute | solution.py:160
  19.3 4.7 %collective-permute-done.5 = bf16[96,1024]{1,0:T(8,128)(2,1)S(1)} collective-permute-done((bf16[96,1024]{1,0:T(8,128)(2,1)S(1)}, bf16[96,1024]{1,0:T(8,128)(2,1)S(1)}, u32[]{:S(2)}, u32[]{:S(2)}) %collective-permute-start.5) | collective-permute-done | bytes 196640 | tf_op jit(solution)/shard_map/ppermute | solution.py:157
  25.4 4.2 %collective-permute-done.6 = bf16[96,1024]{1,0:T(8,128)(2,1)S(1)} collective-permute-done((bf16[96,1024]{1,0:T(8,128)(2,1)S(1)}, bf16[96,1024]{1,0:T(8,128)(2,1)S(1)}, u32[]{:S(2)}, u32[]{:S(2)}) %collective-permute-start.6) | collective-permute-done | bytes 196640 | tf_op jit(solution)/shard_map/ppermute | solution.py:157
  38.2 1.3 %fusion.35.m_ref = f32[128,1]{1,0:T(8,128)} fusion(s32[]{:T(128)} %fusion.46), kind=kLoop, calls=%fused_computation.94 | loop fusion | flops 256 | bytes 516 | tf_op jit(solution)/shard_map/convert_element_type | solution.py:233
  40.2 1.3 %constant_dynamic-update-slice_fusion.2 = bf16[16,96,1024]{2,1,0:T(8,128)(2,1)} fusion(bf16[16,96,1024]{2,1,0:T(8,128)(2,1)} %get-tuple-element.34, bf16[8,96,1024]{2,1,0:T(8,128)(2,1)S(1)} %collective-permute-done.7), kind=kLoop, calls=%fused_computation.97 | loop fusion | bytes 3145728 | tf_op jit(solution)/shard_map/concatenate | solution.py:164
  41.5 2.6 %gather_fusion.1 = bf16[16,96,1024]{2,1,0:T(8,128)(2,1)S(1)} fusion(bf16[16,96,1024]{2,1,0:T(8,128)(2,1)} %constant_dynamic-update-slice_fusion.2, s32[1024]{0:T(1024)S(1)} %pad_clamp_fusion.1), kind=kCustom, calls=%fused_computation.5 | custom fusion | bytes 6291520 | tf_op jit(solution)/shard_map/jit(_take)/gather | solution.py:169
  44.1 2.0 %broadcast_select_fusion.w_ref = bf16[16,96,1024]{2,1,0:T(8,128)(2,1)} fusion(bf16[16,96,1024]{2,1,0:T(8,128)(2,1)S(1)} %gather_fusion.1, pred[16]{0:T(512)(128)(4,1)S(1)} %compare_and_fusion.1), kind=kLoop, calls=%fused_computation.7 | loop fusion | flops 1572864 | bytes 6291472 | tf_op jit(solution)/shard_map/jit(_take)/select_n | solution.py:169
  46.1 6.1 %shard_map.157 = (bf16[128,512]{1,0:T(8,128)(2,1)}, bf16[128,1024]{1,0:T(8,128)(2,1)}, bf16[128,1024]{1,0:T(8,128)(2,1)}, bf16[128,1024]{1,0:T(8,128)(2,1)}, bf1...) custom-call(bf16[128,512]{1,0:T(8,128)(2,1)} %x_ref.1, ...), custom_call_target="tpu_custom_call" | custom-call | flops 1476395008 | bytes 5242880 | tf_op jit(solution)/shard_map/pallas_call | solution.py:117
  52.2 1.1 %copy.25 = bf16[128,1024]{0,1:T(8,128)(2,1)S(1)} copy(bf16[128,1024]{1,0:T(8,128)(2,1)} %get-tuple-element.13) | data formatting | bytes 524288 | tf_op jit(solution)/shard_map/pallas_call | solution.py:117
  53.9 1.1 %copy.26 = bf16[128,1024]{0,1:T(8,128)(2,1)S(1)} copy(bf16[128,1024]{1,0:T(8,128)(2,1)} %get-tuple-element.15) | data formatting | bytes 524288 | tf_op jit(solution)/shard_map/pallas_call | solution.py:117
  57.0 1.4 %fusion.10 = f32[8,64,1024]{2,1,0:T(8,128)S(1)} fusion(bf16[128,1024]{1,0:T(8,128)(2,1)} %get-tuple-element.14, bf16[128,8,2,64]{0,3,2,1:T(8,128)(2,1)S(1)} %get-tuple-element.49, s32[]{:T(128)S(6)} %select_n.181), kind=kOutput, calls=%fused_computation.23 | convolution fusion | flops 134217728 | bytes 2490372 | tf_op jit(solution)/shard_map/dot_general | solution.py:207
  59.1 2.7 %fusion.6 = f32[8,64,1024]{2,1,0:T(8,128)} fusion(bf16[128,1024]{1,0:T(8,128)(2,1)} %get-tuple-element.16, bf16[128,8,2,64]{0,3,2,1:T(8,128)(2,1)S(1)} %get-tuple-element.50, s32[]{:T(128)S(6)} %select_n.181), kind=kOutput, calls=%fused_computation.19 | convolution fusion | flops 134217728 | bytes 2490372 | tf_op jit(solution)/shard_map/dot_general | solution.py:207
  70.4 1.8 %collective-permute-start.17 = (f32[56,1024]{1,0:T(8,128)S(1)}, f32[56,1024]{1,0:T(8,128)S(1)}, u32[]{:S(2)}, u32[]{:S(2)}) collective-permute-start(f32[56,1024]{1,0:T(8,128)S(1)} %get-tuple-element.25), channel_id=1, source_target_pairs={{0,4},{1,5},{4,8},{5,9},{8,12},{9,13},{12,14},{13,15},{14,10},{15,... | collective-permute-start | bytes 688136 | tf_op jit(solution)/shard_map/ppermute | solution.py:182
  72.5 1.4 %collective-permute-start.28 = (f32[48,1024]{1,0:T(8,128)S(1)}, f32[48,1024]{1,0:T(8,128)S(1)}, u32[]{:S(2)}, u32[]{:S(2)}) collective-permute-start(f32[48,1024]{1,0:T(8,128)S(1)} %get-tuple-element.32), channel_id=1, source_target_pairs={{4,0},{5,1},{8,4},{9,5},{12,8},{13,9},{14,12},{15,13},{10,14},{11,... | collective-permute-start | bytes 589832 | tf_op jit(solution)/shard_map/ppermute | solution.py:188
  73.9 3.2 %collective-permute-done.24 = f32[48,1024]{1,0:T(8,128)S(1)} collective-permute-done((f32[48,1024]{1,0:T(8,128)S(1)}, f32[48,1024]{1,0:T(8,128)S(1)}, u32[]{:S(2)}, u32[]{:S(2)}) %collective-permute-start.24) | collective-permute-done | bytes 196640 | tf_op jit(solution)/shard_map/ppermute | solution.py:182
  77.8 4.2 %collective-permute-done.17 = f32[56,1024]{1,0:T(8,128)S(1)} collective-permute-done((f32[56,1024]{1,0:T(8,128)S(1)}, f32[56,1024]{1,0:T(8,128)S(1)}, u32[]{:S(2)}, u32[]{:S(2)}) %collective-permute-start.17) | collective-permute-done | bytes 229408 | tf_op jit(solution)/shard_map/ppermute | solution.py:182
  82.8 1.4 %collective-permute-start.21 = (f32[56,1024]{1,0:T(8,128)S(1)}, f32[56,1024]{1,0:T(8,128)S(1)}, u32[]{:S(2)}, u32[]{:S(2)}) collective-permute-start(f32[56,1024]{1,0:T(8,128)S(1)} %get-tuple-element.24), channel_id=1, source_target_pairs={{4,0},{5,1},{8,4},{9,5},{12,8},{13,9},{14,12},{15,13},{10,14},{11,... | collective-permute-start | bytes 688136 | tf_op jit(solution)/shard_map/ppermute | solution.py:188
  84.2 2.1 %collective-permute-done.25 = f32[48,1024]{1,0:T(8,128)S(1)} collective-permute-done((f32[48,1024]{1,0:T(8,128)S(1)}, f32[48,1024]{1,0:T(8,128)S(1)}, u32[]{:S(2)}, u32[]{:S(2)}) %collective-permute-start.25) | collective-permute-done | bytes 196640 | tf_op jit(solution)/shard_map/ppermute | solution.py:182
  87.0 1.4 %collective-permute-start.29 = (f32[48,1024]{1,0:T(8,128)S(1)}, f32[48,1024]{1,0:T(8,128)S(1)}, u32[]{:S(2)}, u32[]{:S(2)}) collective-permute-start(f32[48,1024]{1,0:T(8,128)S(1)} %get-tuple-element.30), channel_id=1, source_target_pairs={{4,0},{5,1},{8,4},{9,5},{12,8},{13,9},{14,12},{15,13},{10,14},{11,... | collective-permute-start | bytes 589832 | tf_op jit(solution)/shard_map/ppermute | solution.py:188
  88.4 2.8 %collective-permute-done.18 = f32[56,1024]{1,0:T(8,128)S(1)} collective-permute-done((f32[56,1024]{1,0:T(8,128)S(1)}, f32[56,1024]{1,0:T(8,128)S(1)}, u32[]{:S(2)}, u32[]{:S(2)}) %collective-permute-start.18) | collective-permute-done | bytes 229408 | tf_op jit(solution)/shard_map/ppermute | solution.py:182
  91.2 1.6 %collective-permute-start.22 = (f32[56,1024]{1,0:T(8,128)S(1)}, f32[56,1024]{1,0:T(8,128)S(1)}, u32[]{:S(2)}, u32[]{:S(2)}) collective-permute-start(f32[56,1024]{1,0:T(8,128)S(1)} %get-tuple-element.22), channel_id=1, source_target_pairs={{4,0},{5,1},{8,4},{9,5},{12,8},{13,9},{14,12},{15,13},{10,14},{11,... | collective-permute-start | bytes 688136 | tf_op jit(solution)/shard_map/ppermute | solution.py:188
  93.3 2.1 %collective-permute-done.26 = f32[48,1024]{1,0:T(8,128)S(1)} collective-permute-done((f32[48,1024]{1,0:T(8,128)S(1)}, f32[48,1024]{1,0:T(8,128)S(1)}, u32[]{:S(2)}, u32[]{:S(2)}) %collective-permute-start.26) | collective-permute-done | bytes 196640 | tf_op jit(solution)/shard_map/ppermute | solution.py:182
  95.4 1.1 collective-permute-start.27
  97.5 1.3 %collective-permute-done.22 = f32[56,1024]{1,0:T(8,128)S(1)} collective-permute-done((f32[56,1024]{1,0:T(8,128)S(1)}, f32[56,1024]{1,0:T(8,128)S(1)}, u32[]{:S(2)}, u32[]{:S(2)}) %collective-permute-start.22) | collective-permute-done | bytes 229408 | tf_op jit(solution)/shard_map/ppermute | solution.py:188
  98.8 1.4 %collective-permute-start.23 = (f32[56,1024]{1,0:T(8,128)S(1)}, f32[56,1024]{1,0:T(8,128)S(1)}, u32[]{:S(2)}, u32[]{:S(2)}) collective-permute-start(f32[56,1024]{1,0:T(8,128)S(1)} %fusion.13), channel_id=1, source_target_pairs={{4,0},{5,1},{8,4},{9,5},{12,8},{13,9},{14,12},{15,13},{10,14},{11,... | collective-permute-start | bytes 688136 | tf_op jit(solution)/shard_map/ppermute | solution.py:188
  100.3 3.7 %collective-permute-done.27 = f32[48,1024]{1,0:T(8,128)S(1)} collective-permute-done((f32[48,1024]{1,0:T(8,128)S(1)}, f32[48,1024]{1,0:T(8,128)S(1)}, u32[]{:S(2)}, u32[]{:S(2)}) %collective-permute-start.27) | collective-permute-done | bytes 196640 | tf_op jit(solution)/shard_map/ppermute | solution.py:182
  104.5 2.8 %collective-permute-done.23 = f32[56,1024]{1,0:T(8,128)S(1)} collective-permute-done((f32[56,1024]{1,0:T(8,128)S(1)}, f32[56,1024]{1,0:T(8,128)S(1)}, u32[]{:S(2)}, u32[]{:S(2)}) %collective-permute-start.23) | collective-permute-done | bytes 229408 | tf_op jit(solution)/shard_map/ppermute | solution.py:188
  (136 shorter events, 35.8 us)
Async XLA Ops:
  0.6 35.1 %copy-start = (s32[16,16]{1,0:T(8,128)S(1)}, s32[16,16]{1,0:T(8,128)}, u32[]{:S(2)}) copy-start(s32[16,16]{1,0:T(8,128)} %param.21) | copy-start | bytes 3076
  2.4 8.0 %collective-permute-start = (bf16[96,1024]{1,0:T(8,128)(2,1)S(1)}, bf16[96,1024]{1,0:T(8,128)(2,1)S(1)}, u32[]{:S(2)}, u32[]{:S(2)}) collective-permute-start(bf16[96,1024]{1,0:T(8,128)(2,1)S(1)} %constant_dynamic-update-slice_fusion), channel_id=1, source_target_pairs={{4,0},{5,1},{8,4},{9,5},{12,8},{13,9},{14,12},{15,13},{10,14},{11,... | collective-permute-start | bytes 589832 | tf_op jit(solution)/shard_map/ppermute | solution.py:160
  5.4 6.6 %collective-permute-start.3 = (bf16[96,1024]{1,0:T(8,128)(2,1)S(1)}, bf16[96,1024]{1,0:T(8,128)(2,1)S(1)}, u32[]{:S(2)}, u32[]{:S(2)}) collective-permute-start(bf16[96,1024]{1,0:T(8,128)(2,1)S(1)} %constant_dynamic-update-slice_fusion), channel_id=1, source_target_pairs={{0,4},{1,5},{4,8},{5,9},{8,12},{9,13},{12,14},{13,15},{14,10},{15,... | collective-permute-start | bytes 589832 | tf_op jit(solution)/shard_map/ppermute | solution.py:157
  10.4 6.1 %collective-permute-start.1 = (bf16[96,1024]{1,0:T(8,128)(2,1)S(1)}, bf16[96,1024]{1,0:T(8,128)(2,1)S(1)}, u32[]{:S(2)}, u32[]{:S(2)}) collective-permute-start(bf16[96,1024]{1,0:T(8,128)(2,1)S(1)} %collective-permute-done), channel_id=1, source_target_pairs={{4,0},{5,1},{8,4},{9,5},{12,8},{13,9},{14,12},{15,13},{10,14},{11,... | collective-permute-start | bytes 589832 | tf_op jit(solution)/shard_map/ppermute | solution.py:160
  12.1 5.8 %collective-permute-start.4 = (bf16[96,1024]{1,0:T(8,128)(2,1)S(1)}, bf16[96,1024]{1,0:T(8,128)(2,1)S(1)}, u32[]{:S(2)}, u32[]{:S(2)}) collective-permute-start(bf16[96,1024]{1,0:T(8,128)(2,1)S(1)} %collective-permute-done.3), channel_id=1, source_target_pairs={{0,4},{1,5},{4,8},{5,9},{8,12},{9,13},{12,14},{13,15},{14,10},{15,... | collective-permute-start | bytes 589832 | tf_op jit(solution)/shard_map/ppermute | solution.py:157
  16.5 8.1 %collective-permute-start.2 = (bf16[96,1024]{1,0:T(8,128)(2,1)S(1)}, bf16[96,1024]{1,0:T(8,128)(2,1)S(1)}, u32[]{:S(2)}, u32[]{:S(2)}) collective-permute-start(bf16[96,1024]{1,0:T(8,128)(2,1)S(1)} %collective-permute-done.1), channel_id=1, source_target_pairs={{4,0},{5,1},{8,4},{9,5},{12,8},{13,9},{14,12},{15,13},{10,14},{11,... | collective-permute-start | bytes 589832 | tf_op jit(solution)/shard_map/ppermute | solution.py:160
  17.8 6.1 %collective-permute-start.5 = (bf16[96,1024]{1,0:T(8,128)(2,1)S(1)}, bf16[96,1024]{1,0:T(8,128)(2,1)S(1)}, u32[]{:S(2)}, u32[]{:S(2)}) collective-permute-start(bf16[96,1024]{1,0:T(8,128)(2,1)S(1)} %collective-permute-done.4), channel_id=1, source_target_pairs={{0,4},{1,5},{4,8},{5,9},{8,12},{9,13},{12,14},{13,15},{14,10},{15,... | collective-permute-start | bytes 589832 | tf_op jit(solution)/shard_map/ppermute | solution.py:157
  24.0 5.7 %collective-permute-start.6 = (bf16[96,1024]{1,0:T(8,128)(2,1)S(1)}, bf16[96,1024]{1,0:T(8,128)(2,1)S(1)}, u32[]{:S(2)}, u32[]{:S(2)}) collective-permute-start(bf16[96,1024]{1,0:T(8,128)(2,1)S(1)} %collective-permute-done.5), channel_id=1, source_target_pairs={{0,4},{1,5},{4,8},{5,9},{8,12},{9,13},{12,14},{13,15},{14,10},{15,... | collective-permute-start | bytes 589832 | tf_op jit(solution)/shard_map/ppermute | solution.py:157
  32.8 7.3 %collective-permute-start.7 = (bf16[8,96,1024]{2,1,0:T(8,128)(2,1)}, bf16[8,96,1024]{2,1,0:T(8,128)(2,1)S(1)}, u32[]{:S(2)}, u32[]{:S(2)}) collective-permute-start(bf16[8,96,1024]{2,1,0:T(8,128)(2,1)} %get-tuple-element.33), channel_id=1, source_target_pairs={{0,1},{1,0},{2,3},{3,2},{4,5},{5,4},{6,7},{7,6},{8,9},{9,8},{10,11... | collective-permute-start | bytes 4718600 | tf_op jit(solution)/shard_map/ppermute | solution.py:163
  55.7 11.2 %collective-permute-start.9 = (bf16[128,1024]{1,0:T(8,128)(2,1)}, bf16[128,1024]{1,0:T(8,128)(2,1)S(1)}, u32[]{:S(2)}, u32[]{:S(2)}) collective-permute-start(bf16[128,1024]{1,0:T(8,128)(2,1)} %get-tuple-element.14), channel_id=1, source_target_pairs={{0,1},{1,0},{2,3},{3,2},{4,5},{5,4},{6,7},{7,6},{8,9},{9,8},{10,11... | collective-permute-start | bytes 786440 | tf_op jit(solution)/shard_map/ppermute | solution.py:248
  61.9 6.6 %collective-permute-start.11 = (bf16[128,1024]{1,0:T(8,128)(2,1)}, bf16[128,1024]{1,0:T(8,128)(2,1)S(1)}, u32[]{:S(2)}, u32[]{:S(2)}) collective-permute-start(bf16[128,1024]{1,0:T(8,128)(2,1)} %get-tuple-element.16), channel_id=1, source_target_pairs={{0,1},{1,0},{2,3},{3,2},{4,5},{5,4},{6,7},{7,6},{8,9},{9,8},{10,11... | collective-permute-start | bytes 786440 | tf_op jit(solution)/shard_map/ppermute | solution.py:248
  63.6 4.5 %collective-permute-start.14 = (bf16[128,1024]{1,0:T(8,128)(2,1)S(1)}, bf16[128,1024]{1,0:T(8,128)(2,1)S(1)}, u32[]{:S(2)}, u32[]{:S(2)}) collective-permute-start(bf16[128,1024]{1,0:T(8,128)(2,1)S(1)} %copy-done.5), channel_id=1, source_target_pairs={{0,1},{1,0},{2,3},{3,2},{4,5},{5,4},{6,7},{7,6},{8,9},{9,8},{10,11... | collective-permute-start | bytes 786440 | tf_op jit(solution)/shard_map/ppermute | solution.py:248
  64.2 2.5 %collective-permute-start.8 = (bf16[128,8,64]{0,2,1:T(8,128)(2,1)}, bf16[128,8,64]{0,2,1:T(8,128)(2,1)S(1)}, u32[]{:S(2)}, u32[]{:S(2)}) collective-permute-start(bf16[128,8,64]{0,2,1:T(8,128)(2,1)} %dynamic-slice_bitcast_fusion.1), channel_id=1, source_target_pairs={{0,1},{1,0},{2,3},{3,2},{4,5},{5,4},{6,7},{7,6},{8,9},{9,8},{10,11... | collective-permute-start | bytes 393224 | tf_op jit(solution)/shard_map/ppermute | solution.py:245
  64.3 1.3 %collective-permute-start.12 = (f32[1024]{0:T(1024)S(1)}, f32[1024]{0:T(1024)S(1)}, u32[]{:S(2)}, u32[]{:S(2)}) collective-permute-start(f32[1024]{0:T(1024)S(1)} %bitcast.162), channel_id=1, source_target_pairs={{0,1},{1,0},{2,3},{3,2},{4,5},{5,4},{6,7},{7,6},{8,9},{9,8},{10,11... | collective-permute-start | bytes 12296 | tf_op jit(solution)/shard_map/ppermute | solution.py:248
  65.5 2.9 %collective-permute-start.10 = (bf16[128,8,64]{0,2,1:T(8,128)(2,1)}, bf16[128,8,64]{0,2,1:T(8,128)(2,1)S(1)}, u32[]{:S(2)}, u32[]{:S(2)}) collective-permute-start(bf16[128,8,64]{0,2,1:T(8,128)(2,1)} %dynamic-slice_bitcast_fusion), channel_id=1, source_target_pairs={{0,1},{1,0},{2,3},{3,2},{4,5},{5,4},{6,7},{7,6},{8,9},{9,8},{10,11... | collective-permute-start | bytes 393224 | tf_op jit(solution)/shard_map/ppermute | solution.py:245
  66.7 1.3 %collective-permute-start.13 = (bf16[128,8,32]{0,2,1:T(8,128)(2,1)S(1)}, bf16[128,8,32]{0,2,1:T(8,128)(2,1)S(1)}, u32[]{:S(2)}, u32[]{:S(2)}) collective-permute-start(bf16[128,8,32]{0,2,1:T(8,128)(2,1)S(1)} %dynamic-slice_bitcast_fusion.3), channel_id=1, source_target_pairs={{0,1},{1,0},{2,3},{3,2},{4,5},{5,4},{6,7},{7,6},{8,9},{9,8},{10,11... | collective-permute-start | bytes 196616 | tf_op jit(solution)/shard_map/ppermute | solution.py:245
  66.9 3.2 %collective-permute-start.15 = (bf16[128,8,32]{0,2,1:T(8,128)(2,1)S(1)}, bf16[128,8,32]{0,2,1:T(8,128)(2,1)S(1)}, u32[]{:S(2)}, u32[]{:S(2)}) collective-permute-start(bf16[128,8,32]{0,2,1:T(8,128)(2,1)S(1)} %dynamic-slice_bitcast_fusion.2), channel_id=1, source_target_pairs={{0,1},{1,0},{2,3},{3,2},{4,5},{5,4},{6,7},{7,6},{8,9},{9,8},{10,11... | collective-permute-start | bytes 196616 | tf_op jit(solution)/shard_map/ppermute | solution.py:245
  68.0 2.1 %collective-permute-start.16 = (bf16[128,1024]{1,0:T(8,128)(2,1)S(1)}, bf16[128,1024]{1,0:T(8,128)(2,1)S(1)}, u32[]{:S(2)}, u32[]{:S(2)}) collective-permute-start(bf16[128,1024]{1,0:T(8,128)(2,1)S(1)} %copy-done.6), channel_id=1, source_target_pairs={{0,1},{1,0},{2,3},{3,2},{4,5},{5,4},{6,7},{7,6},{8,9},{9,8},{10,11... | collective-permute-start | bytes 786440 | tf_op jit(solution)/shard_map/ppermute | solution.py:248
  69.3 7.8 %collective-permute-start.24 = (f32[48,1024]{1,0:T(8,128)S(1)}, f32[48,1024]{1,0:T(8,128)S(1)}, u32[]{:S(2)}, u32[]{:S(2)}) collective-permute-start(f32[48,1024]{1,0:T(8,128)S(1)} %get-tuple-element.31), channel_id=1, source_target_pairs={{0,4},{1,5},{4,8},{5,9},{8,12},{9,13},{12,14},{13,15},{14,10},{15,... | collective-permute-start | bytes 589832 | tf_op jit(solution)/shard_map/ppermute | solution.py:182
  70.4 11.6 %collective-permute-start.17 = (f32[56,1024]{1,0:T(8,128)S(1)}, f32[56,1024]{1,0:T(8,128)S(1)}, u32[]{:S(2)}, u32[]{:S(2)}) collective-permute-start(f32[56,1024]{1,0:T(8,128)S(1)} %get-tuple-element.25), channel_id=1, source_target_pairs={{0,4},{1,5},{4,8},{5,9},{8,12},{9,13},{12,14},{13,15},{14,10},{15,... | collective-permute-start | bytes 688136 | tf_op jit(solution)/shard_map/ppermute | solution.py:182
  72.2 9.8 %collective-permute-start.20 = (f32[56,1024]{1,0:T(8,128)S(1)}, f32[56,1024]{1,0:T(8,128)S(1)}, u32[]{:S(2)}, u32[]{:S(2)}) collective-permute-start(f32[56,1024]{1,0:T(8,128)S(1)} %get-tuple-element.26), channel_id=1, source_target_pairs={{4,0},{5,1},{8,4},{9,5},{12,8},{13,9},{14,12},{15,13},{10,14},{11,... | collective-permute-start | bytes 688136 | tf_op jit(solution)/shard_map/ppermute | solution.py:188
  72.5 11.7 %collective-permute-start.28 = (f32[48,1024]{1,0:T(8,128)S(1)}, f32[48,1024]{1,0:T(8,128)S(1)}, u32[]{:S(2)}, u32[]{:S(2)}) collective-permute-start(f32[48,1024]{1,0:T(8,128)S(1)} %get-tuple-element.32), channel_id=1, source_target_pairs={{4,0},{5,1},{8,4},{9,5},{12,8},{13,9},{14,12},{15,13},{10,14},{11,... | collective-permute-start | bytes 589832 | tf_op jit(solution)/shard_map/ppermute | solution.py:188
  77.2 9.1 %collective-permute-start.25 = (f32[48,1024]{1,0:T(8,128)S(1)}, f32[48,1024]{1,0:T(8,128)S(1)}, u32[]{:S(2)}, u32[]{:S(2)}) collective-permute-start(f32[48,1024]{1,0:T(8,128)S(1)} %fusion.26), channel_id=1, source_target_pairs={{0,4},{1,5},{4,8},{5,9},{8,12},{9,13},{12,14},{13,15},{14,10},{15,... | collective-permute-start | bytes 589832 | tf_op jit(solution)/shard_map/ppermute | solution.py:182
  82.1 9.1 %collective-permute-start.18 = (f32[56,1024]{1,0:T(8,128)S(1)}, f32[56,1024]{1,0:T(8,128)S(1)}, u32[]{:S(2)}, u32[]{:S(2)}) collective-permute-start(f32[56,1024]{1,0:T(8,128)S(1)} %get-tuple-element.23), channel_id=1, source_target_pairs={{0,4},{1,5},{4,8},{5,9},{8,12},{9,13},{12,14},{13,15},{14,10},{15,... | collective-permute-start | bytes 688136 | tf_op jit(solution)/shard_map/ppermute | solution.py:182
  82.8 8.4 %collective-permute-start.21 = (f32[56,1024]{1,0:T(8,128)S(1)}, f32[56,1024]{1,0:T(8,128)S(1)}, u32[]{:S(2)}, u32[]{:S(2)}) collective-permute-start(f32[56,1024]{1,0:T(8,128)S(1)} %get-tuple-element.24), channel_id=1, source_target_pairs={{4,0},{5,1},{8,4},{9,5},{12,8},{13,9},{14,12},{15,13},{10,14},{11,... | collective-permute-start | bytes 688136 | tf_op jit(solution)/shard_map/ppermute | solution.py:188
  86.3 9.1 %collective-permute-start.26 = (f32[48,1024]{1,0:T(8,128)S(1)}, f32[48,1024]{1,0:T(8,128)S(1)}, u32[]{:S(2)}, u32[]{:S(2)}) collective-permute-start(f32[48,1024]{1,0:T(8,128)S(1)} %get-tuple-element.29), channel_id=1, source_target_pairs={{0,4},{1,5},{4,8},{5,9},{8,12},{9,13},{12,14},{13,15},{14,10},{15,... | collective-permute-start | bytes 589832 | tf_op jit(solution)/shard_map/ppermute | solution.py:182
  87.0 8.4 %collective-permute-start.29 = (f32[48,1024]{1,0:T(8,128)S(1)}, f32[48,1024]{1,0:T(8,128)S(1)}, u32[]{:S(2)}, u32[]{:S(2)}) collective-permute-start(f32[48,1024]{1,0:T(8,128)S(1)} %get-tuple-element.30), channel_id=1, source_target_pairs={{4,0},{5,1},{8,4},{9,5},{12,8},{13,9},{14,12},{15,13},{10,14},{11,... | collective-permute-start | bytes 589832 | tf_op jit(solution)/shard_map/ppermute | solution.py:188
  91.2 7.6 %collective-permute-start.22 = (f32[56,1024]{1,0:T(8,128)S(1)}, f32[56,1024]{1,0:T(8,128)S(1)}, u32[]{:S(2)}, u32[]{:S(2)}) collective-permute-start(f32[56,1024]{1,0:T(8,128)S(1)} %get-tuple-element.22), channel_id=1, source_target_pairs={{4,0},{5,1},{8,4},{9,5},{12,8},{13,9},{14,12},{15,13},{10,14},{11,... | collective-permute-start | bytes 688136 | tf_op jit(solution)/shard_map/ppermute | solution.py:188
  92.9 11.6 %collective-permute-start.19 = (f32[56,1024]{1,0:T(8,128)S(1)}, f32[56,1024]{1,0:T(8,128)S(1)}, u32[]{:S(2)}, u32[]{:S(2)}) collective-permute-start(f32[56,1024]{1,0:T(8,128)S(1)} %get-tuple-element.21), channel_id=1, source_target_pairs={{0,4},{1,5},{4,8},{5,9},{8,12},{9,13},{12,14},{13,15},{14,10},{15,... | collective-permute-start | bytes 688136 | tf_op jit(solution)/shard_map/ppermute | solution.py:182
  95.4 8.5 %collective-permute-start.27 = (f32[48,1024]{1,0:T(8,128)S(1)}, f32[48,1024]{1,0:T(8,128)S(1)}, u32[]{:S(2)}, u32[]{:S(2)}) collective-permute-start(f32[48,1024]{1,0:T(8,128)S(1)} %get-tuple-element.27), channel_id=1, source_target_pairs={{0,4},{1,5},{4,8},{5,9},{8,12},{9,13},{12,14},{13,15},{14,10},{15,... | collective-permute-start | bytes 589832 | tf_op jit(solution)/shard_map/ppermute | solution.py:182
  96.5 7.8 %collective-permute-start.30 = (f32[48,1024]{1,0:T(8,128)S(1)}, f32[48,1024]{1,0:T(8,128)S(1)}, u32[]{:S(2)}, u32[]{:S(2)}) collective-permute-start(f32[48,1024]{1,0:T(8,128)S(1)} %get-tuple-element.28), channel_id=1, source_target_pairs={{4,0},{5,1},{8,4},{9,5},{12,8},{13,9},{14,12},{15,13},{10,14},{11,... | collective-permute-start | bytes 589832 | tf_op jit(solution)/shard_map/ppermute | solution.py:188
  98.8 8.5 %collective-permute-start.23 = (f32[56,1024]{1,0:T(8,128)S(1)}, f32[56,1024]{1,0:T(8,128)S(1)}, u32[]{:S(2)}, u32[]{:S(2)}) collective-permute-start(f32[56,1024]{1,0:T(8,128)S(1)} %fusion.13), channel_id=1, source_target_pairs={{4,0},{5,1},{8,4},{9,5},{12,8},{13,9},{14,12},{15,13},{10,14},{11,... | collective-permute-start | bytes 688136 | tf_op jit(solution)/shard_map/ppermute | solution.py:188
  (14 other events, 141.4 us)

commit v12 on v11

--- a/solution.py
+++ b/solution.py
@@ -166,7 +166,7 @@
     dest_chip, dest_core = dest // 2, dest % 2
     k = (jnp.asarray(place, jnp.int32)[dest_chip] - spot) % chips
     index = jnp.where(dest_core == core, 0, chips) + k
-    return jnp.take(both, index, axis=0)
+    return jnp.take(both, index, axis=0, mode="clip")
 
 
 def ring_reduce_scatter(summed, n_blk):
@@ -239,7 +239,9 @@
     ring_chips = jnp.asarray(snake, jnp.int32)[(spot + jnp.arange(chips, dtype=jnp.int32)) % chips]
 
     def split_cols(f, width):
-        f = jnp.take(f.reshape(rows_dev, chips, 2, width), ring_chips, axis=1)
+        f = jnp.take(
+            f.reshape(rows_dev, chips, 2, width), ring_chips, axis=1, mode="clip"
+        )
         keep = lax.dynamic_index_in_dim(f, core, 2, keepdims=False)
         give = lax.dynamic_index_in_dim(f, 1 - core, 2, keepdims=False)
         return keep, lax.ppermute(give, "blk", partner)

time: 111 us -> 108 us (0.973)
  other arithmetic: 12.1 us -> 9.11 us
  local copies, waits for them, and re-layouts: 21.6 us -> 18.9 us
  waiting for transfers between devices: 38 us -> 40.4 us
  starting transfers between devices: 25.2 us -> 23.9 us
    select_n x5 -> x0, other arithmetic: 3.48 us -> none  [the longest x2 2.66 us: ring_all_gather(): return jnp.take(both, index, axis=0)]
    ppermute x7, waiting for transfers between devices: 4.53 us -> 6.65 us  [backward(): acc = lax.ppermute(acc, 'blk', ccw)]
    ppermute x3, waiting for transfers between devices: 5.39 us -> 7.44 us  [ring_all_gather(): right = lax.ppermute(right, 'blk', ccw)]
    ppermute x7, starting transfers between devices: 8.48 us -> 6.89 us  [backward(): acc = lax.ppermute(acc, 'blk', ccw)]
    ppermute x7, waiting for transfers between devices: 18 us -> 16.5 us  [forward(): acc = lax.ppermute(acc, 'blk', cw) + part[(window - s) % chips]]
  transfers between devices with their start and end apart: 31 -> 31, of which waited for: 15 -> 15; matrix products, arithmetic and copies ran while one was open for 20% -> 25% of each run, Pallas kernels for 0% -> 6%
where the time goes in v12:
time: 108 us; the launch traced here: 107 us
  waiting for transfers between devices  40.4 us (37%)
  starting transfers between devices  23.9 us (22%)
  local copies, waits for them, and re-layouts  18.9 us (17%)
  other arithmetic  9.11 us (8%)
  matrix products  7.08 us (7%)
  Pallas kernels  6.15 us (6%)
  between operations  1.78 us (2%)
    ppermute x7, waiting for transfers between devices, forward(): acc = lax.ppermute(acc, 'blk', cw) + part[(window - s) % chips]  16.5 us
    ppermute x4, waiting for transfers between devices, ring_all_gather(): left = lax.ppermute(left, 'blk', cw)  9.03 us
    ppermute x3, waiting for transfers between devices, ring_all_gather(): right = lax.ppermute(right, 'blk', ccw)  7.44 us
    dot_general x8, matrix products, slots_product(): lax.dot_general(left, right, (((0,), (0,)), ((), ())), preferred_element_...  7.08 us
    ppermute x7, starting transfers between devices, backward(): acc = lax.ppermute(acc, 'blk', ccw)  6.89 us
    ppermute x7, starting transfers between devices, forward(): acc = lax.ppermute(acc, 'blk', cw) + part[(window - s) % chips]  6.71 us
    ppermute x7, waiting for transfers between devices, backward(): acc = lax.ppermute(acc, 'blk', ccw)  6.65 us
    pallas_call x1, Pallas kernels, twin_fused(): pl.pallas_call(functools.partial(twin_body, r_one), out_shape=shapes, in_...  6.15 us
  transfers between devices with their start and end apart: 31, of which 15 were waited for; matrix products, arithmetic and copies ran while one was open for 25% of the time, Pallas kernels for 6%

profile of v12, /device:TPU:0, one launch (start us, length us, event | category | flops | bytes accessed | tf_op | source)
XLA Modules:
  0.0 107.3 jit_solution(8599231485442538090)
XLA Ops:
  0.6 0.9 constant_dynamic-update-slice_fusion.1
  1.5 0.9 constant_dynamic-update-slice_fusion
  2.4 3.0 %collective-permute-start = (bf16[96,1024]{1,0:T(8,128)(2,1)S(1)}, bf16[96,1024]{1,0:T(8,128)(2,1)S(1)}, u32[]{:S(2)}, u32[]{:S(2)}) collective-permute-start(bf16[96,1024]{1,0:T(8,128)(2,1)S(1)} %constant_dynamic-update-slice_fusion), channel_id=1, source_target_pairs={{4,0},{5,1},{8,4},{9,5},{12,8},{13,9},{14,12},{15,13},{10,14},{11,... | collective-permute-start | bytes 589832 | tf_op jit(solution)/shard_map/ppermute | solution.py:160
  6.3 4.1 %collective-permute-done = bf16[96,1024]{1,0:T(8,128)(2,1)S(1)} collective-permute-done((bf16[96,1024]{1,0:T(8,128)(2,1)S(1)}, bf16[96,1024]{1,0:T(8,128)(2,1)S(1)}, u32[]{:S(2)}, u32[]{:S(2)}) %collective-permute-start) | collective-permute-done | bytes 196640 | tf_op jit(solution)/shard_map/ppermute | solution.py:160
  10.4 1.7 %collective-permute-start.1 = (bf16[96,1024]{1,0:T(8,128)(2,1)S(1)}, bf16[96,1024]{1,0:T(8,128)(2,1)S(1)}, u32[]{:S(2)}, u32[]{:S(2)}) collective-permute-start(bf16[96,1024]{1,0:T(8,128)(2,1)S(1)} %collective-permute-done), channel_id=1, source_target_pairs={{4,0},{5,1},{8,4},{9,5},{12,8},{13,9},{14,12},{15,13},{10,14},{11,... | collective-permute-start | bytes 589832 | tf_op jit(solution)/shard_map/ppermute | solution.py:160
  13.2 3.3 %collective-permute-done.1 = bf16[96,1024]{1,0:T(8,128)(2,1)S(1)} collective-permute-done((bf16[96,1024]{1,0:T(8,128)(2,1)S(1)}, bf16[96,1024]{1,0:T(8,128)(2,1)S(1)}, u32[]{:S(2)}, u32[]{:S(2)}) %collective-permute-start.1) | collective-permute-done | bytes 196640 | tf_op jit(solution)/shard_map/ppermute | solution.py:160
  16.5 1.4 %collective-permute-start.2 = (bf16[96,1024]{1,0:T(8,128)(2,1)S(1)}, bf16[96,1024]{1,0:T(8,128)(2,1)S(1)}, u32[]{:S(2)}, u32[]{:S(2)}) collective-permute-start(bf16[96,1024]{1,0:T(8,128)(2,1)S(1)} %collective-permute-done.1), channel_id=1, source_target_pairs={{4,0},{5,1},{8,4},{9,5},{12,8},{13,9},{14,12},{15,13},{10,14},{11,... | collective-permute-start | bytes 589832 | tf_op jit(solution)/shard_map/ppermute | solution.py:160
  19.2 4.7 %collective-permute-done.5 = bf16[96,1024]{1,0:T(8,128)(2,1)S(1)} collective-permute-done((bf16[96,1024]{1,0:T(8,128)(2,1)S(1)}, bf16[96,1024]{1,0:T(8,128)(2,1)S(1)}, u32[]{:S(2)}, u32[]{:S(2)}) %collective-permute-start.5) | collective-permute-done | bytes 196640 | tf_op jit(solution)/shard_map/ppermute | solution.py:157
  25.3 4.3 %collective-permute-done.6 = bf16[96,1024]{1,0:T(8,128)(2,1)S(1)} collective-permute-done((bf16[96,1024]{1,0:T(8,128)(2,1)S(1)}, bf16[96,1024]{1,0:T(8,128)(2,1)S(1)}, u32[]{:S(2)}, u32[]{:S(2)}) %collective-permute-start.6) | collective-permute-done | bytes 196640 | tf_op jit(solution)/shard_map/ppermute | solution.py:157
  40.1 1.3 %fusion.35.m_ref = f32[128,1]{1,0:T(8,128)} fusion(s32[]{:T(128)} %fusion.43), kind=kLoop, calls=%fused_computation.89 | loop fusion | flops 256 | bytes 516 | tf_op jit(solution)/shard_map/convert_element_type | solution.py:233
  41.4 1.6 %constant_dynamic-update-slice_fusion.2 = bf16[16,96,1024]{2,1,0:T(8,128)(2,1)S(1)} fusion(bf16[16,96,1024]{2,1,0:T(8,128)(2,1)S(1)} %get-tuple-element.32, bf16[8,96,1024]{2,1,0:T(8,128)(2,1)} %collective-permute-done.7), kind=kLoop, calls=%fused_computation.92 | loop fusion | bytes 3145728 | tf_op jit(solution)/shard_map/concatenate | solution.py:164
  43.0 2.4 %gather_fusion.1 = bf16[16,96,1024]{2,1,0:T(8,128)(2,1)} fusion(bf16[16,96,1024]{2,1,0:T(8,128)(2,1)S(1)} %constant_dynamic-update-slice_fusion.2, s32[1024]{0:T(1024)S(1)} %pad_clamp_fusion.2), kind=kCustom, calls=%fused_computation.1 | custom fusion | bytes 6291520 | tf_op jit(solution)/shard_map/jit(_take)/gather | solution.py:169
  45.4 6.2 %shard_map.157 = (bf16[128,512]{1,0:T(8,128)(2,1)}, bf16[128,1024]{1,0:T(8,128)(2,1)}, bf16[128,1024]{1,0:T(8,128)(2,1)}, bf16[128,1024]{1,0:T(8,128)(2,1)}, bf1...) custom-call(bf16[128,512]{1,0:T(8,128)(2,1)} %x_ref.1, ...), custom_call_target="tpu_custom_call" | custom-call | flops 1476395008 | bytes 5242880 | tf_op jit(solution)/shard_map/pallas_call | solution.py:117
  51.6 1.2 %copy.19 = bf16[128,1024]{0,1:T(8,128)(2,1)S(1)} copy(bf16[128,1024]{1,0:T(8,128)(2,1)} %get-tuple-element.11) | data formatting | bytes 524288 | tf_op jit(solution)/shard_map/pallas_call | solution.py:117
  53.5 1.4 %fusion.10 = f32[8,64,1024]{2,1,0:T(8,128)S(1)} fusion(bf16[128,1024]{1,0:T(8,128)(2,1)} %get-tuple-element.12, bf16[8,128,2,64]{1,3,2,0:T(8,128)(2,1)S(1)} %gather_fusion.3, s32[]{:T(128)S(6)} %select_n.131), kind=kOutput, calls=%fused_computation.22 | convolution fusion | flops 134217728 | bytes 2490372 | tf_op jit(solution)/shard_map/dot_general | solution.py:207
  55.7 2.8 %fusion.6 = f32[8,64,1024]{2,1,0:T(8,128)} fusion(bf16[128,1024]{1,0:T(8,128)(2,1)} %get-tuple-element.14, bf16[8,128,2,64]{1,3,2,0:T(8,128)(2,1)S(1)} %gather_fusion.4, s32[]{:T(128)S(6)} %select_n.131), kind=kOutput, calls=%fused_computation.18 | convolution fusion | flops 134217728 | bytes 2490372 | tf_op jit(solution)/shard_map/dot_general | solution.py:207
  65.8 1.1 %convolution_add_fusion = f32[8,32,1024]{2,1,0:T(8,128)S(1)} fusion(f32[8,32,1024]{2,1,0:T(8,128)S(1)} %convolution_add_fusion.1, bf16[128,8,32]{0,2,1:T(8,128)(2,1)} %collective-permute-done.15, bf16[128,1024]{1,0:T(8,128)(2,1)S(1)} %collective-permute-done.16), kind=kOutput, calls=%fused_computation.8 | convolution fusion | flops 67371008 | bytes 2424832 | tf_op jit(solution)/shard_map/dot_general | solution.py:207
  67.0 1.8 %collective-permute-start.17 = (f32[56,1024]{1,0:T(8,128)S(1)}, f32[56,1024]{1,0:T(8,128)S(1)}, u32[]{:S(2)}, u32[]{:S(2)}) collective-permute-start(f32[56,1024]{1,0:T(8,128)S(1)} %get-tuple-element.23), channel_id=1, source_target_pairs={{0,4},{1,5},{4,8},{5,9},{8,12},{9,13},{12,14},{13,15},{14,10},{15,... | collective-permute-start | bytes 688136 | tf_op jit(solution)/shard_map/ppermute | solution.py:182
  69.1 1.4 %collective-permute-start.28 = (f32[48,1024]{1,0:T(8,128)S(1)}, f32[48,1024]{1,0:T(8,128)S(1)}, u32[]{:S(2)}, u32[]{:S(2)}) collective-permute-start(f32[48,1024]{1,0:T(8,128)S(1)} %get-tuple-element.30), channel_id=1, source_target_pairs={{4,0},{5,1},{8,4},{9,5},{12,8},{13,9},{14,12},{15,13},{10,14},{11,... | collective-permute-start | bytes 589832 | tf_op jit(solution)/shard_map/ppermute | solution.py:188
  70.5 2.4 %collective-permute-done.24 = f32[48,1024]{1,0:T(8,128)S(1)} collective-permute-done((f32[48,1024]{1,0:T(8,128)S(1)}, f32[48,1024]{1,0:T(8,128)S(1)}, u32[]{:S(2)}, u32[]{:S(2)}) %collective-permute-start.24) | collective-permute-done | bytes 196640 | tf_op jit(solution)/shard_map/ppermute | solution.py:182
  73.6 4.2 %collective-permute-done.17 = f32[56,1024]{1,0:T(8,128)S(1)} collective-permute-done((f32[56,1024]{1,0:T(8,128)S(1)}, f32[56,1024]{1,0:T(8,128)S(1)}, u32[]{:S(2)}, u32[]{:S(2)}) %collective-permute-start.17) | collective-permute-done | bytes 229408 | tf_op jit(solution)/shard_map/ppermute | solution.py:182
  77.9 1.1 %collective-permute-start.18 = (f32[56,1024]{1,0:T(8,128)S(1)}, f32[56,1024]{1,0:T(8,128)S(1)}, u32[]{:S(2)}, u32[]{:S(2)}) collective-permute-start(f32[56,1024]{1,0:T(8,128)S(1)} %get-tuple-element.21), channel_id=1, source_target_pairs={{0,4},{1,5},{4,8},{5,9},{8,12},{9,13},{12,14},{13,15},{14,10},{15,... | collective-permute-start | bytes 688136 | tf_op jit(solution)/shard_map/ppermute | solution.py:182
  79.0 0.9 collective-permute-start.21
  80.7 1.3 %collective-permute-done.25 = f32[48,1024]{1,0:T(8,128)S(1)} collective-permute-done((f32[48,1024]{1,0:T(8,128)S(1)}, f32[48,1024]{1,0:T(8,128)S(1)}, u32[]{:S(2)}, u32[]{:S(2)}) %collective-permute-start.25) | collective-permute-done | bytes 196640 | tf_op jit(solution)/shard_map/ppermute | solution.py:182
  82.8 1.4 %collective-permute-start.29 = (f32[48,1024]{1,0:T(8,128)S(1)}, f32[48,1024]{1,0:T(8,128)S(1)}, u32[]{:S(2)}, u32[]{:S(2)}) collective-permute-start(f32[48,1024]{1,0:T(8,128)S(1)} %get-tuple-element.28), channel_id=1, source_target_pairs={{4,0},{5,1},{8,4},{9,5},{12,8},{13,9},{14,12},{15,13},{10,14},{11,... | collective-permute-start | bytes 589832 | tf_op jit(solution)/shard_map/ppermute | solution.py:188
  84.2 2.8 %collective-permute-done.18 = f32[56,1024]{1,0:T(8,128)S(1)} collective-permute-done((f32[56,1024]{1,0:T(8,128)S(1)}, f32[56,1024]{1,0:T(8,128)S(1)}, u32[]{:S(2)}, u32[]{:S(2)}) %collective-permute-start.18) | collective-permute-done | bytes 229408 | tf_op jit(solution)/shard_map/ppermute | solution.py:182
  87.0 1.6 %collective-permute-start.22 = (f32[56,1024]{1,0:T(8,128)S(1)}, f32[56,1024]{1,0:T(8,128)S(1)}, u32[]{:S(2)}, u32[]{:S(2)}) collective-permute-start(f32[56,1024]{1,0:T(8,128)S(1)} %get-tuple-element.20), channel_id=1, source_target_pairs={{4,0},{5,1},{8,4},{9,5},{12,8},{13,9},{14,12},{15,13},{10,14},{11,... | collective-permute-start | bytes 688136 | tf_op jit(solution)/shard_map/ppermute | solution.py:188
  89.1 2.1 %collective-permute-done.26 = f32[48,1024]{1,0:T(8,128)S(1)} collective-permute-done((f32[48,1024]{1,0:T(8,128)S(1)}, f32[48,1024]{1,0:T(8,128)S(1)}, u32[]{:S(2)}, u32[]{:S(2)}) %collective-permute-start.26) | collective-permute-done | bytes 196640 | tf_op jit(solution)/shard_map/ppermute | solution.py:182
  91.2 1.3 %collective-permute-start.27 = (f32[48,1024]{1,0:T(8,128)S(1)}, f32[48,1024]{1,0:T(8,128)S(1)}, u32[]{:S(2)}, u32[]{:S(2)}) collective-permute-start(f32[48,1024]{1,0:T(8,128)S(1)} %get-tuple-element.25), channel_id=1, source_target_pairs={{0,4},{1,5},{4,8},{5,9},{8,12},{9,13},{12,14},{13,15},{14,10},{15,... | collective-permute-start | bytes 589832 | tf_op jit(solution)/shard_map/ppermute | solution.py:182
  93.3 2.2 %collective-permute-done.22 = f32[56,1024]{1,0:T(8,128)S(1)} collective-permute-done((f32[56,1024]{1,0:T(8,128)S(1)}, f32[56,1024]{1,0:T(8,128)S(1)}, u32[]{:S(2)}, u32[]{:S(2)}) %collective-permute-start.22) | collective-permute-done | bytes 229408 | tf_op jit(solution)/shard_map/ppermute | solution.py:188
  96.0 3.7 %collective-permute-done.27 = f32[48,1024]{1,0:T(8,128)S(1)} collective-permute-done((f32[48,1024]{1,0:T(8,128)S(1)}, f32[48,1024]{1,0:T(8,128)S(1)}, u32[]{:S(2)}, u32[]{:S(2)}) %collective-permute-start.27) | collective-permute-done | bytes 196640 | tf_op jit(solution)/shard_map/ppermute | solution.py:182
  100.4 3.1 %collective-permute-done.23 = f32[56,1024]{1,0:T(8,128)S(1)} collective-permute-done((f32[56,1024]{1,0:T(8,128)S(1)}, f32[56,1024]{1,0:T(8,128)S(1)}, u32[]{:S(2)}, u32[]{:S(2)}) %collective-permute-start.23) | collective-permute-done | bytes 229408 | tf_op jit(solution)/shard_map/ppermute | solution.py:188
  (131 shorter events, 32.1 us)
Async XLA Ops:
  0.6 37.7 %copy-start = (s32[16,16]{1,0:T(8,128)S(1)}, s32[16,16]{1,0:T(8,128)}, u32[]{:S(2)}) copy-start(s32[16,16]{1,0:T(8,128)} %param.17) | copy-start | bytes 3076
  2.4 8.0 %collective-permute-start = (bf16[96,1024]{1,0:T(8,128)(2,1)S(1)}, bf16[96,1024]{1,0:T(8,128)(2,1)S(1)}, u32[]{:S(2)}, u32[]{:S(2)}) collective-permute-start(bf16[96,1024]{1,0:T(8,128)(2,1)S(1)} %constant_dynamic-update-slice_fusion), channel_id=1, source_target_pairs={{4,0},{5,1},{8,4},{9,5},{12,8},{13,9},{14,12},{15,13},{10,14},{11,... | collective-permute-start | bytes 589832 | tf_op jit(solution)/shard_map/ppermute | solution.py:160
  5.4 6.6 %collective-permute-start.3 = (bf16[96,1024]{1,0:T(8,128)(2,1)S(1)}, bf16[96,1024]{1,0:T(8,128)(2,1)S(1)}, u32[]{:S(2)}, u32[]{:S(2)}) collective-permute-start(bf16[96,1024]{1,0:T(8,128)(2,1)S(1)} %constant_dynamic-update-slice_fusion), channel_id=1, source_target_pairs={{0,4},{1,5},{4,8},{5,9},{8,12},{9,13},{12,14},{13,15},{14,10},{15,... | collective-permute-start | bytes 589832 | tf_op jit(solution)/shard_map/ppermute | solution.py:157
  10.4 6.1 %collective-permute-start.1 = (bf16[96,1024]{1,0:T(8,128)(2,1)S(1)}, bf16[96,1024]{1,0:T(8,128)(2,1)S(1)}, u32[]{:S(2)}, u32[]{:S(2)}) collective-permute-start(bf16[96,1024]{1,0:T(8,128)(2,1)S(1)} %collective-permute-done), channel_id=1, source_target_pairs={{4,0},{5,1},{8,4},{9,5},{12,8},{13,9},{14,12},{15,13},{10,14},{11,... | collective-permute-start | bytes 589832 | tf_op jit(solution)/shard_map/ppermute | solution.py:160
  12.1 5.8 %collective-permute-start.4 = (bf16[96,1024]{1,0:T(8,128)(2,1)S(1)}, bf16[96,1024]{1,0:T(8,128)(2,1)S(1)}, u32[]{:S(2)}, u32[]{:S(2)}) collective-permute-start(bf16[96,1024]{1,0:T(8,128)(2,1)S(1)} %collective-permute-done.3), channel_id=1, source_target_pairs={{0,4},{1,5},{4,8},{5,9},{8,12},{9,13},{12,14},{13,15},{14,10},{15,... | collective-permute-start | bytes 589832 | tf_op jit(solution)/shard_map/ppermute | solution.py:157
  16.5 8.1 %collective-permute-start.2 = (bf16[96,1024]{1,0:T(8,128)(2,1)S(1)}, bf16[96,1024]{1,0:T(8,128)(2,1)S(1)}, u32[]{:S(2)}, u32[]{:S(2)}) collective-permute-start(bf16[96,1024]{1,0:T(8,128)(2,1)S(1)} %collective-permute-done.1), channel_id=1, source_target_pairs={{4,0},{5,1},{8,4},{9,5},{12,8},{13,9},{14,12},{15,13},{10,14},{11,... | collective-permute-start | bytes 589832 | tf_op jit(solution)/shard_map/ppermute | solution.py:160
  17.8 6.1 %collective-permute-start.5 = (bf16[96,1024]{1,0:T(8,128)(2,1)S(1)}, bf16[96,1024]{1,0:T(8,128)(2,1)S(1)}, u32[]{:S(2)}, u32[]{:S(2)}) collective-permute-start(bf16[96,1024]{1,0:T(8,128)(2,1)S(1)} %collective-permute-done.4), channel_id=1, source_target_pairs={{0,4},{1,5},{4,8},{5,9},{8,12},{9,13},{12,14},{13,15},{14,10},{15,... | collective-permute-start | bytes 589832 | tf_op jit(solution)/shard_map/ppermute | solution.py:157
  24.0 5.7 %collective-permute-start.6 = (bf16[96,1024]{1,0:T(8,128)(2,1)S(1)}, bf16[96,1024]{1,0:T(8,128)(2,1)S(1)}, u32[]{:S(2)}, u32[]{:S(2)}) collective-permute-start(bf16[96,1024]{1,0:T(8,128)(2,1)S(1)} %collective-permute-done.5), channel_id=1, source_target_pairs={{0,4},{1,5},{4,8},{5,9},{8,12},{9,13},{12,14},{13,15},{14,10},{15,... | collective-permute-start | bytes 589832 | tf_op jit(solution)/shard_map/ppermute | solution.py:157
  32.5 8.9 %collective-permute-start.7 = (bf16[8,96,1024]{2,1,0:T(8,128)(2,1)}, bf16[8,96,1024]{2,1,0:T(8,128)(2,1)}, u32[]{:S(2)}, u32[]{:S(2)}) collective-permute-start(bf16[8,96,1024]{2,1,0:T(8,128)(2,1)} %get-tuple-element.31), channel_id=1, source_target_pairs={{0,1},{1,0},{2,3},{3,2},{4,5},{5,4},{6,7},{7,6},{8,9},{9,8},{10,11... | collective-permute-start | bytes 4718600 | tf_op jit(solution)/shard_map/ppermute | solution.py:163
  35.8 30.0 %collective-permute-start.15 = (bf16[128,8,32]{0,2,1:T(8,128)(2,1)}, bf16[128,8,32]{0,2,1:T(8,128)(2,1)}, u32[]{:S(2)}, u32[]{:S(2)}) collective-permute-start(bf16[128,8,32]{0,2,1:T(8,128)(2,1)} %dynamic-slice_bitcast_fusion.2), channel_id=1, source_target_pairs={{0,1},{1,0},{2,3},{3,2},{4,5},{5,4},{6,7},{7,6},{8,9},{9,8},{10,11... | collective-permute-start | bytes 196616 | tf_op jit(solution)/shard_map/ppermute | solution.py:247
  53.4 9.1 %collective-permute-start.9 = (bf16[128,1024]{1,0:T(8,128)(2,1)}, bf16[128,1024]{1,0:T(8,128)(2,1)S(1)}, u32[]{:S(2)}, u32[]{:S(2)}) collective-permute-start(bf16[128,1024]{1,0:T(8,128)(2,1)} %get-tuple-element.12), channel_id=1, source_target_pairs={{0,1},{1,0},{2,3},{3,2},{4,5},{5,4},{6,7},{7,6},{8,9},{9,8},{10,11... | collective-permute-start | bytes 786440 | tf_op jit(solution)/shard_map/ppermute | solution.py:250
  58.5 5.8 %collective-permute-start.11 = (bf16[128,1024]{1,0:T(8,128)(2,1)}, bf16[128,1024]{1,0:T(8,128)(2,1)S(1)}, u32[]{:S(2)}, u32[]{:S(2)}) collective-permute-start(bf16[128,1024]{1,0:T(8,128)(2,1)} %get-tuple-element.14), channel_id=1, source_target_pairs={{0,1},{1,0},{2,3},{3,2},{4,5},{5,4},{6,7},{7,6},{8,9},{9,8},{10,11... | collective-permute-start | bytes 786440 | tf_op jit(solution)/shard_map/ppermute | solution.py:250
  59.0 1.6 %collective-permute-start.12 = (f32[1024]{0:T(1024)S(1)}, f32[1024]{0:T(1024)}, u32[]{:S(2)}, u32[]{:S(2)}) collective-permute-start(f32[1024]{0:T(1024)S(1)} %bitcast.188), channel_id=1, source_target_pairs={{0,1},{1,0},{2,3},{3,2},{4,5},{5,4},{6,7},{7,6},{8,9},{9,8},{10,11... | collective-permute-start | bytes 12296 | tf_op jit(solution)/shard_map/ppermute | solution.py:250
  60.0 3.9 %collective-permute-start.14 = (bf16[128,1024]{1,0:T(8,128)(2,1)S(1)}, bf16[128,1024]{1,0:T(8,128)(2,1)S(1)}, u32[]{:S(2)}, u32[]{:S(2)}) collective-permute-start(bf16[128,1024]{1,0:T(8,128)(2,1)S(1)} %copy-done.5), channel_id=1, source_target_pairs={{0,1},{1,0},{2,3},{3,2},{4,5},{5,4},{6,7},{7,6},{8,9},{9,8},{10,11... | collective-permute-start | bytes 786440 | tf_op jit(solution)/shard_map/ppermute | solution.py:250
  60.6 1.4 %collective-permute-start.8 = (bf16[128,8,64]{0,2,1:T(8,128)(2,1)S(1)}, bf16[128,8,64]{0,2,1:T(8,128)(2,1)S(1)}, u32[]{:S(2)}, u32[]{:S(2)}) collective-permute-start(bf16[128,8,64]{0,2,1:T(8,128)(2,1)S(1)} %dynamic-slice_bitcast_fusion.1), channel_id=1, source_target_pairs={{0,1},{1,0},{2,3},{3,2},{4,5},{5,4},{6,7},{7,6},{8,9},{9,8},{10,11... | collective-permute-start | bytes 393224 | tf_op jit(solution)/shard_map/ppermute | solution.py:247
  62.0 2.2 %collective-permute-start.10 = (bf16[128,8,64]{0,2,1:T(8,128)(2,1)S(1)}, bf16[128,8,64]{0,2,1:T(8,128)(2,1)S(1)}, u32[]{:S(2)}, u32[]{:S(2)}) collective-permute-start(bf16[128,8,64]{0,2,1:T(8,128)(2,1)S(1)} %dynamic-slice_bitcast_fusion), channel_id=1, source_target_pairs={{0,1},{1,0},{2,3},{3,2},{4,5},{5,4},{6,7},{7,6},{8,9},{9,8},{10,11... | collective-permute-start | bytes 393224 | tf_op jit(solution)/shard_map/ppermute | solution.py:247
  62.5 1.3 %collective-permute-start.13 = (bf16[128,8,32]{0,2,1:T(8,128)(2,1)S(1)}, bf16[128,8,32]{0,2,1:T(8,128)(2,1)S(1)}, u32[]{:S(2)}, u32[]{:S(2)}) collective-permute-start(bf16[128,8,32]{0,2,1:T(8,128)(2,1)S(1)} %dynamic-slice_bitcast_fusion.3), channel_id=1, source_target_pairs={{0,1},{1,0},{2,3},{3,2},{4,5},{5,4},{6,7},{7,6},{8,9},{9,8},{10,11... | collective-permute-start | bytes 196616 | tf_op jit(solution)/shard_map/ppermute | solution.py:247
  63.7 2.1 %collective-permute-start.16 = (bf16[128,1024]{1,0:T(8,128)(2,1)S(1)}, bf16[128,1024]{1,0:T(8,128)(2,1)S(1)}, u32[]{:S(2)}, u32[]{:S(2)}) collective-permute-start(bf16[128,1024]{1,0:T(8,128)(2,1)S(1)} %copy-done.7), channel_id=1, source_target_pairs={{0,1},{1,0},{2,3},{3,2},{4,5},{5,4},{6,7},{7,6},{8,9},{9,8},{10,11... | collective-permute-start | bytes 786440 | tf_op jit(solution)/shard_map/ppermute | solution.py:250
  65.1 7.8 %collective-permute-start.24 = (f32[48,1024]{1,0:T(8,128)S(1)}, f32[48,1024]{1,0:T(8,128)S(1)}, u32[]{:S(2)}, u32[]{:S(2)}) collective-permute-start(f32[48,1024]{1,0:T(8,128)S(1)} %get-tuple-element.29), channel_id=1, source_target_pairs={{0,4},{1,5},{4,8},{5,9},{8,12},{9,13},{12,14},{13,15},{14,10},{15,... | collective-permute-start | bytes 589832 | tf_op jit(solution)/shard_map/ppermute | solution.py:182
  67.0 10.8 %collective-permute-start.17 = (f32[56,1024]{1,0:T(8,128)S(1)}, f32[56,1024]{1,0:T(8,128)S(1)}, u32[]{:S(2)}, u32[]{:S(2)}) collective-permute-start(f32[56,1024]{1,0:T(8,128)S(1)} %get-tuple-element.23), channel_id=1, source_target_pairs={{0,4},{1,5},{4,8},{5,9},{8,12},{9,13},{12,14},{13,15},{14,10},{15,... | collective-permute-start | bytes 688136 | tf_op jit(solution)/shard_map/ppermute | solution.py:182
  68.8 9.0 %collective-permute-start.20 = (f32[56,1024]{1,0:T(8,128)S(1)}, f32[56,1024]{1,0:T(8,128)S(1)}, u32[]{:S(2)}, u32[]{:S(2)}) collective-permute-start(f32[56,1024]{1,0:T(8,128)S(1)} %get-tuple-element.24), channel_id=1, source_target_pairs={{4,0},{5,1},{8,4},{9,5},{12,8},{13,9},{14,12},{15,13},{10,14},{11,... | collective-permute-start | bytes 688136 | tf_op jit(solution)/shard_map/ppermute | solution.py:188
  69.1 11.6 %collective-permute-start.28 = (f32[48,1024]{1,0:T(8,128)S(1)}, f32[48,1024]{1,0:T(8,128)S(1)}, u32[]{:S(2)}, u32[]{:S(2)}) collective-permute-start(f32[48,1024]{1,0:T(8,128)S(1)} %get-tuple-element.30), channel_id=1, source_target_pairs={{4,0},{5,1},{8,4},{9,5},{12,8},{13,9},{14,12},{15,13},{10,14},{11,... | collective-permute-start | bytes 589832 | tf_op jit(solution)/shard_map/ppermute | solution.py:188
  72.9 9.1 %collective-permute-start.25 = (f32[48,1024]{1,0:T(8,128)S(1)}, f32[48,1024]{1,0:T(8,128)S(1)}, u32[]{:S(2)}, u32[]{:S(2)}) collective-permute-start(f32[48,1024]{1,0:T(8,128)S(1)} %fusion.26), channel_id=1, source_target_pairs={{0,4},{1,5},{4,8},{5,9},{8,12},{9,13},{12,14},{13,15},{14,10},{15,... | collective-permute-start | bytes 589832 | tf_op jit(solution)/shard_map/ppermute | solution.py:182
  77.9 9.1 %collective-permute-start.18 = (f32[56,1024]{1,0:T(8,128)S(1)}, f32[56,1024]{1,0:T(8,128)S(1)}, u32[]{:S(2)}, u32[]{:S(2)}) collective-permute-start(f32[56,1024]{1,0:T(8,128)S(1)} %get-tuple-element.21), channel_id=1, source_target_pairs={{0,4},{1,5},{4,8},{5,9},{8,12},{9,13},{12,14},{13,15},{14,10},{15,... | collective-permute-start | bytes 688136 | tf_op jit(solution)/shard_map/ppermute | solution.py:182
  79.0 7.9 %collective-permute-start.21 = (f32[56,1024]{1,0:T(8,128)S(1)}, f32[56,1024]{1,0:T(8,128)S(1)}, u32[]{:S(2)}, u32[]{:S(2)}) collective-permute-start(f32[56,1024]{1,0:T(8,128)S(1)} %get-tuple-element.22), channel_id=1, source_target_pairs={{4,0},{5,1},{8,4},{9,5},{12,8},{13,9},{14,12},{15,13},{10,14},{11,... | collective-permute-start | bytes 688136 | tf_op jit(solution)/shard_map/ppermute | solution.py:188
  82.1 9.1 %collective-permute-start.26 = (f32[48,1024]{1,0:T(8,128)S(1)}, f32[48,1024]{1,0:T(8,128)S(1)}, u32[]{:S(2)}, u32[]{:S(2)}) collective-permute-start(f32[48,1024]{1,0:T(8,128)S(1)} %get-tuple-element.27), channel_id=1, source_target_pairs={{0,4},{1,5},{4,8},{5,9},{8,12},{9,13},{12,14},{13,15},{14,10},{15,... | collective-permute-start | bytes 589832 | tf_op jit(solution)/shard_map/ppermute | solution.py:182
  82.8 8.4 %collective-permute-start.29 = (f32[48,1024]{1,0:T(8,128)S(1)}, f32[48,1024]{1,0:T(8,128)S(1)}, u32[]{:S(2)}, u32[]{:S(2)}) collective-permute-start(f32[48,1024]{1,0:T(8,128)S(1)} %get-tuple-element.28), channel_id=1, source_target_pairs={{4,0},{5,1},{8,4},{9,5},{12,8},{13,9},{14,12},{15,13},{10,14},{11,... | collective-permute-start | bytes 589832 | tf_op jit(solution)/shard_map/ppermute | solution.py:188
  87.0 8.5 %collective-permute-start.22 = (f32[56,1024]{1,0:T(8,128)S(1)}, f32[56,1024]{1,0:T(8,128)S(1)}, u32[]{:S(2)}, u32[]{:S(2)}) collective-permute-start(f32[56,1024]{1,0:T(8,128)S(1)} %get-tuple-element.20), channel_id=1, source_target_pairs={{4,0},{5,1},{8,4},{9,5},{12,8},{13,9},{14,12},{15,13},{10,14},{11,... | collective-permute-start | bytes 688136 | tf_op jit(solution)/shard_map/ppermute | solution.py:188
  88.7 11.8 %collective-permute-start.19 = (f32[56,1024]{1,0:T(8,128)S(1)}, f32[56,1024]{1,0:T(8,128)S(1)}, u32[]{:S(2)}, u32[]{:S(2)}) collective-permute-start(f32[56,1024]{1,0:T(8,128)S(1)} %get-tuple-element.19), channel_id=1, source_target_pairs={{0,4},{1,5},{4,8},{5,9},{8,12},{9,13},{12,14},{13,15},{14,10},{15,... | collective-permute-start | bytes 688136 | tf_op jit(solution)/shard_map/ppermute | solution.py:182
  91.2 8.5 %collective-permute-start.27 = (f32[48,1024]{1,0:T(8,128)S(1)}, f32[48,1024]{1,0:T(8,128)S(1)}, u32[]{:S(2)}, u32[]{:S(2)}) collective-permute-start(f32[48,1024]{1,0:T(8,128)S(1)} %get-tuple-element.25), channel_id=1, source_target_pairs={{0,4},{1,5},{4,8},{5,9},{8,12},{9,13},{12,14},{13,15},{14,10},{15,... | collective-permute-start | bytes 589832 | tf_op jit(solution)/shard_map/ppermute | solution.py:182
  92.5 7.8 %collective-permute-start.30 = (f32[48,1024]{1,0:T(8,128)S(1)}, f32[48,1024]{1,0:T(8,128)S(1)}, u32[]{:S(2)}, u32[]{:S(2)}) collective-permute-start(f32[48,1024]{1,0:T(8,128)S(1)} %get-tuple-element.26), channel_id=1, source_target_pairs={{4,0},{5,1},{8,4},{9,5},{12,8},{13,9},{14,12},{15,13},{10,14},{11,... | collective-permute-start | bytes 589832 | tf_op jit(solution)/shard_map/ppermute | solution.py:188
  95.5 8.0 %collective-permute-start.23 = (f32[56,1024]{1,0:T(8,128)S(1)}, f32[56,1024]{1,0:T(8,128)S(1)}, u32[]{:S(2)}, u32[]{:S(2)}) collective-permute-start(f32[56,1024]{1,0:T(8,128)S(1)} %fusion.13), channel_id=1, source_target_pairs={{4,0},{5,1},{8,4},{9,5},{12,8},{13,9},{14,12},{15,13},{10,14},{11,... | collective-permute-start | bytes 688136 | tf_op jit(solution)/shard_map/ppermute | solution.py:188
  (14 other events, 113.9 us)

commit v13 on v12

--- a/solution.py
+++ b/solution.py
@@ -61,11 +61,17 @@
     return jnp.maximum(a, 0.0) + jnp.log1p(jnp.exp(-jnp.abs(a)))
 
 
-def twin_body(r_one, x_ref, z_ref, y_ref, m_ref, w_ref, wo_ref,
+def twin_body(r_one, sel_ref, x_ref, z_ref, y_ref, m_ref, mine_ref, other_ref, wo_ref,
               es_ref, g1_ref, ea1_ref, ec1_ref, g2_ref, h1_ref, ea2_ref, g3_ref):
-    blocks, width, hidden = w_ref.shape
-    w1 = w_ref[:, :r_one, :].reshape(blocks * r_one, hidden)
-    w2 = w_ref[:, r_one:, :].reshape(blocks * (width - r_one), hidden)
+    chips = mine_ref.shape[0]
+    ones, twos = [], []
+    for b in range(sel_ref.shape[0]):
+        i = sel_ref[b]
+        block = jnp.where(i < chips, mine_ref[i % chips], other_ref[i % chips])
+        ones.append(block[:r_one])
+        twos.append(block[r_one:])
+    w1 = jnp.concatenate(ones, axis=0)
+    w2 = jnp.concatenate(twos, axis=0)
     wo = wo_ref[...]
     mask = m_ref[...]
     a1 = jnp.dot(x_ref[...], w1, preferred_element_type=jnp.float32)
@@ -98,9 +104,9 @@
     ea2_ref[...] = ea2
 
 
-def twin_fused(x_rows, z_rows, y_rows, mask, w_blocks, r_one, w_three):
+def twin_fused(x_rows, z_rows, y_rows, mask, mine, other, sel, r_one, w_three):
     rows, assets = x_rows.shape
-    blocks, width, hidden = w_blocks.shape
+    chips, width, hidden = mine.shape
     bf, f32 = jnp.bfloat16, jnp.float32
     shapes = (
         jax.ShapeDtypeStruct((rows, assets), bf),
@@ -113,16 +119,17 @@
         jax.ShapeDtypeStruct((1, hidden), f32),
     )
     vmem = pl.BlockSpec(memory_space=pltpu.VMEM)
+    smem = pl.BlockSpec(memory_space=pltpu.SMEM)
     flops = 2 * rows * hidden * (3 * assets + 4 * hidden)
     e_slope, g_one, e_aone, e_cone, g_two, h_one, e_atwo, grad_three = pl.pallas_call(
         functools.partial(twin_body, r_one),
         out_shape=shapes,
-        in_specs=[vmem] * 6,
+        in_specs=[smem] + [vmem] * 7,
         out_specs=[vmem] * 8,
         cost_estimate=pl.CostEstimate(
             flops=flops, transcendentals=6 * rows * hidden,
-            bytes_accessed=2 * blocks * width * hidden + 16 * rows * hidden),
-    )(x_rows, z_rows, y_rows.astype(f32)[:, None], mask[:, None], w_blocks,
+            bytes_accessed=4 * chips * width * hidden + 16 * rows * hidden),
+    )(sel, x_rows, z_rows, y_rows.astype(f32)[:, None], mask[:, None], mine, other,
       w_three.astype(f32)[None, :])
     return (e_slope, g_one, e_aone, e_cone, g_two, h_one, e_atwo, grad_three[0])
 
@@ -161,12 +168,11 @@
             rel[s] = right
     mine = jnp.stack(rel)
     other = lax.ppermute(mine, "blk", partner)
-    both = jnp.concatenate([mine, other], axis=0)
     dest = jnp.arange(n_blk, dtype=jnp.int32)
     dest_chip, dest_core = dest // 2, dest % 2
     k = (jnp.asarray(place, jnp.int32)[dest_chip] - spot) % chips
     index = jnp.where(dest_core == core, 0, chips) + k
-    return jnp.take(both, index, axis=0, mode="clip")
+    return mine, other, index
 
 
 def ring_reduce_scatter(summed, n_blk):
@@ -219,21 +225,23 @@
     rows_dev = paths.shape[0]
     r_one, r_two = w_first.shape[0], w_second.shape[0]
     hidden = w_first.shape[1]
-    gathered = ring_all_gather(jnp.concatenate([w_first, w_second], axis=0), n_blk)
-    if r_one % 16 or r_two % 16:
-        gathered = jnp.concatenate(
-            [gathered[:, :r_one].reshape(1, n_blk * r_one, hidden),
-             gathered[:, r_one:].reshape(1, n_blk * r_two, hidden)], axis=1)
-        split_at = n_blk * r_one
-    else:
-        split_at = r_one
+    mine, other, index = ring_all_gather(jnp.concatenate([w_first, w_second], axis=0), n_blk)
+    fused = r_one % 16 == 0 and r_two % 16 == 0
+    if not fused:
+        gathered = jnp.take(
+            jnp.concatenate([mine, other], axis=0), index, axis=0, mode="clip"
+        )
+        w_one = gathered[:, :r_one].reshape(n_blk * r_one, hidden)
+        w_two = gathered[:, r_one:].reshape(n_blk * r_two, hidden)
     sending = lax.dynamic_index_in_dim(counts, position, 0, keepdims=False)
     x_rows, z_rows, y_rows = (paths, deltas, payoffs)
     total = jnp.sum(sending)
     mask = (jnp.arange(rows_dev, dtype=jnp.int32) < total).astype(jnp.float32)
-    e_slope, g_one, e_aone, e_cone, g_two, h_one, e_atwo, grad_three = twin_fused(
-        x_rows, z_rows, y_rows, mask, gathered, split_at, w_out
-    )
+    if fused:
+        terms = twin_fused(x_rows, z_rows, y_rows, mask, mine, other, index, r_one, w_out)
+    else:
+        terms = twin_terms(x_rows, z_rows, y_rows, mask, w_one, w_two, w_out)
+    e_slope, g_one, e_aone, e_cone, g_two, h_one, e_atwo, grad_three = terms
     chip = position // 2
     spot = jnp.asarray(place, jnp.int32)[chip]
     ring_chips = jnp.asarray(snake, jnp.int32)[(spot + jnp.arange(chips, dtype=jnp.int32)) % chips]

time: 108 us -> 107 us (level)
  local copies, waits for them, and re-layouts: 18.9 us -> 12.1 us
  matrix products: 7.08 us -> 10.1 us
  waiting for transfers between devices: 40.4 us -> 42.9 us
    ppermute x7, waiting for transfers between devices: 6.65 us -> 11.3 us  [backward(): acc = lax.ppermute(acc, 'blk', ccw)]
    ppermute x7, waiting for transfers between devices: 16.5 us -> 12.2 us  [forward(): acc = lax.ppermute(acc, 'blk', cw) + part[(window - s) % chips]]
    unnamed x39 -> x37, local copies, waits for them, and re-layouts: 6.12 us -> 2.3 us
    ppermute x7, starting transfers between devices: 6.89 us -> 3.28 us  [backward(): acc = lax.ppermute(acc, 'blk', ccw)]
    ppermute x7, starting transfers between devices: 6.71 us -> 9.79 us  [forward(): acc = lax.ppermute(acc, 'blk', cw) + part[(window - s) % chips]]
    dot_general x8, matrix products: 7.08 us -> 10.1 us  [slots_product(): lax.dot_general(left, right, (((0,), (0,)), ((), ())), preferred_element_...]
    gather x1 -> x0, local copies, waits for them, and re-layouts: 2.4 us -> none  [ring_all_gather(): return jnp.take(both, index, axis=0, mode='clip')]
    concatenate x1 -> x0, local copies, waits for them, and re-layouts: 1.6 us -> none  [ring_all_gather(): both = jnp.concatenate([mine, other], axis=0)]
  transfers between devices with their start and end apart: 31 -> 31, of which waited for: 15 -> 16; matrix products, arithmetic and copies ran while one was open for 25% -> 24% of each run, Pallas kernels for 6% -> 6%
where the time goes in v13:
time: 107 us
  waiting for transfers between devices  42.9 us (40%)
  starting transfers between devices  23.5 us (22%)
  local copies, waits for them, and re-layouts  12.1 us (11%)
  matrix products  10.1 us (9%)
  other arithmetic  10 us (9%)
  Pallas kernels  6.14 us (6%)
  between operations  1.85 us (2%)
    ppermute x7, waiting for transfers between devices, forward(): acc = lax.ppermute(acc, 'blk', cw) + part[(window - s) % chips]  12.2 us
    ppermute x7, waiting for transfers between devices, backward(): acc = lax.ppermute(acc, 'blk', ccw)  11.3 us
    ppermute x4, waiting for transfers between devices, ring_all_gather(): left = lax.ppermute(left, 'blk', cw)  10.4 us
    dot_general x8, matrix products, slots_product(): lax.dot_general(left, right, (((0,), (0,)), ((), ())), preferred_element_...  10.1 us
    ppermute x7, starting transfers between devices, forward(): acc = lax.ppermute(acc, 'blk', cw) + part[(window - s) % chips]  9.79 us
    ppermute x3, waiting for transfers between devices, ring_all_gather(): right = lax.ppermute(right, 'blk', ccw)  8.84 us
    pallas_call x1, Pallas kernels, twin_fused(): pl.pallas_call(functools.partial(twin_body, r_one), out_shape=shapes, in_...  6.14 us
    ppermute x3, starting transfers between devices, ring_all_gather(): right = lax.ppermute(right, 'blk', ccw)  6.07 us
  transfers between devices with their start and end apart: 31, of which 16 were waited for; matrix products, arithmetic and copies ran while one was open for 24% of the time, Pallas kernels for 6%

profile of v13, /device:TPU:0, one launch (start us, length us, event | category | flops | bytes accessed | tf_op | source)
XLA Modules:
  0.0 106.5 jit_solution(8752277923640828858)
XLA Ops:
  2.4 3.0 %collective-permute-start = (bf16[96,1024]{1,0:T(8,128)(2,1)S(1)}, bf16[96,1024]{1,0:T(8,128)(2,1)S(1)}, u32[]{:S(2)}, u32[]{:S(2)}) collective-permute-start(bf16[96,1024]{1,0:T(8,128)(2,1)S(1)} %constant_dynamic-update-slice_fusion), channel_id=1, source_target_pairs={{4,0},{5,1},{8,4},{9,5},{12,8},{13,9},{14,12},{15,13},{10,14},{11,... | collective-permute-start | bytes 589832 | tf_op jit(solution)/shard_map/ppermute | solution.py:167
  5.6 4.8 %collective-permute-done = bf16[96,1024]{1,0:T(8,128)(2,1)S(1)} collective-permute-done((bf16[96,1024]{1,0:T(8,128)(2,1)S(1)}, bf16[96,1024]{1,0:T(8,128)(2,1)S(1)}, u32[]{:S(2)}, u32[]{:S(2)}) %collective-permute-start) | collective-permute-done | bytes 196640 | tf_op jit(solution)/shard_map/ppermute | solution.py:167
  10.4 1.7 %collective-permute-start.1 = (bf16[96,1024]{1,0:T(8,128)(2,1)S(1)}, bf16[96,1024]{1,0:T(8,128)(2,1)S(1)}, u32[]{:S(2)}, u32[]{:S(2)}) collective-permute-start(bf16[96,1024]{1,0:T(8,128)(2,1)S(1)} %collective-permute-done), channel_id=1, source_target_pairs={{4,0},{5,1},{8,4},{9,5},{12,8},{13,9},{14,12},{15,13},{10,14},{11,... | collective-permute-start | bytes 589832 | tf_op jit(solution)/shard_map/ppermute | solution.py:167
  12.4 4.0 %collective-permute-done.1 = bf16[96,1024]{1,0:T(8,128)(2,1)S(1)} collective-permute-done((bf16[96,1024]{1,0:T(8,128)(2,1)S(1)}, bf16[96,1024]{1,0:T(8,128)(2,1)S(1)}, u32[]{:S(2)}, u32[]{:S(2)}) %collective-permute-start.1) | collective-permute-done | bytes 196640 | tf_op jit(solution)/shard_map/ppermute | solution.py:167
  16.5 1.4 %collective-permute-start.2 = (bf16[96,1024]{1,0:T(8,128)(2,1)S(1)}, bf16[96,1024]{1,0:T(8,128)(2,1)S(1)}, u32[]{:S(2)}, u32[]{:S(2)}) collective-permute-start(bf16[96,1024]{1,0:T(8,128)(2,1)S(1)} %collective-permute-done.1), channel_id=1, source_target_pairs={{4,0},{5,1},{8,4},{9,5},{12,8},{13,9},{14,12},{15,13},{10,14},{11,... | collective-permute-start | bytes 589832 | tf_op jit(solution)/shard_map/ppermute | solution.py:167
  18.5 5.4 %collective-permute-done.5 = bf16[96,1024]{1,0:T(8,128)(2,1)S(1)} collective-permute-done((bf16[96,1024]{1,0:T(8,128)(2,1)S(1)}, bf16[96,1024]{1,0:T(8,128)(2,1)S(1)}, u32[]{:S(2)}, u32[]{:S(2)}) %collective-permute-start.5) | collective-permute-done | bytes 196640 | tf_op jit(solution)/shard_map/ppermute | solution.py:164
  24.6 5.0 %collective-permute-done.6 = bf16[96,1024]{1,0:T(8,128)(2,1)S(1)} collective-permute-done((bf16[96,1024]{1,0:T(8,128)(2,1)S(1)}, bf16[96,1024]{1,0:T(8,128)(2,1)S(1)}, u32[]{:S(2)}, u32[]{:S(2)}) %collective-permute-start.6) | collective-permute-done | bytes 196640 | tf_op jit(solution)/shard_map/ppermute | solution.py:164
  36.9 1.3 %fusion.42.m_ref = f32[128,1]{1,0:T(8,128)} fusion(s32[]{:T(128)} %fusion.51), kind=kLoop, calls=%fused_computation.83 | loop fusion | flops 256 | bytes 516 | tf_op jit(solution)/shard_map/convert_element_type | solution.py:239
  38.1 1.2 %fusion.47.sel_ref = s32[16]{0:T(128)} fusion(s32[16]{0:T(128)S(1)} %gather_fusion, s32[]{:T(128)} %bitcast.1, s32[]{:T(128)S(6)} %select_n.100), kind=kLoop, calls=%fused_computation.112 | loop fusion | flops 336 | bytes 136 | tf_op jit(solution)/shard_map/add | solution.py:174
  39.3 1.2 %copy-done.12 = bf16[8,96,1024]{2,1,0:T(8,128)(2,1)} copy-done((bf16[8,96,1024]{2,1,0:T(8,128)(2,1)}, bf16[8,96,1024]{2,1,0:T(8,128)(2,1)S(1)}, u32[]{:S(2)}) %copy-start.12) | copy-done | bytes 1572888
  40.5 6.1 %shard_map.157 = (bf16[128,512]{1,0:T(8,128)(2,1)}, bf16[128,1024]{1,0:T(8,128)(2,1)}, bf16[128,1024]{1,0:T(8,128)(2,1)}, bf16[128,1024]{1,0:T(8,128)(2,1)}, bf1...) custom-call(s32[16]{0:T(128)} %fusion.47.sel_ref, ...), custom_call_target="tpu_custom_call" | custom-call | flops 1476395008 | bytes 5242880 | tf_op jit(solution)/shard_map/pallas_call | solution.py:124
  46.6 1.1 %copy.19 = bf16[128,1024]{0,1:T(8,128)(2,1)S(1)} copy(bf16[128,1024]{1,0:T(8,128)(2,1)} %get-tuple-element.11) | data formatting | bytes 524288 | tf_op jit(solution)/shard_map/pallas_call | solution.py:124
  49.3 1.4 %fusion.17 = f32[8,64,1024]{2,1,0:T(8,128)S(1)} fusion(bf16[128,1024]{1,0:T(8,128)(2,1)} %get-tuple-element.12, bf16[8,128,2,64]{1,3,2,0:T(8,128)(2,1)S(1)} %gather_fusion.2, s32[]{:T(128)S(6)} %select_n.110), kind=kOutput, calls=%fused_computation.24 | convolution fusion | flops 134217728 | bytes 2490372 | tf_op jit(solution)/shard_map/dot_general | solution.py:213
  51.5 2.7 %fusion.13 = f32[8,64,1024]{2,1,0:T(8,128)} fusion(bf16[128,1024]{1,0:T(8,128)(2,1)} %get-tuple-element.14, bf16[8,128,2,64]{1,3,2,0:T(8,128)(2,1)S(1)} %gather_fusion.3, s32[]{:T(128)S(6)} %select_n.110), kind=kOutput, calls=%fused_computation.20 | convolution fusion | flops 134217728 | bytes 2490372 | tf_op jit(solution)/shard_map/dot_general | solution.py:213
  54.5 1.2 %fusion.4 = f32[8,32,1024]{2,1,0:T(8,128)S(1)} fusion(bf16[128,1024]{1,0:T(8,128)(2,1)} %get-tuple-element.18, bf16[8,128,2,32]{1,3,2,0:T(8,128)(2,1)S(1)} %gather_fusion.5, s32[]{:T(128)S(6)} %select_n.110), kind=kOutput, calls=%fused_computation.13 | convolution fusion | flops 67108864 | bytes 1376260 | tf_op jit(solution)/shard_map/dot_general | solution.py:213
  60.4 1.4 %fusion.15 = f32[8,64,1024]{2,1,0:T(8,128)S(1)} fusion(bf16[128,8,64]{0,2,1:T(8,128)(2,1)S(1)} %collective-permute-done.8, bf16[128,1024]{1,0:T(8,128)(2,1)} %collective-permute-done.9), kind=kOutput, calls=%fused_computation.22 | convolution fusion | flops 134217728 | bytes 2490368 | tf_op jit(solution)/shard_map/dot_general | solution.py:213
  62.1 1.5 %add_add_fusion = f32[8,64,1024]{2,1,0:T(8,128)S(1)} fusion(f32[8,64,1024]{2,1,0:T(8,128)S(1)} %copy-done.3, f32[8,64,1024]{2,1,0:T(8,128)S(1)} %fusion.17, f32[8,64,1024]{2,1,0:T(8,128)S(1)} %fusion.15, bf16[128,8,64]{0,2,1:T(8,128)(2,1)S(1)} %collective-permute-done.10, bf16[128,1024]{1,0:T(8,128)(2,1)} %collective-permute-done.11), kind=kOutput, calls=%fused_computation.6 | convolution fusion | flops 135790592 | bytes 8781824 | tf_op jit(solution)/shard_map/dot_general | solution.py:213
  64.7 1.3 %fusion.2 = f32[8,32,1024]{2,1,0:T(8,128)S(1)} fusion(bf16[128,8,32]{0,2,1:T(8,128)(2,1)} %collective-permute-done.15, bf16[128,1024]{1,0:T(8,128)(2,1)} %collective-permute-done.16), kind=kOutput, calls=%fused_computation.11 | convolution fusion | flops 67108864 | bytes 1376256 | tf_op jit(solution)/shard_map/dot_general | solution.py:213
  66.4 1.8 %collective-permute-start.17 = (f32[56,1024]{1,0:T(8,128)S(1)}, f32[56,1024]{1,0:T(8,128)S(1)}, u32[]{:S(2)}, u32[]{:S(2)}) collective-permute-start(f32[56,1024]{1,0:T(8,128)S(1)} %get-tuple-element.23), channel_id=1, source_target_pairs={{0,4},{1,5},{4,8},{5,9},{8,12},{9,13},{12,14},{13,15},{14,10},{15,... | collective-permute-start | bytes 688136 | tf_op jit(solution)/shard_map/ppermute | solution.py:188
  68.4 1.4 %collective-permute-start.28 = (f32[48,1024]{1,0:T(8,128)S(1)}, f32[48,1024]{1,0:T(8,128)S(1)}, u32[]{:S(2)}, u32[]{:S(2)}) collective-permute-start(f32[48,1024]{1,0:T(8,128)S(1)} %get-tuple-element.30), channel_id=1, source_target_pairs={{4,0},{5,1},{8,4},{9,5},{12,8},{13,9},{14,12},{15,13},{10,14},{11,... | collective-permute-start | bytes 589832 | tf_op jit(solution)/shard_map/ppermute | solution.py:194
  69.8 1.6 %collective-permute-done.24 = f32[48,1024]{1,0:T(8,128)S(1)} collective-permute-done((f32[48,1024]{1,0:T(8,128)S(1)}, f32[48,1024]{1,0:T(8,128)S(1)}, u32[]{:S(2)}, u32[]{:S(2)}) %collective-permute-start.24) | collective-permute-done | bytes 196640 | tf_op jit(solution)/shard_map/ppermute | solution.py:188
  72.0 4.3 %collective-permute-done.17 = f32[56,1024]{1,0:T(8,128)S(1)} collective-permute-done((f32[56,1024]{1,0:T(8,128)S(1)}, f32[56,1024]{1,0:T(8,128)S(1)}, u32[]{:S(2)}, u32[]{:S(2)}) %collective-permute-start.17) | collective-permute-done | bytes 229408 | tf_op jit(solution)/shard_map/ppermute | solution.py:188
  76.8 1.6 %collective-permute-start.18 = (f32[56,1024]{1,0:T(8,128)S(1)}, f32[56,1024]{1,0:T(8,128)S(1)}, u32[]{:S(2)}, u32[]{:S(2)}) collective-permute-start(f32[56,1024]{1,0:T(8,128)S(1)} %get-tuple-element.21), channel_id=1, source_target_pairs={{0,4},{1,5},{4,8},{5,9},{8,12},{9,13},{12,14},{13,15},{14,10},{15,... | collective-permute-start | bytes 688136 | tf_op jit(solution)/shard_map/ppermute | solution.py:188
  78.8 1.9 %collective-permute-done.28 = f32[48,1024]{1,0:T(8,128)S(1)} collective-permute-done((f32[48,1024]{1,0:T(8,128)S(1)}, f32[48,1024]{1,0:T(8,128)S(1)}, u32[]{:S(2)}, u32[]{:S(2)}) %collective-permute-start.28) | collective-permute-done | bytes 196640 | tf_op jit(solution)/shard_map/ppermute | solution.py:194
  80.8 1.6 %collective-permute-start.26 = (f32[48,1024]{1,0:T(8,128)S(1)}, f32[48,1024]{1,0:T(8,128)S(1)}, u32[]{:S(2)}, u32[]{:S(2)}) collective-permute-start(f32[48,1024]{1,0:T(8,128)S(1)} %get-tuple-element.27), channel_id=1, source_target_pairs={{0,4},{1,5},{4,8},{5,9},{8,12},{9,13},{12,14},{13,15},{14,10},{15,... | collective-permute-start | bytes 589832 | tf_op jit(solution)/shard_map/ppermute | solution.py:188
  82.9 2.6 %collective-permute-done.18 = f32[56,1024]{1,0:T(8,128)S(1)} collective-permute-done((f32[56,1024]{1,0:T(8,128)S(1)}, f32[56,1024]{1,0:T(8,128)S(1)}, u32[]{:S(2)}, u32[]{:S(2)}) %collective-permute-start.18) | collective-permute-done | bytes 229408 | tf_op jit(solution)/shard_map/ppermute | solution.py:188
  87.2 1.5 %collective-permute-start.19 = (f32[56,1024]{1,0:T(8,128)S(1)}, f32[56,1024]{1,0:T(8,128)S(1)}, u32[]{:S(2)}, u32[]{:S(2)}) collective-permute-start(f32[56,1024]{1,0:T(8,128)S(1)} %get-tuple-element.19), channel_id=1, source_target_pairs={{0,4},{1,5},{4,8},{5,9},{8,12},{9,13},{12,14},{13,15},{14,10},{15,... | collective-permute-start | bytes 688136 | tf_op jit(solution)/shard_map/ppermute | solution.py:188
  90.4 2.0 %collective-permute-start.27 = (f32[48,1024]{1,0:T(8,128)S(1)}, f32[48,1024]{1,0:T(8,128)S(1)}, u32[]{:S(2)}, u32[]{:S(2)}) collective-permute-start(f32[48,1024]{1,0:T(8,128)S(1)} %get-tuple-element.25), channel_id=1, source_target_pairs={{0,4},{1,5},{4,8},{5,9},{8,12},{9,13},{12,14},{13,15},{14,10},{15,... | collective-permute-start | bytes 589832 | tf_op jit(solution)/shard_map/ppermute | solution.py:188
  92.5 2.8 %collective-permute-done.22 = f32[56,1024]{1,0:T(8,128)S(1)} collective-permute-done((f32[56,1024]{1,0:T(8,128)S(1)}, f32[56,1024]{1,0:T(8,128)S(1)}, u32[]{:S(2)}, u32[]{:S(2)}) %collective-permute-start.22) | collective-permute-done | bytes 229408 | tf_op jit(solution)/shard_map/ppermute | solution.py:194
  95.4 2.7 %collective-permute-done.27 = f32[48,1024]{1,0:T(8,128)S(1)} collective-permute-done((f32[48,1024]{1,0:T(8,128)S(1)}, f32[48,1024]{1,0:T(8,128)S(1)}, u32[]{:S(2)}, u32[]{:S(2)}) %collective-permute-start.27) | collective-permute-done | bytes 196640 | tf_op jit(solution)/shard_map/ppermute | solution.py:188
  98.1 2.1 %collective-permute-done.30 = f32[48,1024]{1,0:T(8,128)S(1)} collective-permute-done((f32[48,1024]{1,0:T(8,128)S(1)}, f32[48,1024]{1,0:T(8,128)S(1)}, u32[]{:S(2)}, u32[]{:S(2)}) %collective-permute-start.30) | collective-permute-done | bytes 196640 | tf_op jit(solution)/shard_map/ppermute | solution.py:194
  100.3 2.4 %collective-permute-done.23 = f32[56,1024]{1,0:T(8,128)S(1)} collective-permute-done((f32[56,1024]{1,0:T(8,128)S(1)}, f32[56,1024]{1,0:T(8,128)S(1)}, u32[]{:S(2)}, u32[]{:S(2)}) %collective-permute-start.23) | collective-permute-done | bytes 229408 | tf_op jit(solution)/shard_map/ppermute | solution.py:194
  (126 shorter events, 28.7 us)
Async XLA Ops:
  0.6 35.0 %copy-start = (s32[16,16]{1,0:T(8,128)S(1)}, s32[16,16]{1,0:T(8,128)}, u32[]{:S(2)}) copy-start(s32[16,16]{1,0:T(8,128)} %param.17) | copy-start | bytes 3076
  2.4 8.0 %collective-permute-start = (bf16[96,1024]{1,0:T(8,128)(2,1)S(1)}, bf16[96,1024]{1,0:T(8,128)(2,1)S(1)}, u32[]{:S(2)}, u32[]{:S(2)}) collective-permute-start(bf16[96,1024]{1,0:T(8,128)(2,1)S(1)} %constant_dynamic-update-slice_fusion), channel_id=1, source_target_pairs={{4,0},{5,1},{8,4},{9,5},{12,8},{13,9},{14,12},{15,13},{10,14},{11,... | collective-permute-start | bytes 589832 | tf_op jit(solution)/shard_map/ppermute | solution.py:167
  5.4 6.6 %collective-permute-start.3 = (bf16[96,1024]{1,0:T(8,128)(2,1)S(1)}, bf16[96,1024]{1,0:T(8,128)(2,1)S(1)}, u32[]{:S(2)}, u32[]{:S(2)}) collective-permute-start(bf16[96,1024]{1,0:T(8,128)(2,1)S(1)} %constant_dynamic-update-slice_fusion), channel_id=1, source_target_pairs={{0,4},{1,5},{4,8},{5,9},{8,12},{9,13},{12,14},{13,15},{14,10},{15,... | collective-permute-start | bytes 589832 | tf_op jit(solution)/shard_map/ppermute | solution.py:164
  10.4 6.1 %collective-permute-start.1 = (bf16[96,1024]{1,0:T(8,128)(2,1)S(1)}, bf16[96,1024]{1,0:T(8,128)(2,1)S(1)}, u32[]{:S(2)}, u32[]{:S(2)}) collective-permute-start(bf16[96,1024]{1,0:T(8,128)(2,1)S(1)} %collective-permute-done), channel_id=1, source_target_pairs={{4,0},{5,1},{8,4},{9,5},{12,8},{13,9},{14,12},{15,13},{10,14},{11,... | collective-permute-start | bytes 589832 | tf_op jit(solution)/shard_map/ppermute | solution.py:167
  12.1 5.8 %collective-permute-start.4 = (bf16[96,1024]{1,0:T(8,128)(2,1)S(1)}, bf16[96,1024]{1,0:T(8,128)(2,1)S(1)}, u32[]{:S(2)}, u32[]{:S(2)}) collective-permute-start(bf16[96,1024]{1,0:T(8,128)(2,1)S(1)} %collective-permute-done.3), channel_id=1, source_target_pairs={{0,4},{1,5},{4,8},{5,9},{8,12},{9,13},{12,14},{13,15},{14,10},{15,... | collective-permute-start | bytes 589832 | tf_op jit(solution)/shard_map/ppermute | solution.py:164
  16.5 8.1 %collective-permute-start.2 = (bf16[96,1024]{1,0:T(8,128)(2,1)S(1)}, bf16[96,1024]{1,0:T(8,128)(2,1)S(1)}, u32[]{:S(2)}, u32[]{:S(2)}) collective-permute-start(bf16[96,1024]{1,0:T(8,128)(2,1)S(1)} %collective-permute-done.1), channel_id=1, source_target_pairs={{4,0},{5,1},{8,4},{9,5},{12,8},{13,9},{14,12},{15,13},{10,14},{11,... | collective-permute-start | bytes 589832 | tf_op jit(solution)/shard_map/ppermute | solution.py:167
  17.9 6.1 %collective-permute-start.5 = (bf16[96,1024]{1,0:T(8,128)(2,1)S(1)}, bf16[96,1024]{1,0:T(8,128)(2,1)S(1)}, u32[]{:S(2)}, u32[]{:S(2)}) collective-permute-start(bf16[96,1024]{1,0:T(8,128)(2,1)S(1)} %collective-permute-done.4), channel_id=1, source_target_pairs={{0,4},{1,5},{4,8},{5,9},{8,12},{9,13},{12,14},{13,15},{14,10},{15,... | collective-permute-start | bytes 589832 | tf_op jit(solution)/shard_map/ppermute | solution.py:164
  24.0 5.7 %collective-permute-start.6 = (bf16[96,1024]{1,0:T(8,128)(2,1)S(1)}, bf16[96,1024]{1,0:T(8,128)(2,1)S(1)}, u32[]{:S(2)}, u32[]{:S(2)}) collective-permute-start(bf16[96,1024]{1,0:T(8,128)(2,1)S(1)} %collective-permute-done.5), channel_id=1, source_target_pairs={{0,4},{1,5},{4,8},{5,9},{8,12},{9,13},{12,14},{13,15},{14,10},{15,... | collective-permute-start | bytes 589832 | tf_op jit(solution)/shard_map/ppermute | solution.py:164
  29.8 9.6 %collective-permute-start.7 = (bf16[8,96,1024]{2,1,0:T(8,128)(2,1)S(1)}, bf16[8,96,1024]{2,1,0:T(8,128)(2,1)S(1)}, u32[]{:S(2)}, u32[]{:S(2)}) collective-permute-start(bf16[8,96,1024]{2,1,0:T(8,128)(2,1)S(1)} %bitcast_dynamic-update-slice_fusion.mine_ref), channel_id=1, source_target_pairs={{0,1},{1,0},{2,3},{3,2},{4,5},{5,4},{6,7},{7,6},{8,9},{9,8},{10,11... | collective-permute-start | bytes 4718600 | tf_op jit(solution)/shard_map/ppermute | solution.py:170
  33.3 31.3 %collective-permute-start.15 = (bf16[128,8,32]{0,2,1:T(8,128)(2,1)}, bf16[128,8,32]{0,2,1:T(8,128)(2,1)}, u32[]{:S(2)}, u32[]{:S(2)}) collective-permute-start(bf16[128,8,32]{0,2,1:T(8,128)(2,1)} %dynamic-slice_bitcast_fusion.2), channel_id=1, source_target_pairs={{0,1},{1,0},{2,3},{3,2},{4,5},{5,4},{6,7},{7,6},{8,9},{9,8},{10,11... | collective-permute-start | bytes 196616 | tf_op jit(solution)/shard_map/ppermute | solution.py:255
  49.0 11.1 %collective-permute-start.9 = (bf16[128,1024]{1,0:T(8,128)(2,1)}, bf16[128,1024]{1,0:T(8,128)(2,1)}, u32[]{:S(2)}, u32[]{:S(2)}) collective-permute-start(bf16[128,1024]{1,0:T(8,128)(2,1)} %get-tuple-element.12), channel_id=1, source_target_pairs={{0,1},{1,0},{2,3},{3,2},{4,5},{5,4},{6,7},{7,6},{8,9},{9,8},{10,11... | collective-permute-start | bytes 786440 | tf_op jit(solution)/shard_map/ppermute | solution.py:258
  54.2 7.9 %collective-permute-start.11 = (bf16[128,1024]{1,0:T(8,128)(2,1)}, bf16[128,1024]{1,0:T(8,128)(2,1)}, u32[]{:S(2)}, u32[]{:S(2)}) collective-permute-start(bf16[128,1024]{1,0:T(8,128)(2,1)} %get-tuple-element.14), channel_id=1, source_target_pairs={{0,1},{1,0},{2,3},{3,2},{4,5},{5,4},{6,7},{7,6},{8,9},{9,8},{10,11... | collective-permute-start | bytes 786440 | tf_op jit(solution)/shard_map/ppermute | solution.py:258
  55.7 8.9 %collective-permute-start.16 = (bf16[128,1024]{1,0:T(8,128)(2,1)}, bf16[128,1024]{1,0:T(8,128)(2,1)}, u32[]{:S(2)}, u32[]{:S(2)}) collective-permute-start(bf16[128,1024]{1,0:T(8,128)(2,1)} %get-tuple-element.18), channel_id=1, source_target_pairs={{0,1},{1,0},{2,3},{3,2},{4,5},{5,4},{6,7},{7,6},{8,9},{9,8},{10,11... | collective-permute-start | bytes 786440 | tf_op jit(solution)/shard_map/ppermute | solution.py:258
  56.0 1.9 %collective-permute-start.12 = (f32[1024]{0:T(1024)}, f32[1024]{0:T(1024)}, u32[]{:S(2)}, u32[]{:S(2)}) collective-permute-start(f32[1024]{0:T(1024)} %bitcast.27), channel_id=1, source_target_pairs={{0,1},{1,0},{2,3},{3,2},{4,5},{5,4},{6,7},{7,6},{8,9},{9,8},{10,11... | collective-permute-start | bytes 12296 | tf_op jit(solution)/shard_map/ppermute | solution.py:258
  57.9 1.9 %collective-permute-start.8 = (bf16[128,8,64]{0,2,1:T(8,128)(2,1)}, bf16[128,8,64]{0,2,1:T(8,128)(2,1)S(1)}, u32[]{:S(2)}, u32[]{:S(2)}) collective-permute-start(bf16[128,8,64]{0,2,1:T(8,128)(2,1)} %dynamic-slice_bitcast_fusion.1), channel_id=1, source_target_pairs={{0,1},{1,0},{2,3},{3,2},{4,5},{5,4},{6,7},{7,6},{8,9},{9,8},{10,11... | collective-permute-start | bytes 393224 | tf_op jit(solution)/shard_map/ppermute | solution.py:255
  59.9 1.9 %collective-permute-start.10 = (bf16[128,8,64]{0,2,1:T(8,128)(2,1)S(1)}, bf16[128,8,64]{0,2,1:T(8,128)(2,1)S(1)}, u32[]{:S(2)}, u32[]{:S(2)}) collective-permute-start(bf16[128,8,64]{0,2,1:T(8,128)(2,1)S(1)} %dynamic-slice_bitcast_fusion), channel_id=1, source_target_pairs={{0,1},{1,0},{2,3},{3,2},{4,5},{5,4},{6,7},{7,6},{8,9},{9,8},{10,11... | collective-permute-start | bytes 393224 | tf_op jit(solution)/shard_map/ppermute | solution.py:255
  60.2 4.2 %collective-permute-start.13 = (bf16[128,8,32]{0,2,1:T(8,128)(2,1)S(1)}, bf16[128,8,32]{0,2,1:T(8,128)(2,1)S(1)}, u32[]{:S(2)}, u32[]{:S(2)}) collective-permute-start(bf16[128,8,32]{0,2,1:T(8,128)(2,1)S(1)} %dynamic-slice_bitcast_fusion.3), channel_id=1, source_target_pairs={{0,1},{1,0},{2,3},{3,2},{4,5},{5,4},{6,7},{7,6},{8,9},{9,8},{10,11... | collective-permute-start | bytes 196616 | tf_op jit(solution)/shard_map/ppermute | solution.py:255
  61.8 2.6 %collective-permute-start.14 = (bf16[128,1024]{1,0:T(8,128)(2,1)S(1)}, bf16[128,1024]{1,0:T(8,128)(2,1)S(1)}, u32[]{:S(2)}, u32[]{:S(2)}) collective-permute-start(bf16[128,1024]{1,0:T(8,128)(2,1)S(1)} %copy-done.5), channel_id=1, source_target_pairs={{0,1},{1,0},{2,3},{3,2},{4,5},{5,4},{6,7},{7,6},{8,9},{9,8},{10,11... | collective-permute-start | bytes 786440 | tf_op jit(solution)/shard_map/ppermute | solution.py:258
  63.6 7.8 %collective-permute-start.24 = (f32[48,1024]{1,0:T(8,128)S(1)}, f32[48,1024]{1,0:T(8,128)S(1)}, u32[]{:S(2)}, u32[]{:S(2)}) collective-permute-start(f32[48,1024]{1,0:T(8,128)S(1)} %get-tuple-element.29), channel_id=1, source_target_pairs={{0,4},{1,5},{4,8},{5,9},{8,12},{9,13},{12,14},{13,15},{14,10},{15,... | collective-permute-start | bytes 589832 | tf_op jit(solution)/shard_map/ppermute | solution.py:188
  66.4 10.0 %collective-permute-start.17 = (f32[56,1024]{1,0:T(8,128)S(1)}, f32[56,1024]{1,0:T(8,128)S(1)}, u32[]{:S(2)}, u32[]{:S(2)}) collective-permute-start(f32[56,1024]{1,0:T(8,128)S(1)} %get-tuple-element.23), channel_id=1, source_target_pairs={{0,4},{1,5},{4,8},{5,9},{8,12},{9,13},{12,14},{13,15},{14,10},{15,... | collective-permute-start | bytes 688136 | tf_op jit(solution)/shard_map/ppermute | solution.py:188
  68.2 8.5 %collective-permute-start.20 = (f32[56,1024]{1,0:T(8,128)S(1)}, f32[56,1024]{1,0:T(8,128)S(1)}, u32[]{:S(2)}, u32[]{:S(2)}) collective-permute-start(f32[56,1024]{1,0:T(8,128)S(1)} %get-tuple-element.24), channel_id=1, source_target_pairs={{4,0},{5,1},{8,4},{9,5},{12,8},{13,9},{14,12},{15,13},{10,14},{11,... | collective-permute-start | bytes 688136 | tf_op jit(solution)/shard_map/ppermute | solution.py:194
  68.4 12.3 %collective-permute-start.28 = (f32[48,1024]{1,0:T(8,128)S(1)}, f32[48,1024]{1,0:T(8,128)S(1)}, u32[]{:S(2)}, u32[]{:S(2)}) collective-permute-start(f32[48,1024]{1,0:T(8,128)S(1)} %get-tuple-element.30), channel_id=1, source_target_pairs={{4,0},{5,1},{8,4},{9,5},{12,8},{13,9},{14,12},{15,13},{10,14},{11,... | collective-permute-start | bytes 589832 | tf_op jit(solution)/shard_map/ppermute | solution.py:194
  71.5 9.3 %collective-permute-start.25 = (f32[48,1024]{1,0:T(8,128)S(1)}, f32[48,1024]{1,0:T(8,128)S(1)}, u32[]{:S(2)}, u32[]{:S(2)}) collective-permute-start(f32[48,1024]{1,0:T(8,128)S(1)} %fusion.33), channel_id=1, source_target_pairs={{0,4},{1,5},{4,8},{5,9},{8,12},{9,13},{12,14},{13,15},{14,10},{15,... | collective-permute-start | bytes 589832 | tf_op jit(solution)/shard_map/ppermute | solution.py:188
  76.8 8.7 %collective-permute-start.18 = (f32[56,1024]{1,0:T(8,128)S(1)}, f32[56,1024]{1,0:T(8,128)S(1)}, u32[]{:S(2)}, u32[]{:S(2)}) collective-permute-start(f32[56,1024]{1,0:T(8,128)S(1)} %get-tuple-element.21), channel_id=1, source_target_pairs={{0,4},{1,5},{4,8},{5,9},{8,12},{9,13},{12,14},{13,15},{14,10},{15,... | collective-permute-start | bytes 688136 | tf_op jit(solution)/shard_map/ppermute | solution.py:188
  78.4 8.2 %collective-permute-start.21 = (f32[56,1024]{1,0:T(8,128)S(1)}, f32[56,1024]{1,0:T(8,128)S(1)}, u32[]{:S(2)}, u32[]{:S(2)}) collective-permute-start(f32[56,1024]{1,0:T(8,128)S(1)} %get-tuple-element.22), channel_id=1, source_target_pairs={{4,0},{5,1},{8,4},{9,5},{12,8},{13,9},{14,12},{15,13},{10,14},{11,... | collective-permute-start | bytes 688136 | tf_op jit(solution)/shard_map/ppermute | solution.py:194
  80.8 8.8 %collective-permute-start.26 = (f32[48,1024]{1,0:T(8,128)S(1)}, f32[48,1024]{1,0:T(8,128)S(1)}, u32[]{:S(2)}, u32[]{:S(2)}) collective-permute-start(f32[48,1024]{1,0:T(8,128)S(1)} %get-tuple-element.27), channel_id=1, source_target_pairs={{0,4},{1,5},{4,8},{5,9},{8,12},{9,13},{12,14},{13,15},{14,10},{15,... | collective-permute-start | bytes 589832 | tf_op jit(solution)/shard_map/ppermute | solution.py:188
  82.5 7.9 %collective-permute-start.29 = (f32[48,1024]{1,0:T(8,128)S(1)}, f32[48,1024]{1,0:T(8,128)S(1)}, u32[]{:S(2)}, u32[]{:S(2)}) collective-permute-start(f32[48,1024]{1,0:T(8,128)S(1)} %get-tuple-element.28), channel_id=1, source_target_pairs={{4,0},{5,1},{8,4},{9,5},{12,8},{13,9},{14,12},{15,13},{10,14},{11,... | collective-permute-start | bytes 589832 | tf_op jit(solution)/shard_map/ppermute | solution.py:194
  86.6 8.7 %collective-permute-start.22 = (f32[56,1024]{1,0:T(8,128)S(1)}, f32[56,1024]{1,0:T(8,128)S(1)}, u32[]{:S(2)}, u32[]{:S(2)}) collective-permute-start(f32[56,1024]{1,0:T(8,128)S(1)} %get-tuple-element.20), channel_id=1, source_target_pairs={{4,0},{5,1},{8,4},{9,5},{12,8},{13,9},{14,12},{15,13},{10,14},{11,... | collective-permute-start | bytes 688136 | tf_op jit(solution)/shard_map/ppermute | solution.py:194
  87.2 13.1 %collective-permute-start.19 = (f32[56,1024]{1,0:T(8,128)S(1)}, f32[56,1024]{1,0:T(8,128)S(1)}, u32[]{:S(2)}, u32[]{:S(2)}) collective-permute-start(f32[56,1024]{1,0:T(8,128)S(1)} %get-tuple-element.19), channel_id=1, source_target_pairs={{0,4},{1,5},{4,8},{5,9},{8,12},{9,13},{12,14},{13,15},{14,10},{15,... | collective-permute-start | bytes 688136 | tf_op jit(solution)/shard_map/ppermute | solution.py:188
  90.4 7.7 %collective-permute-start.27 = (f32[48,1024]{1,0:T(8,128)S(1)}, f32[48,1024]{1,0:T(8,128)S(1)}, u32[]{:S(2)}, u32[]{:S(2)}) collective-permute-start(f32[48,1024]{1,0:T(8,128)S(1)} %get-tuple-element.25), channel_id=1, source_target_pairs={{0,4},{1,5},{4,8},{5,9},{8,12},{9,13},{12,14},{13,15},{14,10},{15,... | collective-permute-start | bytes 589832 | tf_op jit(solution)/shard_map/ppermute | solution.py:188
  92.4 7.8 %collective-permute-start.30 = (f32[48,1024]{1,0:T(8,128)S(1)}, f32[48,1024]{1,0:T(8,128)S(1)}, u32[]{:S(2)}, u32[]{:S(2)}) collective-permute-start(f32[48,1024]{1,0:T(8,128)S(1)} %get-tuple-element.26), channel_id=1, source_target_pairs={{4,0},{5,1},{8,4},{9,5},{12,8},{13,9},{14,12},{15,13},{10,14},{11,... | collective-permute-start | bytes 589832 | tf_op jit(solution)/shard_map/ppermute | solution.py:194
  95.3 7.4 %collective-permute-start.23 = (f32[56,1024]{1,0:T(8,128)S(1)}, f32[56,1024]{1,0:T(8,128)S(1)}, u32[]{:S(2)}, u32[]{:S(2)}) collective-permute-start(f32[56,1024]{1,0:T(8,128)S(1)} %fusion.20), channel_id=1, source_target_pairs={{4,0},{5,1},{8,4},{9,5},{12,8},{13,9},{14,12},{15,13},{10,14},{11,... | collective-permute-start | bytes 688136 | tf_op jit(solution)/shard_map/ppermute | solution.py:194
  (13 other events, 120.5 us)

commit v14 on v13

--- a/solution.py
+++ b/solution.py
@@ -98,9 +98,9 @@
     es_ref[...] = ed
     g1_ref[...] = g1
     ea1_ref[...] = ea1
-    ec1_ref[...] = ec1
+    ec1_ref[...] = ec1.astype(jnp.float32).T.astype(jnp.bfloat16)
     g2_ref[...] = g2
-    h1_ref[...] = h1
+    h1_ref[...] = h1.astype(jnp.float32).T.astype(jnp.bfloat16)
     ea2_ref[...] = ea2
 
 
@@ -112,9 +112,9 @@
         jax.ShapeDtypeStruct((rows, assets), bf),
         jax.ShapeDtypeStruct((rows, hidden), bf),
         jax.ShapeDtypeStruct((rows, hidden), bf),
+        jax.ShapeDtypeStruct((hidden, rows), bf),
         jax.ShapeDtypeStruct((rows, hidden), bf),
-        jax.ShapeDtypeStruct((rows, hidden), bf),
-        jax.ShapeDtypeStruct((rows, hidden), bf),
+        jax.ShapeDtypeStruct((hidden, rows), bf),
         jax.ShapeDtypeStruct((rows, hidden), bf),
         jax.ShapeDtypeStruct((1, hidden), f32),
     )
@@ -242,6 +242,8 @@
     else:
         terms = twin_terms(x_rows, z_rows, y_rows, mask, w_one, w_two, w_out)
     e_slope, g_one, e_aone, e_cone, g_two, h_one, e_atwo, grad_three = terms
+    if not fused:
+        e_cone, h_one = e_cone.T, h_one.T
     chip = position // 2
     spot = jnp.asarray(place, jnp.int32)[chip]
     ring_chips = jnp.asarray(snake, jnp.int32)[(spot + jnp.arange(chips, dtype=jnp.int32)) % chips]
@@ -257,18 +259,29 @@
     def swap(f):
         return lax.ppermute(f, "blk", partner)
 
+    def split_rows(f, width):
+        f = jnp.take(f.reshape(chips, 2, width, rows_dev), ring_chips, axis=0, mode="clip")
+        keep = lax.dynamic_index_in_dim(f, core, 1, keepdims=False)
+        give = lax.dynamic_index_in_dim(f, 1 - core, 1, keepdims=False)
+        return keep, lax.ppermute(give, "blk", partner)
+
+    def rows_first(left, right):
+        return lax.dot_general(
+            left, right, (((2,), (0,)), ((), ())), preferred_element_type=jnp.float32
+        )
+
     x_keep, x_got = split_cols(x_rows, r_one)
-    h_keep, h_got = split_cols(h_one, r_two)
+    h_keep, h_got = split_rows(h_one, r_two)
     g2_got = swap(g_two)
     g1_got = swap(g_one)
     ed_keep, ed_got = split_cols(e_slope, r_one)
-    ec_keep, ec_got = split_cols(e_cone, r_two)
+    ec_keep, ec_got = split_rows(e_cone, r_two)
     ea2_got = swap(e_atwo)
     ea1_got = swap(e_aone)
     chip_out = grad_three + swap(grad_three)
     part_two = (
-        slots_product(ec_keep, g_two) + slots_product(ec_got, g2_got)
-        + slots_product(h_keep, e_atwo) + slots_product(h_got, ea2_got)
+        rows_first(ec_keep, g_two) + rows_first(ec_got, g2_got)
+        + rows_first(h_keep, e_atwo) + rows_first(h_got, ea2_got)
     )
     part_one = (
         slots_product(ed_keep, g_one) + slots_product(ed_got, g1_got)

time: 107 us -> 107 us (level)
    dot_general x8 -> x4, matrix products: 10.1 us -> 3.12 us  [slots_product(): lax.dot_general(left, right, (((0,), (0,)), ((), ())), preferred_element_...]
    dot_general x0 -> x4, matrix products: none -> 6.93 us  [rows_first(): lax.dot_general(left, right, (((2,), (0,)), ((), ())), preferred_element_...]
    gather x0 -> x2, local copies, waits for them, and re-layouts: none -> 2.19 us  [split_rows(): jnp.take(f.reshape(chips, 2, width, rows_dev), ring_chips, axis=0, mode='...]
    pallas_call x3 -> x1, local copies, waits for them, and re-layouts: 2.32 us -> 1.02 us  [twin_fused(): pl.pallas_call(functools.partial(twin_body, r_one), out_shape=shapes, in_...]
    gather x4 -> x2, local copies, waits for them, and re-layouts: 2.35 us -> 1.15 us  [split_cols(): jnp.take(f.reshape(rows_dev, chips, 2, width), ring_chips, axis=1, mode='...]
where the time goes in v14:
time: 107 us; the launch traced here: 106 us
  waiting for transfers between devices  42.9 us (40%)
  starting transfers between devices  23.5 us (22%)
  local copies, waits for them, and re-layouts  11.7 us (11%)
  matrix products  10.1 us (9%)
  other arithmetic  10 us (9%)
  Pallas kernels  6.4 us (6%)
  between operations  1.83 us (2%)
    ppermute x7, waiting for transfers between devices, forward(): acc = lax.ppermute(acc, 'blk', cw) + part[(window - s) % chips]  12.2 us
    ppermute x7, waiting for transfers between devices, backward(): acc = lax.ppermute(acc, 'blk', ccw)  11.3 us
    ppermute x4, waiting for transfers between devices, ring_all_gather(): left = lax.ppermute(left, 'blk', cw)  10.4 us
    ppermute x7, starting transfers between devices, forward(): acc = lax.ppermute(acc, 'blk', cw) + part[(window - s) % chips]  9.66 us
    ppermute x3, waiting for transfers between devices, ring_all_gather(): right = lax.ppermute(right, 'blk', ccw)  8.84 us
    dot_general x4, matrix products, rows_first(): lax.dot_general(left, right, (((2,), (0,)), ((), ())), preferred_element_...  6.93 us
    pallas_call x1, Pallas kernels, twin_fused(): pl.pallas_call(functools.partial(twin_body, r_one), out_shape=shapes, in_...  6.4 us
    ppermute x3, starting transfers between devices, ring_all_gather(): right = lax.ppermute(right, 'blk', ccw)  6.07 us
  transfers between devices with their start and end apart: 31, of which 16 were waited for; matrix products, arithmetic and copies ran while one was open for 24% of the time, Pallas kernels for 6%

profile of v14, /device:TPU:0, one launch (start us, length us, event | category | flops | bytes accessed | tf_op | source)
XLA Modules:
  0.0 106.4 jit_solution(14996923686859484945)
XLA Ops:
  2.4 3.0 %collective-permute-start = (bf16[96,1024]{1,0:T(8,128)(2,1)S(1)}, bf16[96,1024]{1,0:T(8,128)(2,1)S(1)}, u32[]{:S(2)}, u32[]{:S(2)}) collective-permute-start(bf16[96,1024]{1,0:T(8,128)(2,1)S(1)} %constant_dynamic-update-slice_fusion), channel_id=1, source_target_pairs={{4,0},{5,1},{8,4},{9,5},{12,8},{13,9},{14,12},{15,13},{10,14},{11,... | collective-permute-start | bytes 589832 | tf_op jit(solution)/shard_map/ppermute | solution.py:167
  5.6 4.8 %collective-permute-done = bf16[96,1024]{1,0:T(8,128)(2,1)S(1)} collective-permute-done((bf16[96,1024]{1,0:T(8,128)(2,1)S(1)}, bf16[96,1024]{1,0:T(8,128)(2,1)S(1)}, u32[]{:S(2)}, u32[]{:S(2)}) %collective-permute-start) | collective-permute-done | bytes 196640 | tf_op jit(solution)/shard_map/ppermute | solution.py:167
  10.4 1.7 %collective-permute-start.1 = (bf16[96,1024]{1,0:T(8,128)(2,1)S(1)}, bf16[96,1024]{1,0:T(8,128)(2,1)S(1)}, u32[]{:S(2)}, u32[]{:S(2)}) collective-permute-start(bf16[96,1024]{1,0:T(8,128)(2,1)S(1)} %collective-permute-done), channel_id=1, source_target_pairs={{4,0},{5,1},{8,4},{9,5},{12,8},{13,9},{14,12},{15,13},{10,14},{11,... | collective-permute-start | bytes 589832 | tf_op jit(solution)/shard_map/ppermute | solution.py:167
  12.4 4.0 %collective-permute-done.1 = bf16[96,1024]{1,0:T(8,128)(2,1)S(1)} collective-permute-done((bf16[96,1024]{1,0:T(8,128)(2,1)S(1)}, bf16[96,1024]{1,0:T(8,128)(2,1)S(1)}, u32[]{:S(2)}, u32[]{:S(2)}) %collective-permute-start.1) | collective-permute-done | bytes 196640 | tf_op jit(solution)/shard_map/ppermute | solution.py:167
  16.5 1.4 %collective-permute-start.2 = (bf16[96,1024]{1,0:T(8,128)(2,1)S(1)}, bf16[96,1024]{1,0:T(8,128)(2,1)S(1)}, u32[]{:S(2)}, u32[]{:S(2)}) collective-permute-start(bf16[96,1024]{1,0:T(8,128)(2,1)S(1)} %collective-permute-done.1), channel_id=1, source_target_pairs={{4,0},{5,1},{8,4},{9,5},{12,8},{13,9},{14,12},{15,13},{10,14},{11,... | collective-permute-start | bytes 589832 | tf_op jit(solution)/shard_map/ppermute | solution.py:167
  18.5 5.4 %collective-permute-done.5 = bf16[96,1024]{1,0:T(8,128)(2,1)S(1)} collective-permute-done((bf16[96,1024]{1,0:T(8,128)(2,1)S(1)}, bf16[96,1024]{1,0:T(8,128)(2,1)S(1)}, u32[]{:S(2)}, u32[]{:S(2)}) %collective-permute-start.5) | collective-permute-done | bytes 196640 | tf_op jit(solution)/shard_map/ppermute | solution.py:164
  24.6 5.0 %collective-permute-done.6 = bf16[96,1024]{1,0:T(8,128)(2,1)S(1)} collective-permute-done((bf16[96,1024]{1,0:T(8,128)(2,1)S(1)}, bf16[96,1024]{1,0:T(8,128)(2,1)S(1)}, u32[]{:S(2)}, u32[]{:S(2)}) %collective-permute-start.6) | collective-permute-done | bytes 196640 | tf_op jit(solution)/shard_map/ppermute | solution.py:164
  36.9 1.3 %fusion.42.m_ref = f32[128,1]{1,0:T(8,128)} fusion(s32[]{:T(128)} %fusion.51), kind=kLoop, calls=%fused_computation.83 | loop fusion | flops 256 | bytes 516 | tf_op jit(solution)/shard_map/convert_element_type | solution.py:239
  38.1 1.2 %fusion.47.sel_ref = s32[16]{0:T(128)} fusion(s32[16]{0:T(128)S(1)} %gather_fusion, s32[]{:T(128)} %bitcast.1, s32[]{:T(128)S(6)} %select_n.100), kind=kLoop, calls=%fused_computation.112 | loop fusion | flops 336 | bytes 136 | tf_op jit(solution)/shard_map/add | solution.py:174
  39.3 1.2 %copy-done.12 = bf16[8,96,1024]{2,1,0:T(8,128)(2,1)} copy-done((bf16[8,96,1024]{2,1,0:T(8,128)(2,1)}, bf16[8,96,1024]{2,1,0:T(8,128)(2,1)S(1)}, u32[]{:S(2)}) %copy-start.12) | copy-done | bytes 1572888
  40.5 6.4 %shard_map.157 = (bf16[128,512]{1,0:T(8,128)(2,1)}, bf16[128,1024]{1,0:T(8,128)(2,1)}, bf16[128,1024]{1,0:T(8,128)(2,1)}, bf16[1024,128]{1,0:T(8,128)(2,1)}, bf1...) custom-call(s32[16]{0:T(128)} %fusion.47.sel_ref, ...), custom_call_target="tpu_custom_call" | custom-call | flops 1476395008 | bytes 5242880 | tf_op jit(solution)/shard_map/pallas_call | solution.py:124
  46.9 1.6 %gather_fusion.2 = bf16[8,2,64,128]{3,2,1,0:T(8,128)(2,1)S(1)} fusion(bf16[8,2,64,128]{3,2,1,0:T(8,128)(2,1)} %bitcast.159, s32[1024]{0:T(1024)S(1)} %pad_clamp_fusion), kind=kCustom, calls=%fused_computation.2 | custom fusion | bytes 524320 | tf_op jit(solution)/shard_map/jit(_take)/gather | solution.py:263
  49.4 1.4 %fusion.17 = f32[8,64,1024]{2,1,0:T(8,128)S(1)} fusion(bf16[128,1024]{1,0:T(8,128)(2,1)} %get-tuple-element.12, bf16[8,2,64,128]{3,2,1,0:T(8,128)(2,1)S(1)} %gather_fusion.2, s32[]{:T(128)S(6)} %select_n.110), kind=kOutput, calls=%fused_computation.24 | convolution fusion | flops 134217728 | bytes 2490372 | tf_op jit(solution)/shard_map/dot_general | solution.py:269
  51.4 2.7 %fusion.13 = f32[8,64,1024]{2,1,0:T(8,128)} fusion(bf16[128,1024]{1,0:T(8,128)(2,1)} %get-tuple-element.14, bf16[8,2,64,128]{3,2,1,0:T(8,128)(2,1)S(1)} %gather_fusion.3, s32[]{:T(128)S(6)} %select_n.110), kind=kOutput, calls=%fused_computation.20 | convolution fusion | flops 134217728 | bytes 2490372 | tf_op jit(solution)/shard_map/dot_general | solution.py:269
  54.4 1.2 %fusion.4 = f32[8,32,1024]{2,1,0:T(8,128)S(1)} fusion(bf16[128,1024]{1,0:T(8,128)(2,1)} %get-tuple-element.18, bf16[8,128,2,32]{1,3,2,0:T(8,128)(2,1)S(1)} %gather_fusion.5, s32[]{:T(128)S(6)} %select_n.110), kind=kOutput, calls=%fused_computation.13 | convolution fusion | flops 67108864 | bytes 1376260 | tf_op jit(solution)/shard_map/dot_general | solution.py:213
  60.3 1.4 %fusion.15 = f32[8,64,1024]{2,1,0:T(8,128)S(1)} fusion(bf16[8,64,128]{2,1,0:T(8,128)(2,1)S(1)} %collective-permute-done.8, bf16[128,1024]{1,0:T(8,128)(2,1)} %collective-permute-done.9), kind=kOutput, calls=%fused_computation.22 | convolution fusion | flops 134217728 | bytes 2490368 | tf_op jit(solution)/shard_map/dot_general | solution.py:269
  62.1 1.5 %add_add_fusion = f32[8,64,1024]{2,1,0:T(8,128)S(1)} fusion(f32[8,64,1024]{2,1,0:T(8,128)S(1)} %copy-done.3, f32[8,64,1024]{2,1,0:T(8,128)S(1)} %fusion.17, f32[8,64,1024]{2,1,0:T(8,128)S(1)} %fusion.15, bf16[8,64,128]{2,1,0:T(8,128)(2,1)S(1)} %collective-permute-done.10, bf16[128,1024]{1,0:T(8,128)(2,1)} %collective-permute-done.11), kind=kOutput, calls=%fused_computation.6 | convolution fusion | flops 135790592 | bytes 8781824 | tf_op jit(solution)/shard_map/dot_general | solution.py:269
  64.6 1.3 %fusion.2 = f32[8,32,1024]{2,1,0:T(8,128)S(1)} fusion(bf16[128,8,32]{0,2,1:T(8,128)(2,1)} %collective-permute-done.15, bf16[128,1024]{1,0:T(8,128)(2,1)} %collective-permute-done.16), kind=kOutput, calls=%fused_computation.11 | convolution fusion | flops 67108864 | bytes 1376256 | tf_op jit(solution)/shard_map/dot_general | solution.py:213
  66.3 1.8 %collective-permute-start.17 = (f32[56,1024]{1,0:T(8,128)S(1)}, f32[56,1024]{1,0:T(8,128)S(1)}, u32[]{:S(2)}, u32[]{:S(2)}) collective-permute-start(f32[56,1024]{1,0:T(8,128)S(1)} %get-tuple-element.23), channel_id=1, source_target_pairs={{0,4},{1,5},{4,8},{5,9},{8,12},{9,13},{12,14},{13,15},{14,10},{15,... | collective-permute-start | bytes 688136 | tf_op jit(solution)/shard_map/ppermute | solution.py:188
  68.3 1.4 %collective-permute-start.28 = (f32[48,1024]{1,0:T(8,128)S(1)}, f32[48,1024]{1,0:T(8,128)S(1)}, u32[]{:S(2)}, u32[]{:S(2)}) collective-permute-start(f32[48,1024]{1,0:T(8,128)S(1)} %get-tuple-element.30), channel_id=1, source_target_pairs={{4,0},{5,1},{8,4},{9,5},{12,8},{13,9},{14,12},{15,13},{10,14},{11,... | collective-permute-start | bytes 589832 | tf_op jit(solution)/shard_map/ppermute | solution.py:194
  69.7 1.6 %collective-permute-done.24 = f32[48,1024]{1,0:T(8,128)S(1)} collective-permute-done((f32[48,1024]{1,0:T(8,128)S(1)}, f32[48,1024]{1,0:T(8,128)S(1)}, u32[]{:S(2)}, u32[]{:S(2)}) %collective-permute-start.24) | collective-permute-done | bytes 196640 | tf_op jit(solution)/shard_map/ppermute | solution.py:188
  72.0 4.3 %collective-permute-done.17 = f32[56,1024]{1,0:T(8,128)S(1)} collective-permute-done((f32[56,1024]{1,0:T(8,128)S(1)}, f32[56,1024]{1,0:T(8,128)S(1)}, u32[]{:S(2)}, u32[]{:S(2)}) %collective-permute-start.17) | collective-permute-done | bytes 229408 | tf_op jit(solution)/shard_map/ppermute | solution.py:188
  76.6 1.6 %collective-permute-start.18 = (f32[56,1024]{1,0:T(8,128)S(1)}, f32[56,1024]{1,0:T(8,128)S(1)}, u32[]{:S(2)}, u32[]{:S(2)}) collective-permute-start(f32[56,1024]{1,0:T(8,128)S(1)} %get-tuple-element.21), channel_id=1, source_target_pairs={{0,4},{1,5},{4,8},{5,9},{8,12},{9,13},{12,14},{13,15},{14,10},{15,... | collective-permute-start | bytes 688136 | tf_op jit(solution)/shard_map/ppermute | solution.py:188
  78.7 2.0 %collective-permute-done.28 = f32[48,1024]{1,0:T(8,128)S(1)} collective-permute-done((f32[48,1024]{1,0:T(8,128)S(1)}, f32[48,1024]{1,0:T(8,128)S(1)}, u32[]{:S(2)}, u32[]{:S(2)}) %collective-permute-start.28) | collective-permute-done | bytes 196640 | tf_op jit(solution)/shard_map/ppermute | solution.py:194
  80.8 1.6 %collective-permute-start.26 = (f32[48,1024]{1,0:T(8,128)S(1)}, f32[48,1024]{1,0:T(8,128)S(1)}, u32[]{:S(2)}, u32[]{:S(2)}) collective-permute-start(f32[48,1024]{1,0:T(8,128)S(1)} %get-tuple-element.27), channel_id=1, source_target_pairs={{0,4},{1,5},{4,8},{5,9},{8,12},{9,13},{12,14},{13,15},{14,10},{15,... | collective-permute-start | bytes 589832 | tf_op jit(solution)/shard_map/ppermute | solution.py:188
  82.8 2.6 %collective-permute-done.18 = f32[56,1024]{1,0:T(8,128)S(1)} collective-permute-done((f32[56,1024]{1,0:T(8,128)S(1)}, f32[56,1024]{1,0:T(8,128)S(1)}, u32[]{:S(2)}, u32[]{:S(2)}) %collective-permute-start.18) | collective-permute-done | bytes 229408 | tf_op jit(solution)/shard_map/ppermute | solution.py:188
  87.1 1.5 %collective-permute-start.19 = (f32[56,1024]{1,0:T(8,128)S(1)}, f32[56,1024]{1,0:T(8,128)S(1)}, u32[]{:S(2)}, u32[]{:S(2)}) collective-permute-start(f32[56,1024]{1,0:T(8,128)S(1)} %get-tuple-element.19), channel_id=1, source_target_pairs={{0,4},{1,5},{4,8},{5,9},{8,12},{9,13},{12,14},{13,15},{14,10},{15,... | collective-permute-start | bytes 688136 | tf_op jit(solution)/shard_map/ppermute | solution.py:188
  90.4 1.9 %collective-permute-start.27 = (f32[48,1024]{1,0:T(8,128)S(1)}, f32[48,1024]{1,0:T(8,128)S(1)}, u32[]{:S(2)}, u32[]{:S(2)}) collective-permute-start(f32[48,1024]{1,0:T(8,128)S(1)} %get-tuple-element.25), channel_id=1, source_target_pairs={{0,4},{1,5},{4,8},{5,9},{8,12},{9,13},{12,14},{13,15},{14,10},{15,... | collective-permute-start | bytes 589832 | tf_op jit(solution)/shard_map/ppermute | solution.py:188
  92.5 2.8 %collective-permute-done.22 = f32[56,1024]{1,0:T(8,128)S(1)} collective-permute-done((f32[56,1024]{1,0:T(8,128)S(1)}, f32[56,1024]{1,0:T(8,128)S(1)}, u32[]{:S(2)}, u32[]{:S(2)}) %collective-permute-start.22) | collective-permute-done | bytes 229408 | tf_op jit(solution)/shard_map/ppermute | solution.py:194
  95.3 2.7 %collective-permute-done.27 = f32[48,1024]{1,0:T(8,128)S(1)} collective-permute-done((f32[48,1024]{1,0:T(8,128)S(1)}, f32[48,1024]{1,0:T(8,128)S(1)}, u32[]{:S(2)}, u32[]{:S(2)}) %collective-permute-start.27) | collective-permute-done | bytes 196640 | tf_op jit(solution)/shard_map/ppermute | solution.py:188
  98.0 2.1 %collective-permute-done.30 = f32[48,1024]{1,0:T(8,128)S(1)} collective-permute-done((f32[48,1024]{1,0:T(8,128)S(1)}, f32[48,1024]{1,0:T(8,128)S(1)}, u32[]{:S(2)}, u32[]{:S(2)}) %collective-permute-start.30) | collective-permute-done | bytes 196640 | tf_op jit(solution)/shard_map/ppermute | solution.py:194
  100.2 2.4 %collective-permute-done.23 = f32[56,1024]{1,0:T(8,128)S(1)} collective-permute-done((f32[56,1024]{1,0:T(8,128)S(1)}, f32[56,1024]{1,0:T(8,128)S(1)}, u32[]{:S(2)}, u32[]{:S(2)}) %collective-permute-start.23) | collective-permute-done | bytes 229408 | tf_op jit(solution)/shard_map/ppermute | solution.py:194
  (124 shorter events, 27.9 us)
Async XLA Ops:
  0.6 35.0 %copy-start = (s32[16,16]{1,0:T(8,128)S(1)}, s32[16,16]{1,0:T(8,128)}, u32[]{:S(2)}) copy-start(s32[16,16]{1,0:T(8,128)} %param.17) | copy-start | bytes 3076
  2.4 8.0 %collective-permute-start = (bf16[96,1024]{1,0:T(8,128)(2,1)S(1)}, bf16[96,1024]{1,0:T(8,128)(2,1)S(1)}, u32[]{:S(2)}, u32[]{:S(2)}) collective-permute-start(bf16[96,1024]{1,0:T(8,128)(2,1)S(1)} %constant_dynamic-update-slice_fusion), channel_id=1, source_target_pairs={{4,0},{5,1},{8,4},{9,5},{12,8},{13,9},{14,12},{15,13},{10,14},{11,... | collective-permute-start | bytes 589832 | tf_op jit(solution)/shard_map/ppermute | solution.py:167
  5.4 6.6 %collective-permute-start.3 = (bf16[96,1024]{1,0:T(8,128)(2,1)S(1)}, bf16[96,1024]{1,0:T(8,128)(2,1)S(1)}, u32[]{:S(2)}, u32[]{:S(2)}) collective-permute-start(bf16[96,1024]{1,0:T(8,128)(2,1)S(1)} %constant_dynamic-update-slice_fusion), channel_id=1, source_target_pairs={{0,4},{1,5},{4,8},{5,9},{8,12},{9,13},{12,14},{13,15},{14,10},{15,... | collective-permute-start | bytes 589832 | tf_op jit(solution)/shard_map/ppermute | solution.py:164
  10.4 6.1 %collective-permute-start.1 = (bf16[96,1024]{1,0:T(8,128)(2,1)S(1)}, bf16[96,1024]{1,0:T(8,128)(2,1)S(1)}, u32[]{:S(2)}, u32[]{:S(2)}) collective-permute-start(bf16[96,1024]{1,0:T(8,128)(2,1)S(1)} %collective-permute-done), channel_id=1, source_target_pairs={{4,0},{5,1},{8,4},{9,5},{12,8},{13,9},{14,12},{15,13},{10,14},{11,... | collective-permute-start | bytes 589832 | tf_op jit(solution)/shard_map/ppermute | solution.py:167
  12.1 5.8 %collective-permute-start.4 = (bf16[96,1024]{1,0:T(8,128)(2,1)S(1)}, bf16[96,1024]{1,0:T(8,128)(2,1)S(1)}, u32[]{:S(2)}, u32[]{:S(2)}) collective-permute-start(bf16[96,1024]{1,0:T(8,128)(2,1)S(1)} %collective-permute-done.3), channel_id=1, source_target_pairs={{0,4},{1,5},{4,8},{5,9},{8,12},{9,13},{12,14},{13,15},{14,10},{15,... | collective-permute-start | bytes 589832 | tf_op jit(solution)/shard_map/ppermute | solution.py:164
  16.5 8.1 %collective-permute-start.2 = (bf16[96,1024]{1,0:T(8,128)(2,1)S(1)}, bf16[96,1024]{1,0:T(8,128)(2,1)S(1)}, u32[]{:S(2)}, u32[]{:S(2)}) collective-permute-start(bf16[96,1024]{1,0:T(8,128)(2,1)S(1)} %collective-permute-done.1), channel_id=1, source_target_pairs={{4,0},{5,1},{8,4},{9,5},{12,8},{13,9},{14,12},{15,13},{10,14},{11,... | collective-permute-start | bytes 589832 | tf_op jit(solution)/shard_map/ppermute | solution.py:167
  17.9 6.1 %collective-permute-start.5 = (bf16[96,1024]{1,0:T(8,128)(2,1)S(1)}, bf16[96,1024]{1,0:T(8,128)(2,1)S(1)}, u32[]{:S(2)}, u32[]{:S(2)}) collective-permute-start(bf16[96,1024]{1,0:T(8,128)(2,1)S(1)} %collective-permute-done.4), channel_id=1, source_target_pairs={{0,4},{1,5},{4,8},{5,9},{8,12},{9,13},{12,14},{13,15},{14,10},{15,... | collective-permute-start | bytes 589832 | tf_op jit(solution)/shard_map/ppermute | solution.py:164
  24.0 5.7 %collective-permute-start.6 = (bf16[96,1024]{1,0:T(8,128)(2,1)S(1)}, bf16[96,1024]{1,0:T(8,128)(2,1)S(1)}, u32[]{:S(2)}, u32[]{:S(2)}) collective-permute-start(bf16[96,1024]{1,0:T(8,128)(2,1)S(1)} %collective-permute-done.5), channel_id=1, source_target_pairs={{0,4},{1,5},{4,8},{5,9},{8,12},{9,13},{12,14},{13,15},{14,10},{15,... | collective-permute-start | bytes 589832 | tf_op jit(solution)/shard_map/ppermute | solution.py:164
  29.8 9.6 %collective-permute-start.7 = (bf16[8,96,1024]{2,1,0:T(8,128)(2,1)S(1)}, bf16[8,96,1024]{2,1,0:T(8,128)(2,1)S(1)}, u32[]{:S(2)}, u32[]{:S(2)}) collective-permute-start(bf16[8,96,1024]{2,1,0:T(8,128)(2,1)S(1)} %bitcast_dynamic-update-slice_fusion.mine_ref), channel_id=1, source_target_pairs={{0,1},{1,0},{2,3},{3,2},{4,5},{5,4},{6,7},{7,6},{8,9},{9,8},{10,11... | collective-permute-start | bytes 4718600 | tf_op jit(solution)/shard_map/ppermute | solution.py:170
  33.3 31.2 %collective-permute-start.15 = (bf16[128,8,32]{0,2,1:T(8,128)(2,1)}, bf16[128,8,32]{0,2,1:T(8,128)(2,1)}, u32[]{:S(2)}, u32[]{:S(2)}) collective-permute-start(bf16[128,8,32]{0,2,1:T(8,128)(2,1)} %dynamic-slice_bitcast_fusion.2), channel_id=1, source_target_pairs={{0,1},{1,0},{2,3},{3,2},{4,5},{5,4},{6,7},{7,6},{8,9},{9,8},{10,11... | collective-permute-start | bytes 196616 | tf_op jit(solution)/shard_map/ppermute | solution.py:257
  49.1 11.0 %collective-permute-start.9 = (bf16[128,1024]{1,0:T(8,128)(2,1)}, bf16[128,1024]{1,0:T(8,128)(2,1)}, u32[]{:S(2)}, u32[]{:S(2)}) collective-permute-start(bf16[128,1024]{1,0:T(8,128)(2,1)} %get-tuple-element.12), channel_id=1, source_target_pairs={{0,1},{1,0},{2,3},{3,2},{4,5},{5,4},{6,7},{7,6},{8,9},{9,8},{10,11... | collective-permute-start | bytes 786440 | tf_op jit(solution)/shard_map/ppermute | solution.py:260
  54.1 8.0 %collective-permute-start.11 = (bf16[128,1024]{1,0:T(8,128)(2,1)}, bf16[128,1024]{1,0:T(8,128)(2,1)}, u32[]{:S(2)}, u32[]{:S(2)}) collective-permute-start(bf16[128,1024]{1,0:T(8,128)(2,1)} %get-tuple-element.14), channel_id=1, source_target_pairs={{0,1},{1,0},{2,3},{3,2},{4,5},{5,4},{6,7},{7,6},{8,9},{9,8},{10,11... | collective-permute-start | bytes 786440 | tf_op jit(solution)/shard_map/ppermute | solution.py:260
  55.6 8.9 %collective-permute-start.16 = (bf16[128,1024]{1,0:T(8,128)(2,1)}, bf16[128,1024]{1,0:T(8,128)(2,1)}, u32[]{:S(2)}, u32[]{:S(2)}) collective-permute-start(bf16[128,1024]{1,0:T(8,128)(2,1)} %get-tuple-element.18), channel_id=1, source_target_pairs={{0,1},{1,0},{2,3},{3,2},{4,5},{5,4},{6,7},{7,6},{8,9},{9,8},{10,11... | collective-permute-start | bytes 786440 | tf_op jit(solution)/shard_map/ppermute | solution.py:260
  55.9 1.9 %collective-permute-start.12 = (f32[1024]{0:T(1024)}, f32[1024]{0:T(1024)}, u32[]{:S(2)}, u32[]{:S(2)}) collective-permute-start(f32[1024]{0:T(1024)} %bitcast.23), channel_id=1, source_target_pairs={{0,1},{1,0},{2,3},{3,2},{4,5},{5,4},{6,7},{7,6},{8,9},{9,8},{10,11... | collective-permute-start | bytes 12296 | tf_op jit(solution)/shard_map/ppermute | solution.py:260
  57.9 1.9 %collective-permute-start.8 = (bf16[8,64,128]{2,1,0:T(8,128)(2,1)}, bf16[8,64,128]{2,1,0:T(8,128)(2,1)S(1)}, u32[]{:S(2)}, u32[]{:S(2)}) collective-permute-start(bf16[8,64,128]{2,1,0:T(8,128)(2,1)} %dynamic-slice_bitcast_fusion.1), channel_id=1, source_target_pairs={{0,1},{1,0},{2,3},{3,2},{4,5},{5,4},{6,7},{7,6},{8,9},{9,8},{10,11... | collective-permute-start | bytes 393224 | tf_op jit(solution)/shard_map/ppermute | solution.py:266
  59.8 1.9 %collective-permute-start.10 = (bf16[8,64,128]{2,1,0:T(8,128)(2,1)S(1)}, bf16[8,64,128]{2,1,0:T(8,128)(2,1)S(1)}, u32[]{:S(2)}, u32[]{:S(2)}) collective-permute-start(bf16[8,64,128]{2,1,0:T(8,128)(2,1)S(1)} %dynamic-slice_bitcast_fusion), channel_id=1, source_target_pairs={{0,1},{1,0},{2,3},{3,2},{4,5},{5,4},{6,7},{7,6},{8,9},{9,8},{10,11... | collective-permute-start | bytes 393224 | tf_op jit(solution)/shard_map/ppermute | solution.py:266
  60.1 4.1 %collective-permute-start.13 = (bf16[128,8,32]{0,2,1:T(8,128)(2,1)S(1)}, bf16[128,8,32]{0,2,1:T(8,128)(2,1)S(1)}, u32[]{:S(2)}, u32[]{:S(2)}) collective-permute-start(bf16[128,8,32]{0,2,1:T(8,128)(2,1)S(1)} %dynamic-slice_bitcast_fusion.3), channel_id=1, source_target_pairs={{0,1},{1,0},{2,3},{3,2},{4,5},{5,4},{6,7},{7,6},{8,9},{9,8},{10,11... | collective-permute-start | bytes 196616 | tf_op jit(solution)/shard_map/ppermute | solution.py:257
  61.7 2.6 %collective-permute-start.14 = (bf16[128,1024]{1,0:T(8,128)(2,1)S(1)}, bf16[128,1024]{1,0:T(8,128)(2,1)S(1)}, u32[]{:S(2)}, u32[]{:S(2)}) collective-permute-start(bf16[128,1024]{1,0:T(8,128)(2,1)S(1)} %copy-done.5), channel_id=1, source_target_pairs={{0,1},{1,0},{2,3},{3,2},{4,5},{5,4},{6,7},{7,6},{8,9},{9,8},{10,11... | collective-permute-start | bytes 786440 | tf_op jit(solution)/shard_map/ppermute | solution.py:260
  63.6 7.8 %collective-permute-start.24 = (f32[48,1024]{1,0:T(8,128)S(1)}, f32[48,1024]{1,0:T(8,128)S(1)}, u32[]{:S(2)}, u32[]{:S(2)}) collective-permute-start(f32[48,1024]{1,0:T(8,128)S(1)} %get-tuple-element.29), channel_id=1, source_target_pairs={{0,4},{1,5},{4,8},{5,9},{8,12},{9,13},{12,14},{13,15},{14,10},{15,... | collective-permute-start | bytes 589832 | tf_op jit(solution)/shard_map/ppermute | solution.py:188
  66.3 10.0 %collective-permute-start.17 = (f32[56,1024]{1,0:T(8,128)S(1)}, f32[56,1024]{1,0:T(8,128)S(1)}, u32[]{:S(2)}, u32[]{:S(2)}) collective-permute-start(f32[56,1024]{1,0:T(8,128)S(1)} %get-tuple-element.23), channel_id=1, source_target_pairs={{0,4},{1,5},{4,8},{5,9},{8,12},{9,13},{12,14},{13,15},{14,10},{15,... | collective-permute-start | bytes 688136 | tf_op jit(solution)/shard_map/ppermute | solution.py:188
  68.1 8.5 %collective-permute-start.20 = (f32[56,1024]{1,0:T(8,128)S(1)}, f32[56,1024]{1,0:T(8,128)S(1)}, u32[]{:S(2)}, u32[]{:S(2)}) collective-permute-start(f32[56,1024]{1,0:T(8,128)S(1)} %get-tuple-element.24), channel_id=1, source_target_pairs={{4,0},{5,1},{8,4},{9,5},{12,8},{13,9},{14,12},{15,13},{10,14},{11,... | collective-permute-start | bytes 688136 | tf_op jit(solution)/shard_map/ppermute | solution.py:194
  68.3 12.4 %collective-permute-start.28 = (f32[48,1024]{1,0:T(8,128)S(1)}, f32[48,1024]{1,0:T(8,128)S(1)}, u32[]{:S(2)}, u32[]{:S(2)}) collective-permute-start(f32[48,1024]{1,0:T(8,128)S(1)} %get-tuple-element.30), channel_id=1, source_target_pairs={{4,0},{5,1},{8,4},{9,5},{12,8},{13,9},{14,12},{15,13},{10,14},{11,... | collective-permute-start | bytes 589832 | tf_op jit(solution)/shard_map/ppermute | solution.py:194
  71.4 9.3 %collective-permute-start.25 = (f32[48,1024]{1,0:T(8,128)S(1)}, f32[48,1024]{1,0:T(8,128)S(1)}, u32[]{:S(2)}, u32[]{:S(2)}) collective-permute-start(f32[48,1024]{1,0:T(8,128)S(1)} %fusion.33), channel_id=1, source_target_pairs={{0,4},{1,5},{4,8},{5,9},{8,12},{9,13},{12,14},{13,15},{14,10},{15,... | collective-permute-start | bytes 589832 | tf_op jit(solution)/shard_map/ppermute | solution.py:188
  76.6 8.8 %collective-permute-start.18 = (f32[56,1024]{1,0:T(8,128)S(1)}, f32[56,1024]{1,0:T(8,128)S(1)}, u32[]{:S(2)}, u32[]{:S(2)}) collective-permute-start(f32[56,1024]{1,0:T(8,128)S(1)} %get-tuple-element.21), channel_id=1, source_target_pairs={{0,4},{1,5},{4,8},{5,9},{8,12},{9,13},{12,14},{13,15},{14,10},{15,... | collective-permute-start | bytes 688136 | tf_op jit(solution)/shard_map/ppermute | solution.py:188
  78.3 8.2 %collective-permute-start.21 = (f32[56,1024]{1,0:T(8,128)S(1)}, f32[56,1024]{1,0:T(8,128)S(1)}, u32[]{:S(2)}, u32[]{:S(2)}) collective-permute-start(f32[56,1024]{1,0:T(8,128)S(1)} %get-tuple-element.22), channel_id=1, source_target_pairs={{4,0},{5,1},{8,4},{9,5},{12,8},{13,9},{14,12},{15,13},{10,14},{11,... | collective-permute-start | bytes 688136 | tf_op jit(solution)/shard_map/ppermute | solution.py:194
  80.8 8.9 %collective-permute-start.26 = (f32[48,1024]{1,0:T(8,128)S(1)}, f32[48,1024]{1,0:T(8,128)S(1)}, u32[]{:S(2)}, u32[]{:S(2)}) collective-permute-start(f32[48,1024]{1,0:T(8,128)S(1)} %get-tuple-element.27), channel_id=1, source_target_pairs={{0,4},{1,5},{4,8},{5,9},{8,12},{9,13},{12,14},{13,15},{14,10},{15,... | collective-permute-start | bytes 589832 | tf_op jit(solution)/shard_map/ppermute | solution.py:188
  82.3 8.0 %collective-permute-start.29 = (f32[48,1024]{1,0:T(8,128)S(1)}, f32[48,1024]{1,0:T(8,128)S(1)}, u32[]{:S(2)}, u32[]{:S(2)}) collective-permute-start(f32[48,1024]{1,0:T(8,128)S(1)} %get-tuple-element.28), channel_id=1, source_target_pairs={{4,0},{5,1},{8,4},{9,5},{12,8},{13,9},{14,12},{15,13},{10,14},{11,... | collective-permute-start | bytes 589832 | tf_op jit(solution)/shard_map/ppermute | solution.py:194
  86.5 8.7 %collective-permute-start.22 = (f32[56,1024]{1,0:T(8,128)S(1)}, f32[56,1024]{1,0:T(8,128)S(1)}, u32[]{:S(2)}, u32[]{:S(2)}) collective-permute-start(f32[56,1024]{1,0:T(8,128)S(1)} %get-tuple-element.20), channel_id=1, source_target_pairs={{4,0},{5,1},{8,4},{9,5},{12,8},{13,9},{14,12},{15,13},{10,14},{11,... | collective-permute-start | bytes 688136 | tf_op jit(solution)/shard_map/ppermute | solution.py:194
  87.1 13.1 %collective-permute-start.19 = (f32[56,1024]{1,0:T(8,128)S(1)}, f32[56,1024]{1,0:T(8,128)S(1)}, u32[]{:S(2)}, u32[]{:S(2)}) collective-permute-start(f32[56,1024]{1,0:T(8,128)S(1)} %get-tuple-element.19), channel_id=1, source_target_pairs={{0,4},{1,5},{4,8},{5,9},{8,12},{9,13},{12,14},{13,15},{14,10},{15,... | collective-permute-start | bytes 688136 | tf_op jit(solution)/shard_map/ppermute | solution.py:188
  90.4 7.6 %collective-permute-start.27 = (f32[48,1024]{1,0:T(8,128)S(1)}, f32[48,1024]{1,0:T(8,128)S(1)}, u32[]{:S(2)}, u32[]{:S(2)}) collective-permute-start(f32[48,1024]{1,0:T(8,128)S(1)} %get-tuple-element.25), channel_id=1, source_target_pairs={{0,4},{1,5},{4,8},{5,9},{8,12},{9,13},{12,14},{13,15},{14,10},{15,... | collective-permute-start | bytes 589832 | tf_op jit(solution)/shard_map/ppermute | solution.py:188
  92.3 7.8 %collective-permute-start.30 = (f32[48,1024]{1,0:T(8,128)S(1)}, f32[48,1024]{1,0:T(8,128)S(1)}, u32[]{:S(2)}, u32[]{:S(2)}) collective-permute-start(f32[48,1024]{1,0:T(8,128)S(1)} %get-tuple-element.26), channel_id=1, source_target_pairs={{4,0},{5,1},{8,4},{9,5},{12,8},{13,9},{14,12},{15,13},{10,14},{11,... | collective-permute-start | bytes 589832 | tf_op jit(solution)/shard_map/ppermute | solution.py:194
  95.3 7.4 %collective-permute-start.23 = (f32[56,1024]{1,0:T(8,128)S(1)}, f32[56,1024]{1,0:T(8,128)S(1)}, u32[]{:S(2)}, u32[]{:S(2)}) collective-permute-start(f32[56,1024]{1,0:T(8,128)S(1)} %fusion.20), channel_id=1, source_target_pairs={{4,0},{5,1},{8,4},{9,5},{12,8},{13,9},{14,12},{15,13},{10,14},{11,... | collective-permute-start | bytes 688136 | tf_op jit(solution)/shard_map/ppermute | solution.py:194
  (13 other events, 122.2 us)

commit v15 on v14

--- a/solution.py
+++ b/solution.py
@@ -61,19 +61,22 @@
     return jnp.maximum(a, 0.0) + jnp.log1p(jnp.exp(-jnp.abs(a)))
 
 
-def twin_body(r_one, sel_ref, x_ref, z_ref, y_ref, m_ref, mine_ref, other_ref, wo_ref,
+def twin_body(r_one, place, par_ref, x_ref, z_ref, y_ref, mine_ref, other_ref, wo_ref,
               es_ref, g1_ref, ea1_ref, ec1_ref, g2_ref, h1_ref, ea2_ref, g3_ref):
     chips = mine_ref.shape[0]
+    total, core, spot = par_ref[0], par_ref[1], par_ref[2]
+    rows = x_ref.shape[0]
+    mask = (lax.broadcasted_iota(jnp.int32, (rows, 1), 0) < total).astype(jnp.float32)
     ones, twos = [], []
-    for b in range(sel_ref.shape[0]):
-        i = sel_ref[b]
-        block = jnp.where(i < chips, mine_ref[i % chips], other_ref[i % chips])
+    for b in range(2 * chips):
+        k = (place[b // 2] - spot + chips) % chips
+        same = (b % 2) == core
+        block = jnp.where(same, mine_ref[k], other_ref[k])
         ones.append(block[:r_one])
         twos.append(block[r_one:])
     w1 = jnp.concatenate(ones, axis=0)
     w2 = jnp.concatenate(twos, axis=0)
     wo = wo_ref[...]
-    mask = m_ref[...]
     a1 = jnp.dot(x_ref[...], w1, preferred_element_type=jnp.float32)
     s1 = _sigmoid(a1)
     h1 = _softplus(a1).astype(jnp.bfloat16)
@@ -104,7 +107,7 @@
     ea2_ref[...] = ea2
 
 
-def twin_fused(x_rows, z_rows, y_rows, mask, mine, other, sel, r_one, w_three):
+def twin_fused(x_rows, z_rows, y_rows, params, place, mine, other, r_one, w_three):
     rows, assets = x_rows.shape
     chips, width, hidden = mine.shape
     bf, f32 = jnp.bfloat16, jnp.float32
@@ -122,14 +125,14 @@
     smem = pl.BlockSpec(memory_space=pltpu.SMEM)
     flops = 2 * rows * hidden * (3 * assets + 4 * hidden)
     e_slope, g_one, e_aone, e_cone, g_two, h_one, e_atwo, grad_three = pl.pallas_call(
-        functools.partial(twin_body, r_one),
+        functools.partial(twin_body, r_one, place),
         out_shape=shapes,
-        in_specs=[smem] + [vmem] * 7,
+        in_specs=[smem] + [vmem] * 6,
         out_specs=[vmem] * 8,
         cost_estimate=pl.CostEstimate(
             flops=flops, transcendentals=6 * rows * hidden,
             bytes_accessed=4 * chips * width * hidden + 16 * rows * hidden),
-    )(sel, x_rows, z_rows, y_rows.astype(f32)[:, None], mask[:, None], mine, other,
+    )(params, x_rows, z_rows, y_rows.astype(f32)[:, None], mine, other,
       w_three.astype(f32)[None, :])
     return (e_slope, g_one, e_aone, e_cone, g_two, h_one, e_atwo, grad_three[0])
 
@@ -238,7 +241,9 @@
     total = jnp.sum(sending)
     mask = (jnp.arange(rows_dev, dtype=jnp.int32) < total).astype(jnp.float32)
     if fused:
-        terms = twin_fused(x_rows, z_rows, y_rows, mask, mine, other, index, r_one, w_out)
+        spot = jnp.asarray(place, jnp.int32)[position // 2]
+        params = jnp.stack([total, core, spot]).astype(jnp.int32)
+        terms = twin_fused(x_rows, z_rows, y_rows, params, place, mine, other, r_one, w_out)
     else:
         terms = twin_terms(x_rows, z_rows, y_rows, mask, w_one, w_two, w_out)
     e_slope, g_one, e_aone, e_cone, g_two, h_one, e_atwo, grad_three = terms

time: 107 us -> 105 us (0.981)
    another operation x0 -> x1, other arithmetic: none -> 1.81 us  [per_device(): params = jnp.stack([total, core, spot]).astype(jnp.int32)]
    convert_element_type x1 -> x0, other arithmetic: 1.28 us -> none  [per_device(): mask = (jnp.arange(rows_dev, dtype=jnp.int32) < total).astype(jnp.float32)]
    add x1 -> x0, other arithmetic: 1.17 us -> none  [ring_all_gather(): index = jnp.where(dest_core == core, 0, chips) + k]
    unnamed x37 -> x39, local copies, waits for them, and re-layouts: 2.3 us -> 2.3 us
  transfers between devices with their start and end apart: 31 -> 31, of which waited for: 16 -> 16; matrix products, arithmetic and copies ran while one was open for 24% -> 23% of each run, Pallas kernels for 6% -> 6%
where the time goes in v15:
time: 105 us
  waiting for transfers between devices  42.9 us (41%)
  starting transfers between devices  23.5 us (22%)
  local copies, waits for them, and re-layouts  11.1 us (11%)
  matrix products  10.1 us (10%)
  other arithmetic  9.26 us (9%)
  Pallas kernels  6.37 us (6%)
  between operations  1.82 us (2%)
    ppermute x7, waiting for transfers between devices, forward(): acc = lax.ppermute(acc, 'blk', cw) + part[(window - s) % chips]  12.3 us
    ppermute x7, waiting for transfers between devices, backward(): acc = lax.ppermute(acc, 'blk', ccw)  11.3 us
    ppermute x4, waiting for transfers between devices, ring_all_gather(): left = lax.ppermute(left, 'blk', cw)  10.4 us
    ppermute x7, starting transfers between devices, forward(): acc = lax.ppermute(acc, 'blk', cw) + part[(window - s) % chips]  9.71 us
    ppermute x3, waiting for transfers between devices, ring_all_gather(): right = lax.ppermute(right, 'blk', ccw)  8.84 us
    dot_general x4, matrix products, rows_first(): lax.dot_general(left, right, (((2,), (0,)), ((), ())), preferred_element_...  6.98 us
    pallas_call x1, Pallas kernels, twin_fused(): pl.pallas_call(functools.partial(twin_body, r_one, place), out_shape=shap...  6.37 us
    ppermute x3, starting transfers between devices, ring_all_gather(): right = lax.ppermute(right, 'blk', ccw)  6.07 us
  transfers between devices with their start and end apart: 31, of which 16 were waited for; matrix products, arithmetic and copies ran while one was open for 23% of the time, Pallas kernels for 6%

profile of v15, /device:TPU:0, one launch (start us, length us, event | category | flops | bytes accessed | tf_op | source)
XLA Modules:
  0.0 105.0 jit_solution(14369303444841555338)
XLA Ops:
  2.4 3.0 %collective-permute-start = (bf16[96,1024]{1,0:T(8,128)(2,1)S(1)}, bf16[96,1024]{1,0:T(8,128)(2,1)S(1)}, u32[]{:S(2)}, u32[]{:S(2)}) collective-permute-start(bf16[96,1024]{1,0:T(8,128)(2,1)S(1)} %constant_dynamic-update-slice_fusion), channel_id=1, source_target_pairs={{4,0},{5,1},{8,4},{9,5},{12,8},{13,9},{14,12},{15,13},{10,14},{11,... | collective-permute-start | bytes 589832 | tf_op jit(solution)/shard_map/ppermute | solution.py:170
  5.6 4.8 %collective-permute-done = bf16[96,1024]{1,0:T(8,128)(2,1)S(1)} collective-permute-done((bf16[96,1024]{1,0:T(8,128)(2,1)S(1)}, bf16[96,1024]{1,0:T(8,128)(2,1)S(1)}, u32[]{:S(2)}, u32[]{:S(2)}) %collective-permute-start) | collective-permute-done | bytes 196640 | tf_op jit(solution)/shard_map/ppermute | solution.py:170
  10.4 1.7 %collective-permute-start.1 = (bf16[96,1024]{1,0:T(8,128)(2,1)S(1)}, bf16[96,1024]{1,0:T(8,128)(2,1)S(1)}, u32[]{:S(2)}, u32[]{:S(2)}) collective-permute-start(bf16[96,1024]{1,0:T(8,128)(2,1)S(1)} %collective-permute-done), channel_id=1, source_target_pairs={{4,0},{5,1},{8,4},{9,5},{12,8},{13,9},{14,12},{15,13},{10,14},{11,... | collective-permute-start | bytes 589832 | tf_op jit(solution)/shard_map/ppermute | solution.py:170
  12.4 4.0 %collective-permute-done.1 = bf16[96,1024]{1,0:T(8,128)(2,1)S(1)} collective-permute-done((bf16[96,1024]{1,0:T(8,128)(2,1)S(1)}, bf16[96,1024]{1,0:T(8,128)(2,1)S(1)}, u32[]{:S(2)}, u32[]{:S(2)}) %collective-permute-start.1) | collective-permute-done | bytes 196640 | tf_op jit(solution)/shard_map/ppermute | solution.py:170
  16.5 1.4 %collective-permute-start.2 = (bf16[96,1024]{1,0:T(8,128)(2,1)S(1)}, bf16[96,1024]{1,0:T(8,128)(2,1)S(1)}, u32[]{:S(2)}, u32[]{:S(2)}) collective-permute-start(bf16[96,1024]{1,0:T(8,128)(2,1)S(1)} %collective-permute-done.1), channel_id=1, source_target_pairs={{4,0},{5,1},{8,4},{9,5},{12,8},{13,9},{14,12},{15,13},{10,14},{11,... | collective-permute-start | bytes 589832 | tf_op jit(solution)/shard_map/ppermute | solution.py:170
  18.5 5.4 %collective-permute-done.5 = bf16[96,1024]{1,0:T(8,128)(2,1)S(1)} collective-permute-done((bf16[96,1024]{1,0:T(8,128)(2,1)S(1)}, bf16[96,1024]{1,0:T(8,128)(2,1)S(1)}, u32[]{:S(2)}, u32[]{:S(2)}) %collective-permute-start.5) | collective-permute-done | bytes 196640 | tf_op jit(solution)/shard_map/ppermute | solution.py:167
  24.6 5.0 %collective-permute-done.6 = bf16[96,1024]{1,0:T(8,128)(2,1)S(1)} collective-permute-done((bf16[96,1024]{1,0:T(8,128)(2,1)S(1)}, bf16[96,1024]{1,0:T(8,128)(2,1)S(1)}, u32[]{:S(2)}, u32[]{:S(2)}) %collective-permute-start.6) | collective-permute-done | bytes 196640 | tf_op jit(solution)/shard_map/ppermute | solution.py:167
  36.1 1.8 %pad_add_fusion.par_ref = s32[3]{0:T(128)} fusion(s32[1]{0:T(128)} %dynamic_slice.37, s32[1]{0:T(128)} %bitcast.1, s32[1]{0:T(128)} %bitcast), kind=kLoop, calls=%fused_computation.101 | loop fusion | flops 6 | bytes 24 | tf_op jit(solution)/shard_map/stack | solution.py:245
  38.0 1.1 %copy-done.12 = bf16[8,96,1024]{2,1,0:T(8,128)(2,1)} copy-done((bf16[8,96,1024]{2,1,0:T(8,128)(2,1)}, bf16[8,96,1024]{2,1,0:T(8,128)(2,1)S(1)}, u32[]{:S(2)}) %copy-start.12) | copy-done | bytes 1572888
  39.1 6.4 %shard_map.148 = (bf16[128,512]{1,0:T(8,128)(2,1)}, bf16[128,1024]{1,0:T(8,128)(2,1)}, bf16[128,1024]{1,0:T(8,128)(2,1)}, bf16[1024,128]{1,0:T(8,128)(2,1)}, bf1...) custom-call(s32[3]{0:T(128)} %pad_add_fusion.par_ref, ...), custom_call_target="tpu_custom_call" | custom-call | flops 1476395008 | bytes 5242880 | tf_op jit(solution)/shard_map/pallas_call | solution.py:127
  45.5 1.6 %gather_fusion.1 = bf16[8,2,64,128]{3,2,1,0:T(8,128)(2,1)S(1)} fusion(bf16[8,2,64,128]{3,2,1,0:T(8,128)(2,1)} %bitcast.159, s32[1024]{0:T(1024)S(1)} %pad_clamp_fusion), kind=kCustom, calls=%fused_computation.1 | custom fusion | bytes 524320 | tf_op jit(solution)/shard_map/jit(_take)/gather | solution.py:268
  48.0 1.4 %fusion.17 = f32[8,64,1024]{2,1,0:T(8,128)S(1)} fusion(bf16[128,1024]{1,0:T(8,128)(2,1)} %get-tuple-element.12, bf16[8,2,64,128]{3,2,1,0:T(8,128)(2,1)S(1)} %gather_fusion.1, s32[]{:T(128)S(6)} %select_n.67), kind=kOutput, calls=%fused_computation.23 | convolution fusion | flops 134217728 | bytes 2490372 | tf_op jit(solution)/shard_map/dot_general | solution.py:274
  50.0 2.7 %fusion.13 = f32[8,64,1024]{2,1,0:T(8,128)} fusion(bf16[128,1024]{1,0:T(8,128)(2,1)} %get-tuple-element.14, bf16[8,2,64,128]{3,2,1,0:T(8,128)(2,1)S(1)} %gather_fusion.2, s32[]{:T(128)S(6)} %select_n.67), kind=kOutput, calls=%fused_computation.19 | convolution fusion | flops 134217728 | bytes 2490372 | tf_op jit(solution)/shard_map/dot_general | solution.py:274
  53.0 1.2 %fusion.4 = f32[8,32,1024]{2,1,0:T(8,128)S(1)} fusion(bf16[128,1024]{1,0:T(8,128)(2,1)} %get-tuple-element.18, bf16[8,128,2,32]{1,3,2,0:T(8,128)(2,1)S(1)} %gather_fusion.4, s32[]{:T(128)S(6)} %select_n.67), kind=kOutput, calls=%fused_computation.12 | convolution fusion | flops 67108864 | bytes 1376260 | tf_op jit(solution)/shard_map/dot_general | solution.py:216
  58.9 1.4 %fusion.15 = f32[8,64,1024]{2,1,0:T(8,128)S(1)} fusion(bf16[8,64,128]{2,1,0:T(8,128)(2,1)S(1)} %collective-permute-done.8, bf16[128,1024]{1,0:T(8,128)(2,1)} %collective-permute-done.9), kind=kOutput, calls=%fused_computation.21 | convolution fusion | flops 134217728 | bytes 2490368 | tf_op jit(solution)/shard_map/dot_general | solution.py:274
  60.6 1.5 %add_add_fusion = f32[8,64,1024]{2,1,0:T(8,128)S(1)} fusion(f32[8,64,1024]{2,1,0:T(8,128)S(1)} %copy-done.2, f32[8,64,1024]{2,1,0:T(8,128)S(1)} %fusion.17, f32[8,64,1024]{2,1,0:T(8,128)S(1)} %fusion.15, bf16[8,64,128]{2,1,0:T(8,128)(2,1)S(1)} %collective-permute-done.10, bf16[128,1024]{1,0:T(8,128)(2,1)} %collective-permute-done.11), kind=kOutput, calls=%fused_computation.5 | convolution fusion | flops 135790592 | bytes 8781824 | tf_op jit(solution)/shard_map/dot_general | solution.py:274
  63.2 1.3 %fusion.2 = f32[8,32,1024]{2,1,0:T(8,128)S(1)} fusion(bf16[128,8,32]{0,2,1:T(8,128)(2,1)} %collective-permute-done.15, bf16[128,1024]{1,0:T(8,128)(2,1)} %collective-permute-done.16), kind=kOutput, calls=%fused_computation.10 | convolution fusion | flops 67108864 | bytes 1376256 | tf_op jit(solution)/shard_map/dot_general | solution.py:216
  64.9 1.8 %collective-permute-start.17 = (f32[56,1024]{1,0:T(8,128)S(1)}, f32[56,1024]{1,0:T(8,128)S(1)}, u32[]{:S(2)}, u32[]{:S(2)}) collective-permute-start(f32[56,1024]{1,0:T(8,128)S(1)} %get-tuple-element.23), channel_id=1, source_target_pairs={{0,4},{1,5},{4,8},{5,9},{8,12},{9,13},{12,14},{13,15},{14,10},{15,... | collective-permute-start | bytes 688136 | tf_op jit(solution)/shard_map/ppermute | solution.py:191
  67.0 1.4 %collective-permute-start.28 = (f32[48,1024]{1,0:T(8,128)S(1)}, f32[48,1024]{1,0:T(8,128)S(1)}, u32[]{:S(2)}, u32[]{:S(2)}) collective-permute-start(f32[48,1024]{1,0:T(8,128)S(1)} %get-tuple-element.30), channel_id=1, source_target_pairs={{4,0},{5,1},{8,4},{9,5},{12,8},{13,9},{14,12},{15,13},{10,14},{11,... | collective-permute-start | bytes 589832 | tf_op jit(solution)/shard_map/ppermute | solution.py:197
  68.3 1.6 %collective-permute-done.24 = f32[48,1024]{1,0:T(8,128)S(1)} collective-permute-done((f32[48,1024]{1,0:T(8,128)S(1)}, f32[48,1024]{1,0:T(8,128)S(1)}, u32[]{:S(2)}, u32[]{:S(2)}) %collective-permute-start.24) | collective-permute-done | bytes 196640 | tf_op jit(solution)/shard_map/ppermute | solution.py:191
  70.5 4.3 %collective-permute-done.17 = f32[56,1024]{1,0:T(8,128)S(1)} collective-permute-done((f32[56,1024]{1,0:T(8,128)S(1)}, f32[56,1024]{1,0:T(8,128)S(1)}, u32[]{:S(2)}, u32[]{:S(2)}) %collective-permute-start.17) | collective-permute-done | bytes 229408 | tf_op jit(solution)/shard_map/ppermute | solution.py:191
  75.3 1.6 %collective-permute-start.18 = (f32[56,1024]{1,0:T(8,128)S(1)}, f32[56,1024]{1,0:T(8,128)S(1)}, u32[]{:S(2)}, u32[]{:S(2)}) collective-permute-start(f32[56,1024]{1,0:T(8,128)S(1)} %get-tuple-element.21), channel_id=1, source_target_pairs={{0,4},{1,5},{4,8},{5,9},{8,12},{9,13},{12,14},{13,15},{14,10},{15,... | collective-permute-start | bytes 688136 | tf_op jit(solution)/shard_map/ppermute | solution.py:191
  77.4 1.9 %collective-permute-done.28 = f32[48,1024]{1,0:T(8,128)S(1)} collective-permute-done((f32[48,1024]{1,0:T(8,128)S(1)}, f32[48,1024]{1,0:T(8,128)S(1)}, u32[]{:S(2)}, u32[]{:S(2)}) %collective-permute-start.28) | collective-permute-done | bytes 196640 | tf_op jit(solution)/shard_map/ppermute | solution.py:197
  79.4 1.6 %collective-permute-start.26 = (f32[48,1024]{1,0:T(8,128)S(1)}, f32[48,1024]{1,0:T(8,128)S(1)}, u32[]{:S(2)}, u32[]{:S(2)}) collective-permute-start(f32[48,1024]{1,0:T(8,128)S(1)} %get-tuple-element.27), channel_id=1, source_target_pairs={{0,4},{1,5},{4,8},{5,9},{8,12},{9,13},{12,14},{13,15},{14,10},{15,... | collective-permute-start | bytes 589832 | tf_op jit(solution)/shard_map/ppermute | solution.py:191
  81.4 2.6 %collective-permute-done.18 = f32[56,1024]{1,0:T(8,128)S(1)} collective-permute-done((f32[56,1024]{1,0:T(8,128)S(1)}, f32[56,1024]{1,0:T(8,128)S(1)}, u32[]{:S(2)}, u32[]{:S(2)}) %collective-permute-start.18) | collective-permute-done | bytes 229408 | tf_op jit(solution)/shard_map/ppermute | solution.py:191
  84.0 1.0 collective-permute-done.21
  85.7 1.5 %collective-permute-start.19 = (f32[56,1024]{1,0:T(8,128)S(1)}, f32[56,1024]{1,0:T(8,128)S(1)}, u32[]{:S(2)}, u32[]{:S(2)}) collective-permute-start(f32[56,1024]{1,0:T(8,128)S(1)} %get-tuple-element.19), channel_id=1, source_target_pairs={{0,4},{1,5},{4,8},{5,9},{8,12},{9,13},{12,14},{13,15},{14,10},{15,... | collective-permute-start | bytes 688136 | tf_op jit(solution)/shard_map/ppermute | solution.py:191
  89.0 2.0 %collective-permute-start.27 = (f32[48,1024]{1,0:T(8,128)S(1)}, f32[48,1024]{1,0:T(8,128)S(1)}, u32[]{:S(2)}, u32[]{:S(2)}) collective-permute-start(f32[48,1024]{1,0:T(8,128)S(1)} %get-tuple-element.25), channel_id=1, source_target_pairs={{0,4},{1,5},{4,8},{5,9},{8,12},{9,13},{12,14},{13,15},{14,10},{15,... | collective-permute-start | bytes 589832 | tf_op jit(solution)/shard_map/ppermute | solution.py:191
  91.0 2.8 %collective-permute-done.22 = f32[56,1024]{1,0:T(8,128)S(1)} collective-permute-done((f32[56,1024]{1,0:T(8,128)S(1)}, f32[56,1024]{1,0:T(8,128)S(1)}, u32[]{:S(2)}, u32[]{:S(2)}) %collective-permute-start.22) | collective-permute-done | bytes 229408 | tf_op jit(solution)/shard_map/ppermute | solution.py:197
  93.9 2.7 %collective-permute-done.27 = f32[48,1024]{1,0:T(8,128)S(1)} collective-permute-done((f32[48,1024]{1,0:T(8,128)S(1)}, f32[48,1024]{1,0:T(8,128)S(1)}, u32[]{:S(2)}, u32[]{:S(2)}) %collective-permute-start.27) | collective-permute-done | bytes 196640 | tf_op jit(solution)/shard_map/ppermute | solution.py:191
  96.6 2.1 %collective-permute-done.30 = f32[48,1024]{1,0:T(8,128)S(1)} collective-permute-done((f32[48,1024]{1,0:T(8,128)S(1)}, f32[48,1024]{1,0:T(8,128)S(1)}, u32[]{:S(2)}, u32[]{:S(2)}) %collective-permute-start.30) | collective-permute-done | bytes 196640 | tf_op jit(solution)/shard_map/ppermute | solution.py:197
  98.8 2.4 %collective-permute-done.23 = f32[56,1024]{1,0:T(8,128)S(1)} collective-permute-done((f32[56,1024]{1,0:T(8,128)S(1)}, f32[56,1024]{1,0:T(8,128)S(1)}, u32[]{:S(2)}, u32[]{:S(2)}) %collective-permute-start.23) | collective-permute-done | bytes 229408 | tf_op jit(solution)/shard_map/ppermute | solution.py:197
  (122 shorter events, 26.1 us)
Async XLA Ops:
  0.6 34.3 %copy-start = (s32[16,16]{1,0:T(8,128)S(1)}, s32[16,16]{1,0:T(8,128)}, u32[]{:S(2)}) copy-start(s32[16,16]{1,0:T(8,128)} %param.16) | copy-start | bytes 3076
  2.4 8.0 %collective-permute-start = (bf16[96,1024]{1,0:T(8,128)(2,1)S(1)}, bf16[96,1024]{1,0:T(8,128)(2,1)S(1)}, u32[]{:S(2)}, u32[]{:S(2)}) collective-permute-start(bf16[96,1024]{1,0:T(8,128)(2,1)S(1)} %constant_dynamic-update-slice_fusion), channel_id=1, source_target_pairs={{4,0},{5,1},{8,4},{9,5},{12,8},{13,9},{14,12},{15,13},{10,14},{11,... | collective-permute-start | bytes 589832 | tf_op jit(solution)/shard_map/ppermute | solution.py:170
  5.4 6.6 %collective-permute-start.3 = (bf16[96,1024]{1,0:T(8,128)(2,1)S(1)}, bf16[96,1024]{1,0:T(8,128)(2,1)S(1)}, u32[]{:S(2)}, u32[]{:S(2)}) collective-permute-start(bf16[96,1024]{1,0:T(8,128)(2,1)S(1)} %constant_dynamic-update-slice_fusion), channel_id=1, source_target_pairs={{0,4},{1,5},{4,8},{5,9},{8,12},{9,13},{12,14},{13,15},{14,10},{15,... | collective-permute-start | bytes 589832 | tf_op jit(solution)/shard_map/ppermute | solution.py:167
  10.4 6.1 %collective-permute-start.1 = (bf16[96,1024]{1,0:T(8,128)(2,1)S(1)}, bf16[96,1024]{1,0:T(8,128)(2,1)S(1)}, u32[]{:S(2)}, u32[]{:S(2)}) collective-permute-start(bf16[96,1024]{1,0:T(8,128)(2,1)S(1)} %collective-permute-done), channel_id=1, source_target_pairs={{4,0},{5,1},{8,4},{9,5},{12,8},{13,9},{14,12},{15,13},{10,14},{11,... | collective-permute-start | bytes 589832 | tf_op jit(solution)/shard_map/ppermute | solution.py:170
  12.1 5.8 %collective-permute-start.4 = (bf16[96,1024]{1,0:T(8,128)(2,1)S(1)}, bf16[96,1024]{1,0:T(8,128)(2,1)S(1)}, u32[]{:S(2)}, u32[]{:S(2)}) collective-permute-start(bf16[96,1024]{1,0:T(8,128)(2,1)S(1)} %collective-permute-done.3), channel_id=1, source_target_pairs={{0,4},{1,5},{4,8},{5,9},{8,12},{9,13},{12,14},{13,15},{14,10},{15,... | collective-permute-start | bytes 589832 | tf_op jit(solution)/shard_map/ppermute | solution.py:167
  16.5 8.1 %collective-permute-start.2 = (bf16[96,1024]{1,0:T(8,128)(2,1)S(1)}, bf16[96,1024]{1,0:T(8,128)(2,1)S(1)}, u32[]{:S(2)}, u32[]{:S(2)}) collective-permute-start(bf16[96,1024]{1,0:T(8,128)(2,1)S(1)} %collective-permute-done.1), channel_id=1, source_target_pairs={{4,0},{5,1},{8,4},{9,5},{12,8},{13,9},{14,12},{15,13},{10,14},{11,... | collective-permute-start | bytes 589832 | tf_op jit(solution)/shard_map/ppermute | solution.py:170
  17.9 6.1 %collective-permute-start.5 = (bf16[96,1024]{1,0:T(8,128)(2,1)S(1)}, bf16[96,1024]{1,0:T(8,128)(2,1)S(1)}, u32[]{:S(2)}, u32[]{:S(2)}) collective-permute-start(bf16[96,1024]{1,0:T(8,128)(2,1)S(1)} %collective-permute-done.4), channel_id=1, source_target_pairs={{0,4},{1,5},{4,8},{5,9},{8,12},{9,13},{12,14},{13,15},{14,10},{15,... | collective-permute-start | bytes 589832 | tf_op jit(solution)/shard_map/ppermute | solution.py:167
  24.0 5.7 %collective-permute-start.6 = (bf16[96,1024]{1,0:T(8,128)(2,1)S(1)}, bf16[96,1024]{1,0:T(8,128)(2,1)S(1)}, u32[]{:S(2)}, u32[]{:S(2)}) collective-permute-start(bf16[96,1024]{1,0:T(8,128)(2,1)S(1)} %collective-permute-done.5), channel_id=1, source_target_pairs={{0,4},{1,5},{4,8},{5,9},{8,12},{9,13},{12,14},{13,15},{14,10},{15,... | collective-permute-start | bytes 589832 | tf_op jit(solution)/shard_map/ppermute | solution.py:167
  29.8 8.2 %collective-permute-start.7 = (bf16[8,96,1024]{2,1,0:T(8,128)(2,1)S(1)}, bf16[8,96,1024]{2,1,0:T(8,128)(2,1)S(1)}, u32[]{:S(2)}, u32[]{:S(2)}) collective-permute-start(bf16[8,96,1024]{2,1,0:T(8,128)(2,1)S(1)} %bitcast_dynamic-update-slice_fusion.mine_ref), channel_id=1, source_target_pairs={{0,1},{1,0},{2,3},{3,2},{4,5},{5,4},{6,7},{7,6},{8,9},{9,8},{10,11... | collective-permute-start | bytes 4718600 | tf_op jit(solution)/shard_map/ppermute | solution.py:173
  33.3 29.8 %collective-permute-start.15 = (bf16[128,8,32]{0,2,1:T(8,128)(2,1)}, bf16[128,8,32]{0,2,1:T(8,128)(2,1)}, u32[]{:S(2)}, u32[]{:S(2)}) collective-permute-start(bf16[128,8,32]{0,2,1:T(8,128)(2,1)} %dynamic-slice_bitcast_fusion.2), channel_id=1, source_target_pairs={{0,1},{1,0},{2,3},{3,2},{4,5},{5,4},{6,7},{7,6},{8,9},{9,8},{10,11... | collective-permute-start | bytes 196616 | tf_op jit(solution)/shard_map/ppermute | solution.py:262
  47.8 10.9 %collective-permute-start.9 = (bf16[128,1024]{1,0:T(8,128)(2,1)}, bf16[128,1024]{1,0:T(8,128)(2,1)}, u32[]{:S(2)}, u32[]{:S(2)}) collective-permute-start(bf16[128,1024]{1,0:T(8,128)(2,1)} %get-tuple-element.12), channel_id=1, source_target_pairs={{0,1},{1,0},{2,3},{3,2},{4,5},{5,4},{6,7},{7,6},{8,9},{9,8},{10,11... | collective-permute-start | bytes 786440 | tf_op jit(solution)/shard_map/ppermute | solution.py:265
  52.7 7.9 %collective-permute-start.11 = (bf16[128,1024]{1,0:T(8,128)(2,1)}, bf16[128,1024]{1,0:T(8,128)(2,1)}, u32[]{:S(2)}, u32[]{:S(2)}) collective-permute-start(bf16[128,1024]{1,0:T(8,128)(2,1)} %get-tuple-element.14), channel_id=1, source_target_pairs={{0,1},{1,0},{2,3},{3,2},{4,5},{5,4},{6,7},{7,6},{8,9},{9,8},{10,11... | collective-permute-start | bytes 786440 | tf_op jit(solution)/shard_map/ppermute | solution.py:265
  54.3 8.9 %collective-permute-start.16 = (bf16[128,1024]{1,0:T(8,128)(2,1)}, bf16[128,1024]{1,0:T(8,128)(2,1)}, u32[]{:S(2)}, u32[]{:S(2)}) collective-permute-start(bf16[128,1024]{1,0:T(8,128)(2,1)} %get-tuple-element.18), channel_id=1, source_target_pairs={{0,1},{1,0},{2,3},{3,2},{4,5},{5,4},{6,7},{7,6},{8,9},{9,8},{10,11... | collective-permute-start | bytes 786440 | tf_op jit(solution)/shard_map/ppermute | solution.py:265
  54.6 1.9 %collective-permute-start.12 = (f32[1024]{0:T(1024)S(1)}, f32[1024]{0:T(1024)}, u32[]{:S(2)}, u32[]{:S(2)}) collective-permute-start(f32[1024]{0:T(1024)S(1)} %bitcast.160), channel_id=1, source_target_pairs={{0,1},{1,0},{2,3},{3,2},{4,5},{5,4},{6,7},{7,6},{8,9},{9,8},{10,11... | collective-permute-start | bytes 12296 | tf_op jit(solution)/shard_map/ppermute | solution.py:265
  56.5 1.8 %collective-permute-start.8 = (bf16[8,64,128]{2,1,0:T(8,128)(2,1)}, bf16[8,64,128]{2,1,0:T(8,128)(2,1)S(1)}, u32[]{:S(2)}, u32[]{:S(2)}) collective-permute-start(bf16[8,64,128]{2,1,0:T(8,128)(2,1)} %dynamic-slice_bitcast_fusion.1), channel_id=1, source_target_pairs={{0,1},{1,0},{2,3},{3,2},{4,5},{5,4},{6,7},{7,6},{8,9},{9,8},{10,11... | collective-permute-start | bytes 393224 | tf_op jit(solution)/shard_map/ppermute | solution.py:271
  58.4 1.9 %collective-permute-start.10 = (bf16[8,64,128]{2,1,0:T(8,128)(2,1)S(1)}, bf16[8,64,128]{2,1,0:T(8,128)(2,1)S(1)}, u32[]{:S(2)}, u32[]{:S(2)}) collective-permute-start(bf16[8,64,128]{2,1,0:T(8,128)(2,1)S(1)} %dynamic-slice_bitcast_fusion), channel_id=1, source_target_pairs={{0,1},{1,0},{2,3},{3,2},{4,5},{5,4},{6,7},{7,6},{8,9},{9,8},{10,11... | collective-permute-start | bytes 393224 | tf_op jit(solution)/shard_map/ppermute | solution.py:271
  58.7 4.2 %collective-permute-start.13 = (bf16[128,8,32]{0,2,1:T(8,128)(2,1)S(1)}, bf16[128,8,32]{0,2,1:T(8,128)(2,1)S(1)}, u32[]{:S(2)}, u32[]{:S(2)}) collective-permute-start(bf16[128,8,32]{0,2,1:T(8,128)(2,1)S(1)} %dynamic-slice_bitcast_fusion.3), channel_id=1, source_target_pairs={{0,1},{1,0},{2,3},{3,2},{4,5},{5,4},{6,7},{7,6},{8,9},{9,8},{10,11... | collective-permute-start | bytes 196616 | tf_op jit(solution)/shard_map/ppermute | solution.py:262
  60.3 2.6 %collective-permute-start.14 = (bf16[128,1024]{1,0:T(8,128)(2,1)S(1)}, bf16[128,1024]{1,0:T(8,128)(2,1)S(1)}, u32[]{:S(2)}, u32[]{:S(2)}) collective-permute-start(bf16[128,1024]{1,0:T(8,128)(2,1)S(1)} %copy-done.4), channel_id=1, source_target_pairs={{0,1},{1,0},{2,3},{3,2},{4,5},{5,4},{6,7},{7,6},{8,9},{9,8},{10,11... | collective-permute-start | bytes 786440 | tf_op jit(solution)/shard_map/ppermute | solution.py:265
  62.2 7.8 %collective-permute-start.24 = (f32[48,1024]{1,0:T(8,128)S(1)}, f32[48,1024]{1,0:T(8,128)S(1)}, u32[]{:S(2)}, u32[]{:S(2)}) collective-permute-start(f32[48,1024]{1,0:T(8,128)S(1)} %get-tuple-element.29), channel_id=1, source_target_pairs={{0,4},{1,5},{4,8},{5,9},{8,12},{9,13},{12,14},{13,15},{14,10},{15,... | collective-permute-start | bytes 589832 | tf_op jit(solution)/shard_map/ppermute | solution.py:191
  64.9 10.0 %collective-permute-start.17 = (f32[56,1024]{1,0:T(8,128)S(1)}, f32[56,1024]{1,0:T(8,128)S(1)}, u32[]{:S(2)}, u32[]{:S(2)}) collective-permute-start(f32[56,1024]{1,0:T(8,128)S(1)} %get-tuple-element.23), channel_id=1, source_target_pairs={{0,4},{1,5},{4,8},{5,9},{8,12},{9,13},{12,14},{13,15},{14,10},{15,... | collective-permute-start | bytes 688136 | tf_op jit(solution)/shard_map/ppermute | solution.py:191
  66.7 8.5 %collective-permute-start.20 = (f32[56,1024]{1,0:T(8,128)S(1)}, f32[56,1024]{1,0:T(8,128)S(1)}, u32[]{:S(2)}, u32[]{:S(2)}) collective-permute-start(f32[56,1024]{1,0:T(8,128)S(1)} %get-tuple-element.24), channel_id=1, source_target_pairs={{4,0},{5,1},{8,4},{9,5},{12,8},{13,9},{14,12},{15,13},{10,14},{11,... | collective-permute-start | bytes 688136 | tf_op jit(solution)/shard_map/ppermute | solution.py:197
  67.0 12.3 %collective-permute-start.28 = (f32[48,1024]{1,0:T(8,128)S(1)}, f32[48,1024]{1,0:T(8,128)S(1)}, u32[]{:S(2)}, u32[]{:S(2)}) collective-permute-start(f32[48,1024]{1,0:T(8,128)S(1)} %get-tuple-element.30), channel_id=1, source_target_pairs={{4,0},{5,1},{8,4},{9,5},{12,8},{13,9},{14,12},{15,13},{10,14},{11,... | collective-permute-start | bytes 589832 | tf_op jit(solution)/shard_map/ppermute | solution.py:197
  70.0 9.3 %collective-permute-start.25 = (f32[48,1024]{1,0:T(8,128)S(1)}, f32[48,1024]{1,0:T(8,128)S(1)}, u32[]{:S(2)}, u32[]{:S(2)}) collective-permute-start(f32[48,1024]{1,0:T(8,128)S(1)} %fusion.33), channel_id=1, source_target_pairs={{0,4},{1,5},{4,8},{5,9},{8,12},{9,13},{12,14},{13,15},{14,10},{15,... | collective-permute-start | bytes 589832 | tf_op jit(solution)/shard_map/ppermute | solution.py:191
  75.3 8.7 %collective-permute-start.18 = (f32[56,1024]{1,0:T(8,128)S(1)}, f32[56,1024]{1,0:T(8,128)S(1)}, u32[]{:S(2)}, u32[]{:S(2)}) collective-permute-start(f32[56,1024]{1,0:T(8,128)S(1)} %get-tuple-element.21), channel_id=1, source_target_pairs={{0,4},{1,5},{4,8},{5,9},{8,12},{9,13},{12,14},{13,15},{14,10},{15,... | collective-permute-start | bytes 688136 | tf_op jit(solution)/shard_map/ppermute | solution.py:191
  76.9 8.2 %collective-permute-start.21 = (f32[56,1024]{1,0:T(8,128)S(1)}, f32[56,1024]{1,0:T(8,128)S(1)}, u32[]{:S(2)}, u32[]{:S(2)}) collective-permute-start(f32[56,1024]{1,0:T(8,128)S(1)} %get-tuple-element.22), channel_id=1, source_target_pairs={{4,0},{5,1},{8,4},{9,5},{12,8},{13,9},{14,12},{15,13},{10,14},{11,... | collective-permute-start | bytes 688136 | tf_op jit(solution)/shard_map/ppermute | solution.py:197
  79.4 8.9 %collective-permute-start.26 = (f32[48,1024]{1,0:T(8,128)S(1)}, f32[48,1024]{1,0:T(8,128)S(1)}, u32[]{:S(2)}, u32[]{:S(2)}) collective-permute-start(f32[48,1024]{1,0:T(8,128)S(1)} %get-tuple-element.27), channel_id=1, source_target_pairs={{0,4},{1,5},{4,8},{5,9},{8,12},{9,13},{12,14},{13,15},{14,10},{15,... | collective-permute-start | bytes 589832 | tf_op jit(solution)/shard_map/ppermute | solution.py:191
  81.0 8.0 %collective-permute-start.29 = (f32[48,1024]{1,0:T(8,128)S(1)}, f32[48,1024]{1,0:T(8,128)S(1)}, u32[]{:S(2)}, u32[]{:S(2)}) collective-permute-start(f32[48,1024]{1,0:T(8,128)S(1)} %get-tuple-element.28), channel_id=1, source_target_pairs={{4,0},{5,1},{8,4},{9,5},{12,8},{13,9},{14,12},{15,13},{10,14},{11,... | collective-permute-start | bytes 589832 | tf_op jit(solution)/shard_map/ppermute | solution.py:197
  85.1 8.7 %collective-permute-start.22 = (f32[56,1024]{1,0:T(8,128)S(1)}, f32[56,1024]{1,0:T(8,128)S(1)}, u32[]{:S(2)}, u32[]{:S(2)}) collective-permute-start(f32[56,1024]{1,0:T(8,128)S(1)} %get-tuple-element.20), channel_id=1, source_target_pairs={{4,0},{5,1},{8,4},{9,5},{12,8},{13,9},{14,12},{15,13},{10,14},{11,... | collective-permute-start | bytes 688136 | tf_op jit(solution)/shard_map/ppermute | solution.py:197
  85.7 13.1 %collective-permute-start.19 = (f32[56,1024]{1,0:T(8,128)S(1)}, f32[56,1024]{1,0:T(8,128)S(1)}, u32[]{:S(2)}, u32[]{:S(2)}) collective-permute-start(f32[56,1024]{1,0:T(8,128)S(1)} %get-tuple-element.19), channel_id=1, source_target_pairs={{0,4},{1,5},{4,8},{5,9},{8,12},{9,13},{12,14},{13,15},{14,10},{15,... | collective-permute-start | bytes 688136 | tf_op jit(solution)/shard_map/ppermute | solution.py:191
  89.0 7.7 %collective-permute-start.27 = (f32[48,1024]{1,0:T(8,128)S(1)}, f32[48,1024]{1,0:T(8,128)S(1)}, u32[]{:S(2)}, u32[]{:S(2)}) collective-permute-start(f32[48,1024]{1,0:T(8,128)S(1)} %get-tuple-element.25), channel_id=1, source_target_pairs={{0,4},{1,5},{4,8},{5,9},{8,12},{9,13},{12,14},{13,15},{14,10},{15,... | collective-permute-start | bytes 589832 | tf_op jit(solution)/shard_map/ppermute | solution.py:191
  90.9 7.8 %collective-permute-start.30 = (f32[48,1024]{1,0:T(8,128)S(1)}, f32[48,1024]{1,0:T(8,128)S(1)}, u32[]{:S(2)}, u32[]{:S(2)}) collective-permute-start(f32[48,1024]{1,0:T(8,128)S(1)} %get-tuple-element.26), channel_id=1, source_target_pairs={{4,0},{5,1},{8,4},{9,5},{12,8},{13,9},{14,12},{15,13},{10,14},{11,... | collective-permute-start | bytes 589832 | tf_op jit(solution)/shard_map/ppermute | solution.py:197
  93.9 7.4 %collective-permute-start.23 = (f32[56,1024]{1,0:T(8,128)S(1)}, f32[56,1024]{1,0:T(8,128)S(1)}, u32[]{:S(2)}, u32[]{:S(2)}) collective-permute-start(f32[56,1024]{1,0:T(8,128)S(1)} %fusion.20), channel_id=1, source_target_pairs={{4,0},{5,1},{8,4},{9,5},{12,8},{13,9},{14,12},{15,13},{10,14},{11,... | collective-permute-start | bytes 688136 | tf_op jit(solution)/shard_map/ppermute | solution.py:197
  (14 other events, 123.9 us)

commit v16 on v15

--- a/solution.py
+++ b/solution.py
@@ -153,7 +153,7 @@
     return chips, snake, place, cw, ccw, partner
 
 
-def ring_all_gather(x, n_blk):
+def ring_all_gather(x, n_blk, extra):
     chips, snake, place, cw, ccw, partner = ring_plan(n_blk)
     ahead = chips // 2
     behind = chips - 1 - ahead
@@ -165,6 +165,8 @@
     left = right = x
     for s in range(1, ahead + 1):
         left = lax.ppermute(left, "blk", cw)
+        if s == 1:
+            left, extra = lax.optimization_barrier((left, extra))
         rel[chips - s] = left
         if s <= behind:
             right = lax.ppermute(right, "blk", ccw)
@@ -175,7 +177,7 @@
     dest_chip, dest_core = dest // 2, dest % 2
     k = (jnp.asarray(place, jnp.int32)[dest_chip] - spot) % chips
     index = jnp.where(dest_core == core, 0, chips) + k
-    return mine, other, index
+    return mine, other, index, extra
 
 
 def ring_reduce_scatter(summed, n_blk):
@@ -228,7 +230,13 @@
     rows_dev = paths.shape[0]
     r_one, r_two = w_first.shape[0], w_second.shape[0]
     hidden = w_first.shape[1]
-    mine, other, index = ring_all_gather(jnp.concatenate([w_first, w_second], axis=0), n_blk)
+    total = jnp.sum(lax.dynamic_index_in_dim(counts, position, 0, keepdims=False))
+    params = jnp.stack(
+        [total, core, jnp.asarray(place, jnp.int32)[position // 2]]
+    ).astype(jnp.int32)
+    mine, other, index, params = ring_all_gather(
+        jnp.concatenate([w_first, w_second], axis=0), n_blk, params
+    )
     fused = r_one % 16 == 0 and r_two % 16 == 0
     if not fused:
         gathered = jnp.take(
@@ -241,8 +249,6 @@
     total = jnp.sum(sending)
     mask = (jnp.arange(rows_dev, dtype=jnp.int32) < total).astype(jnp.float32)
     if fused:
-        spot = jnp.asarray(place, jnp.int32)[position // 2]
-        params = jnp.stack([total, core, spot]).astype(jnp.int32)
         terms = twin_fused(x_rows, z_rows, y_rows, params, place, mine, other, r_one, w_out)
     else:
         terms = twin_terms(x_rows, z_rows, y_rows, mask, w_one, w_two, w_out)

time: 105 us -> 101 us (0.962)
  waiting for transfers between devices: 42.9 us -> 35.7 us
  starting transfers between devices: 23.5 us -> 26.3 us
    ppermute x3, waiting for transfers between devices: 8.84 us -> 0.01 us  [ring_all_gather(): right = lax.ppermute(right, 'blk', ccw)]
    ppermute x4, starting transfers between devices: 1.76 us -> 8.15 us  [ring_all_gather(): left = lax.ppermute(left, 'blk', cw)]
    ppermute x3, starting transfers between devices: 6.07 us -> 0.79 us  [ring_all_gather(): right = lax.ppermute(right, 'blk', ccw)]
    ppermute x7, waiting for transfers between devices: 12.3 us -> 7.99 us  [forward(): acc = lax.ppermute(acc, 'blk', cw) + part[(window - s) % chips]]
    ppermute x7, waiting for transfers between devices: 11.3 us -> 15 us  [backward(): acc = lax.ppermute(acc, 'blk', ccw)]
    ppermute x7, starting transfers between devices: 9.71 us -> 12 us  [forward(): acc = lax.ppermute(acc, 'blk', cw) + part[(window - s) % chips]]
    ppermute x4, waiting for transfers between devices: 10.4 us -> 12.7 us  [ring_all_gather(): left = lax.ppermute(left, 'blk', cw)]
    unnamed x39 -> x35, local copies, waits for them, and re-layouts: 2.3 us -> 1.14 us
  transfers between devices with their start and end apart: 31 -> 31, of which waited for: 16 -> 15; matrix products, arithmetic and copies ran while one was open for 23% -> 25% of each run, Pallas kernels for 6% -> 6%
where the time goes in v16:
time: 101 us; the launch traced here: 100 us
  waiting for transfers between devices  35.7 us (35%)
  starting transfers between devices  26.3 us (26%)
  local copies, waits for them, and re-layouts  10.4 us (10%)
  matrix products  10 us (10%)
  other arithmetic  9.42 us (9%)
  Pallas kernels  6.36 us (6%)
  between operations  1.78 us (2%)
    ppermute x7, waiting for transfers between devices, backward(): acc = lax.ppermute(acc, 'blk', ccw)  15 us
    ppermute x4, waiting for transfers between devices, ring_all_gather(): left = lax.ppermute(left, 'blk', cw)  12.7 us
    ppermute x7, starting transfers between devices, forward(): acc = lax.ppermute(acc, 'blk', cw) + part[(window - s) % chips]  12 us
    ppermute x4, starting transfers between devices, ring_all_gather(): left = lax.ppermute(left, 'blk', cw)  8.15 us
    ppermute x7, waiting for transfers between devices, forward(): acc = lax.ppermute(acc, 'blk', cw) + part[(window - s) % chips]  7.99 us
    dot_general x4, matrix products, rows_first(): lax.dot_general(left, right, (((2,), (0,)), ((), ())), preferred_element_...  6.92 us
    pallas_call x1, Pallas kernels, twin_fused(): pl.pallas_call(functools.partial(twin_body, r_one, place), out_shape=shap...  6.36 us
    dot_general x4, matrix products, slots_product(): lax.dot_general(left, right, (((0,), (0,)), ((), ())), preferred_element_...  3.13 us
  transfers between devices with their start and end apart: 31, of which 15 were waited for; matrix products, arithmetic and copies ran while one was open for 25% of the time, Pallas kernels for 6%

profile of v16, /device:TPU:0, one launch (start us, length us, event | category | flops | bytes accessed | tf_op | source)
XLA Modules:
  0.0 100.1 jit_solution(15897523799428129868)
XLA Ops:
  2.4 3.1 %collective-permute-start = (bf16[96,1024]{1,0:T(8,128)(2,1)S(1)}, bf16[96,1024]{1,0:T(8,128)(2,1)S(1)}, u32[]{:S(2)}, u32[]{:S(2)}) collective-permute-start(bf16[96,1024]{1,0:T(8,128)(2,1)S(1)} %constant_dynamic-update-slice_fusion), channel_id=1, source_target_pairs={{0,4},{1,5},{4,8},{5,9},{8,12},{9,13},{12,14},{13,15},{14,10},{15,... | collective-permute-start | bytes 589832 | tf_op jit(solution)/shard_map/ppermute | solution.py:167
  7.4 1.9 %pad_add_fusion.par_ref = s32[3]{0:T(128)} fusion(s32[1]{0:T(128)} %dynamic_slice.37, s32[1]{0:T(128)} %bitcast.1, s32[1]{0:T(128)} %bitcast), kind=kLoop, calls=%fused_computation.101 | loop fusion | flops 6 | bytes 24 | tf_op jit(solution)/shard_map/stack | solution.py:234
  10.3 1.8 %collective-permute-start.4 = (bf16[96,1024]{1,0:T(8,128)(2,1)S(1)}, bf16[96,1024]{1,0:T(8,128)(2,1)S(1)}, u32[]{:S(2)}, u32[]{:S(2)}) collective-permute-start(bf16[96,1024]{1,0:T(8,128)(2,1)S(1)} %collective-permute-done), channel_id=1, source_target_pairs={{0,4},{1,5},{4,8},{5,9},{8,12},{9,13},{12,14},{13,15},{14,10},{15,... | collective-permute-start | bytes 589832 | tf_op jit(solution)/shard_map/ppermute | solution.py:167
  12.4 4.0 %collective-permute-done.4 = bf16[96,1024]{1,0:T(8,128)(2,1)S(1)} collective-permute-done((bf16[96,1024]{1,0:T(8,128)(2,1)S(1)}, bf16[96,1024]{1,0:T(8,128)(2,1)S(1)}, u32[]{:S(2)}, u32[]{:S(2)}) %collective-permute-start.4) | collective-permute-done | bytes 196640 | tf_op jit(solution)/shard_map/ppermute | solution.py:167
  16.4 1.5 %collective-permute-start.5 = (bf16[96,1024]{1,0:T(8,128)(2,1)S(1)}, bf16[96,1024]{1,0:T(8,128)(2,1)S(1)}, u32[]{:S(2)}, u32[]{:S(2)}) collective-permute-start(bf16[96,1024]{1,0:T(8,128)(2,1)S(1)} %collective-permute-done.4), channel_id=1, source_target_pairs={{0,4},{1,5},{4,8},{5,9},{8,12},{9,13},{12,14},{13,15},{14,10},{15,... | collective-permute-start | bytes 589832 | tf_op jit(solution)/shard_map/ppermute | solution.py:167
  18.5 3.7 %collective-permute-done.5 = bf16[96,1024]{1,0:T(8,128)(2,1)S(1)} collective-permute-done((bf16[96,1024]{1,0:T(8,128)(2,1)S(1)}, bf16[96,1024]{1,0:T(8,128)(2,1)S(1)}, u32[]{:S(2)}, u32[]{:S(2)}) %collective-permute-start.5) | collective-permute-done | bytes 196640 | tf_op jit(solution)/shard_map/ppermute | solution.py:167
  22.2 1.8 %collective-permute-start.6 = (bf16[96,1024]{1,0:T(8,128)(2,1)S(1)}, bf16[96,1024]{1,0:T(8,128)(2,1)S(1)}, u32[]{:S(2)}, u32[]{:S(2)}) collective-permute-start(bf16[96,1024]{1,0:T(8,128)(2,1)S(1)} %collective-permute-done.5), channel_id=1, source_target_pairs={{0,4},{1,5},{4,8},{5,9},{8,12},{9,13},{12,14},{13,15},{14,10},{15,... | collective-permute-start | bytes 589832 | tf_op jit(solution)/shard_map/ppermute | solution.py:167
  24.0 3.9 %collective-permute-done.6 = bf16[96,1024]{1,0:T(8,128)(2,1)S(1)} collective-permute-done((bf16[96,1024]{1,0:T(8,128)(2,1)S(1)}, bf16[96,1024]{1,0:T(8,128)(2,1)S(1)}, u32[]{:S(2)}, u32[]{:S(2)}) %collective-permute-start.6) | collective-permute-done | bytes 196640 | tf_op jit(solution)/shard_map/ppermute | solution.py:167
  33.2 6.4 %shard_map.148 = (bf16[128,512]{1,0:T(8,128)(2,1)}, bf16[128,1024]{1,0:T(8,128)(2,1)}, bf16[128,1024]{1,0:T(8,128)(2,1)}, bf16[1024,128]{1,0:T(8,128)(2,1)}, bf1...) custom-call(s32[3]{0:T(128)} %pad_add_fusion.par_ref, ...), custom_call_target="tpu_custom_call" | custom-call | flops 1476395008 | bytes 5242880 | tf_op jit(solution)/shard_map/pallas_call | solution.py:127
  39.6 1.6 %gather_fusion.1 = bf16[8,2,64,128]{3,2,1,0:T(8,128)(2,1)S(1)} fusion(bf16[8,2,64,128]{3,2,1,0:T(8,128)(2,1)} %bitcast.159, s32[1024]{0:T(1024)S(1)} %pad_clamp_fusion), kind=kCustom, calls=%fused_computation.1 | custom fusion | bytes 524320 | tf_op jit(solution)/shard_map/jit(_take)/gather | solution.py:274
  41.9 1.4 %fusion.17 = f32[8,64,1024]{2,1,0:T(8,128)S(1)} fusion(bf16[128,1024]{1,0:T(8,128)(2,1)} %get-tuple-element.16, bf16[8,2,64,128]{3,2,1,0:T(8,128)(2,1)S(1)} %gather_fusion.1, s32[]{:T(128)S(6)} %select_n.67), kind=kOutput, calls=%fused_computation.23 | convolution fusion | flops 134217728 | bytes 2490372 | tf_op jit(solution)/shard_map/dot_general | solution.py:280
  44.0 2.7 %fusion.13 = f32[8,64,1024]{2,1,0:T(8,128)} fusion(bf16[128,1024]{1,0:T(8,128)(2,1)} %get-tuple-element.18, bf16[8,2,64,128]{3,2,1,0:T(8,128)(2,1)S(1)} %gather_fusion.2, s32[]{:T(128)S(6)} %select_n.67), kind=kOutput, calls=%fused_computation.19 | convolution fusion | flops 134217728 | bytes 2490372 | tf_op jit(solution)/shard_map/dot_general | solution.py:280
  52.9 1.4 %fusion.15 = f32[8,64,1024]{2,1,0:T(8,128)S(1)} fusion(bf16[8,64,128]{2,1,0:T(8,128)(2,1)S(1)} %collective-permute-done.8, bf16[128,1024]{1,0:T(8,128)(2,1)} %collective-permute-done.9), kind=kOutput, calls=%fused_computation.21 | convolution fusion | flops 134217728 | bytes 2490368 | tf_op jit(solution)/shard_map/dot_general | solution.py:280
  54.8 1.5 %add_add_fusion = f32[8,64,1024]{2,1,0:T(8,128)S(1)} fusion(f32[8,64,1024]{2,1,0:T(8,128)S(1)} %copy-done.2, f32[8,64,1024]{2,1,0:T(8,128)S(1)} %fusion.17, f32[8,64,1024]{2,1,0:T(8,128)S(1)} %fusion.15, bf16[8,64,128]{2,1,0:T(8,128)(2,1)S(1)} %collective-permute-done.10, bf16[128,1024]{1,0:T(8,128)(2,1)} %collective-permute-done.11), kind=kOutput, calls=%fused_computation.5 | convolution fusion | flops 135790592 | bytes 8781824 | tf_op jit(solution)/shard_map/dot_general | solution.py:280
  56.3 1.8 %collective-permute-start.24 = (f32[48,1024]{1,0:T(8,128)S(1)}, f32[48,1024]{1,0:T(8,128)S(1)}, u32[]{:S(2)}, u32[]{:S(2)}) collective-permute-start(f32[48,1024]{1,0:T(8,128)S(1)} %get-tuple-element.33), channel_id=1, source_target_pairs={{0,4},{1,5},{4,8},{5,9},{8,12},{9,13},{12,14},{13,15},{14,10},{15,... | collective-permute-start | bytes 589832 | tf_op jit(solution)/shard_map/ppermute | solution.py:193
  58.4 1.3 %fusion.2 = f32[8,32,1024]{2,1,0:T(8,128)S(1)} fusion(bf16[128,8,32]{0,2,1:T(8,128)(2,1)} %collective-permute-done.15, bf16[128,1024]{1,0:T(8,128)(2,1)} %collective-permute-done.16), kind=kOutput, calls=%fused_computation.10 | convolution fusion | flops 67108864 | bytes 1376256 | tf_op jit(solution)/shard_map/dot_general | solution.py:218
  60.1 1.6 %collective-permute-start.17 = (f32[56,1024]{1,0:T(8,128)S(1)}, f32[56,1024]{1,0:T(8,128)S(1)}, u32[]{:S(2)}, u32[]{:S(2)}) collective-permute-start(f32[56,1024]{1,0:T(8,128)S(1)} %get-tuple-element.27), channel_id=1, source_target_pairs={{0,4},{1,5},{4,8},{5,9},{8,12},{9,13},{12,14},{13,15},{14,10},{15,... | collective-permute-start | bytes 688136 | tf_op jit(solution)/shard_map/ppermute | solution.py:193
  62.4 1.4 %collective-permute-done.24 = f32[48,1024]{1,0:T(8,128)S(1)} collective-permute-done((f32[48,1024]{1,0:T(8,128)S(1)}, f32[48,1024]{1,0:T(8,128)S(1)}, u32[]{:S(2)}, u32[]{:S(2)}) %collective-permute-start.24) | collective-permute-done | bytes 196640 | tf_op jit(solution)/shard_map/ppermute | solution.py:193
  63.8 2.1 %collective-permute-start.25 = (f32[48,1024]{1,0:T(8,128)S(1)}, f32[48,1024]{1,0:T(8,128)S(1)}, u32[]{:S(2)}, u32[]{:S(2)}) collective-permute-start(f32[48,1024]{1,0:T(8,128)S(1)} %fusion.33), channel_id=1, source_target_pairs={{0,4},{1,5},{4,8},{5,9},{8,12},{9,13},{12,14},{13,15},{14,10},{15,... | collective-permute-start | bytes 589832 | tf_op jit(solution)/shard_map/ppermute | solution.py:193
  65.9 2.8 %collective-permute-done.17 = f32[56,1024]{1,0:T(8,128)S(1)} collective-permute-done((f32[56,1024]{1,0:T(8,128)S(1)}, f32[56,1024]{1,0:T(8,128)S(1)}, u32[]{:S(2)}, u32[]{:S(2)}) %collective-permute-start.17) | collective-permute-done | bytes 229408 | tf_op jit(solution)/shard_map/ppermute | solution.py:193
  68.7 1.6 %collective-permute-done.20 = f32[56,1024]{1,0:T(8,128)S(1)} collective-permute-done((f32[56,1024]{1,0:T(8,128)S(1)}, f32[56,1024]{1,0:T(8,128)S(1)}, u32[]{:S(2)}, u32[]{:S(2)}) %collective-permute-start.20) | collective-permute-done | bytes 229408 | tf_op jit(solution)/shard_map/ppermute | solution.py:199
  70.3 1.6 %collective-permute-start.18 = (f32[56,1024]{1,0:T(8,128)S(1)}, f32[56,1024]{1,0:T(8,128)S(1)}, u32[]{:S(2)}, u32[]{:S(2)}) collective-permute-start(f32[56,1024]{1,0:T(8,128)S(1)} %get-tuple-element.25), channel_id=1, source_target_pairs={{0,4},{1,5},{4,8},{5,9},{8,12},{9,13},{12,14},{13,15},{14,10},{15,... | collective-permute-start | bytes 688136 | tf_op jit(solution)/shard_map/ppermute | solution.py:193
  72.4 1.8 %collective-permute-done.28 = f32[48,1024]{1,0:T(8,128)S(1)} collective-permute-done((f32[48,1024]{1,0:T(8,128)S(1)}, f32[48,1024]{1,0:T(8,128)S(1)}, u32[]{:S(2)}, u32[]{:S(2)}) %collective-permute-start.28) | collective-permute-done | bytes 196640 | tf_op jit(solution)/shard_map/ppermute | solution.py:199
  74.3 1.6 %collective-permute-start.26 = (f32[48,1024]{1,0:T(8,128)S(1)}, f32[48,1024]{1,0:T(8,128)S(1)}, u32[]{:S(2)}, u32[]{:S(2)}) collective-permute-start(f32[48,1024]{1,0:T(8,128)S(1)} %get-tuple-element.31), channel_id=1, source_target_pairs={{0,4},{1,5},{4,8},{5,9},{8,12},{9,13},{12,14},{13,15},{14,10},{15,... | collective-permute-start | bytes 589832 | tf_op jit(solution)/shard_map/ppermute | solution.py:193
  76.4 2.6 %collective-permute-done.18 = f32[56,1024]{1,0:T(8,128)S(1)} collective-permute-done((f32[56,1024]{1,0:T(8,128)S(1)}, f32[56,1024]{1,0:T(8,128)S(1)}, u32[]{:S(2)}, u32[]{:S(2)}) %collective-permute-start.18) | collective-permute-done | bytes 229408 | tf_op jit(solution)/shard_map/ppermute | solution.py:193
  80.7 1.6 %collective-permute-start.19 = (f32[56,1024]{1,0:T(8,128)S(1)}, f32[56,1024]{1,0:T(8,128)S(1)}, u32[]{:S(2)}, u32[]{:S(2)}) collective-permute-start(f32[56,1024]{1,0:T(8,128)S(1)} %get-tuple-element.23), channel_id=1, source_target_pairs={{0,4},{1,5},{4,8},{5,9},{8,12},{9,13},{12,14},{13,15},{14,10},{15,... | collective-permute-start | bytes 688136 | tf_op jit(solution)/shard_map/ppermute | solution.py:193
  82.3 2.1 %collective-permute-done.29 = f32[48,1024]{1,0:T(8,128)S(1)} collective-permute-done((f32[48,1024]{1,0:T(8,128)S(1)}, f32[48,1024]{1,0:T(8,128)S(1)}, u32[]{:S(2)}, u32[]{:S(2)}) %collective-permute-start.29) | collective-permute-done | bytes 196640 | tf_op jit(solution)/shard_map/ppermute | solution.py:199
  84.4 1.6 %collective-permute-start.27 = (f32[48,1024]{1,0:T(8,128)S(1)}, f32[48,1024]{1,0:T(8,128)S(1)}, u32[]{:S(2)}, u32[]{:S(2)}) collective-permute-start(f32[48,1024]{1,0:T(8,128)S(1)} %get-tuple-element.29), channel_id=1, source_target_pairs={{0,4},{1,5},{4,8},{5,9},{8,12},{9,13},{12,14},{13,15},{14,10},{15,... | collective-permute-start | bytes 589832 | tf_op jit(solution)/shard_map/ppermute | solution.py:193
  86.5 2.8 %collective-permute-done.22 = f32[56,1024]{1,0:T(8,128)S(1)} collective-permute-done((f32[56,1024]{1,0:T(8,128)S(1)}, f32[56,1024]{1,0:T(8,128)S(1)}, u32[]{:S(2)}, u32[]{:S(2)}) %collective-permute-start.22) | collective-permute-done | bytes 229408 | tf_op jit(solution)/shard_map/ppermute | solution.py:199
  89.4 1.2 %collective-permute-done.27 = f32[48,1024]{1,0:T(8,128)S(1)} collective-permute-done((f32[48,1024]{1,0:T(8,128)S(1)}, f32[48,1024]{1,0:T(8,128)S(1)}, u32[]{:S(2)}, u32[]{:S(2)}) %collective-permute-start.27) | collective-permute-done | bytes 196640 | tf_op jit(solution)/shard_map/ppermute | solution.py:193
  90.6 3.2 %collective-permute-done.30 = f32[48,1024]{1,0:T(8,128)S(1)} collective-permute-done((f32[48,1024]{1,0:T(8,128)S(1)}, f32[48,1024]{1,0:T(8,128)S(1)}, u32[]{:S(2)}, u32[]{:S(2)}) %collective-permute-start.30) | collective-permute-done | bytes 196640 | tf_op jit(solution)/shard_map/ppermute | solution.py:199
  93.9 2.4 %collective-permute-done.23 = f32[56,1024]{1,0:T(8,128)S(1)} collective-permute-done((f32[56,1024]{1,0:T(8,128)S(1)}, f32[56,1024]{1,0:T(8,128)S(1)}, u32[]{:S(2)}, u32[]{:S(2)}) %collective-permute-start.23) | collective-permute-done | bytes 229408 | tf_op jit(solution)/shard_map/ppermute | solution.py:199
  (118 shorter events, 26.7 us)
Async XLA Ops:
  2.4 7.9 %collective-permute-start = (bf16[96,1024]{1,0:T(8,128)(2,1)S(1)}, bf16[96,1024]{1,0:T(8,128)(2,1)S(1)}, u32[]{:S(2)}, u32[]{:S(2)}) collective-permute-start(bf16[96,1024]{1,0:T(8,128)(2,1)S(1)} %constant_dynamic-update-slice_fusion), channel_id=1, source_target_pairs={{0,4},{1,5},{4,8},{5,9},{8,12},{9,13},{12,14},{13,15},{14,10},{15,... | collective-permute-start | bytes 589832 | tf_op jit(solution)/shard_map/ppermute | solution.py:167
  5.5 6.6 %collective-permute-start.1 = (bf16[96,1024]{1,0:T(8,128)(2,1)S(1)}, bf16[96,1024]{1,0:T(8,128)(2,1)S(1)}, u32[]{:S(2)}, u32[]{:S(2)}) collective-permute-start(bf16[96,1024]{1,0:T(8,128)(2,1)S(1)} %constant_dynamic-update-slice_fusion), channel_id=1, source_target_pairs={{4,0},{5,1},{8,4},{9,5},{12,8},{13,9},{14,12},{15,13},{10,14},{11,... | collective-permute-start | bytes 589832 | tf_op jit(solution)/shard_map/ppermute | solution.py:172
  9.3 19.7 %copy-start.1 = (s32[8]{0:T(128)S(1)}, s32[8]{0:T(128)}, u32[]{:S(2)}) copy-start(s32[8]{0:T(128)} %constant.103.clone) | copy-start | bytes 100
  10.3 6.1 %collective-permute-start.4 = (bf16[96,1024]{1,0:T(8,128)(2,1)S(1)}, bf16[96,1024]{1,0:T(8,128)(2,1)S(1)}, u32[]{:S(2)}, u32[]{:S(2)}) collective-permute-start(bf16[96,1024]{1,0:T(8,128)(2,1)S(1)} %collective-permute-done), channel_id=1, source_target_pairs={{0,4},{1,5},{4,8},{5,9},{8,12},{9,13},{12,14},{13,15},{14,10},{15,... | collective-permute-start | bytes 589832 | tf_op jit(solution)/shard_map/ppermute | solution.py:167
  12.1 5.8 %collective-permute-start.2 = (bf16[96,1024]{1,0:T(8,128)(2,1)S(1)}, bf16[96,1024]{1,0:T(8,128)(2,1)S(1)}, u32[]{:S(2)}, u32[]{:S(2)}) collective-permute-start(bf16[96,1024]{1,0:T(8,128)(2,1)S(1)} %collective-permute-done.1), channel_id=1, source_target_pairs={{4,0},{5,1},{8,4},{9,5},{12,8},{13,9},{14,12},{15,13},{10,14},{11,... | collective-permute-start | bytes 589832 | tf_op jit(solution)/shard_map/ppermute | solution.py:172
  16.4 5.8 %collective-permute-start.5 = (bf16[96,1024]{1,0:T(8,128)(2,1)S(1)}, bf16[96,1024]{1,0:T(8,128)(2,1)S(1)}, u32[]{:S(2)}, u32[]{:S(2)}) collective-permute-start(bf16[96,1024]{1,0:T(8,128)(2,1)S(1)} %collective-permute-done.4), channel_id=1, source_target_pairs={{0,4},{1,5},{4,8},{5,9},{8,12},{9,13},{12,14},{13,15},{14,10},{15,... | collective-permute-start | bytes 589832 | tf_op jit(solution)/shard_map/ppermute | solution.py:167
  17.9 6.1 %collective-permute-start.3 = (bf16[96,1024]{1,0:T(8,128)(2,1)S(1)}, bf16[96,1024]{1,0:T(8,128)(2,1)S(1)}, u32[]{:S(2)}, u32[]{:S(2)}) collective-permute-start(bf16[96,1024]{1,0:T(8,128)(2,1)S(1)} %collective-permute-done.2), channel_id=1, source_target_pairs={{4,0},{5,1},{8,4},{9,5},{12,8},{13,9},{14,12},{15,13},{10,14},{11,... | collective-permute-start | bytes 589832 | tf_op jit(solution)/shard_map/ppermute | solution.py:172
  22.2 5.7 %collective-permute-start.6 = (bf16[96,1024]{1,0:T(8,128)(2,1)S(1)}, bf16[96,1024]{1,0:T(8,128)(2,1)S(1)}, u32[]{:S(2)}, u32[]{:S(2)}) collective-permute-start(bf16[96,1024]{1,0:T(8,128)(2,1)S(1)} %collective-permute-done.5), channel_id=1, source_target_pairs={{0,4},{1,5},{4,8},{5,9},{8,12},{9,13},{12,14},{13,15},{14,10},{15,... | collective-permute-start | bytes 589832 | tf_op jit(solution)/shard_map/ppermute | solution.py:167
  28.0 5.2 %collective-permute-start.7 = (bf16[8,96,1024]{2,1,0:T(8,128)(2,1)S(1)}, bf16[8,96,1024]{2,1,0:T(8,128)(2,1)}, u32[]{:S(2)}, u32[]{:S(2)}) collective-permute-start(bf16[8,96,1024]{2,1,0:T(8,128)(2,1)S(1)} %bitcast_dynamic-update-slice_fusion.mine_ref), channel_id=1, source_target_pairs={{0,1},{1,0},{2,3},{3,2},{4,5},{5,4},{6,7},{7,6},{8,9},{9,8},{10,11... | collective-permute-start | bytes 4718600 | tf_op jit(solution)/shard_map/ppermute | solution.py:175
  30.9 27.5 %collective-permute-start.15 = (bf16[128,8,32]{0,2,1:T(8,128)(2,1)}, bf16[128,8,32]{0,2,1:T(8,128)(2,1)}, u32[]{:S(2)}, u32[]{:S(2)}) collective-permute-start(bf16[128,8,32]{0,2,1:T(8,128)(2,1)} %dynamic-slice_bitcast_fusion.2), channel_id=1, source_target_pairs={{0,1},{1,0},{2,3},{3,2},{4,5},{5,4},{6,7},{7,6},{8,9},{9,8},{10,11... | collective-permute-start | bytes 196616 | tf_op jit(solution)/shard_map/ppermute | solution.py:268
  41.9 10.9 %collective-permute-start.9 = (bf16[128,1024]{1,0:T(8,128)(2,1)}, bf16[128,1024]{1,0:T(8,128)(2,1)}, u32[]{:S(2)}, u32[]{:S(2)}) collective-permute-start(bf16[128,1024]{1,0:T(8,128)(2,1)} %get-tuple-element.16), channel_id=1, source_target_pairs={{0,1},{1,0},{2,3},{3,2},{4,5},{5,4},{6,7},{7,6},{8,9},{9,8},{10,11... | collective-permute-start | bytes 786440 | tf_op jit(solution)/shard_map/ppermute | solution.py:271
  46.7 8.1 %collective-permute-start.11 = (bf16[128,1024]{1,0:T(8,128)(2,1)}, bf16[128,1024]{1,0:T(8,128)(2,1)}, u32[]{:S(2)}, u32[]{:S(2)}) collective-permute-start(bf16[128,1024]{1,0:T(8,128)(2,1)} %get-tuple-element.18), channel_id=1, source_target_pairs={{0,1},{1,0},{2,3},{3,2},{4,5},{5,4},{6,7},{7,6},{8,9},{9,8},{10,11... | collective-permute-start | bytes 786440 | tf_op jit(solution)/shard_map/ppermute | solution.py:271
  48.4 10.1 %collective-permute-start.16 = (bf16[128,1024]{1,0:T(8,128)(2,1)}, bf16[128,1024]{1,0:T(8,128)(2,1)}, u32[]{:S(2)}, u32[]{:S(2)}) collective-permute-start(bf16[128,1024]{1,0:T(8,128)(2,1)} %get-tuple-element.22), channel_id=1, source_target_pairs={{0,1},{1,0},{2,3},{3,2},{4,5},{5,4},{6,7},{7,6},{8,9},{9,8},{10,11... | collective-permute-start | bytes 786440 | tf_op jit(solution)/shard_map/ppermute | solution.py:271
  48.5 2.1 %collective-permute-start.12 = (f32[1024]{0:T(1024)S(1)}, f32[1024]{0:T(1024)}, u32[]{:S(2)}, u32[]{:S(2)}) collective-permute-start(f32[1024]{0:T(1024)S(1)} %bitcast.160), channel_id=1, source_target_pairs={{0,1},{1,0},{2,3},{3,2},{4,5},{5,4},{6,7},{7,6},{8,9},{9,8},{10,11... | collective-permute-start | bytes 12296 | tf_op jit(solution)/shard_map/ppermute | solution.py:271
  50.6 1.7 %collective-permute-start.8 = (bf16[8,64,128]{2,1,0:T(8,128)(2,1)}, bf16[8,64,128]{2,1,0:T(8,128)(2,1)S(1)}, u32[]{:S(2)}, u32[]{:S(2)}) collective-permute-start(bf16[8,64,128]{2,1,0:T(8,128)(2,1)} %dynamic-slice_bitcast_fusion.1), channel_id=1, source_target_pairs={{0,1},{1,0},{2,3},{3,2},{4,5},{5,4},{6,7},{7,6},{8,9},{9,8},{10,11... | collective-permute-start | bytes 393224 | tf_op jit(solution)/shard_map/ppermute | solution.py:277
  52.3 1.9 %collective-permute-start.10 = (bf16[8,64,128]{2,1,0:T(8,128)(2,1)S(1)}, bf16[8,64,128]{2,1,0:T(8,128)(2,1)S(1)}, u32[]{:S(2)}, u32[]{:S(2)}) collective-permute-start(bf16[8,64,128]{2,1,0:T(8,128)(2,1)S(1)} %dynamic-slice_bitcast_fusion), channel_id=1, source_target_pairs={{0,1},{1,0},{2,3},{3,2},{4,5},{5,4},{6,7},{7,6},{8,9},{9,8},{10,11... | collective-permute-start | bytes 393224 | tf_op jit(solution)/shard_map/ppermute | solution.py:277
  52.8 5.3 %collective-permute-start.13 = (bf16[128,8,32]{0,2,1:T(8,128)(2,1)S(1)}, bf16[128,8,32]{0,2,1:T(8,128)(2,1)S(1)}, u32[]{:S(2)}, u32[]{:S(2)}) collective-permute-start(bf16[128,8,32]{0,2,1:T(8,128)(2,1)S(1)} %dynamic-slice_bitcast_fusion.3), channel_id=1, source_target_pairs={{0,1},{1,0},{2,3},{3,2},{4,5},{5,4},{6,7},{7,6},{8,9},{9,8},{10,11... | collective-permute-start | bytes 196616 | tf_op jit(solution)/shard_map/ppermute | solution.py:268
  54.3 3.9 %collective-permute-start.14 = (bf16[128,1024]{1,0:T(8,128)(2,1)S(1)}, bf16[128,1024]{1,0:T(8,128)(2,1)S(1)}, u32[]{:S(2)}, u32[]{:S(2)}) collective-permute-start(bf16[128,1024]{1,0:T(8,128)(2,1)S(1)} %copy-done.4), channel_id=1, source_target_pairs={{0,1},{1,0},{2,3},{3,2},{4,5},{5,4},{6,7},{7,6},{8,9},{9,8},{10,11... | collective-permute-start | bytes 786440 | tf_op jit(solution)/shard_map/ppermute | solution.py:271
  56.3 7.5 %collective-permute-start.24 = (f32[48,1024]{1,0:T(8,128)S(1)}, f32[48,1024]{1,0:T(8,128)S(1)}, u32[]{:S(2)}, u32[]{:S(2)}) collective-permute-start(f32[48,1024]{1,0:T(8,128)S(1)} %get-tuple-element.33), channel_id=1, source_target_pairs={{0,4},{1,5},{4,8},{5,9},{8,12},{9,13},{12,14},{13,15},{14,10},{15,... | collective-permute-start | bytes 589832 | tf_op jit(solution)/shard_map/ppermute | solution.py:193
  60.1 8.6 %collective-permute-start.17 = (f32[56,1024]{1,0:T(8,128)S(1)}, f32[56,1024]{1,0:T(8,128)S(1)}, u32[]{:S(2)}, u32[]{:S(2)}) collective-permute-start(f32[56,1024]{1,0:T(8,128)S(1)} %get-tuple-element.27), channel_id=1, source_target_pairs={{0,4},{1,5},{4,8},{5,9},{8,12},{9,13},{12,14},{13,15},{14,10},{15,... | collective-permute-start | bytes 688136 | tf_op jit(solution)/shard_map/ppermute | solution.py:193
  61.7 8.5 %collective-permute-start.20 = (f32[56,1024]{1,0:T(8,128)S(1)}, f32[56,1024]{1,0:T(8,128)S(1)}, u32[]{:S(2)}, u32[]{:S(2)}) collective-permute-start(f32[56,1024]{1,0:T(8,128)S(1)} %get-tuple-element.28), channel_id=1, source_target_pairs={{4,0},{5,1},{8,4},{9,5},{12,8},{13,9},{14,12},{15,13},{10,14},{11,... | collective-permute-start | bytes 688136 | tf_op jit(solution)/shard_map/ppermute | solution.py:199
  62.2 12.0 %collective-permute-start.28 = (f32[48,1024]{1,0:T(8,128)S(1)}, f32[48,1024]{1,0:T(8,128)S(1)}, u32[]{:S(2)}, u32[]{:S(2)}) collective-permute-start(f32[48,1024]{1,0:T(8,128)S(1)} %get-tuple-element.34), channel_id=1, source_target_pairs={{4,0},{5,1},{8,4},{9,5},{12,8},{13,9},{14,12},{15,13},{10,14},{11,... | collective-permute-start | bytes 589832 | tf_op jit(solution)/shard_map/ppermute | solution.py:199
  63.8 10.4 %collective-permute-start.25 = (f32[48,1024]{1,0:T(8,128)S(1)}, f32[48,1024]{1,0:T(8,128)S(1)}, u32[]{:S(2)}, u32[]{:S(2)}) collective-permute-start(f32[48,1024]{1,0:T(8,128)S(1)} %fusion.33), channel_id=1, source_target_pairs={{0,4},{1,5},{4,8},{5,9},{8,12},{9,13},{12,14},{13,15},{14,10},{15,... | collective-permute-start | bytes 589832 | tf_op jit(solution)/shard_map/ppermute | solution.py:193
  70.3 8.6 %collective-permute-start.18 = (f32[56,1024]{1,0:T(8,128)S(1)}, f32[56,1024]{1,0:T(8,128)S(1)}, u32[]{:S(2)}, u32[]{:S(2)}) collective-permute-start(f32[56,1024]{1,0:T(8,128)S(1)} %get-tuple-element.25), channel_id=1, source_target_pairs={{0,4},{1,5},{4,8},{5,9},{8,12},{9,13},{12,14},{13,15},{14,10},{15,... | collective-permute-start | bytes 688136 | tf_op jit(solution)/shard_map/ppermute | solution.py:193
  72.0 8.1 %collective-permute-start.21 = (f32[56,1024]{1,0:T(8,128)S(1)}, f32[56,1024]{1,0:T(8,128)S(1)}, u32[]{:S(2)}, u32[]{:S(2)}) collective-permute-start(f32[56,1024]{1,0:T(8,128)S(1)} %get-tuple-element.26), channel_id=1, source_target_pairs={{4,0},{5,1},{8,4},{9,5},{12,8},{13,9},{14,12},{15,13},{10,14},{11,... | collective-permute-start | bytes 688136 | tf_op jit(solution)/shard_map/ppermute | solution.py:199
  74.3 8.0 %collective-permute-start.26 = (f32[48,1024]{1,0:T(8,128)S(1)}, f32[48,1024]{1,0:T(8,128)S(1)}, u32[]{:S(2)}, u32[]{:S(2)}) collective-permute-start(f32[48,1024]{1,0:T(8,128)S(1)} %get-tuple-element.31), channel_id=1, source_target_pairs={{0,4},{1,5},{4,8},{5,9},{8,12},{9,13},{12,14},{13,15},{14,10},{15,... | collective-permute-start | bytes 589832 | tf_op jit(solution)/shard_map/ppermute | solution.py:193
  75.9 8.4 %collective-permute-start.29 = (f32[48,1024]{1,0:T(8,128)S(1)}, f32[48,1024]{1,0:T(8,128)S(1)}, u32[]{:S(2)}, u32[]{:S(2)}) collective-permute-start(f32[48,1024]{1,0:T(8,128)S(1)} %get-tuple-element.32), channel_id=1, source_target_pairs={{4,0},{5,1},{8,4},{9,5},{12,8},{13,9},{14,12},{15,13},{10,14},{11,... | collective-permute-start | bytes 589832 | tf_op jit(solution)/shard_map/ppermute | solution.py:199
  80.2 9.1 %collective-permute-start.22 = (f32[56,1024]{1,0:T(8,128)S(1)}, f32[56,1024]{1,0:T(8,128)S(1)}, u32[]{:S(2)}, u32[]{:S(2)}) collective-permute-start(f32[56,1024]{1,0:T(8,128)S(1)} %get-tuple-element.24), channel_id=1, source_target_pairs={{4,0},{5,1},{8,4},{9,5},{12,8},{13,9},{14,12},{15,13},{10,14},{11,... | collective-permute-start | bytes 688136 | tf_op jit(solution)/shard_map/ppermute | solution.py:199
  80.7 13.2 %collective-permute-start.19 = (f32[56,1024]{1,0:T(8,128)S(1)}, f32[56,1024]{1,0:T(8,128)S(1)}, u32[]{:S(2)}, u32[]{:S(2)}) collective-permute-start(f32[56,1024]{1,0:T(8,128)S(1)} %get-tuple-element.23), channel_id=1, source_target_pairs={{0,4},{1,5},{4,8},{5,9},{8,12},{9,13},{12,14},{13,15},{14,10},{15,... | collective-permute-start | bytes 688136 | tf_op jit(solution)/shard_map/ppermute | solution.py:193
  84.4 6.2 %collective-permute-start.27 = (f32[48,1024]{1,0:T(8,128)S(1)}, f32[48,1024]{1,0:T(8,128)S(1)}, u32[]{:S(2)}, u32[]{:S(2)}) collective-permute-start(f32[48,1024]{1,0:T(8,128)S(1)} %get-tuple-element.29), channel_id=1, source_target_pairs={{0,4},{1,5},{4,8},{5,9},{8,12},{9,13},{12,14},{13,15},{14,10},{15,... | collective-permute-start | bytes 589832 | tf_op jit(solution)/shard_map/ppermute | solution.py:193
  86.0 7.8 %collective-permute-start.30 = (f32[48,1024]{1,0:T(8,128)S(1)}, f32[48,1024]{1,0:T(8,128)S(1)}, u32[]{:S(2)}, u32[]{:S(2)}) collective-permute-start(f32[48,1024]{1,0:T(8,128)S(1)} %get-tuple-element.30), channel_id=1, source_target_pairs={{4,0},{5,1},{8,4},{9,5},{12,8},{13,9},{14,12},{15,13},{10,14},{11,... | collective-permute-start | bytes 589832 | tf_op jit(solution)/shard_map/ppermute | solution.py:199
  89.3 7.0 %collective-permute-start.23 = (f32[56,1024]{1,0:T(8,128)S(1)}, f32[56,1024]{1,0:T(8,128)S(1)}, u32[]{:S(2)}, u32[]{:S(2)}) collective-permute-start(f32[56,1024]{1,0:T(8,128)S(1)} %fusion.20), channel_id=1, source_target_pairs={{4,0},{5,1},{8,4},{9,5},{12,8},{13,9},{14,12},{15,13},{10,14},{11,... | collective-permute-start | bytes 688136 | tf_op jit(solution)/shard_map/ppermute | solution.py:199
  (12 other events, 65.6 us)

commit v17 on v16

--- a/solution.py
+++ b/solution.py
@@ -98,7 +98,7 @@
     ea2 = (eg2 * wo * s2 * (1.0 - s2) + ev * wo * s2).astype(jnp.bfloat16)
     eh1 = _nt(ea2, w2)
     ea1 = (es1 * s1 * (1.0 - s1) + eh1 * s1).astype(jnp.bfloat16)
-    es_ref[...] = ed
+    es_ref[...] = ed.astype(jnp.float32).T.astype(jnp.bfloat16)
     g1_ref[...] = g1
     ea1_ref[...] = ea1
     ec1_ref[...] = ec1.astype(jnp.float32).T.astype(jnp.bfloat16)
@@ -112,7 +112,7 @@
     chips, width, hidden = mine.shape
     bf, f32 = jnp.bfloat16, jnp.float32
     shapes = (
-        jax.ShapeDtypeStruct((rows, assets), bf),
+        jax.ShapeDtypeStruct((assets, rows), bf),
         jax.ShapeDtypeStruct((rows, hidden), bf),
         jax.ShapeDtypeStruct((rows, hidden), bf),
         jax.ShapeDtypeStruct((hidden, rows), bf),
@@ -254,7 +254,7 @@
         terms = twin_terms(x_rows, z_rows, y_rows, mask, w_one, w_two, w_out)
     e_slope, g_one, e_aone, e_cone, g_two, h_one, e_atwo, grad_three = terms
     if not fused:
-        e_cone, h_one = e_cone.T, h_one.T
+        e_cone, h_one, e_slope = e_cone.T, h_one.T, e_slope.T
     chip = position // 2
     spot = jnp.asarray(place, jnp.int32)[chip]
     ring_chips = jnp.asarray(snake, jnp.int32)[(spot + jnp.arange(chips, dtype=jnp.int32)) % chips]
@@ -285,7 +285,7 @@
     h_keep, h_got = split_rows(h_one, r_two)
     g2_got = swap(g_two)
     g1_got = swap(g_one)
-    ed_keep, ed_got = split_cols(e_slope, r_one)
+    ed_keep, ed_got = split_rows(e_slope, r_one)
     ec_keep, ec_got = split_rows(e_cone, r_two)
     ea2_got = swap(e_atwo)
     ea1_got = swap(e_aone)
@@ -295,7 +295,7 @@
         + rows_first(h_keep, e_atwo) + rows_first(h_got, ea2_got)
     )
     part_one = (
-        slots_product(ed_keep, g_one) + slots_product(ed_got, g1_got)
+        rows_first(ed_keep, g_one) + rows_first(ed_got, g1_got)
         + slots_product(x_keep, e_aone) + slots_product(x_got, ea1_got)
     )
     own_row = jnp.arange(chips, dtype=jnp.int32)[:, None] == chip

time: 101 us -> 101 us (level)
    gather x2 -> x3, local copies, waits for them, and re-layouts: 2.19 us -> 3.66 us  [split_rows(): jnp.take(f.reshape(chips, 2, width, rows_dev), ring_chips, axis=0, mode='...]
    pallas_call x1 -> x0, local copies, waits for them, and re-layouts: 1.02 us -> none  [twin_fused(): pl.pallas_call(functools.partial(twin_body, r_one, place), out_shape=shap...]
    dot_general x4 -> x2, matrix products: 3.13 us -> 2.5 us  [slots_product(): lax.dot_general(left, right, (((0,), (0,)), ((), ())), preferred_element_...]
    dot_general x4 -> x6, matrix products: 6.92 us -> 7.53 us  [rows_first(): lax.dot_general(left, right, (((2,), (0,)), ((), ())), preferred_element_...]
where the time goes in v17:
time: 101 us; the launch traced here: 100 us
  waiting for transfers between devices  35.7 us (35%)
  starting transfers between devices  26.3 us (26%)
  local copies, waits for them, and re-layouts  11 us (11%)
  matrix products  10 us (10%)
  other arithmetic  9.42 us (9%)
  Pallas kernels  6.36 us (6%)
  between operations  1.75 us (2%)
    ppermute x7, waiting for transfers between devices, backward(): acc = lax.ppermute(acc, 'blk', ccw)  15.1 us
    ppermute x4, waiting for transfers between devices, ring_all_gather(): left = lax.ppermute(left, 'blk', cw)  12.7 us
    ppermute x7, starting transfers between devices, forward(): acc = lax.ppermute(acc, 'blk', cw) + part[(window - s) % chips]  12.1 us
    ppermute x4, starting transfers between devices, ring_all_gather(): left = lax.ppermute(left, 'blk', cw)  8.15 us
    ppermute x7, waiting for transfers between devices, forward(): acc = lax.ppermute(acc, 'blk', cw) + part[(window - s) % chips]  7.85 us
    dot_general x6, matrix products, rows_first(): lax.dot_general(left, right, (((2,), (0,)), ((), ())), preferred_element_...  7.53 us
    pallas_call x1, Pallas kernels, twin_fused(): pl.pallas_call(functools.partial(twin_body, r_one, place), out_shape=shap...  6.36 us
    gather x3, local copies, waits for them, and re-layouts, split_rows(): jnp.take(f.reshape(chips, 2, width, rows_dev), ring_chips, axis=0, mode='...  3.66 us
  transfers between devices with their start and end apart: 31, of which 15 were waited for; matrix products, arithmetic and copies ran while one was open for 25% of the time, Pallas kernels for 6%

profile of v17, /device:TPU:0, one launch (start us, length us, event | category | flops | bytes accessed | tf_op | source)
XLA Modules:
  0.0 100.5 jit_solution(1810872020340579199)
XLA Ops:
  2.4 3.1 %collective-permute-start = (bf16[96,1024]{1,0:T(8,128)(2,1)S(1)}, bf16[96,1024]{1,0:T(8,128)(2,1)S(1)}, u32[]{:S(2)}, u32[]{:S(2)}) collective-permute-start(bf16[96,1024]{1,0:T(8,128)(2,1)S(1)} %constant_dynamic-update-slice_fusion), channel_id=1, source_target_pairs={{0,4},{1,5},{4,8},{5,9},{8,12},{9,13},{12,14},{13,15},{14,10},{15,... | collective-permute-start | bytes 589832 | tf_op jit(solution)/shard_map/ppermute | solution.py:167
  7.4 1.9 %pad_add_fusion.par_ref = s32[3]{0:T(128)} fusion(s32[1]{0:T(128)} %dynamic_slice.38, s32[1]{0:T(128)} %bitcast.1, s32[1]{0:T(128)} %bitcast), kind=kLoop, calls=%fused_computation.101 | loop fusion | flops 6 | bytes 24 | tf_op jit(solution)/shard_map/stack | solution.py:234
  10.3 1.8 %collective-permute-start.4 = (bf16[96,1024]{1,0:T(8,128)(2,1)S(1)}, bf16[96,1024]{1,0:T(8,128)(2,1)S(1)}, u32[]{:S(2)}, u32[]{:S(2)}) collective-permute-start(bf16[96,1024]{1,0:T(8,128)(2,1)S(1)} %collective-permute-done), channel_id=1, source_target_pairs={{0,4},{1,5},{4,8},{5,9},{8,12},{9,13},{12,14},{13,15},{14,10},{15,... | collective-permute-start | bytes 589832 | tf_op jit(solution)/shard_map/ppermute | solution.py:167
  12.4 4.0 %collective-permute-done.4 = bf16[96,1024]{1,0:T(8,128)(2,1)S(1)} collective-permute-done((bf16[96,1024]{1,0:T(8,128)(2,1)S(1)}, bf16[96,1024]{1,0:T(8,128)(2,1)S(1)}, u32[]{:S(2)}, u32[]{:S(2)}) %collective-permute-start.4) | collective-permute-done | bytes 196640 | tf_op jit(solution)/shard_map/ppermute | solution.py:167
  16.4 1.5 %collective-permute-start.5 = (bf16[96,1024]{1,0:T(8,128)(2,1)S(1)}, bf16[96,1024]{1,0:T(8,128)(2,1)S(1)}, u32[]{:S(2)}, u32[]{:S(2)}) collective-permute-start(bf16[96,1024]{1,0:T(8,128)(2,1)S(1)} %collective-permute-done.4), channel_id=1, source_target_pairs={{0,4},{1,5},{4,8},{5,9},{8,12},{9,13},{12,14},{13,15},{14,10},{15,... | collective-permute-start | bytes 589832 | tf_op jit(solution)/shard_map/ppermute | solution.py:167
  18.5 3.7 %collective-permute-done.5 = bf16[96,1024]{1,0:T(8,128)(2,1)S(1)} collective-permute-done((bf16[96,1024]{1,0:T(8,128)(2,1)S(1)}, bf16[96,1024]{1,0:T(8,128)(2,1)S(1)}, u32[]{:S(2)}, u32[]{:S(2)}) %collective-permute-start.5) | collective-permute-done | bytes 196640 | tf_op jit(solution)/shard_map/ppermute | solution.py:167
  22.2 1.8 %collective-permute-start.6 = (bf16[96,1024]{1,0:T(8,128)(2,1)S(1)}, bf16[96,1024]{1,0:T(8,128)(2,1)S(1)}, u32[]{:S(2)}, u32[]{:S(2)}) collective-permute-start(bf16[96,1024]{1,0:T(8,128)(2,1)S(1)} %collective-permute-done.5), channel_id=1, source_target_pairs={{0,4},{1,5},{4,8},{5,9},{8,12},{9,13},{12,14},{13,15},{14,10},{15,... | collective-permute-start | bytes 589832 | tf_op jit(solution)/shard_map/ppermute | solution.py:167
  24.0 3.9 %collective-permute-done.6 = bf16[96,1024]{1,0:T(8,128)(2,1)S(1)} collective-permute-done((bf16[96,1024]{1,0:T(8,128)(2,1)S(1)}, bf16[96,1024]{1,0:T(8,128)(2,1)S(1)}, u32[]{:S(2)}, u32[]{:S(2)}) %collective-permute-start.6) | collective-permute-done | bytes 196640 | tf_op jit(solution)/shard_map/ppermute | solution.py:167
  33.2 6.4 %shard_map.148 = (bf16[512,128]{1,0:T(8,128)(2,1)}, bf16[128,1024]{1,0:T(8,128)(2,1)}, bf16[128,1024]{1,0:T(8,128)(2,1)}, bf16[1024,128]{1,0:T(8,128)(2,1)}, bf1...) custom-call(s32[3]{0:T(128)} %pad_add_fusion.par_ref, ...), custom_call_target="tpu_custom_call" | custom-call | flops 1476395008 | bytes 5242880 | tf_op jit(solution)/shard_map/pallas_call | solution.py:127
  39.6 1.6 %gather_fusion.1 = bf16[8,2,64,128]{3,2,1,0:T(8,128)(2,1)S(1)} fusion(bf16[8,2,64,128]{3,2,1,0:T(8,128)(2,1)} %bitcast.150, s32[1024]{0:T(1024)S(1)} %pad_clamp_fusion), kind=kCustom, calls=%fused_computation.1 | custom fusion | bytes 524320 | tf_op jit(solution)/shard_map/jit(_take)/gather | solution.py:274
  41.9 1.4 %fusion.17 = f32[8,64,1024]{2,1,0:T(8,128)S(1)} fusion(bf16[128,1024]{1,0:T(8,128)(2,1)} %get-tuple-element.16, bf16[8,2,64,128]{3,2,1,0:T(8,128)(2,1)S(1)} %gather_fusion.1, s32[]{:T(128)S(6)} %select_n.68), kind=kOutput, calls=%fused_computation.23 | convolution fusion | flops 134217728 | bytes 2490372 | tf_op jit(solution)/shard_map/dot_general | solution.py:280
  44.6 2.7 %fusion.13 = f32[8,64,1024]{2,1,0:T(8,128)} fusion(bf16[128,1024]{1,0:T(8,128)(2,1)} %get-tuple-element.18, bf16[8,2,64,128]{3,2,1,0:T(8,128)(2,1)S(1)} %gather_fusion.2, s32[]{:T(128)S(6)} %select_n.68), kind=kOutput, calls=%fused_computation.19 | convolution fusion | flops 134217728 | bytes 2490372 | tf_op jit(solution)/shard_map/dot_general | solution.py:280
  49.6 1.5 %gather_fusion.3 = bf16[8,2,32,128]{3,2,1,0:T(8,128)(2,1)S(1)} fusion(bf16[8,2,32,128]{3,2,1,0:T(8,128)(2,1)} %bitcast.151, s32[1024]{0:T(1024)S(1)} %pad_clamp_fusion), kind=kCustom, calls=%fused_computation.3 | custom fusion | bytes 262176 | tf_op jit(solution)/shard_map/jit(_take)/gather | solution.py:274
  53.3 1.4 %fusion.15 = f32[8,64,1024]{2,1,0:T(8,128)S(1)} fusion(bf16[8,64,128]{2,1,0:T(8,128)(2,1)S(1)} %collective-permute-done.8, bf16[128,1024]{1,0:T(8,128)(2,1)} %collective-permute-done.9), kind=kOutput, calls=%fused_computation.21 | convolution fusion | flops 134217728 | bytes 2490368 | tf_op jit(solution)/shard_map/dot_general | solution.py:280
  55.2 1.5 %add_add_fusion = f32[8,64,1024]{2,1,0:T(8,128)S(1)} fusion(f32[8,64,1024]{2,1,0:T(8,128)S(1)} %copy-done.2, f32[8,64,1024]{2,1,0:T(8,128)S(1)} %fusion.17, f32[8,64,1024]{2,1,0:T(8,128)S(1)} %fusion.15, bf16[8,64,128]{2,1,0:T(8,128)(2,1)S(1)} %collective-permute-done.10, bf16[128,1024]{1,0:T(8,128)(2,1)} %collective-permute-done.11), kind=kOutput, calls=%fused_computation.5 | convolution fusion | flops 135790592 | bytes 8781824 | tf_op jit(solution)/shard_map/dot_general | solution.py:280
  56.7 1.8 %collective-permute-start.24 = (f32[48,1024]{1,0:T(8,128)S(1)}, f32[48,1024]{1,0:T(8,128)S(1)}, u32[]{:S(2)}, u32[]{:S(2)}) collective-permute-start(f32[48,1024]{1,0:T(8,128)S(1)} %get-tuple-element.33), channel_id=1, source_target_pairs={{0,4},{1,5},{4,8},{5,9},{8,12},{9,13},{12,14},{13,15},{14,10},{15,... | collective-permute-start | bytes 589832 | tf_op jit(solution)/shard_map/ppermute | solution.py:193
  58.8 1.3 %fusion.2 = f32[8,32,1024]{2,1,0:T(8,128)S(1)} fusion(bf16[128,8,32]{0,2,1:T(8,128)(2,1)} %collective-permute-done.15, bf16[128,1024]{1,0:T(8,128)(2,1)} %collective-permute-done.16), kind=kOutput, calls=%fused_computation.10 | convolution fusion | flops 67108864 | bytes 1376256 | tf_op jit(solution)/shard_map/dot_general | solution.py:218
  60.5 1.6 %collective-permute-start.17 = (f32[56,1024]{1,0:T(8,128)S(1)}, f32[56,1024]{1,0:T(8,128)S(1)}, u32[]{:S(2)}, u32[]{:S(2)}) collective-permute-start(f32[56,1024]{1,0:T(8,128)S(1)} %get-tuple-element.27), channel_id=1, source_target_pairs={{0,4},{1,5},{4,8},{5,9},{8,12},{9,13},{12,14},{13,15},{14,10},{15,... | collective-permute-start | bytes 688136 | tf_op jit(solution)/shard_map/ppermute | solution.py:193
  62.8 1.4 %collective-permute-done.24 = f32[48,1024]{1,0:T(8,128)S(1)} collective-permute-done((f32[48,1024]{1,0:T(8,128)S(1)}, f32[48,1024]{1,0:T(8,128)S(1)}, u32[]{:S(2)}, u32[]{:S(2)}) %collective-permute-start.24) | collective-permute-done | bytes 196640 | tf_op jit(solution)/shard_map/ppermute | solution.py:193
  64.2 2.1 %collective-permute-start.25 = (f32[48,1024]{1,0:T(8,128)S(1)}, f32[48,1024]{1,0:T(8,128)S(1)}, u32[]{:S(2)}, u32[]{:S(2)}) collective-permute-start(f32[48,1024]{1,0:T(8,128)S(1)} %fusion.33), channel_id=1, source_target_pairs={{0,4},{1,5},{4,8},{5,9},{8,12},{9,13},{12,14},{13,15},{14,10},{15,... | collective-permute-start | bytes 589832 | tf_op jit(solution)/shard_map/ppermute | solution.py:193
  66.4 2.8 %collective-permute-done.17 = f32[56,1024]{1,0:T(8,128)S(1)} collective-permute-done((f32[56,1024]{1,0:T(8,128)S(1)}, f32[56,1024]{1,0:T(8,128)S(1)}, u32[]{:S(2)}, u32[]{:S(2)}) %collective-permute-start.17) | collective-permute-done | bytes 229408 | tf_op jit(solution)/shard_map/ppermute | solution.py:193
  69.1 1.6 %collective-permute-done.20 = f32[56,1024]{1,0:T(8,128)S(1)} collective-permute-done((f32[56,1024]{1,0:T(8,128)S(1)}, f32[56,1024]{1,0:T(8,128)S(1)}, u32[]{:S(2)}, u32[]{:S(2)}) %collective-permute-start.20) | collective-permute-done | bytes 229408 | tf_op jit(solution)/shard_map/ppermute | solution.py:199
  70.8 1.6 %collective-permute-start.18 = (f32[56,1024]{1,0:T(8,128)S(1)}, f32[56,1024]{1,0:T(8,128)S(1)}, u32[]{:S(2)}, u32[]{:S(2)}) collective-permute-start(f32[56,1024]{1,0:T(8,128)S(1)} %get-tuple-element.25), channel_id=1, source_target_pairs={{0,4},{1,5},{4,8},{5,9},{8,12},{9,13},{12,14},{13,15},{14,10},{15,... | collective-permute-start | bytes 688136 | tf_op jit(solution)/shard_map/ppermute | solution.py:193
  72.8 1.9 %collective-permute-done.28 = f32[48,1024]{1,0:T(8,128)S(1)} collective-permute-done((f32[48,1024]{1,0:T(8,128)S(1)}, f32[48,1024]{1,0:T(8,128)S(1)}, u32[]{:S(2)}, u32[]{:S(2)}) %collective-permute-start.28) | collective-permute-done | bytes 196640 | tf_op jit(solution)/shard_map/ppermute | solution.py:199
  74.8 1.6 %collective-permute-start.26 = (f32[48,1024]{1,0:T(8,128)S(1)}, f32[48,1024]{1,0:T(8,128)S(1)}, u32[]{:S(2)}, u32[]{:S(2)}) collective-permute-start(f32[48,1024]{1,0:T(8,128)S(1)} %get-tuple-element.31), channel_id=1, source_target_pairs={{0,4},{1,5},{4,8},{5,9},{8,12},{9,13},{12,14},{13,15},{14,10},{15,... | collective-permute-start | bytes 589832 | tf_op jit(solution)/shard_map/ppermute | solution.py:193
  76.9 2.5 %collective-permute-done.18 = f32[56,1024]{1,0:T(8,128)S(1)} collective-permute-done((f32[56,1024]{1,0:T(8,128)S(1)}, f32[56,1024]{1,0:T(8,128)S(1)}, u32[]{:S(2)}, u32[]{:S(2)}) %collective-permute-start.18) | collective-permute-done | bytes 229408 | tf_op jit(solution)/shard_map/ppermute | solution.py:193
  81.1 1.6 %collective-permute-start.19 = (f32[56,1024]{1,0:T(8,128)S(1)}, f32[56,1024]{1,0:T(8,128)S(1)}, u32[]{:S(2)}, u32[]{:S(2)}) collective-permute-start(f32[56,1024]{1,0:T(8,128)S(1)} %get-tuple-element.23), channel_id=1, source_target_pairs={{0,4},{1,5},{4,8},{5,9},{8,12},{9,13},{12,14},{13,15},{14,10},{15,... | collective-permute-start | bytes 688136 | tf_op jit(solution)/shard_map/ppermute | solution.py:193
  82.7 2.1 %collective-permute-done.29 = f32[48,1024]{1,0:T(8,128)S(1)} collective-permute-done((f32[48,1024]{1,0:T(8,128)S(1)}, f32[48,1024]{1,0:T(8,128)S(1)}, u32[]{:S(2)}, u32[]{:S(2)}) %collective-permute-start.29) | collective-permute-done | bytes 196640 | tf_op jit(solution)/shard_map/ppermute | solution.py:199
  84.9 1.6 %collective-permute-start.27 = (f32[48,1024]{1,0:T(8,128)S(1)}, f32[48,1024]{1,0:T(8,128)S(1)}, u32[]{:S(2)}, u32[]{:S(2)}) collective-permute-start(f32[48,1024]{1,0:T(8,128)S(1)} %get-tuple-element.29), channel_id=1, source_target_pairs={{0,4},{1,5},{4,8},{5,9},{8,12},{9,13},{12,14},{13,15},{14,10},{15,... | collective-permute-start | bytes 589832 | tf_op jit(solution)/shard_map/ppermute | solution.py:193
  86.9 2.8 %collective-permute-done.22 = f32[56,1024]{1,0:T(8,128)S(1)} collective-permute-done((f32[56,1024]{1,0:T(8,128)S(1)}, f32[56,1024]{1,0:T(8,128)S(1)}, u32[]{:S(2)}, u32[]{:S(2)}) %collective-permute-start.22) | collective-permute-done | bytes 229408 | tf_op jit(solution)/shard_map/ppermute | solution.py:199
  91.0 3.2 %collective-permute-done.30 = f32[48,1024]{1,0:T(8,128)S(1)} collective-permute-done((f32[48,1024]{1,0:T(8,128)S(1)}, f32[48,1024]{1,0:T(8,128)S(1)}, u32[]{:S(2)}, u32[]{:S(2)}) %collective-permute-start.30) | collective-permute-done | bytes 196640 | tf_op jit(solution)/shard_map/ppermute | solution.py:199
  94.3 2.4 %collective-permute-done.23 = f32[56,1024]{1,0:T(8,128)S(1)} collective-permute-done((f32[56,1024]{1,0:T(8,128)S(1)}, f32[56,1024]{1,0:T(8,128)S(1)}, u32[]{:S(2)}, u32[]{:S(2)}) %collective-permute-start.23) | collective-permute-done | bytes 229408 | tf_op jit(solution)/shard_map/ppermute | solution.py:199
  (117 shorter events, 26.9 us)
Async XLA Ops:
  2.4 7.9 %collective-permute-start = (bf16[96,1024]{1,0:T(8,128)(2,1)S(1)}, bf16[96,1024]{1,0:T(8,128)(2,1)S(1)}, u32[]{:S(2)}, u32[]{:S(2)}) collective-permute-start(bf16[96,1024]{1,0:T(8,128)(2,1)S(1)} %constant_dynamic-update-slice_fusion), channel_id=1, source_target_pairs={{0,4},{1,5},{4,8},{5,9},{8,12},{9,13},{12,14},{13,15},{14,10},{15,... | collective-permute-start | bytes 589832 | tf_op jit(solution)/shard_map/ppermute | solution.py:167
  5.5 6.6 %collective-permute-start.1 = (bf16[96,1024]{1,0:T(8,128)(2,1)S(1)}, bf16[96,1024]{1,0:T(8,128)(2,1)S(1)}, u32[]{:S(2)}, u32[]{:S(2)}) collective-permute-start(bf16[96,1024]{1,0:T(8,128)(2,1)S(1)} %constant_dynamic-update-slice_fusion), channel_id=1, source_target_pairs={{4,0},{5,1},{8,4},{9,5},{12,8},{13,9},{14,12},{15,13},{10,14},{11,... | collective-permute-start | bytes 589832 | tf_op jit(solution)/shard_map/ppermute | solution.py:172
  9.3 19.7 %copy-start.1 = (s32[8]{0:T(128)S(1)}, s32[8]{0:T(128)}, u32[]{:S(2)}) copy-start(s32[8]{0:T(128)} %constant.105.clone) | copy-start | bytes 100
  10.3 6.1 %collective-permute-start.4 = (bf16[96,1024]{1,0:T(8,128)(2,1)S(1)}, bf16[96,1024]{1,0:T(8,128)(2,1)S(1)}, u32[]{:S(2)}, u32[]{:S(2)}) collective-permute-start(bf16[96,1024]{1,0:T(8,128)(2,1)S(1)} %collective-permute-done), channel_id=1, source_target_pairs={{0,4},{1,5},{4,8},{5,9},{8,12},{9,13},{12,14},{13,15},{14,10},{15,... | collective-permute-start | bytes 589832 | tf_op jit(solution)/shard_map/ppermute | solution.py:167
  12.1 5.8 %collective-permute-start.2 = (bf16[96,1024]{1,0:T(8,128)(2,1)S(1)}, bf16[96,1024]{1,0:T(8,128)(2,1)S(1)}, u32[]{:S(2)}, u32[]{:S(2)}) collective-permute-start(bf16[96,1024]{1,0:T(8,128)(2,1)S(1)} %collective-permute-done.1), channel_id=1, source_target_pairs={{4,0},{5,1},{8,4},{9,5},{12,8},{13,9},{14,12},{15,13},{10,14},{11,... | collective-permute-start | bytes 589832 | tf_op jit(solution)/shard_map/ppermute | solution.py:172
  16.4 5.8 %collective-permute-start.5 = (bf16[96,1024]{1,0:T(8,128)(2,1)S(1)}, bf16[96,1024]{1,0:T(8,128)(2,1)S(1)}, u32[]{:S(2)}, u32[]{:S(2)}) collective-permute-start(bf16[96,1024]{1,0:T(8,128)(2,1)S(1)} %collective-permute-done.4), channel_id=1, source_target_pairs={{0,4},{1,5},{4,8},{5,9},{8,12},{9,13},{12,14},{13,15},{14,10},{15,... | collective-permute-start | bytes 589832 | tf_op jit(solution)/shard_map/ppermute | solution.py:167
  17.9 6.1 %collective-permute-start.3 = (bf16[96,1024]{1,0:T(8,128)(2,1)S(1)}, bf16[96,1024]{1,0:T(8,128)(2,1)S(1)}, u32[]{:S(2)}, u32[]{:S(2)}) collective-permute-start(bf16[96,1024]{1,0:T(8,128)(2,1)S(1)} %collective-permute-done.2), channel_id=1, source_target_pairs={{4,0},{5,1},{8,4},{9,5},{12,8},{13,9},{14,12},{15,13},{10,14},{11,... | collective-permute-start | bytes 589832 | tf_op jit(solution)/shard_map/ppermute | solution.py:172
  22.2 5.7 %collective-permute-start.6 = (bf16[96,1024]{1,0:T(8,128)(2,1)S(1)}, bf16[96,1024]{1,0:T(8,128)(2,1)S(1)}, u32[]{:S(2)}, u32[]{:S(2)}) collective-permute-start(bf16[96,1024]{1,0:T(8,128)(2,1)S(1)} %collective-permute-done.5), channel_id=1, source_target_pairs={{0,4},{1,5},{4,8},{5,9},{8,12},{9,13},{12,14},{13,15},{14,10},{15,... | collective-permute-start | bytes 589832 | tf_op jit(solution)/shard_map/ppermute | solution.py:167
  28.0 5.2 %collective-permute-start.7 = (bf16[8,96,1024]{2,1,0:T(8,128)(2,1)S(1)}, bf16[8,96,1024]{2,1,0:T(8,128)(2,1)}, u32[]{:S(2)}, u32[]{:S(2)}) collective-permute-start(bf16[8,96,1024]{2,1,0:T(8,128)(2,1)S(1)} %bitcast_dynamic-update-slice_fusion.mine_ref), channel_id=1, source_target_pairs={{0,1},{1,0},{2,3},{3,2},{4,5},{5,4},{6,7},{7,6},{8,9},{9,8},{10,11... | collective-permute-start | bytes 4718600 | tf_op jit(solution)/shard_map/ppermute | solution.py:175
  30.9 28.0 %collective-permute-start.15 = (bf16[128,8,32]{0,2,1:T(8,128)(2,1)}, bf16[128,8,32]{0,2,1:T(8,128)(2,1)}, u32[]{:S(2)}, u32[]{:S(2)}) collective-permute-start(bf16[128,8,32]{0,2,1:T(8,128)(2,1)} %dynamic-slice_bitcast_fusion.2), channel_id=1, source_target_pairs={{0,1},{1,0},{2,3},{3,2},{4,5},{5,4},{6,7},{7,6},{8,9},{9,8},{10,11... | collective-permute-start | bytes 196616 | tf_op jit(solution)/shard_map/ppermute | solution.py:268
  41.9 11.3 %collective-permute-start.9 = (bf16[128,1024]{1,0:T(8,128)(2,1)}, bf16[128,1024]{1,0:T(8,128)(2,1)}, u32[]{:S(2)}, u32[]{:S(2)}) collective-permute-start(bf16[128,1024]{1,0:T(8,128)(2,1)} %get-tuple-element.16), channel_id=1, source_target_pairs={{0,1},{1,0},{2,3},{3,2},{4,5},{5,4},{6,7},{7,6},{8,9},{9,8},{10,11... | collective-permute-start | bytes 786440 | tf_op jit(solution)/shard_map/ppermute | solution.py:271
  47.3 7.9 %collective-permute-start.11 = (bf16[128,1024]{1,0:T(8,128)(2,1)}, bf16[128,1024]{1,0:T(8,128)(2,1)}, u32[]{:S(2)}, u32[]{:S(2)}) collective-permute-start(bf16[128,1024]{1,0:T(8,128)(2,1)} %get-tuple-element.18), channel_id=1, source_target_pairs={{0,1},{1,0},{2,3},{3,2},{4,5},{5,4},{6,7},{7,6},{8,9},{9,8},{10,11... | collective-permute-start | bytes 786440 | tf_op jit(solution)/shard_map/ppermute | solution.py:271
  49.0 9.9 %collective-permute-start.16 = (bf16[128,1024]{1,0:T(8,128)(2,1)}, bf16[128,1024]{1,0:T(8,128)(2,1)}, u32[]{:S(2)}, u32[]{:S(2)}) collective-permute-start(bf16[128,1024]{1,0:T(8,128)(2,1)} %get-tuple-element.22), channel_id=1, source_target_pairs={{0,1},{1,0},{2,3},{3,2},{4,5},{5,4},{6,7},{7,6},{8,9},{9,8},{10,11... | collective-permute-start | bytes 786440 | tf_op jit(solution)/shard_map/ppermute | solution.py:271
  49.1 2.0 %collective-permute-start.12 = (f32[1024]{0:T(1024)S(1)}, f32[1024]{0:T(1024)}, u32[]{:S(2)}, u32[]{:S(2)}) collective-permute-start(f32[1024]{0:T(1024)S(1)} %bitcast.152), channel_id=1, source_target_pairs={{0,1},{1,0},{2,3},{3,2},{4,5},{5,4},{6,7},{7,6},{8,9},{9,8},{10,11... | collective-permute-start | bytes 12296 | tf_op jit(solution)/shard_map/ppermute | solution.py:271
  51.1 1.7 %collective-permute-start.8 = (bf16[8,64,128]{2,1,0:T(8,128)(2,1)}, bf16[8,64,128]{2,1,0:T(8,128)(2,1)S(1)}, u32[]{:S(2)}, u32[]{:S(2)}) collective-permute-start(bf16[8,64,128]{2,1,0:T(8,128)(2,1)} %dynamic-slice_bitcast_fusion.1), channel_id=1, source_target_pairs={{0,1},{1,0},{2,3},{3,2},{4,5},{5,4},{6,7},{7,6},{8,9},{9,8},{10,11... | collective-permute-start | bytes 393224 | tf_op jit(solution)/shard_map/ppermute | solution.py:277
  52.8 1.9 %collective-permute-start.10 = (bf16[8,64,128]{2,1,0:T(8,128)(2,1)}, bf16[8,64,128]{2,1,0:T(8,128)(2,1)S(1)}, u32[]{:S(2)}, u32[]{:S(2)}) collective-permute-start(bf16[8,64,128]{2,1,0:T(8,128)(2,1)} %dynamic-slice_bitcast_fusion), channel_id=1, source_target_pairs={{0,1},{1,0},{2,3},{3,2},{4,5},{5,4},{6,7},{7,6},{8,9},{9,8},{10,11... | collective-permute-start | bytes 393224 | tf_op jit(solution)/shard_map/ppermute | solution.py:277
  53.2 5.3 %collective-permute-start.13 = (bf16[8,32,128]{2,1,0:T(8,128)(2,1)S(1)}, bf16[8,32,128]{2,1,0:T(8,128)(2,1)S(1)}, u32[]{:S(2)}, u32[]{:S(2)}) collective-permute-start(bf16[8,32,128]{2,1,0:T(8,128)(2,1)S(1)} %dynamic-slice_bitcast_fusion.3), channel_id=1, source_target_pairs={{0,1},{1,0},{2,3},{3,2},{4,5},{5,4},{6,7},{7,6},{8,9},{9,8},{10,11... | collective-permute-start | bytes 196616 | tf_op jit(solution)/shard_map/ppermute | solution.py:277
  54.7 3.8 %collective-permute-start.14 = (bf16[128,1024]{1,0:T(8,128)(2,1)S(1)}, bf16[128,1024]{1,0:T(8,128)(2,1)S(1)}, u32[]{:S(2)}, u32[]{:S(2)}) collective-permute-start(bf16[128,1024]{1,0:T(8,128)(2,1)S(1)} %copy-done.4), channel_id=1, source_target_pairs={{0,1},{1,0},{2,3},{3,2},{4,5},{5,4},{6,7},{7,6},{8,9},{9,8},{10,11... | collective-permute-start | bytes 786440 | tf_op jit(solution)/shard_map/ppermute | solution.py:271
  56.7 7.5 %collective-permute-start.24 = (f32[48,1024]{1,0:T(8,128)S(1)}, f32[48,1024]{1,0:T(8,128)S(1)}, u32[]{:S(2)}, u32[]{:S(2)}) collective-permute-start(f32[48,1024]{1,0:T(8,128)S(1)} %get-tuple-element.33), channel_id=1, source_target_pairs={{0,4},{1,5},{4,8},{5,9},{8,12},{9,13},{12,14},{13,15},{14,10},{15,... | collective-permute-start | bytes 589832 | tf_op jit(solution)/shard_map/ppermute | solution.py:193
  60.5 8.6 %collective-permute-start.17 = (f32[56,1024]{1,0:T(8,128)S(1)}, f32[56,1024]{1,0:T(8,128)S(1)}, u32[]{:S(2)}, u32[]{:S(2)}) collective-permute-start(f32[56,1024]{1,0:T(8,128)S(1)} %get-tuple-element.27), channel_id=1, source_target_pairs={{0,4},{1,5},{4,8},{5,9},{8,12},{9,13},{12,14},{13,15},{14,10},{15,... | collective-permute-start | bytes 688136 | tf_op jit(solution)/shard_map/ppermute | solution.py:193
  62.2 8.5 %collective-permute-start.20 = (f32[56,1024]{1,0:T(8,128)S(1)}, f32[56,1024]{1,0:T(8,128)S(1)}, u32[]{:S(2)}, u32[]{:S(2)}) collective-permute-start(f32[56,1024]{1,0:T(8,128)S(1)} %get-tuple-element.28), channel_id=1, source_target_pairs={{4,0},{5,1},{8,4},{9,5},{12,8},{13,9},{14,12},{15,13},{10,14},{11,... | collective-permute-start | bytes 688136 | tf_op jit(solution)/shard_map/ppermute | solution.py:199
  62.6 12.1 %collective-permute-start.28 = (f32[48,1024]{1,0:T(8,128)S(1)}, f32[48,1024]{1,0:T(8,128)S(1)}, u32[]{:S(2)}, u32[]{:S(2)}) collective-permute-start(f32[48,1024]{1,0:T(8,128)S(1)} %get-tuple-element.34), channel_id=1, source_target_pairs={{4,0},{5,1},{8,4},{9,5},{12,8},{13,9},{14,12},{15,13},{10,14},{11,... | collective-permute-start | bytes 589832 | tf_op jit(solution)/shard_map/ppermute | solution.py:199
  64.2 10.5 %collective-permute-start.25 = (f32[48,1024]{1,0:T(8,128)S(1)}, f32[48,1024]{1,0:T(8,128)S(1)}, u32[]{:S(2)}, u32[]{:S(2)}) collective-permute-start(f32[48,1024]{1,0:T(8,128)S(1)} %fusion.33), channel_id=1, source_target_pairs={{0,4},{1,5},{4,8},{5,9},{8,12},{9,13},{12,14},{13,15},{14,10},{15,... | collective-permute-start | bytes 589832 | tf_op jit(solution)/shard_map/ppermute | solution.py:193
  70.8 8.6 %collective-permute-start.18 = (f32[56,1024]{1,0:T(8,128)S(1)}, f32[56,1024]{1,0:T(8,128)S(1)}, u32[]{:S(2)}, u32[]{:S(2)}) collective-permute-start(f32[56,1024]{1,0:T(8,128)S(1)} %get-tuple-element.25), channel_id=1, source_target_pairs={{0,4},{1,5},{4,8},{5,9},{8,12},{9,13},{12,14},{13,15},{14,10},{15,... | collective-permute-start | bytes 688136 | tf_op jit(solution)/shard_map/ppermute | solution.py:193
  72.4 8.2 %collective-permute-start.21 = (f32[56,1024]{1,0:T(8,128)S(1)}, f32[56,1024]{1,0:T(8,128)S(1)}, u32[]{:S(2)}, u32[]{:S(2)}) collective-permute-start(f32[56,1024]{1,0:T(8,128)S(1)} %get-tuple-element.26), channel_id=1, source_target_pairs={{4,0},{5,1},{8,4},{9,5},{12,8},{13,9},{14,12},{15,13},{10,14},{11,... | collective-permute-start | bytes 688136 | tf_op jit(solution)/shard_map/ppermute | solution.py:199
  74.8 7.9 %collective-permute-start.26 = (f32[48,1024]{1,0:T(8,128)S(1)}, f32[48,1024]{1,0:T(8,128)S(1)}, u32[]{:S(2)}, u32[]{:S(2)}) collective-permute-start(f32[48,1024]{1,0:T(8,128)S(1)} %get-tuple-element.31), channel_id=1, source_target_pairs={{0,4},{1,5},{4,8},{5,9},{8,12},{9,13},{12,14},{13,15},{14,10},{15,... | collective-permute-start | bytes 589832 | tf_op jit(solution)/shard_map/ppermute | solution.py:193
  76.4 8.4 %collective-permute-start.29 = (f32[48,1024]{1,0:T(8,128)S(1)}, f32[48,1024]{1,0:T(8,128)S(1)}, u32[]{:S(2)}, u32[]{:S(2)}) collective-permute-start(f32[48,1024]{1,0:T(8,128)S(1)} %get-tuple-element.32), channel_id=1, source_target_pairs={{4,0},{5,1},{8,4},{9,5},{12,8},{13,9},{14,12},{15,13},{10,14},{11,... | collective-permute-start | bytes 589832 | tf_op jit(solution)/shard_map/ppermute | solution.py:199
  80.7 9.1 %collective-permute-start.22 = (f32[56,1024]{1,0:T(8,128)S(1)}, f32[56,1024]{1,0:T(8,128)S(1)}, u32[]{:S(2)}, u32[]{:S(2)}) collective-permute-start(f32[56,1024]{1,0:T(8,128)S(1)} %get-tuple-element.24), channel_id=1, source_target_pairs={{4,0},{5,1},{8,4},{9,5},{12,8},{13,9},{14,12},{15,13},{10,14},{11,... | collective-permute-start | bytes 688136 | tf_op jit(solution)/shard_map/ppermute | solution.py:199
  81.1 13.2 %collective-permute-start.19 = (f32[56,1024]{1,0:T(8,128)S(1)}, f32[56,1024]{1,0:T(8,128)S(1)}, u32[]{:S(2)}, u32[]{:S(2)}) collective-permute-start(f32[56,1024]{1,0:T(8,128)S(1)} %get-tuple-element.23), channel_id=1, source_target_pairs={{0,4},{1,5},{4,8},{5,9},{8,12},{9,13},{12,14},{13,15},{14,10},{15,... | collective-permute-start | bytes 688136 | tf_op jit(solution)/shard_map/ppermute | solution.py:193
  84.9 6.2 %collective-permute-start.27 = (f32[48,1024]{1,0:T(8,128)S(1)}, f32[48,1024]{1,0:T(8,128)S(1)}, u32[]{:S(2)}, u32[]{:S(2)}) collective-permute-start(f32[48,1024]{1,0:T(8,128)S(1)} %get-tuple-element.29), channel_id=1, source_target_pairs={{0,4},{1,5},{4,8},{5,9},{8,12},{9,13},{12,14},{13,15},{14,10},{15,... | collective-permute-start | bytes 589832 | tf_op jit(solution)/shard_map/ppermute | solution.py:193
  86.5 7.8 %collective-permute-start.30 = (f32[48,1024]{1,0:T(8,128)S(1)}, f32[48,1024]{1,0:T(8,128)S(1)}, u32[]{:S(2)}, u32[]{:S(2)}) collective-permute-start(f32[48,1024]{1,0:T(8,128)S(1)} %get-tuple-element.30), channel_id=1, source_target_pairs={{4,0},{5,1},{8,4},{9,5},{12,8},{13,9},{14,12},{15,13},{10,14},{11,... | collective-permute-start | bytes 589832 | tf_op jit(solution)/shard_map/ppermute | solution.py:199
  89.7 6.9 %collective-permute-start.23 = (f32[56,1024]{1,0:T(8,128)S(1)}, f32[56,1024]{1,0:T(8,128)S(1)}, u32[]{:S(2)}, u32[]{:S(2)}) collective-permute-start(f32[56,1024]{1,0:T(8,128)S(1)} %fusion.20), channel_id=1, source_target_pairs={{4,0},{5,1},{8,4},{9,5},{12,8},{13,9},{14,12},{15,13},{10,14},{11,... | collective-permute-start | bytes 688136 | tf_op jit(solution)/shard_map/ppermute | solution.py:199
  (12 other events, 67.6 us)

commit v18 on v16

--- a/solution.py
+++ b/solution.py
@@ -180,36 +180,37 @@
     return mine, other, index, extra
 
 
-def ring_reduce_scatter(summed, n_blk):
+def ring_reduce_scatter(summed, n_blk, got=(None, None)):
     chips, snake, place, cw, ccw, partner = ring_plan(n_blk)
     ahead = chips // 2
     behind = chips - 1 - ahead
     rows = summed.shape[1]
     split = (rows // 16) * 8
 
-    def forward(part, window):
+    def forward(part, window, got=None):
         acc = part[window % chips]
         for s in range(1, window + 1):
-            acc = lax.ppermute(acc, "blk", cw) + part[(window - s) % chips]
+            sent = lax.ppermute(acc, "blk", cw) if got is None or s > 1 else got
+            acc = sent + part[(window - s) % chips]
         return acc
 
-    def backward(part, window):
+    def backward(part, window, got=None):
         acc = part[chips - window]
         for s in range(1, window + 1):
-            acc = lax.ppermute(acc, "blk", ccw)
+            acc = lax.ppermute(acc, "blk", ccw) if got is None or s > 1 else got
             if s < window:
                 acc = acc + part[chips - window + s]
         return acc
 
-    def both_ways(part, one, other):
-        total = forward(part, one)
+    def both_ways(part, one, other, got=(None, None)):
+        total = forward(part, one, got[0])
         if other:
-            total = total + backward(part, other)
+            total = total + backward(part, other, got[1])
         return total
 
     if split == 0 or behind == ahead:
         return both_ways(summed, ahead, behind)
-    first = both_ways(summed[:, :split], ahead, behind)
+    first = both_ways(summed[:, :split], ahead, behind, got)
     second = both_ways(summed[:, split:], behind, ahead)
     return jnp.concatenate([first, second], axis=0)
 
@@ -294,6 +295,15 @@
         rows_first(ec_keep, g_two) + rows_first(ec_got, g2_got)
         + rows_first(h_keep, e_atwo) + rows_first(h_got, ea2_got)
     )
+    total_rows = r_one + r_two + chips
+    split = (total_rows // 16) * 8
+    ahead, behind = chips // 2, chips - 1 - chips // 2
+    got = (None, None)
+    if 0 < split <= r_two and behind and behind != ahead:
+        head = part_two[:, :split]
+        got = (lax.ppermute(head[ahead], "blk", cw),
+               lax.ppermute(head[chips - behind], "blk", ccw))
+        got, e_aone, ea1_got = lax.optimization_barrier((got, e_aone, ea1_got))
     part_one = (
         slots_product(ed_keep, g_one) + slots_product(ed_got, g1_got)
         + slots_product(x_keep, e_aone) + slots_product(x_got, ea1_got)
@@ -303,7 +313,7 @@
     summed = jnp.concatenate(
         [part_two, jnp.broadcast_to(outs, (chips,) + outs.shape), part_one], axis=1
     )
-    reduced = ring_reduce_scatter(summed, n_blk)
+    reduced = ring_reduce_scatter(summed, n_blk, got)
     grad_two = reduced[:r_two]
     grad_out = jnp.sum(reduced[r_two:r_two + chips], axis=0)
     grad_one = reduced[r_two + chips:]

time: 101 us -> 105 us (1.040)
  waiting for transfers between devices: 35.7 us -> 43.9 us
  matrix products: 10 us -> 7.02 us
    ppermute x3, waiting for transfers between devices: 0.01 us -> 5.43 us  [ring_all_gather(): right = lax.ppermute(right, 'blk', ccw)]
    ppermute x14, waiting for transfers between devices: 23 us -> 28.2 us  [the longest x6 10.8 us: backward(): acc = lax.ppermute(acc, 'blk', ccw) if got is None or s > 1 else got]
    ppermute x4, waiting for transfers between devices: 12.7 us -> 9.44 us  [ring_all_gather(): left = lax.ppermute(left, 'blk', cw)]
    dot_general x4, matrix products: 6.92 us -> 5.02 us  [rows_first(): lax.dot_general(left, right, (((2,), (0,)), ((), ())), preferred_element_...]
    dot_general x4, matrix products: 3.13 us -> 2 us  [slots_product(): lax.dot_general(left, right, (((0,), (0,)), ((), ())), preferred_element_...]
  transfers between devices with their start and end apart: 31 -> 31, of which waited for: 15 -> 16; matrix products, arithmetic and copies ran while one was open for 25% -> 20% of each run, Pallas kernels for 6% -> 6%
where the time goes in v18:
time: 105 us
  waiting for transfers between devices  43.9 us (42%)
  starting transfers between devices  25.9 us (25%)
  local copies, waits for them, and re-layouts  11.1 us (11%)
  other arithmetic  8.53 us (8%)
  matrix products  7.02 us (7%)
  Pallas kernels  6.37 us (6%)
  between operations  1.76 us (2%)
    ppermute x6, waiting for transfers between devices, backward(): acc = lax.ppermute(acc, 'blk', ccw) if got is None or s > 1 else got  10.8 us
    ppermute x6, waiting for transfers between devices, forward(): sent = lax.ppermute(acc, 'blk', cw) if got is None or s > 1 else got  10.8 us
    ppermute x6, starting transfers between devices, forward(): sent = lax.ppermute(acc, 'blk', cw) if got is None or s > 1 else got  9.94 us
    ppermute x4, waiting for transfers between devices, ring_all_gather(): left = lax.ppermute(left, 'blk', cw)  9.44 us
    ppermute x4, starting transfers between devices, ring_all_gather(): left = lax.ppermute(left, 'blk', cw)  8.48 us
    pallas_call x1, Pallas kernels, twin_fused(): pl.pallas_call(functools.partial(twin_body, r_one, place), out_shape=shap...  6.37 us
    ppermute x3, waiting for transfers between devices, ring_all_gather(): right = lax.ppermute(right, 'blk', ccw)  5.43 us
    dot_general x4, matrix products, rows_first(): lax.dot_general(left, right, (((2,), (0,)), ((), ())), preferred_element_...  5.02 us
  transfers between devices with their start and end apart: 31, of which 16 were waited for; matrix products, arithmetic and copies ran while one was open for 20% of the time, Pallas kernels for 6%

profile of v18, /device:TPU:0, one launch (start us, length us, event | category | flops | bytes accessed | tf_op | source)
XLA Modules:
  0.0 104.5 jit_solution(13527189167723589398)
XLA Ops:
  2.4 3.1 %collective-permute-start = (bf16[96,1024]{1,0:T(8,128)(2,1)S(1)}, bf16[96,1024]{1,0:T(8,128)(2,1)S(1)}, u32[]{:S(2)}, u32[]{:S(2)}) collective-permute-start(bf16[96,1024]{1,0:T(8,128)(2,1)S(1)} %constant_dynamic-update-slice_fusion), channel_id=1, source_target_pairs={{0,4},{1,5},{4,8},{5,9},{8,12},{9,13},{12,14},{13,15},{14,10},{15,... | collective-permute-start | bytes 589832 | tf_op jit(solution)/shard_map/ppermute | solution.py:167
  5.5 1.2 %dynamic_slice.37 = s32[1]{0:T(128)} dynamic-slice(s32[8]{0:T(128)} %constant.102.clone, s32[]{:T(128)S(6)} %select_n.64), dynamic_slice_sizes={1} | dynamic-slice | bytes 12 | tf_op jit(solution)/shard_map/dynamic_slice | solution.py:236
  7.4 1.9 %pad_add_fusion.par_ref = s32[3]{0:T(128)} fusion(s32[1]{0:T(128)} %dynamic_slice.37, s32[1]{0:T(128)} %bitcast.1, s32[1]{0:T(128)} %bitcast), kind=kLoop, calls=%fused_computation.100 | loop fusion | flops 6 | bytes 24 | tf_op jit(solution)/shard_map/stack | solution.py:235
  10.3 1.8 %collective-permute-start.4 = (bf16[96,1024]{1,0:T(8,128)(2,1)S(1)}, bf16[96,1024]{1,0:T(8,128)(2,1)S(1)}, u32[]{:S(2)}, u32[]{:S(2)}) collective-permute-start(bf16[96,1024]{1,0:T(8,128)(2,1)S(1)} %collective-permute-done), channel_id=1, source_target_pairs={{0,4},{1,5},{4,8},{5,9},{8,12},{9,13},{12,14},{13,15},{14,10},{15,... | collective-permute-start | bytes 589832 | tf_op jit(solution)/shard_map/ppermute | solution.py:167
  12.4 5.4 %collective-permute-done.2 = bf16[96,1024]{1,0:T(8,128)(2,1)S(1)} collective-permute-done((bf16[96,1024]{1,0:T(8,128)(2,1)S(1)}, bf16[96,1024]{1,0:T(8,128)(2,1)S(1)}, u32[]{:S(2)}, u32[]{:S(2)}) %collective-permute-start.2) | collective-permute-done | bytes 196640 | tf_op jit(solution)/shard_map/ppermute | solution.py:172
  18.2 1.7 %collective-permute-start.5 = (bf16[96,1024]{1,0:T(8,128)(2,1)S(1)}, bf16[96,1024]{1,0:T(8,128)(2,1)S(1)}, u32[]{:S(2)}, u32[]{:S(2)}) collective-permute-start(bf16[96,1024]{1,0:T(8,128)(2,1)S(1)} %collective-permute-done.4), channel_id=1, source_target_pairs={{0,4},{1,5},{4,8},{5,9},{8,12},{9,13},{12,14},{13,15},{14,10},{15,... | collective-permute-start | bytes 589832 | tf_op jit(solution)/shard_map/ppermute | solution.py:167
  19.9 4.7 %collective-permute-done.5 = bf16[96,1024]{1,0:T(8,128)(2,1)S(1)} collective-permute-done((bf16[96,1024]{1,0:T(8,128)(2,1)S(1)}, bf16[96,1024]{1,0:T(8,128)(2,1)S(1)}, u32[]{:S(2)}, u32[]{:S(2)}) %collective-permute-start.5) | collective-permute-done | bytes 196640 | tf_op jit(solution)/shard_map/ppermute | solution.py:167
  24.5 1.9 %collective-permute-start.6 = (bf16[96,1024]{1,0:T(8,128)(2,1)S(1)}, bf16[96,1024]{1,0:T(8,128)(2,1)S(1)}, u32[]{:S(2)}, u32[]{:S(2)}) collective-permute-start(bf16[96,1024]{1,0:T(8,128)(2,1)S(1)} %collective-permute-done.5), channel_id=1, source_target_pairs={{0,4},{1,5},{4,8},{5,9},{8,12},{9,13},{12,14},{13,15},{14,10},{15,... | collective-permute-start | bytes 589832 | tf_op jit(solution)/shard_map/ppermute | solution.py:167
  26.5 3.7 %collective-permute-done.6 = bf16[96,1024]{1,0:T(8,128)(2,1)S(1)} collective-permute-done((bf16[96,1024]{1,0:T(8,128)(2,1)S(1)}, bf16[96,1024]{1,0:T(8,128)(2,1)S(1)}, u32[]{:S(2)}, u32[]{:S(2)}) %collective-permute-start.6) | collective-permute-done | bytes 196640 | tf_op jit(solution)/shard_map/ppermute | solution.py:167
  35.5 6.4 %shard_map.148 = (bf16[128,512]{1,0:T(8,128)(2,1)}, bf16[128,1024]{1,0:T(8,128)(2,1)}, bf16[128,1024]{1,0:T(8,128)(2,1)}, bf16[1024,128]{1,0:T(8,128)(2,1)}, bf1...) custom-call(s32[3]{0:T(128)} %pad_add_fusion.par_ref, ...), custom_call_target="tpu_custom_call" | custom-call | flops 1476395008 | bytes 5242880 | tf_op jit(solution)/shard_map/pallas_call | solution.py:127
  41.9 1.5 %gather_fusion.2 = bf16[8,2,64,128]{3,2,1,0:T(8,128)(2,1)S(1)} fusion(bf16[8,2,64,128]{3,2,1,0:T(8,128)(2,1)} %bitcast.159, s32[1024]{0:T(1024)S(1)} %pad_clamp_fusion), kind=kCustom, calls=%fused_computation.2 | custom fusion | bytes 524320 | tf_op jit(solution)/shard_map/jit(_take)/gather | solution.py:275
  43.4 1.5 %gather_fusion.1 = bf16[8,2,64,128]{3,2,1,0:T(8,128)(2,1)S(1)} fusion(bf16[8,2,64,128]{3,2,1,0:T(8,128)(2,1)} %bitcast.158, s32[1024]{0:T(1024)S(1)} %pad_clamp_fusion), kind=kCustom, calls=%fused_computation.1 | custom fusion | bytes 524320 | tf_op jit(solution)/shard_map/jit(_take)/gather | solution.py:275
  45.7 1.4 %fusion.15 = f32[8,64,1024]{2,1,0:T(8,128)S(1)} fusion(bf16[128,1024]{1,0:T(8,128)(2,1)} %get-tuple-element.20, bf16[8,2,64,128]{3,2,1,0:T(8,128)(2,1)S(1)} %gather_fusion.1, s32[]{:T(128)S(6)} %select_n.67), kind=kOutput, calls=%fused_computation.22 | convolution fusion | flops 134217728 | bytes 2490372 | tf_op jit(solution)/shard_map/dot_general | solution.py:281
  47.8 1.8 %fusion.11 = f32[8,64,1024]{2,1,0:T(8,128)} fusion(bf16[128,1024]{1,0:T(8,128)(2,1)S(1)} %copy-done.6, bf16[8,2,64,128]{3,2,1,0:T(8,128)(2,1)S(1)} %gather_fusion.2, s32[]{:T(128)S(6)} %select_n.67), kind=kOutput, calls=%fused_computation.18 | convolution fusion | flops 134217728 | bytes 2490372 | tf_op jit(solution)/shard_map/dot_general | solution.py:281
  53.8 1.3 %fusion.13 = f32[8,64,1024]{2,1,0:T(8,128)S(1)} fusion(bf16[8,64,128]{2,1,0:T(8,128)(2,1)} %collective-permute-done.8, bf16[128,1024]{1,0:T(8,128)(2,1)S(1)} %collective-permute-done.9), kind=kOutput, calls=%fused_computation.20 | convolution fusion | flops 134217728 | bytes 2490368 | tf_op jit(solution)/shard_map/dot_general | solution.py:281
  56.0 2.0 %collective-permute-start.15 = (f32[48,1024]{1,0:T(8,128)S(1)}, f32[48,1024]{1,0:T(8,128)S(1)}, u32[]{:S(2)}, u32[]{:S(2)}) collective-permute-start(f32[48,1024]{1,0:T(8,128)S(1)} %get-tuple-element.42), channel_id=1, source_target_pairs={{0,4},{1,5},{4,8},{5,9},{8,12},{9,13},{12,14},{13,15},{14,10},{15,... | collective-permute-start | bytes 589832 | tf_op jit(solution)/shard_map/ppermute | solution.py:304
  58.4 4.8 %collective-permute-done.15 = f32[48,1024]{1,0:T(8,128)S(1)} collective-permute-done((f32[48,1024]{1,0:T(8,128)S(1)}, f32[48,1024]{1,0:T(8,128)S(1)}, u32[]{:S(2)}, u32[]{:S(2)}) %collective-permute-start.15) | collective-permute-done | bytes 196640 | tf_op jit(solution)/shard_map/ppermute | solution.py:304
  63.2 1.7 %collective-permute-done.16 = f32[48,1024]{1,0:T(8,128)S(1)} collective-permute-done((f32[48,1024]{1,0:T(8,128)S(1)}, f32[48,1024]{1,0:T(8,128)S(1)}, u32[]{:S(2)}, u32[]{:S(2)}) %collective-permute-start.16) | collective-permute-done | bytes 196640 | tf_op jit(solution)/shard_map/ppermute | solution.py:305
  65.5 1.1 %convolution_add_fusion = f32[8,32,1024]{2,1,0:T(8,128)S(1)} fusion(f32[8,32,1024]{2,1,0:T(8,128)S(1)} %fusion, bf16[128,8,32]{0,2,1:T(8,128)(2,1)} %collective-permute-done.18, bf16[128,1024]{1,0:T(8,128)(2,1)S(1)} %collective-permute-done.17), kind=kOutput, calls=%fused_computation.6 | convolution fusion | flops 67371008 | bytes 2424832 | tf_op jit(solution)/shard_map/dot_general | solution.py:219
  66.7 1.6 %collective-permute-start.19 = (f32[56,1024]{1,0:T(8,128)S(1)}, f32[56,1024]{1,0:T(8,128)S(1)}, u32[]{:S(2)}, u32[]{:S(2)}) collective-permute-start(f32[56,1024]{1,0:T(8,128)S(1)} %get-tuple-element.35), channel_id=1, source_target_pairs={{0,4},{1,5},{4,8},{5,9},{8,12},{9,13},{12,14},{13,15},{14,10},{15,... | collective-permute-start | bytes 688136 | tf_op jit(solution)/shard_map/ppermute | solution.py:193
  68.8 1.6 %collective-permute-start.26 = (f32[48,1024]{1,0:T(8,128)S(1)}, f32[48,1024]{1,0:T(8,128)S(1)}, u32[]{:S(2)}, u32[]{:S(2)}) collective-permute-start(f32[48,1024]{1,0:T(8,128)S(1)} %fusion.31), channel_id=1, source_target_pairs={{0,4},{1,5},{4,8},{5,9},{8,12},{9,13},{12,14},{13,15},{14,10},{15,... | collective-permute-start | bytes 589832 | tf_op jit(solution)/shard_map/ppermute | solution.py:193
  70.4 4.9 %collective-permute-done.19 = f32[56,1024]{1,0:T(8,128)S(1)} collective-permute-done((f32[56,1024]{1,0:T(8,128)S(1)}, f32[56,1024]{1,0:T(8,128)S(1)}, u32[]{:S(2)}, u32[]{:S(2)}) %collective-permute-start.19) | collective-permute-done | bytes 229408 | tf_op jit(solution)/shard_map/ppermute | solution.py:193
  75.3 1.6 %collective-permute-start.20 = (f32[56,1024]{1,0:T(8,128)S(1)}, f32[56,1024]{1,0:T(8,128)S(1)}, u32[]{:S(2)}, u32[]{:S(2)}) collective-permute-start(f32[56,1024]{1,0:T(8,128)S(1)} %get-tuple-element.33), channel_id=1, source_target_pairs={{0,4},{1,5},{4,8},{5,9},{8,12},{9,13},{12,14},{13,15},{14,10},{15,... | collective-permute-start | bytes 688136 | tf_op jit(solution)/shard_map/ppermute | solution.py:193
  77.4 2.1 %collective-permute-done.26 = f32[48,1024]{1,0:T(8,128)S(1)} collective-permute-done((f32[48,1024]{1,0:T(8,128)S(1)}, f32[48,1024]{1,0:T(8,128)S(1)}, u32[]{:S(2)}, u32[]{:S(2)}) %collective-permute-start.26) | collective-permute-done | bytes 196640 | tf_op jit(solution)/shard_map/ppermute | solution.py:193
  79.5 1.6 %collective-permute-start.27 = (f32[48,1024]{1,0:T(8,128)S(1)}, f32[48,1024]{1,0:T(8,128)S(1)}, u32[]{:S(2)}, u32[]{:S(2)}) collective-permute-start(f32[48,1024]{1,0:T(8,128)S(1)} %get-tuple-element.39), channel_id=1, source_target_pairs={{0,4},{1,5},{4,8},{5,9},{8,12},{9,13},{12,14},{13,15},{14,10},{15,... | collective-permute-start | bytes 589832 | tf_op jit(solution)/shard_map/ppermute | solution.py:193
  81.6 2.8 %collective-permute-done.20 = f32[56,1024]{1,0:T(8,128)S(1)} collective-permute-done((f32[56,1024]{1,0:T(8,128)S(1)}, f32[56,1024]{1,0:T(8,128)S(1)}, u32[]{:S(2)}, u32[]{:S(2)}) %collective-permute-start.20) | collective-permute-done | bytes 229408 | tf_op jit(solution)/shard_map/ppermute | solution.py:193
  86.8 2.8 %collective-permute-done.29 = f32[48,1024]{1,0:T(8,128)S(1)} collective-permute-done((f32[48,1024]{1,0:T(8,128)S(1)}, f32[48,1024]{1,0:T(8,128)S(1)}, u32[]{:S(2)}, u32[]{:S(2)}) %collective-permute-start.29) | collective-permute-done | bytes 196640 | tf_op jit(solution)/shard_map/ppermute | solution.py:200
  89.9 1.9 %collective-permute-start.28 = (f32[48,1024]{1,0:T(8,128)S(1)}, f32[48,1024]{1,0:T(8,128)S(1)}, u32[]{:S(2)}, u32[]{:S(2)}) collective-permute-start(f32[48,1024]{1,0:T(8,128)S(1)} %get-tuple-element.37), channel_id=1, source_target_pairs={{0,4},{1,5},{4,8},{5,9},{8,12},{9,13},{12,14},{13,15},{14,10},{15,... | collective-permute-start | bytes 589832 | tf_op jit(solution)/shard_map/ppermute | solution.py:193
  91.7 1.6 %collective-permute-start.21 = (f32[56,1024]{1,0:T(8,128)S(1)}, f32[56,1024]{1,0:T(8,128)S(1)}, u32[]{:S(2)}, u32[]{:S(2)}) collective-permute-start(f32[56,1024]{1,0:T(8,128)S(1)} %get-tuple-element.31), channel_id=1, source_target_pairs={{0,4},{1,5},{4,8},{5,9},{8,12},{9,13},{12,14},{13,15},{14,10},{15,... | collective-permute-start | bytes 688136 | tf_op jit(solution)/shard_map/ppermute | solution.py:193
  93.3 1.2 %collective-permute-done.24 = f32[56,1024]{1,0:T(8,128)S(1)} collective-permute-done((f32[56,1024]{1,0:T(8,128)S(1)}, f32[56,1024]{1,0:T(8,128)S(1)}, u32[]{:S(2)}, u32[]{:S(2)}) %collective-permute-start.24) | collective-permute-done | bytes 229408 | tf_op jit(solution)/shard_map/ppermute | solution.py:200
  94.8 3.5 %collective-permute-done.30 = f32[48,1024]{1,0:T(8,128)S(1)} collective-permute-done((f32[48,1024]{1,0:T(8,128)S(1)}, f32[48,1024]{1,0:T(8,128)S(1)}, u32[]{:S(2)}, u32[]{:S(2)}) %collective-permute-start.30) | collective-permute-done | bytes 196640 | tf_op jit(solution)/shard_map/ppermute | solution.py:200
  98.3 2.4 %collective-permute-done.25 = f32[56,1024]{1,0:T(8,128)S(1)} collective-permute-done((f32[56,1024]{1,0:T(8,128)S(1)}, f32[56,1024]{1,0:T(8,128)S(1)}, u32[]{:S(2)}, u32[]{:S(2)}) %collective-permute-start.25) | collective-permute-done | bytes 229408 | tf_op jit(solution)/shard_map/ppermute | solution.py:200
  (122 shorter events, 24.3 us)
Async XLA Ops:
  2.4 7.9 %collective-permute-start = (bf16[96,1024]{1,0:T(8,128)(2,1)S(1)}, bf16[96,1024]{1,0:T(8,128)(2,1)S(1)}, u32[]{:S(2)}, u32[]{:S(2)}) collective-permute-start(bf16[96,1024]{1,0:T(8,128)(2,1)S(1)} %constant_dynamic-update-slice_fusion), channel_id=1, source_target_pairs={{0,4},{1,5},{4,8},{5,9},{8,12},{9,13},{12,14},{13,15},{14,10},{15,... | collective-permute-start | bytes 589832 | tf_op jit(solution)/shard_map/ppermute | solution.py:167
  5.5 6.6 %collective-permute-start.1 = (bf16[96,1024]{1,0:T(8,128)(2,1)S(1)}, bf16[96,1024]{1,0:T(8,128)(2,1)S(1)}, u32[]{:S(2)}, u32[]{:S(2)}) collective-permute-start(bf16[96,1024]{1,0:T(8,128)(2,1)S(1)} %constant_dynamic-update-slice_fusion), channel_id=1, source_target_pairs={{4,0},{5,1},{8,4},{9,5},{12,8},{13,9},{14,12},{15,13},{10,14},{11,... | collective-permute-start | bytes 589832 | tf_op jit(solution)/shard_map/ppermute | solution.py:172
  9.3 22.0 %copy-start.1 = (s32[8]{0:T(128)S(1)}, s32[8]{0:T(128)}, u32[]{:S(2)}) copy-start(s32[8]{0:T(128)} %constant.103.clone) | copy-start | bytes 100
  10.3 7.8 %collective-permute-start.4 = (bf16[96,1024]{1,0:T(8,128)(2,1)S(1)}, bf16[96,1024]{1,0:T(8,128)(2,1)S(1)}, u32[]{:S(2)}, u32[]{:S(2)}) collective-permute-start(bf16[96,1024]{1,0:T(8,128)(2,1)S(1)} %collective-permute-done), channel_id=1, source_target_pairs={{0,4},{1,5},{4,8},{5,9},{8,12},{9,13},{12,14},{13,15},{14,10},{15,... | collective-permute-start | bytes 589832 | tf_op jit(solution)/shard_map/ppermute | solution.py:167
  12.1 5.7 %collective-permute-start.2 = (bf16[96,1024]{1,0:T(8,128)(2,1)S(1)}, bf16[96,1024]{1,0:T(8,128)(2,1)S(1)}, u32[]{:S(2)}, u32[]{:S(2)}) collective-permute-start(bf16[96,1024]{1,0:T(8,128)(2,1)S(1)} %collective-permute-done.1), channel_id=1, source_target_pairs={{4,0},{5,1},{8,4},{9,5},{12,8},{13,9},{14,12},{15,13},{10,14},{11,... | collective-permute-start | bytes 589832 | tf_op jit(solution)/shard_map/ppermute | solution.py:172
  17.8 8.7 %collective-permute-start.3 = (bf16[96,1024]{1,0:T(8,128)(2,1)S(1)}, bf16[96,1024]{1,0:T(8,128)(2,1)S(1)}, u32[]{:S(2)}, u32[]{:S(2)}) collective-permute-start(bf16[96,1024]{1,0:T(8,128)(2,1)S(1)} %collective-permute-done.2), channel_id=1, source_target_pairs={{4,0},{5,1},{8,4},{9,5},{12,8},{13,9},{14,12},{15,13},{10,14},{11,... | collective-permute-start | bytes 589832 | tf_op jit(solution)/shard_map/ppermute | solution.py:172
  18.2 6.4 %collective-permute-start.5 = (bf16[96,1024]{1,0:T(8,128)(2,1)S(1)}, bf16[96,1024]{1,0:T(8,128)(2,1)S(1)}, u32[]{:S(2)}, u32[]{:S(2)}) collective-permute-start(bf16[96,1024]{1,0:T(8,128)(2,1)S(1)} %collective-permute-done.4), channel_id=1, source_target_pairs={{0,4},{1,5},{4,8},{5,9},{8,12},{9,13},{12,14},{13,15},{14,10},{15,... | collective-permute-start | bytes 589832 | tf_op jit(solution)/shard_map/ppermute | solution.py:167
  24.5 5.7 %collective-permute-start.6 = (bf16[96,1024]{1,0:T(8,128)(2,1)S(1)}, bf16[96,1024]{1,0:T(8,128)(2,1)S(1)}, u32[]{:S(2)}, u32[]{:S(2)}) collective-permute-start(bf16[96,1024]{1,0:T(8,128)(2,1)S(1)} %collective-permute-done.5), channel_id=1, source_target_pairs={{0,4},{1,5},{4,8},{5,9},{8,12},{9,13},{12,14},{13,15},{14,10},{15,... | collective-permute-start | bytes 589832 | tf_op jit(solution)/shard_map/ppermute | solution.py:167
  30.3 5.2 %collective-permute-start.7 = (bf16[8,96,1024]{2,1,0:T(8,128)(2,1)S(1)}, bf16[8,96,1024]{2,1,0:T(8,128)(2,1)}, u32[]{:S(2)}, u32[]{:S(2)}) collective-permute-start(bf16[8,96,1024]{2,1,0:T(8,128)(2,1)S(1)} %bitcast_dynamic-update-slice_fusion.mine_ref), channel_id=1, source_target_pairs={{0,1},{1,0},{2,3},{3,2},{4,5},{5,4},{6,7},{7,6},{8,9},{9,8},{10,11... | collective-permute-start | bytes 4718600 | tf_op jit(solution)/shard_map/ppermute | solution.py:175
  33.2 32.3 %collective-permute-start.18 = (bf16[128,8,32]{0,2,1:T(8,128)(2,1)}, bf16[128,8,32]{0,2,1:T(8,128)(2,1)}, u32[]{:S(2)}, u32[]{:S(2)}) collective-permute-start(bf16[128,8,32]{0,2,1:T(8,128)(2,1)} %dynamic-slice_bitcast_fusion.2), channel_id=1, source_target_pairs={{0,1},{1,0},{2,3},{3,2},{4,5},{5,4},{6,7},{7,6},{8,9},{9,8},{10,11... | collective-permute-start | bytes 196616 | tf_op jit(solution)/shard_map/ppermute | solution.py:269
  45.7 7.8 %collective-permute-start.9 = (bf16[128,1024]{1,0:T(8,128)(2,1)}, bf16[128,1024]{1,0:T(8,128)(2,1)S(1)}, u32[]{:S(2)}, u32[]{:S(2)}) collective-permute-start(bf16[128,1024]{1,0:T(8,128)(2,1)} %get-tuple-element.20), channel_id=1, source_target_pairs={{0,1},{1,0},{2,3},{3,2},{4,5},{5,4},{6,7},{7,6},{8,9},{9,8},{10,11... | collective-permute-start | bytes 786440 | tf_op jit(solution)/shard_map/ppermute | solution.py:272
  49.6 5.8 %collective-permute-start.11 = (bf16[128,1024]{1,0:T(8,128)(2,1)S(1)}, bf16[128,1024]{1,0:T(8,128)(2,1)S(1)}, u32[]{:S(2)}, u32[]{:S(2)}) collective-permute-start(bf16[128,1024]{1,0:T(8,128)(2,1)S(1)} %copy-done.6), channel_id=1, source_target_pairs={{0,1},{1,0},{2,3},{3,2},{4,5},{5,4},{6,7},{7,6},{8,9},{9,8},{10,11... | collective-permute-start | bytes 786440 | tf_op jit(solution)/shard_map/ppermute | solution.py:272
  50.0 3.2 %collective-permute-start.8 = (bf16[8,64,128]{2,1,0:T(8,128)(2,1)}, bf16[8,64,128]{2,1,0:T(8,128)(2,1)}, u32[]{:S(2)}, u32[]{:S(2)}) collective-permute-start(bf16[8,64,128]{2,1,0:T(8,128)(2,1)} %dynamic-slice_bitcast_fusion.1), channel_id=1, source_target_pairs={{0,1},{1,0},{2,3},{3,2},{4,5},{5,4},{6,7},{7,6},{8,9},{9,8},{10,11... | collective-permute-start | bytes 393224 | tf_op jit(solution)/shard_map/ppermute | solution.py:278
  50.8 1.3 %collective-permute-start.12 = (f32[1024]{0:T(1024)S(1)}, f32[1024]{0:T(1024)S(1)}, u32[]{:S(2)}, u32[]{:S(2)}) collective-permute-start(f32[1024]{0:T(1024)S(1)} %bitcast.160), channel_id=1, source_target_pairs={{0,1},{1,0},{2,3},{3,2},{4,5},{5,4},{6,7},{7,6},{8,9},{9,8},{10,11... | collective-permute-start | bytes 12296 | tf_op jit(solution)/shard_map/ppermute | solution.py:272
  52.2 3.0 %collective-permute-start.10 = (bf16[8,64,128]{2,1,0:T(8,128)(2,1)}, bf16[8,64,128]{2,1,0:T(8,128)(2,1)S(1)}, u32[]{:S(2)}, u32[]{:S(2)}) collective-permute-start(bf16[8,64,128]{2,1,0:T(8,128)(2,1)} %dynamic-slice_bitcast_fusion), channel_id=1, source_target_pairs={{0,1},{1,0},{2,3},{3,2},{4,5},{5,4},{6,7},{7,6},{8,9},{9,8},{10,11... | collective-permute-start | bytes 393224 | tf_op jit(solution)/shard_map/ppermute | solution.py:278
  53.2 5.1 %collective-permute-start.17 = (bf16[128,1024]{1,0:T(8,128)(2,1)S(1)}, bf16[128,1024]{1,0:T(8,128)(2,1)S(1)}, u32[]{:S(2)}, u32[]{:S(2)}) collective-permute-start(bf16[128,1024]{1,0:T(8,128)(2,1)S(1)} %copy-done.5), channel_id=1, source_target_pairs={{0,1},{1,0},{2,3},{3,2},{4,5},{5,4},{6,7},{7,6},{8,9},{9,8},{10,11... | collective-permute-start | bytes 786440 | tf_op jit(solution)/shard_map/ppermute | solution.py:272
  53.5 4.5 %collective-permute-start.13 = (bf16[128,8,32]{0,2,1:T(8,128)(2,1)S(1)}, bf16[128,8,32]{0,2,1:T(8,128)(2,1)S(1)}, u32[]{:S(2)}, u32[]{:S(2)}) collective-permute-start(bf16[128,8,32]{0,2,1:T(8,128)(2,1)S(1)} %dynamic-slice_bitcast_fusion.3), channel_id=1, source_target_pairs={{0,1},{1,0},{2,3},{3,2},{4,5},{5,4},{6,7},{7,6},{8,9},{9,8},{10,11... | collective-permute-start | bytes 196616 | tf_op jit(solution)/shard_map/ppermute | solution.py:269
  55.1 2.9 %collective-permute-start.14 = (bf16[128,1024]{1,0:T(8,128)(2,1)S(1)}, bf16[128,1024]{1,0:T(8,128)(2,1)S(1)}, u32[]{:S(2)}, u32[]{:S(2)}) collective-permute-start(bf16[128,1024]{1,0:T(8,128)(2,1)S(1)} %copy-done.4), channel_id=1, source_target_pairs={{0,1},{1,0},{2,3},{3,2},{4,5},{5,4},{6,7},{7,6},{8,9},{9,8},{10,11... | collective-permute-start | bytes 786440 | tf_op jit(solution)/shard_map/ppermute | solution.py:272
  56.0 7.2 %collective-permute-start.15 = (f32[48,1024]{1,0:T(8,128)S(1)}, f32[48,1024]{1,0:T(8,128)S(1)}, u32[]{:S(2)}, u32[]{:S(2)}) collective-permute-start(f32[48,1024]{1,0:T(8,128)S(1)} %get-tuple-element.42), channel_id=1, source_target_pairs={{0,4},{1,5},{4,8},{5,9},{8,12},{9,13},{12,14},{13,15},{14,10},{15,... | collective-permute-start | bytes 589832 | tf_op jit(solution)/shard_map/ppermute | solution.py:304
  58.0 6.9 %collective-permute-start.16 = (f32[48,1024]{1,0:T(8,128)S(1)}, f32[48,1024]{1,0:T(8,128)S(1)}, u32[]{:S(2)}, u32[]{:S(2)}) collective-permute-start(f32[48,1024]{1,0:T(8,128)S(1)} %get-tuple-element.41), channel_id=1, source_target_pairs={{4,0},{5,1},{8,4},{9,5},{12,8},{13,9},{14,12},{15,13},{10,14},{11,... | collective-permute-start | bytes 589832 | tf_op jit(solution)/shard_map/ppermute | solution.py:305
  66.7 8.6 %collective-permute-start.19 = (f32[56,1024]{1,0:T(8,128)S(1)}, f32[56,1024]{1,0:T(8,128)S(1)}, u32[]{:S(2)}, u32[]{:S(2)}) collective-permute-start(f32[56,1024]{1,0:T(8,128)S(1)} %get-tuple-element.35), channel_id=1, source_target_pairs={{0,4},{1,5},{4,8},{5,9},{8,12},{9,13},{12,14},{13,15},{14,10},{15,... | collective-permute-start | bytes 688136 | tf_op jit(solution)/shard_map/ppermute | solution.py:193
  68.3 7.0 %collective-permute-start.22 = (f32[56,1024]{1,0:T(8,128)S(1)}, f32[56,1024]{1,0:T(8,128)S(1)}, u32[]{:S(2)}, u32[]{:S(2)}) collective-permute-start(f32[56,1024]{1,0:T(8,128)S(1)} %get-tuple-element.36), channel_id=1, source_target_pairs={{4,0},{5,1},{8,4},{9,5},{12,8},{13,9},{14,12},{15,13},{10,14},{11,... | collective-permute-start | bytes 688136 | tf_op jit(solution)/shard_map/ppermute | solution.py:200
  68.8 10.7 %collective-permute-start.26 = (f32[48,1024]{1,0:T(8,128)S(1)}, f32[48,1024]{1,0:T(8,128)S(1)}, u32[]{:S(2)}, u32[]{:S(2)}) collective-permute-start(f32[48,1024]{1,0:T(8,128)S(1)} %fusion.31), channel_id=1, source_target_pairs={{0,4},{1,5},{4,8},{5,9},{8,12},{9,13},{12,14},{13,15},{14,10},{15,... | collective-permute-start | bytes 589832 | tf_op jit(solution)/shard_map/ppermute | solution.py:193
  75.3 9.0 %collective-permute-start.20 = (f32[56,1024]{1,0:T(8,128)S(1)}, f32[56,1024]{1,0:T(8,128)S(1)}, u32[]{:S(2)}, u32[]{:S(2)}) collective-permute-start(f32[56,1024]{1,0:T(8,128)S(1)} %get-tuple-element.33), channel_id=1, source_target_pairs={{0,4},{1,5},{4,8},{5,9},{8,12},{9,13},{12,14},{13,15},{14,10},{15,... | collective-permute-start | bytes 688136 | tf_op jit(solution)/shard_map/ppermute | solution.py:193
  77.0 8.4 %collective-permute-start.23 = (f32[56,1024]{1,0:T(8,128)S(1)}, f32[56,1024]{1,0:T(8,128)S(1)}, u32[]{:S(2)}, u32[]{:S(2)}) collective-permute-start(f32[56,1024]{1,0:T(8,128)S(1)} %get-tuple-element.34), channel_id=1, source_target_pairs={{4,0},{5,1},{8,4},{9,5},{12,8},{13,9},{14,12},{15,13},{10,14},{11,... | collective-permute-start | bytes 688136 | tf_op jit(solution)/shard_map/ppermute | solution.py:200
  79.5 7.3 %collective-permute-start.27 = (f32[48,1024]{1,0:T(8,128)S(1)}, f32[48,1024]{1,0:T(8,128)S(1)}, u32[]{:S(2)}, u32[]{:S(2)}) collective-permute-start(f32[48,1024]{1,0:T(8,128)S(1)} %get-tuple-element.39), channel_id=1, source_target_pairs={{0,4},{1,5},{4,8},{5,9},{8,12},{9,13},{12,14},{13,15},{14,10},{15,... | collective-permute-start | bytes 589832 | tf_op jit(solution)/shard_map/ppermute | solution.py:193
  81.2 8.4 %collective-permute-start.29 = (f32[48,1024]{1,0:T(8,128)S(1)}, f32[48,1024]{1,0:T(8,128)S(1)}, u32[]{:S(2)}, u32[]{:S(2)}) collective-permute-start(f32[48,1024]{1,0:T(8,128)S(1)} %get-tuple-element.40), channel_id=1, source_target_pairs={{4,0},{5,1},{8,4},{9,5},{12,8},{13,9},{14,12},{15,13},{10,14},{11,... | collective-permute-start | bytes 589832 | tf_op jit(solution)/shard_map/ppermute | solution.py:200
  85.5 9.1 %collective-permute-start.24 = (f32[56,1024]{1,0:T(8,128)S(1)}, f32[56,1024]{1,0:T(8,128)S(1)}, u32[]{:S(2)}, u32[]{:S(2)}) collective-permute-start(f32[56,1024]{1,0:T(8,128)S(1)} %get-tuple-element.32), channel_id=1, source_target_pairs={{4,0},{5,1},{8,4},{9,5},{12,8},{13,9},{14,12},{15,13},{10,14},{11,... | collective-permute-start | bytes 688136 | tf_op jit(solution)/shard_map/ppermute | solution.py:200
  89.7 8.6 %collective-permute-start.30 = (f32[48,1024]{1,0:T(8,128)S(1)}, f32[48,1024]{1,0:T(8,128)S(1)}, u32[]{:S(2)}, u32[]{:S(2)}) collective-permute-start(f32[48,1024]{1,0:T(8,128)S(1)} %get-tuple-element.38), channel_id=1, source_target_pairs={{4,0},{5,1},{8,4},{9,5},{12,8},{13,9},{14,12},{15,13},{10,14},{11,... | collective-permute-start | bytes 589832 | tf_op jit(solution)/shard_map/ppermute | solution.py:200
  89.9 8.4 %collective-permute-start.28 = (f32[48,1024]{1,0:T(8,128)S(1)}, f32[48,1024]{1,0:T(8,128)S(1)}, u32[]{:S(2)}, u32[]{:S(2)}) collective-permute-start(f32[48,1024]{1,0:T(8,128)S(1)} %get-tuple-element.37), channel_id=1, source_target_pairs={{0,4},{1,5},{4,8},{5,9},{8,12},{9,13},{12,14},{13,15},{14,10},{15,... | collective-permute-start | bytes 589832 | tf_op jit(solution)/shard_map/ppermute | solution.py:193
  91.7 6.6 %collective-permute-start.21 = (f32[56,1024]{1,0:T(8,128)S(1)}, f32[56,1024]{1,0:T(8,128)S(1)}, u32[]{:S(2)}, u32[]{:S(2)}) collective-permute-start(f32[56,1024]{1,0:T(8,128)S(1)} %get-tuple-element.31), channel_id=1, source_target_pairs={{0,4},{1,5},{4,8},{5,9},{8,12},{9,13},{12,14},{13,15},{14,10},{15,... | collective-permute-start | bytes 688136 | tf_op jit(solution)/shard_map/ppermute | solution.py:193
  94.6 6.2 %collective-permute-start.25 = (f32[56,1024]{1,0:T(8,128)S(1)}, f32[56,1024]{1,0:T(8,128)S(1)}, u32[]{:S(2)}, u32[]{:S(2)}) collective-permute-start(f32[56,1024]{1,0:T(8,128)S(1)} %fusion.18), channel_id=1, source_target_pairs={{4,0},{5,1},{8,4},{9,5},{12,8},{13,9},{14,12},{15,13},{10,14},{11,... | collective-permute-start | bytes 688136 | tf_op jit(solution)/shard_map/ppermute | solution.py:200
  (14 other events, 75.1 us)

commit v19 on v16

--- a/solution.py
+++ b/solution.py
@@ -132,8 +132,7 @@
         cost_estimate=pl.CostEstimate(
             flops=flops, transcendentals=6 * rows * hidden,
             bytes_accessed=4 * chips * width * hidden + 16 * rows * hidden),
-    )(params, x_rows, z_rows, y_rows.astype(f32)[:, None], mine, other,
-      w_three.astype(f32)[None, :])
+    )(params, x_rows, z_rows, y_rows, mine, other, w_three)
     return (e_slope, g_one, e_aone, e_cone, g_two, h_one, e_atwo, grad_three[0])
 
 
@@ -234,9 +233,11 @@
     params = jnp.stack(
         [total, core, jnp.asarray(place, jnp.int32)[position // 2]]
     ).astype(jnp.int32)
-    mine, other, index, params = ring_all_gather(
-        jnp.concatenate([w_first, w_second], axis=0), n_blk, params
-    )
+    side = (params, payoffs.astype(jnp.float32)[:, None], w_out.astype(jnp.float32)[None, :])
+    mine, other, index, side = ring_all_gather(
+        jnp.concatenate([w_first, w_second], axis=0), n_blk, side
+    )
+    params, y_col, out_row = side
     fused = r_one % 16 == 0 and r_two % 16 == 0
     if not fused:
         gathered = jnp.take(
@@ -249,7 +250,7 @@
     total = jnp.sum(sending)
     mask = (jnp.arange(rows_dev, dtype=jnp.int32) < total).astype(jnp.float32)
     if fused:
-        terms = twin_fused(x_rows, z_rows, y_rows, params, place, mine, other, r_one, w_out)
+        terms = twin_fused(x_rows, z_rows, y_col, params, place, mine, other, r_one, out_row)
     else:
         terms = twin_terms(x_rows, z_rows, y_rows, mask, w_one, w_two, w_out)
     e_slope, g_one, e_aone, e_cone, g_two, h_one, e_atwo, grad_three = terms

time: 101 us -> 101 us (level)
  other arithmetic: 9.42 us -> 10.7 us
    broadcast_in_dim x2, other arithmetic: 0.6 us -> 1.96 us  [the longest x1 1.31 us: per_device(): w_out.astype(jnp.float32)[None, :]]
  transfers between devices with their start and end apart: 31 -> 31, of which waited for: 15 -> 14; matrix products, arithmetic and copies ran while one was open for 25% -> 26% of each run, Pallas kernels for 6% -> 6%
where the time goes in v19:
time: 101 us
  waiting for transfers between devices  34.8 us (34%)
  starting transfers between devices  26.4 us (26%)
  other arithmetic  10.7 us (11%)
  local copies, waits for them, and re-layouts  10.4 us (10%)
  matrix products  10 us (10%)
  Pallas kernels  6.36 us (6%)
  between operations  1.78 us (2%)
    ppermute x7, waiting for transfers between devices, backward(): acc = lax.ppermute(acc, 'blk', ccw)  14.9 us
    ppermute x7, starting transfers between devices, forward(): acc = lax.ppermute(acc, 'blk', cw) + part[(window - s) % chips]  12.1 us
    ppermute x4, waiting for transfers between devices, ring_all_gather(): left = lax.ppermute(left, 'blk', cw)  11.7 us
    ppermute x4, starting transfers between devices, ring_all_gather(): left = lax.ppermute(left, 'blk', cw)  8.71 us
    ppermute x7, waiting for transfers between devices, forward(): acc = lax.ppermute(acc, 'blk', cw) + part[(window - s) % chips]  8.14 us
    dot_general x4, matrix products, rows_first(): lax.dot_general(left, right, (((2,), (0,)), ((), ())), preferred_element_...  6.96 us
    pallas_call x1, Pallas kernels, twin_fused(): pl.pallas_call(functools.partial(twin_body, r_one, place), out_shape=shap...  6.36 us
    dot_general x4, matrix products, slots_product(): lax.dot_general(left, right, (((0,), (0,)), ((), ())), preferred_element_...  3.08 us
  transfers between devices with their start and end apart: 31, of which 14 were waited for; matrix products, arithmetic and copies ran while one was open for 26% of the time, Pallas kernels for 6%

profile of v19, /device:TPU:0, one launch (start us, length us, event | category | flops | bytes accessed | tf_op | source)
XLA Modules:
  0.0 100.6 jit_solution(1319045027644828283)
XLA Ops:
  2.4 3.1 %collective-permute-start = (bf16[96,1024]{1,0:T(8,128)(2,1)S(1)}, bf16[96,1024]{1,0:T(8,128)(2,1)S(1)}, u32[]{:S(2)}, u32[]{:S(2)}) collective-permute-start(bf16[96,1024]{1,0:T(8,128)(2,1)S(1)} %constant_dynamic-update-slice_fusion), channel_id=1, source_target_pairs={{0,4},{1,5},{4,8},{5,9},{8,12},{9,13},{12,14},{13,15},{14,10},{15,... | collective-permute-start | bytes 589832 | tf_op jit(solution)/shard_map/ppermute | solution.py:166
  5.6 1.3 %broadcast_in_dim.59 = f32[1024]{0:T(1024)} convert(bf16[1024]{0:T(1024)(128)(2,1)} %param.19) | non-fusion elementwise | flops 1024 | bytes 6144 | tf_op jit(solution)/shard_map/broadcast_in_dim | solution.py:236
  8.8 1.9 %pad_add_fusion.par_ref = s32[3]{0:T(128)} fusion(s32[1]{0:T(128)} %dynamic_slice.37, s32[1]{0:T(128)} %bitcast.1, s32[1]{0:T(128)} %bitcast), kind=kLoop, calls=%fused_computation.101 | loop fusion | flops 6 | bytes 24 | tf_op jit(solution)/shard_map/stack | solution.py:233
  11.3 2.0 %collective-permute-start.4 = (bf16[96,1024]{1,0:T(8,128)(2,1)S(1)}, bf16[96,1024]{1,0:T(8,128)(2,1)S(1)}, u32[]{:S(2)}, u32[]{:S(2)}) collective-permute-start(bf16[96,1024]{1,0:T(8,128)(2,1)S(1)} %collective-permute-done), channel_id=1, source_target_pairs={{0,4},{1,5},{4,8},{5,9},{8,12},{9,13},{12,14},{13,15},{14,10},{15,... | collective-permute-start | bytes 589832 | tf_op jit(solution)/shard_map/ppermute | solution.py:166
  13.4 4.3 %collective-permute-done.4 = bf16[96,1024]{1,0:T(8,128)(2,1)S(1)} collective-permute-done((bf16[96,1024]{1,0:T(8,128)(2,1)S(1)}, bf16[96,1024]{1,0:T(8,128)(2,1)S(1)}, u32[]{:S(2)}, u32[]{:S(2)}) %collective-permute-start.4) | collective-permute-done | bytes 196640 | tf_op jit(solution)/shard_map/ppermute | solution.py:166
  17.7 1.7 %collective-permute-start.5 = (bf16[96,1024]{1,0:T(8,128)(2,1)S(1)}, bf16[96,1024]{1,0:T(8,128)(2,1)S(1)}, u32[]{:S(2)}, u32[]{:S(2)}) collective-permute-start(bf16[96,1024]{1,0:T(8,128)(2,1)S(1)} %collective-permute-done.4), channel_id=1, source_target_pairs={{0,4},{1,5},{4,8},{5,9},{8,12},{9,13},{12,14},{13,15},{14,10},{15,... | collective-permute-start | bytes 589832 | tf_op jit(solution)/shard_map/ppermute | solution.py:166
  19.7 3.6 %collective-permute-done.5 = bf16[96,1024]{1,0:T(8,128)(2,1)S(1)} collective-permute-done((bf16[96,1024]{1,0:T(8,128)(2,1)S(1)}, bf16[96,1024]{1,0:T(8,128)(2,1)S(1)}, u32[]{:S(2)}, u32[]{:S(2)}) %collective-permute-start.5) | collective-permute-done | bytes 196640 | tf_op jit(solution)/shard_map/ppermute | solution.py:166
  23.4 1.9 %collective-permute-start.6 = (bf16[96,1024]{1,0:T(8,128)(2,1)S(1)}, bf16[96,1024]{1,0:T(8,128)(2,1)S(1)}, u32[]{:S(2)}, u32[]{:S(2)}) collective-permute-start(bf16[96,1024]{1,0:T(8,128)(2,1)S(1)} %collective-permute-done.5), channel_id=1, source_target_pairs={{0,4},{1,5},{4,8},{5,9},{8,12},{9,13},{12,14},{13,15},{14,10},{15,... | collective-permute-start | bytes 589832 | tf_op jit(solution)/shard_map/ppermute | solution.py:166
  25.3 3.8 %collective-permute-done.6 = bf16[96,1024]{1,0:T(8,128)(2,1)S(1)} collective-permute-done((bf16[96,1024]{1,0:T(8,128)(2,1)S(1)}, bf16[96,1024]{1,0:T(8,128)(2,1)S(1)}, u32[]{:S(2)}, u32[]{:S(2)}) %collective-permute-start.6) | collective-permute-done | bytes 196640 | tf_op jit(solution)/shard_map/ppermute | solution.py:166
  33.7 6.4 %shard_map.148 = (bf16[128,512]{1,0:T(8,128)(2,1)}, bf16[128,1024]{1,0:T(8,128)(2,1)}, bf16[128,1024]{1,0:T(8,128)(2,1)}, bf16[1024,128]{1,0:T(8,128)(2,1)}, bf1...) custom-call(s32[3]{0:T(128)} %pad_add_fusion.par_ref, ...), custom_call_target="tpu_custom_call" | custom-call | flops 1476395008 | bytes 5242880 | tf_op jit(solution)/shard_map/pallas_call | solution.py:127
  40.1 1.6 %gather_fusion.1 = bf16[8,2,64,128]{3,2,1,0:T(8,128)(2,1)S(1)} fusion(bf16[8,2,64,128]{3,2,1,0:T(8,128)(2,1)} %bitcast.159, s32[1024]{0:T(1024)S(1)} %pad_clamp_fusion), kind=kCustom, calls=%fused_computation.1 | custom fusion | bytes 524320 | tf_op jit(solution)/shard_map/jit(_take)/gather | solution.py:275
  42.4 1.4 %fusion.17 = f32[8,64,1024]{2,1,0:T(8,128)S(1)} fusion(bf16[128,1024]{1,0:T(8,128)(2,1)} %get-tuple-element.20, bf16[8,2,64,128]{3,2,1,0:T(8,128)(2,1)S(1)} %gather_fusion.1, s32[]{:T(128)S(6)} %select_n.67), kind=kOutput, calls=%fused_computation.23 | convolution fusion | flops 134217728 | bytes 2490372 | tf_op jit(solution)/shard_map/dot_general | solution.py:281
  44.4 2.7 %fusion.13 = f32[8,64,1024]{2,1,0:T(8,128)} fusion(bf16[128,1024]{1,0:T(8,128)(2,1)} %get-tuple-element.22, bf16[8,2,64,128]{3,2,1,0:T(8,128)(2,1)S(1)} %gather_fusion.2, s32[]{:T(128)S(6)} %select_n.67), kind=kOutput, calls=%fused_computation.19 | convolution fusion | flops 134217728 | bytes 2490372 | tf_op jit(solution)/shard_map/dot_general | solution.py:281
  53.3 1.4 %fusion.15 = f32[8,64,1024]{2,1,0:T(8,128)S(1)} fusion(bf16[8,64,128]{2,1,0:T(8,128)(2,1)S(1)} %collective-permute-done.8, bf16[128,1024]{1,0:T(8,128)(2,1)} %collective-permute-done.9), kind=kOutput, calls=%fused_computation.21 | convolution fusion | flops 134217728 | bytes 2490368 | tf_op jit(solution)/shard_map/dot_general | solution.py:281
  55.2 1.5 %add_add_fusion = f32[8,64,1024]{2,1,0:T(8,128)S(1)} fusion(f32[8,64,1024]{2,1,0:T(8,128)S(1)} %copy-done.2, f32[8,64,1024]{2,1,0:T(8,128)S(1)} %fusion.17, f32[8,64,1024]{2,1,0:T(8,128)S(1)} %fusion.15, bf16[8,64,128]{2,1,0:T(8,128)(2,1)S(1)} %collective-permute-done.10, bf16[128,1024]{1,0:T(8,128)(2,1)} %collective-permute-done.11), kind=kOutput, calls=%fused_computation.5 | convolution fusion | flops 135790592 | bytes 8781824 | tf_op jit(solution)/shard_map/dot_general | solution.py:281
  56.7 1.9 %collective-permute-start.24 = (f32[48,1024]{1,0:T(8,128)S(1)}, f32[48,1024]{1,0:T(8,128)S(1)}, u32[]{:S(2)}, u32[]{:S(2)}) collective-permute-start(f32[48,1024]{1,0:T(8,128)S(1)} %get-tuple-element.37), channel_id=1, source_target_pairs={{0,4},{1,5},{4,8},{5,9},{8,12},{9,13},{12,14},{13,15},{14,10},{15,... | collective-permute-start | bytes 589832 | tf_op jit(solution)/shard_map/ppermute | solution.py:192
  59.0 1.3 %fusion.2 = f32[8,32,1024]{2,1,0:T(8,128)S(1)} fusion(bf16[128,8,32]{0,2,1:T(8,128)(2,1)} %collective-permute-done.15, bf16[128,1024]{1,0:T(8,128)(2,1)} %collective-permute-done.16), kind=kOutput, calls=%fused_computation.10 | convolution fusion | flops 67108864 | bytes 1376256 | tf_op jit(solution)/shard_map/dot_general | solution.py:217
  60.6 1.6 %collective-permute-start.17 = (f32[56,1024]{1,0:T(8,128)S(1)}, f32[56,1024]{1,0:T(8,128)S(1)}, u32[]{:S(2)}, u32[]{:S(2)}) collective-permute-start(f32[56,1024]{1,0:T(8,128)S(1)} %get-tuple-element.31), channel_id=1, source_target_pairs={{0,4},{1,5},{4,8},{5,9},{8,12},{9,13},{12,14},{13,15},{14,10},{15,... | collective-permute-start | bytes 688136 | tf_op jit(solution)/shard_map/ppermute | solution.py:192
  62.8 1.5 %collective-permute-done.24 = f32[48,1024]{1,0:T(8,128)S(1)} collective-permute-done((f32[48,1024]{1,0:T(8,128)S(1)}, f32[48,1024]{1,0:T(8,128)S(1)}, u32[]{:S(2)}, u32[]{:S(2)}) %collective-permute-start.24) | collective-permute-done | bytes 196640 | tf_op jit(solution)/shard_map/ppermute | solution.py:192
  64.4 2.1 %collective-permute-start.25 = (f32[48,1024]{1,0:T(8,128)S(1)}, f32[48,1024]{1,0:T(8,128)S(1)}, u32[]{:S(2)}, u32[]{:S(2)}) collective-permute-start(f32[48,1024]{1,0:T(8,128)S(1)} %fusion.33), channel_id=1, source_target_pairs={{0,4},{1,5},{4,8},{5,9},{8,12},{9,13},{12,14},{13,15},{14,10},{15,... | collective-permute-start | bytes 589832 | tf_op jit(solution)/shard_map/ppermute | solution.py:192
  66.5 2.8 %collective-permute-done.17 = f32[56,1024]{1,0:T(8,128)S(1)} collective-permute-done((f32[56,1024]{1,0:T(8,128)S(1)}, f32[56,1024]{1,0:T(8,128)S(1)}, u32[]{:S(2)}, u32[]{:S(2)}) %collective-permute-start.17) | collective-permute-done | bytes 229408 | tf_op jit(solution)/shard_map/ppermute | solution.py:192
  69.3 1.5 %collective-permute-done.20 = f32[56,1024]{1,0:T(8,128)S(1)} collective-permute-done((f32[56,1024]{1,0:T(8,128)S(1)}, f32[56,1024]{1,0:T(8,128)S(1)}, u32[]{:S(2)}, u32[]{:S(2)}) %collective-permute-start.20) | collective-permute-done | bytes 229408 | tf_op jit(solution)/shard_map/ppermute | solution.py:198
  70.8 1.6 %collective-permute-start.18 = (f32[56,1024]{1,0:T(8,128)S(1)}, f32[56,1024]{1,0:T(8,128)S(1)}, u32[]{:S(2)}, u32[]{:S(2)}) collective-permute-start(f32[56,1024]{1,0:T(8,128)S(1)} %get-tuple-element.29), channel_id=1, source_target_pairs={{0,4},{1,5},{4,8},{5,9},{8,12},{9,13},{12,14},{13,15},{14,10},{15,... | collective-permute-start | bytes 688136 | tf_op jit(solution)/shard_map/ppermute | solution.py:192
  72.9 1.8 %collective-permute-done.28 = f32[48,1024]{1,0:T(8,128)S(1)} collective-permute-done((f32[48,1024]{1,0:T(8,128)S(1)}, f32[48,1024]{1,0:T(8,128)S(1)}, u32[]{:S(2)}, u32[]{:S(2)}) %collective-permute-start.28) | collective-permute-done | bytes 196640 | tf_op jit(solution)/shard_map/ppermute | solution.py:198
  74.8 1.7 %collective-permute-start.26 = (f32[48,1024]{1,0:T(8,128)S(1)}, f32[48,1024]{1,0:T(8,128)S(1)}, u32[]{:S(2)}, u32[]{:S(2)}) collective-permute-start(f32[48,1024]{1,0:T(8,128)S(1)} %get-tuple-element.35), channel_id=1, source_target_pairs={{0,4},{1,5},{4,8},{5,9},{8,12},{9,13},{12,14},{13,15},{14,10},{15,... | collective-permute-start | bytes 589832 | tf_op jit(solution)/shard_map/ppermute | solution.py:192
  76.9 2.5 %collective-permute-done.18 = f32[56,1024]{1,0:T(8,128)S(1)} collective-permute-done((f32[56,1024]{1,0:T(8,128)S(1)}, f32[56,1024]{1,0:T(8,128)S(1)}, u32[]{:S(2)}, u32[]{:S(2)}) %collective-permute-start.18) | collective-permute-done | bytes 229408 | tf_op jit(solution)/shard_map/ppermute | solution.py:192
  81.2 1.6 %collective-permute-start.19 = (f32[56,1024]{1,0:T(8,128)S(1)}, f32[56,1024]{1,0:T(8,128)S(1)}, u32[]{:S(2)}, u32[]{:S(2)}) collective-permute-start(f32[56,1024]{1,0:T(8,128)S(1)} %get-tuple-element.27), channel_id=1, source_target_pairs={{0,4},{1,5},{4,8},{5,9},{8,12},{9,13},{12,14},{13,15},{14,10},{15,... | collective-permute-start | bytes 688136 | tf_op jit(solution)/shard_map/ppermute | solution.py:192
  82.8 2.1 %collective-permute-done.29 = f32[48,1024]{1,0:T(8,128)S(1)} collective-permute-done((f32[48,1024]{1,0:T(8,128)S(1)}, f32[48,1024]{1,0:T(8,128)S(1)}, u32[]{:S(2)}, u32[]{:S(2)}) %collective-permute-start.29) | collective-permute-done | bytes 196640 | tf_op jit(solution)/shard_map/ppermute | solution.py:198
  84.9 1.6 %collective-permute-start.27 = (f32[48,1024]{1,0:T(8,128)S(1)}, f32[48,1024]{1,0:T(8,128)S(1)}, u32[]{:S(2)}, u32[]{:S(2)}) collective-permute-start(f32[48,1024]{1,0:T(8,128)S(1)} %get-tuple-element.33), channel_id=1, source_target_pairs={{0,4},{1,5},{4,8},{5,9},{8,12},{9,13},{12,14},{13,15},{14,10},{15,... | collective-permute-start | bytes 589832 | tf_op jit(solution)/shard_map/ppermute | solution.py:192
  87.0 2.8 %collective-permute-done.22 = f32[56,1024]{1,0:T(8,128)S(1)} collective-permute-done((f32[56,1024]{1,0:T(8,128)S(1)}, f32[56,1024]{1,0:T(8,128)S(1)}, u32[]{:S(2)}, u32[]{:S(2)}) %collective-permute-start.22) | collective-permute-done | bytes 229408 | tf_op jit(solution)/shard_map/ppermute | solution.py:198
  91.1 3.2 %collective-permute-done.30 = f32[48,1024]{1,0:T(8,128)S(1)} collective-permute-done((f32[48,1024]{1,0:T(8,128)S(1)}, f32[48,1024]{1,0:T(8,128)S(1)}, u32[]{:S(2)}, u32[]{:S(2)}) %collective-permute-start.30) | collective-permute-done | bytes 196640 | tf_op jit(solution)/shard_map/ppermute | solution.py:198
  94.4 2.4 %collective-permute-done.23 = f32[56,1024]{1,0:T(8,128)S(1)} collective-permute-done((f32[56,1024]{1,0:T(8,128)S(1)}, f32[56,1024]{1,0:T(8,128)S(1)}, u32[]{:S(2)}, u32[]{:S(2)}) %collective-permute-start.23) | collective-permute-done | bytes 229408 | tf_op jit(solution)/shard_map/ppermute | solution.py:198
  (114 shorter events, 26.3 us)
Async XLA Ops:
  2.4 8.9 %collective-permute-start = (bf16[96,1024]{1,0:T(8,128)(2,1)S(1)}, bf16[96,1024]{1,0:T(8,128)(2,1)S(1)}, u32[]{:S(2)}, u32[]{:S(2)}) collective-permute-start(bf16[96,1024]{1,0:T(8,128)(2,1)S(1)} %constant_dynamic-update-slice_fusion), channel_id=1, source_target_pairs={{0,4},{1,5},{4,8},{5,9},{8,12},{9,13},{12,14},{13,15},{14,10},{15,... | collective-permute-start | bytes 589832 | tf_op jit(solution)/shard_map/ppermute | solution.py:166
  5.5 7.9 %collective-permute-start.1 = (bf16[96,1024]{1,0:T(8,128)(2,1)S(1)}, bf16[96,1024]{1,0:T(8,128)(2,1)S(1)}, u32[]{:S(2)}, u32[]{:S(2)}) collective-permute-start(bf16[96,1024]{1,0:T(8,128)(2,1)S(1)} %constant_dynamic-update-slice_fusion), channel_id=1, source_target_pairs={{4,0},{5,1},{8,4},{9,5},{12,8},{13,9},{14,12},{15,13},{10,14},{11,... | collective-permute-start | bytes 589832 | tf_op jit(solution)/shard_map/ppermute | solution.py:171
  5.5 24.5 %copy-start.1 = (s32[8]{0:T(128)S(1)}, s32[8]{0:T(128)}, u32[]{:S(2)}) copy-start(s32[8]{0:T(128)} %constant.103.clone) | copy-start | bytes 100
  11.3 6.4 %collective-permute-start.4 = (bf16[96,1024]{1,0:T(8,128)(2,1)S(1)}, bf16[96,1024]{1,0:T(8,128)(2,1)S(1)}, u32[]{:S(2)}, u32[]{:S(2)}) collective-permute-start(bf16[96,1024]{1,0:T(8,128)(2,1)S(1)} %collective-permute-done), channel_id=1, source_target_pairs={{0,4},{1,5},{4,8},{5,9},{8,12},{9,13},{12,14},{13,15},{14,10},{15,... | collective-permute-start | bytes 589832 | tf_op jit(solution)/shard_map/ppermute | solution.py:166
  13.4 6.1 %collective-permute-start.2 = (bf16[96,1024]{1,0:T(8,128)(2,1)S(1)}, bf16[96,1024]{1,0:T(8,128)(2,1)S(1)}, u32[]{:S(2)}, u32[]{:S(2)}) collective-permute-start(bf16[96,1024]{1,0:T(8,128)(2,1)S(1)} %collective-permute-done.1), channel_id=1, source_target_pairs={{4,0},{5,1},{8,4},{9,5},{12,8},{13,9},{14,12},{15,13},{10,14},{11,... | collective-permute-start | bytes 589832 | tf_op jit(solution)/shard_map/ppermute | solution.py:171
  17.7 5.7 %collective-permute-start.5 = (bf16[96,1024]{1,0:T(8,128)(2,1)S(1)}, bf16[96,1024]{1,0:T(8,128)(2,1)S(1)}, u32[]{:S(2)}, u32[]{:S(2)}) collective-permute-start(bf16[96,1024]{1,0:T(8,128)(2,1)S(1)} %collective-permute-done.4), channel_id=1, source_target_pairs={{0,4},{1,5},{4,8},{5,9},{8,12},{9,13},{12,14},{13,15},{14,10},{15,... | collective-permute-start | bytes 589832 | tf_op jit(solution)/shard_map/ppermute | solution.py:166
  19.4 5.8 %collective-permute-start.3 = (bf16[96,1024]{1,0:T(8,128)(2,1)S(1)}, bf16[96,1024]{1,0:T(8,128)(2,1)S(1)}, u32[]{:S(2)}, u32[]{:S(2)}) collective-permute-start(bf16[96,1024]{1,0:T(8,128)(2,1)S(1)} %collective-permute-done.2), channel_id=1, source_target_pairs={{4,0},{5,1},{8,4},{9,5},{12,8},{13,9},{14,12},{15,13},{10,14},{11,... | collective-permute-start | bytes 589832 | tf_op jit(solution)/shard_map/ppermute | solution.py:171
  23.4 5.7 %collective-permute-start.6 = (bf16[96,1024]{1,0:T(8,128)(2,1)S(1)}, bf16[96,1024]{1,0:T(8,128)(2,1)S(1)}, u32[]{:S(2)}, u32[]{:S(2)}) collective-permute-start(bf16[96,1024]{1,0:T(8,128)(2,1)S(1)} %collective-permute-done.5), channel_id=1, source_target_pairs={{0,4},{1,5},{4,8},{5,9},{8,12},{9,13},{12,14},{13,15},{14,10},{15,... | collective-permute-start | bytes 589832 | tf_op jit(solution)/shard_map/ppermute | solution.py:166
  29.1 4.6 %collective-permute-start.7 = (bf16[8,96,1024]{2,1,0:T(8,128)(2,1)S(1)}, bf16[8,96,1024]{2,1,0:T(8,128)(2,1)}, u32[]{:S(2)}, u32[]{:S(2)}) collective-permute-start(bf16[8,96,1024]{2,1,0:T(8,128)(2,1)S(1)} %bitcast_dynamic-update-slice_fusion.mine_ref), channel_id=1, source_target_pairs={{0,1},{1,0},{2,3},{3,2},{4,5},{5,4},{6,7},{7,6},{8,9},{9,8},{10,11... | collective-permute-start | bytes 4718600 | tf_op jit(solution)/shard_map/ppermute | solution.py:174
  31.9 27.0 %collective-permute-start.15 = (bf16[128,8,32]{0,2,1:T(8,128)(2,1)}, bf16[128,8,32]{0,2,1:T(8,128)(2,1)}, u32[]{:S(2)}, u32[]{:S(2)}) collective-permute-start(bf16[128,8,32]{0,2,1:T(8,128)(2,1)} %dynamic-slice_bitcast_fusion.2), channel_id=1, source_target_pairs={{0,1},{1,0},{2,3},{3,2},{4,5},{5,4},{6,7},{7,6},{8,9},{9,8},{10,11... | collective-permute-start | bytes 196616 | tf_op jit(solution)/shard_map/ppermute | solution.py:269
  42.3 10.9 %collective-permute-start.9 = (bf16[128,1024]{1,0:T(8,128)(2,1)}, bf16[128,1024]{1,0:T(8,128)(2,1)}, u32[]{:S(2)}, u32[]{:S(2)}) collective-permute-start(bf16[128,1024]{1,0:T(8,128)(2,1)} %get-tuple-element.20), channel_id=1, source_target_pairs={{0,1},{1,0},{2,3},{3,2},{4,5},{5,4},{6,7},{7,6},{8,9},{9,8},{10,11... | collective-permute-start | bytes 786440 | tf_op jit(solution)/shard_map/ppermute | solution.py:272
  47.1 8.0 %collective-permute-start.11 = (bf16[128,1024]{1,0:T(8,128)(2,1)}, bf16[128,1024]{1,0:T(8,128)(2,1)}, u32[]{:S(2)}, u32[]{:S(2)}) collective-permute-start(bf16[128,1024]{1,0:T(8,128)(2,1)} %get-tuple-element.22), channel_id=1, source_target_pairs={{0,1},{1,0},{2,3},{3,2},{4,5},{5,4},{6,7},{7,6},{8,9},{9,8},{10,11... | collective-permute-start | bytes 786440 | tf_op jit(solution)/shard_map/ppermute | solution.py:272
  48.8 10.1 %collective-permute-start.16 = (bf16[128,1024]{1,0:T(8,128)(2,1)}, bf16[128,1024]{1,0:T(8,128)(2,1)}, u32[]{:S(2)}, u32[]{:S(2)}) collective-permute-start(bf16[128,1024]{1,0:T(8,128)(2,1)} %get-tuple-element.26), channel_id=1, source_target_pairs={{0,1},{1,0},{2,3},{3,2},{4,5},{5,4},{6,7},{7,6},{8,9},{9,8},{10,11... | collective-permute-start | bytes 786440 | tf_op jit(solution)/shard_map/ppermute | solution.py:272
  48.9 2.1 %collective-permute-start.12 = (f32[1024]{0:T(1024)S(1)}, f32[1024]{0:T(1024)}, u32[]{:S(2)}, u32[]{:S(2)}) collective-permute-start(f32[1024]{0:T(1024)S(1)} %bitcast.160), channel_id=1, source_target_pairs={{0,1},{1,0},{2,3},{3,2},{4,5},{5,4},{6,7},{7,6},{8,9},{9,8},{10,11... | collective-permute-start | bytes 12296 | tf_op jit(solution)/shard_map/ppermute | solution.py:272
  51.1 1.7 %collective-permute-start.8 = (bf16[8,64,128]{2,1,0:T(8,128)(2,1)}, bf16[8,64,128]{2,1,0:T(8,128)(2,1)S(1)}, u32[]{:S(2)}, u32[]{:S(2)}) collective-permute-start(bf16[8,64,128]{2,1,0:T(8,128)(2,1)} %dynamic-slice_bitcast_fusion.1), channel_id=1, source_target_pairs={{0,1},{1,0},{2,3},{3,2},{4,5},{5,4},{6,7},{7,6},{8,9},{9,8},{10,11... | collective-permute-start | bytes 393224 | tf_op jit(solution)/shard_map/ppermute | solution.py:278
  52.7 1.9 %collective-permute-start.10 = (bf16[8,64,128]{2,1,0:T(8,128)(2,1)S(1)}, bf16[8,64,128]{2,1,0:T(8,128)(2,1)S(1)}, u32[]{:S(2)}, u32[]{:S(2)}) collective-permute-start(bf16[8,64,128]{2,1,0:T(8,128)(2,1)S(1)} %dynamic-slice_bitcast_fusion), channel_id=1, source_target_pairs={{0,1},{1,0},{2,3},{3,2},{4,5},{5,4},{6,7},{7,6},{8,9},{9,8},{10,11... | collective-permute-start | bytes 393224 | tf_op jit(solution)/shard_map/ppermute | solution.py:278
  53.2 5.4 %collective-permute-start.13 = (bf16[128,8,32]{0,2,1:T(8,128)(2,1)S(1)}, bf16[128,8,32]{0,2,1:T(8,128)(2,1)S(1)}, u32[]{:S(2)}, u32[]{:S(2)}) collective-permute-start(bf16[128,8,32]{0,2,1:T(8,128)(2,1)S(1)} %dynamic-slice_bitcast_fusion.3), channel_id=1, source_target_pairs={{0,1},{1,0},{2,3},{3,2},{4,5},{5,4},{6,7},{7,6},{8,9},{9,8},{10,11... | collective-permute-start | bytes 196616 | tf_op jit(solution)/shard_map/ppermute | solution.py:269
  54.7 4.0 %collective-permute-start.14 = (bf16[128,1024]{1,0:T(8,128)(2,1)S(1)}, bf16[128,1024]{1,0:T(8,128)(2,1)S(1)}, u32[]{:S(2)}, u32[]{:S(2)}) collective-permute-start(bf16[128,1024]{1,0:T(8,128)(2,1)S(1)} %copy-done.4), channel_id=1, source_target_pairs={{0,1},{1,0},{2,3},{3,2},{4,5},{5,4},{6,7},{7,6},{8,9},{9,8},{10,11... | collective-permute-start | bytes 786440 | tf_op jit(solution)/shard_map/ppermute | solution.py:272
  56.7 7.6 %collective-permute-start.24 = (f32[48,1024]{1,0:T(8,128)S(1)}, f32[48,1024]{1,0:T(8,128)S(1)}, u32[]{:S(2)}, u32[]{:S(2)}) collective-permute-start(f32[48,1024]{1,0:T(8,128)S(1)} %get-tuple-element.37), channel_id=1, source_target_pairs={{0,4},{1,5},{4,8},{5,9},{8,12},{9,13},{12,14},{13,15},{14,10},{15,... | collective-permute-start | bytes 589832 | tf_op jit(solution)/shard_map/ppermute | solution.py:192
  60.6 8.7 %collective-permute-start.17 = (f32[56,1024]{1,0:T(8,128)S(1)}, f32[56,1024]{1,0:T(8,128)S(1)}, u32[]{:S(2)}, u32[]{:S(2)}) collective-permute-start(f32[56,1024]{1,0:T(8,128)S(1)} %get-tuple-element.31), channel_id=1, source_target_pairs={{0,4},{1,5},{4,8},{5,9},{8,12},{9,13},{12,14},{13,15},{14,10},{15,... | collective-permute-start | bytes 688136 | tf_op jit(solution)/shard_map/ppermute | solution.py:192
  62.2 8.5 %collective-permute-start.20 = (f32[56,1024]{1,0:T(8,128)S(1)}, f32[56,1024]{1,0:T(8,128)S(1)}, u32[]{:S(2)}, u32[]{:S(2)}) collective-permute-start(f32[56,1024]{1,0:T(8,128)S(1)} %get-tuple-element.32), channel_id=1, source_target_pairs={{4,0},{5,1},{8,4},{9,5},{12,8},{13,9},{14,12},{15,13},{10,14},{11,... | collective-permute-start | bytes 688136 | tf_op jit(solution)/shard_map/ppermute | solution.py:198
  62.7 12.1 %collective-permute-start.28 = (f32[48,1024]{1,0:T(8,128)S(1)}, f32[48,1024]{1,0:T(8,128)S(1)}, u32[]{:S(2)}, u32[]{:S(2)}) collective-permute-start(f32[48,1024]{1,0:T(8,128)S(1)} %get-tuple-element.38), channel_id=1, source_target_pairs={{4,0},{5,1},{8,4},{9,5},{12,8},{13,9},{14,12},{15,13},{10,14},{11,... | collective-permute-start | bytes 589832 | tf_op jit(solution)/shard_map/ppermute | solution.py:198
  64.4 10.3 %collective-permute-start.25 = (f32[48,1024]{1,0:T(8,128)S(1)}, f32[48,1024]{1,0:T(8,128)S(1)}, u32[]{:S(2)}, u32[]{:S(2)}) collective-permute-start(f32[48,1024]{1,0:T(8,128)S(1)} %fusion.33), channel_id=1, source_target_pairs={{0,4},{1,5},{4,8},{5,9},{8,12},{9,13},{12,14},{13,15},{14,10},{15,... | collective-permute-start | bytes 589832 | tf_op jit(solution)/shard_map/ppermute | solution.py:192
  70.8 8.6 %collective-permute-start.18 = (f32[56,1024]{1,0:T(8,128)S(1)}, f32[56,1024]{1,0:T(8,128)S(1)}, u32[]{:S(2)}, u32[]{:S(2)}) collective-permute-start(f32[56,1024]{1,0:T(8,128)S(1)} %get-tuple-element.29), channel_id=1, source_target_pairs={{0,4},{1,5},{4,8},{5,9},{8,12},{9,13},{12,14},{13,15},{14,10},{15,... | collective-permute-start | bytes 688136 | tf_op jit(solution)/shard_map/ppermute | solution.py:192
  72.5 8.2 %collective-permute-start.21 = (f32[56,1024]{1,0:T(8,128)S(1)}, f32[56,1024]{1,0:T(8,128)S(1)}, u32[]{:S(2)}, u32[]{:S(2)}) collective-permute-start(f32[56,1024]{1,0:T(8,128)S(1)} %get-tuple-element.30), channel_id=1, source_target_pairs={{4,0},{5,1},{8,4},{9,5},{12,8},{13,9},{14,12},{15,13},{10,14},{11,... | collective-permute-start | bytes 688136 | tf_op jit(solution)/shard_map/ppermute | solution.py:198
  74.8 8.0 %collective-permute-start.26 = (f32[48,1024]{1,0:T(8,128)S(1)}, f32[48,1024]{1,0:T(8,128)S(1)}, u32[]{:S(2)}, u32[]{:S(2)}) collective-permute-start(f32[48,1024]{1,0:T(8,128)S(1)} %get-tuple-element.35), channel_id=1, source_target_pairs={{0,4},{1,5},{4,8},{5,9},{8,12},{9,13},{12,14},{13,15},{14,10},{15,... | collective-permute-start | bytes 589832 | tf_op jit(solution)/shard_map/ppermute | solution.py:192
  76.5 8.4 %collective-permute-start.29 = (f32[48,1024]{1,0:T(8,128)S(1)}, f32[48,1024]{1,0:T(8,128)S(1)}, u32[]{:S(2)}, u32[]{:S(2)}) collective-permute-start(f32[48,1024]{1,0:T(8,128)S(1)} %get-tuple-element.36), channel_id=1, source_target_pairs={{4,0},{5,1},{8,4},{9,5},{12,8},{13,9},{14,12},{15,13},{10,14},{11,... | collective-permute-start | bytes 589832 | tf_op jit(solution)/shard_map/ppermute | solution.py:198
  80.7 9.1 %collective-permute-start.22 = (f32[56,1024]{1,0:T(8,128)S(1)}, f32[56,1024]{1,0:T(8,128)S(1)}, u32[]{:S(2)}, u32[]{:S(2)}) collective-permute-start(f32[56,1024]{1,0:T(8,128)S(1)} %get-tuple-element.28), channel_id=1, source_target_pairs={{4,0},{5,1},{8,4},{9,5},{12,8},{13,9},{14,12},{15,13},{10,14},{11,... | collective-permute-start | bytes 688136 | tf_op jit(solution)/shard_map/ppermute | solution.py:198
  81.2 13.2 %collective-permute-start.19 = (f32[56,1024]{1,0:T(8,128)S(1)}, f32[56,1024]{1,0:T(8,128)S(1)}, u32[]{:S(2)}, u32[]{:S(2)}) collective-permute-start(f32[56,1024]{1,0:T(8,128)S(1)} %get-tuple-element.27), channel_id=1, source_target_pairs={{0,4},{1,5},{4,8},{5,9},{8,12},{9,13},{12,14},{13,15},{14,10},{15,... | collective-permute-start | bytes 688136 | tf_op jit(solution)/shard_map/ppermute | solution.py:192
  84.9 6.2 %collective-permute-start.27 = (f32[48,1024]{1,0:T(8,128)S(1)}, f32[48,1024]{1,0:T(8,128)S(1)}, u32[]{:S(2)}, u32[]{:S(2)}) collective-permute-start(f32[48,1024]{1,0:T(8,128)S(1)} %get-tuple-element.33), channel_id=1, source_target_pairs={{0,4},{1,5},{4,8},{5,9},{8,12},{9,13},{12,14},{13,15},{14,10},{15,... | collective-permute-start | bytes 589832 | tf_op jit(solution)/shard_map/ppermute | solution.py:192
  86.5 7.8 %collective-permute-start.30 = (f32[48,1024]{1,0:T(8,128)S(1)}, f32[48,1024]{1,0:T(8,128)S(1)}, u32[]{:S(2)}, u32[]{:S(2)}) collective-permute-start(f32[48,1024]{1,0:T(8,128)S(1)} %get-tuple-element.34), channel_id=1, source_target_pairs={{4,0},{5,1},{8,4},{9,5},{12,8},{13,9},{14,12},{15,13},{10,14},{11,... | collective-permute-start | bytes 589832 | tf_op jit(solution)/shard_map/ppermute | solution.py:198
  89.8 6.9 %collective-permute-start.23 = (f32[56,1024]{1,0:T(8,128)S(1)}, f32[56,1024]{1,0:T(8,128)S(1)}, u32[]{:S(2)}, u32[]{:S(2)}) collective-permute-start(f32[56,1024]{1,0:T(8,128)S(1)} %fusion.20), channel_id=1, source_target_pairs={{4,0},{5,1},{8,4},{9,5},{12,8},{13,9},{14,12},{15,13},{10,14},{11,... | collective-permute-start | bytes 688136 | tf_op jit(solution)/shard_map/ppermute | solution.py:198
  (10 other events, 63.6 us)
